TPU v7x, 32 devices: a whole 2x2x4 slice. The times are simulated.
32 devices in a mesh: seq: 16 (over z, y, x), fsdp: 2 (over core).
Axes of the slice: x: 2, y: 2, z: 4, core: 2. Of those that a mesh axis runs over, the one named last changes fastest.
Arguments:
- tokens: bfloat16 [12288, 4096], P('seq'), may hold values from -6 to 6
- norm_gain: float32 [4096], replicated, may hold values from 0.5 to 1.5
- w_zx: bfloat16 [4096, 2, 4096], P('seq', None, 'fsdp'), may hold values from -0.09375 to 0.09375
- w_bc: bfloat16 [4096, 2, 512], P('seq', None, 'fsdp'), may hold values from -0.09375 to 0.09375
- w_dt: bfloat16 [4096, 64], P('seq', 'fsdp'), may hold values from -0.09375 to 0.09375
- conv_x: bfloat16 [4, 4096], P(None, 'fsdp'), may hold values from -3 to 3
- conv_bc: bfloat16 [4, 2, 512], P(None, None, 'fsdp'), may hold values from -3 to 3
- dt_bias: float32 [64], P('fsdp'), may hold values from -4 to -1
- decay_rate: float32 [64], P('fsdp'), may hold values from 8.138021e-05 to 8
- d_skip: float32 [64], P('fsdp'), may hold values from 0.2 to 1
- gated_gain: float32 [4096], P('fsdp'), may hold values from 0.5 to 1.5
- w_out: bfloat16 [4096, 4096], P('fsdp', 'seq'), may hold values from -0.09375 to 0.09375
- prompt_lengths: int32 [8], replicated, may hold values from 1 to 3072, 12288 in all
- pack_order: int32 [8], replicated, may hold values from 0 to 7, each once
- resume_prompt: int32 [1], replicated, may hold values from 0 to 7
- carry_state: float32 [64, 64, 128], P('fsdp'), may hold values from -12 to 12
- carry_conv_x: bfloat16 [3, 4096], P(None, 'fsdp'), may hold values from -6 to 6
- carry_conv_bc: bfloat16 [3, 2, 512], P(None, None, 'fsdp'), may hold values from -6 to 6
Outputs:
- mixed: bfloat16 [12288, 4096], P(('seq', 'fsdp'))
Inputs may be any that keep to these rules, and one draw needn't show every extreme that they name: `prompt_lengths`: they sum to 12288; the longest prompt holds exactly 3072 tokens. `pack_order`: each prompt stands at one place.
All inputs are finite; a program needn't handle non-finite values.
Results may differ from a plain program's by a relative error of at most 0.008.
Values may be sent and summed in bfloat16 or wider, within the bound.
No kernel may reach another device: no remote copies, remote signals or barrier semaphores. Data moves between devices by JAX's collectives and lax.ppermute only.
A program may use at most 128 MiB of HBM per device.

v0:
```python
import jax
import jax.numpy as jnp
from jax import lax
from jax.sharding import PartitionSpec as P

SPAN = 256


EPS = 1e-05


def from_behind(value, axis, steps):
    count = lax.axis_size(axis)
    leading, last = (max(0, -steps), min(count, count - steps))
    return lax.ppermute(value, axis, [(source, source + steps) for source in range(leading, last)])


def product_of(form, left, right):
    if left.dtype == jnp.bfloat16 and right.dtype == jnp.bfloat16:
        return jnp.einsum(form, left, right, preferred_element_type=jnp.float32)
    return jnp.einsum(form, left, right.astype(jnp.float32), precision=lax.Precision.HIGHEST)


def norm_rows(values, row_gain):
    widened = values.astype(jnp.float32)
    factor = lax.rsqrt(jnp.mean(widened * widened, axis=-1, keepdims=True) + EPS)
    return (widened * factor * row_gain[None, :]).astype(jnp.bfloat16)


def layout(prompt_lengths, pack_order, resume_prompt, position):
    prompt_count = pack_order.shape[0]
    slot_ids = jnp.arange(prompt_count, dtype=jnp.int32)
    ordered = jnp.sum(
        jnp.where(pack_order[:, None] == slot_ids[None, :], prompt_lengths[None, :], 0), axis=1
    )
    seg_starts = jnp.cumsum(ordered, dtype=jnp.int32) - ordered
    reached = position[:, None] >= seg_starts[None, :]
    segment = jnp.sum(reached.astype(jnp.int32), axis=1) - 1
    seg_start = jnp.max(jnp.where(reached, seg_starts[None, :], 0), axis=1)
    resume_slot = jnp.sum(jnp.where(pack_order == resume_prompt[0], slot_ids, 0))
    resume_start = jnp.sum(jnp.where(slot_ids == resume_slot, seg_starts, 0))
    return (segment, seg_start, resume_slot, resume_start)


def conv_rows(
    source, prior_rows, weight, carry_rows, segment, seg_start, position, resume_slot, resume_start
):
    row_count = source.shape[0]
    edge_rows = prior_rows.shape[0]
    extended = jnp.concatenate([prior_rows, source], axis=0)
    resumed = (segment == resume_slot)[:, None]
    summed = jnp.zeros(source.shape, jnp.float32)
    for back_by in range(edge_rows + 1):
        shifted = extended[edge_rows - back_by : edge_rows - back_by + row_count].astype(
            jnp.float32
        )
        inside = (position - back_by >= seg_start)[:, None]
        carry_index = position - back_by - resume_start + edge_rows
        from_carry = jnp.zeros(source.shape, jnp.float32)
        for slot_id in range(edge_rows):
            from_carry = from_carry + jnp.where(
                (carry_index == slot_id)[:, None],
                carry_rows[slot_id].astype(jnp.float32)[None, :],
                0.0,
            )
        chosen = jnp.where(inside, shifted, jnp.where(resumed, from_carry, 0.0))
        summed = summed + chosen * weight[edge_rows - back_by].astype(jnp.float32)[None, :]
    return jax.nn.silu(summed).astype(jnp.bfloat16)


def span_pieces(
    x_blocks,
    b_blocks,
    c_blocks,
    dt_blocks,
    head_rate,
    segment,
    starting,
    resumed,
    resume_hit,
    carry_init,
    skip_gain,
):
    block_len = segment.shape[1]
    log_decay = -dt_blocks * head_rate[None, None]
    cumulative = jnp.cumsum(log_decay, axis=1)
    indices = jnp.arange(block_len, dtype=jnp.int32)
    causal = (indices[:, None] >= indices[None, :])[None] & (
        segment[:, :, None] == segment[:, None, :]
    )
    cum_rows = jnp.moveaxis(cumulative, 1, -1)
    log_gap = cum_rows[..., :, None] - cum_rows[..., None, :]
    within = causal[:, None, None]
    decays = jnp.where(within, jnp.exp(jnp.where(within, log_gap, 0.0)), 0.0)
    scores = product_of("cqgn,csgn->cgqs", c_blocks, b_blocks)
    dt_source = jnp.moveaxis(dt_blocks, 1, -1)[..., None, :]
    weights = (scores[:, :, None] * decays * dt_source).astype(jnp.bfloat16)
    direct = product_of("cghqs,csghp->cqghp", weights, x_blocks)
    cum_end = cumulative[:, -1]
    tail_mask = (segment == segment[:, -1:])[:, :, None, None]
    to_end = (
        jnp.where(tail_mask, jnp.exp(jnp.where(tail_mask, cum_end[:, None] - cumulative, 0.0)), 0.0)
        * dt_blocks
    )
    scaled = (x_blocks.astype(jnp.float32) * to_end[..., None]).astype(jnp.bfloat16)
    update = product_of("cqghp,cqgn->cghpn", scaled, b_blocks)
    opened = jnp.any(starting, axis=1)
    span_decay = jnp.where(opened[:, None, None], 0.0, jnp.exp(cum_end))
    hit_mask = resume_hit[:, :, None, None]
    has_hit = jnp.any(resume_hit, axis=1)[:, None, None, None]
    cum_hit = jnp.sum(jnp.where(hit_mask, cumulative - log_decay, 0.0), axis=1, keepdims=True)
    carry_mask = resumed[:, :, None, None] & has_hit
    carry_gain = jnp.where(
        carry_mask, jnp.exp(jnp.where(carry_mask, cumulative - cum_hit, 0.0)), 0.0
    )
    end_gain = carry_gain[:, -1]
    update = update + end_gain[..., None, None] * carry_init[None]
    direct = direct + carry_gain[..., None] * product_of("ghpn,cqgn->cqghp", carry_init, c_blocks)
    direct = direct + skip_gain[None, None, :, :, None] * x_blocks.astype(jnp.float32)
    unopened = jnp.cumsum(starting.astype(jnp.int32), axis=1, dtype=jnp.int32) == 0
    state_gain = jnp.where(unopened[:, :, None, None], jnp.exp(cumulative), 0.0)
    return (direct, state_gain, update, span_decay)


def body(
    tokens,
    norm_gain,
    w_zx,
    w_bc,
    w_dt,
    conv_x,
    conv_bc,
    dt_bias,
    decay_rate,
    d_skip,
    gated_gain,
    w_out,
    prompt_lengths,
    pack_order,
    resume_prompt,
    carry_state,
    carry_conv_x,
    carry_conv_bc,
):
    row_count = tokens.shape[0]
    edge_rows = conv_x.shape[0] - 1
    inner_local = w_zx.shape[2]
    state_cols = w_bc.shape[2]
    head_local = w_dt.shape[1]
    head_width = carry_state.shape[1]
    state_width = carry_state.shape[2]
    group_local = state_cols // state_width
    per_group = head_local // group_local
    span_count = row_count // SPAN
    position = lax.axis_index("seq") * row_count + jnp.arange(row_count, dtype=jnp.int32)
    segment, seg_start, resume_slot, resume_start = layout(
        prompt_lengths, pack_order, resume_prompt, position
    )
    normed = norm_rows(tokens, norm_gain)
    pieces = (
        lax.all_gather(w_zx, "seq", axis=0, tiled=True),
        lax.all_gather(w_bc, "seq", axis=0, tiled=True),
        lax.all_gather(w_dt, "seq", axis=0, tiled=True),
    )
    proj_zx = jnp.einsum("td,dkc->tkc", normed, pieces[0], preferred_element_type=jnp.float32)
    proj_bc = jnp.einsum("td,dkc->tkc", normed, pieces[1], preferred_element_type=jnp.float32)
    proj_dt = jnp.dot(normed, pieces[2], preferred_element_type=jnp.float32)
    proj_zx = proj_zx.astype(jnp.bfloat16)
    proj_bc = proj_bc.astype(jnp.bfloat16)
    proj_dt = proj_dt.astype(jnp.bfloat16)
    conv_in = jnp.concatenate([proj_zx[:, 1], proj_bc[:, 0], proj_bc[:, 1]], axis=1)
    prior_rows = from_behind(conv_in[row_count - edge_rows :], "seq", 1)
    weight = jnp.concatenate([conv_x, conv_bc[:, 0], conv_bc[:, 1]], axis=1)
    carry_rows = jnp.concatenate([carry_conv_x, carry_conv_bc[:, 0], carry_conv_bc[:, 1]], axis=1)
    conv_out = conv_rows(
        conv_in,
        prior_rows,
        weight,
        carry_rows,
        segment,
        seg_start,
        position,
        resume_slot,
        resume_start,
    )
    x_conv = conv_out[:, :inner_local].reshape(span_count, SPAN, group_local, per_group, head_width)
    b_conv = conv_out[:, inner_local : inner_local + state_cols].reshape(
        span_count, SPAN, group_local, state_width
    )
    c_conv = conv_out[:, inner_local + state_cols :].reshape(
        span_count, SPAN, group_local, state_width
    )
    dt_full = jax.nn.softplus(proj_dt.astype(jnp.float32) + dt_bias[None, :]).reshape(
        span_count, SPAN, group_local, per_group
    )
    seg_blocks = segment.reshape(span_count, SPAN)
    starting = (position == seg_start).reshape(span_count, SPAN)
    resumed = (segment == resume_slot).reshape(span_count, SPAN)
    resume_hit = (position == resume_start).reshape(span_count, SPAN)
    head_rate = decay_rate.reshape(group_local, per_group)
    skip_gain = d_skip.reshape(group_local, per_group)
    carry_init = carry_state.reshape(group_local, per_group, head_width, state_width)
    direct, state_gain, update, span_decay = span_pieces(
        x_conv,
        b_conv,
        c_conv,
        dt_full,
        head_rate,
        seg_blocks,
        starting,
        resumed,
        resume_hit,
        carry_init,
        skip_gain,
    )

    def fold_span(carried, pieces):
        return (
            (pieces[1][..., None, None] * carried[0] + pieces[0], pieces[1] * carried[1]),
            carried,
        )

    empty_state = jnp.zeros((group_local, per_group, head_width, state_width), jnp.float32)
    unit_decay = jnp.ones((group_local, per_group), jnp.float32)
    (local_state, local_decay), (prefix_state, prefix_decay) = lax.scan(
        fold_span, (empty_state, unit_decay), (update, span_decay)
    )
    hop_count = lax.axis_size("seq") // 4

    def hop_once(turn_id, carried):
        received = from_behind(carried[1], "seq", 1)
        return (received, local_decay[..., None, None] * received + local_state)

    incoming = lax.fori_loop(0, hop_count, hop_once, (empty_state, local_state))[0]
    entering = prefix_decay[..., None, None] * incoming[None] + prefix_state
    from_state = product_of("cghpn,cqgn->cqghp", entering, c_conv)
    ssd_out = (direct + state_gain[..., None] * from_state).reshape(row_count, inner_local)
    gate_act = jax.nn.silu(proj_zx[:, 0].astype(jnp.float32))
    gated = (ssd_out * gate_act).reshape(row_count, group_local, inner_local // group_local)
    factor = lax.rsqrt(jnp.mean(gated * gated, axis=-1, keepdims=True) + EPS)
    normed_y = ((gated * factor).reshape(row_count, inner_local) * gated_gain[None, :]).astype(
        jnp.bfloat16
    )
    partial_out = jnp.dot(
        normed_y,
        lax.all_gather(w_out, "seq", axis=1, tiled=True),
        preferred_element_type=jnp.float32,
    )
    return lax.psum_scatter(partial_out, "fsdp", scatter_dimension=0, tiled=True).astype(
        jnp.bfloat16
    )


def solution(mesh):
    return jax.shard_map(
        body,
        mesh=mesh,
        in_specs=(
            P("seq", None),
            P(),
            P("seq", None, "fsdp"),
            P("seq", None, "fsdp"),
            P("seq", "fsdp"),
            P(None, "fsdp"),
            P(None, None, "fsdp"),
            P("fsdp"),
            P("fsdp"),
            P("fsdp"),
            P("fsdp"),
            P("fsdp", "seq"),
            P(),
            P(),
            P(),
            P("fsdp", None, None),
            P(None, "fsdp"),
            P(None, None, "fsdp"),
        ),
        out_specs=P(("seq", "fsdp"), None),
        check_vma=False,
    )
```

profile of v0, /device:TPU:0, one launch (start us, length us, event | category | flops | bytes accessed | tf_op | source)
XLA Modules:
  0.0 896.3 jit_solution(3665538155999291183)
XLA Ops:
  6.5 1.8 copy.169
  8.5 3.8 copy.168
  12.4 0.7 all-gather.8.cloned.1.call-update
  14.8 1.3 fusion.97
  16.3 0.9 reduce-window.30
  17.6 44.2 %all_gather.14 = bf16[4096,32]{0,1:T(8,128)(2,1)S(1)} all-gather(bf16[256,32]{0,1:T(8,128)(2,1)S(1)} %copy-done.14), channel_id=1, replica_groups=mesh['seq'=16,'fsdp'=2] {'seq'}, dimensions={0}, use_global_device_ids=true | all-gather | bytes 278528 | tf_op jit(solution)/shard_map/all_gather | solution.py:163
  61.8 4.3 fusion.3
  66.3 4.9 compare_select_fusion
  71.6 3.6 reduce-window.21
  75.5 0.7 fusion.102
  76.6 0.7 fusion.75
  80.6 0.8 fusion.95
  82.5 0.7 compare_and_fusion.1
  83.2 0.9 compare_and_fusion
  84.6 16.8 %all-gather.6.cloned.1.call-done = bf16[4096,2,256]{0,2,1:T(8,128)(2,1)} async-done(((bf16[256,2,256]{0,2,1:T(8,128)(2,1)}), bf16[4096,2,256]{0,2,1:T(8,128)(2,1)}) %all-gather.6.cloned.1.call-update) | async-done | bytes 4194320 | tf_op jit(solution)/shard_map/all_gather | solution.py:162
  101.4 7.5 fusion.44
  108.9 344.2 %all-gather.4.cloned.1.call-done = bf16[4096,2,2048]{2,0,1:T(8,128)(2,1)} async-done(((bf16[256,2,2048]{2,0,1:T(8,128)(2,1)}), bf16[4096,2,2048]{2,0,1:T(8,128)(2,1)}) %all-gather.4.cloned.1.call-update) | async-done | bytes 33554448 | tf_op jit(solution)/shard_map/all_gather | solution.py:161
  453.2 32.0 %fusion.27 = bf16[768,2,2048]{2,0,1:T(8,128)(2,1)S(1)} fusion(bf16[4096,2,2048]{2,0,1:T(8,128)(2,1)} %all-gather.4.cloned.1.call-done, bf16[768,4096]{1,0:T(8,128)(2,1)} %param.22, f32[4096]{0:T(1024)S(1)} %copy-done.19, f32[768]{0:T(1024)S(1)} %add_rsqrt_fusion.1), kind=kOutput, calls=%fused_computation.44 | convolution fusion | flops 25785532416 | bytes 46156800 | tf_op jit(solution)/shard_map/td,dkc->tkc/dot_general | solution.py:165
  485.2 4.0 slice_convert_fusion
  489.8 1.8 copy-done.1
  491.9 3.3 collective-permute-start.1
  496.0 0.7 copy.182
  496.8 0.7 copy.187
  497.5 0.7 copy.179
  498.2 11.6 %reshape.326 = f32[3,256,2,16,64]{4,3,2,1,0:T(8,128)} reshape(f32[768,1,2048]{2,0,1:T(8,128)} %get-tuple-element.137) | data formatting | bytes 12582912 | tf_op jit(solution)/shard_map/convert_element_type | solution.py:238
  509.8 11.0 %copy.198 = f32[3,256,2,16,64]{1,4,3,2,0:T(8,128)} copy(f32[3,256,2,16,64]{4,3,2,1,0:T(8,128)} %reshape.326) | data formatting | bytes 12582912 | tf_op jit(solution)/shard_map/convert_element_type | solution.py:238
  520.8 3.3 maximum_maximum_fusion
  524.1 28.6 %multiply_convert_fusion.2 = bf16[768,2560]{1,0:T(8,128)(2,1)S(1)} fusion(bf16[771,2560]{1,0:T(8,128)(2,1)S(1)} %maximum_maximum_fusion, f32[2560]{0:T(1024)S(1)} %get-tuple-element.104, f32[2560]{0:T(1024)S(1)} %get-tuple-element.105, f32[2560]{0:T(1024)S(1)} %get-tuple-element.106, f32[2560]{0:T(1024)S(1)} %get-tuple-element.103, ...), kind=kLoop, calls=%fused_computation.23 | loop fusion | flops 96337920 | bytes 19745536 | tf_op jit(solution)/shard_map/convert_element_type | solution.py:68
  552.7 2.1 slice.142
  555.0 10.2 %reshape.325 = bf16[3,256,2,16,64]{4,3,2,1,0:T(8,128)(2,1)} reshape(bf16[768,2048]{1,0:T(8,128)(2,1)} %slice.142) | data formatting | bytes 6291456 | tf_op jit(solution)/shard_map/reshape | solution.py:186
  565.2 8.2 copy.180
  573.4 4.6 multiply_add_fusion.1
  578.0 7.9 while.32
  578.1 1.0 bitcast_dynamic-update-slice_fusion.6
  579.1 1.4 bitcast_add_fusion.3
  580.6 1.0 bitcast_dynamic-update-slice_fusion.6
  581.6 1.4 bitcast_add_fusion.3
  583.1 1.0 bitcast_dynamic-update-slice_fusion.6
  584.1 1.4 bitcast_add_fusion.3
  586.0 1.0 copy.277
  587.0 1.5 fusion.54
  588.5 5.3 fusion.58
  593.8 120.8 %while.31 = (s32[]{:T(128)}, f32[2,16,64,128]{3,2,1,0:T(8,128)}, f32[2,16,64,128]{3,2,1,0:T(8,128)S(1)}, f32[2,16]{1,0:T(2,128)S(1)}, f32[2,16,64,128]{3,2,1,0:T(8,128)S(1)}) while((s32[]{:T(128)}, f32[2,16,64,128]{3,2,1,0:T(8,128)}, f32[2,16,64,128]{3,2,1,0:T(8,128)S(1)}, f32[2,16]{1,0:T(2,128)S(1)}, ...), condition=%wide.region_17.18_spmd.clone, body=%wide.region_16.17_spmd.sunk.clone | while | flops 524290 | bytes 11534593 | solution.py:234
  593.8 3.5 collective-permute-start
  597.3 21.7 %collective-permute-done = f32[2,16,64,128]{3,2,1,0:T(8,128)S(1)} collective-permute-done((f32[2,16,64,128]{3,2,1,0:T(8,128)S(1)}, f32[2,16,64,128]{3,2,1,0:T(8,128)S(1)}, u32[]{:S(2)}, u32[]{:S(2)}) %collective-permute-start) | collective-permute-done | bytes 1048608 | tf_op jit(solution)/shard_map/while/body/eval_jaxpr/ppermute | solution.py:15
  619.2 0.8 copy-done
  620.0 4.4 collective-permute-start
  624.4 20.8 %collective-permute-done = f32[2,16,64,128]{3,2,1,0:T(8,128)S(1)} collective-permute-done((f32[2,16,64,128]{3,2,1,0:T(8,128)S(1)}, f32[2,16,64,128]{3,2,1,0:T(8,128)S(1)}, u32[]{:S(2)}, u32[]{:S(2)}) %collective-permute-start) | collective-permute-done | bytes 1048608 | tf_op jit(solution)/shard_map/while/body/eval_jaxpr/ppermute | solution.py:15
  645.5 0.8 copy-done
  646.3 4.4 collective-permute-start
  650.7 20.0 %collective-permute-done = f32[2,16,64,128]{3,2,1,0:T(8,128)S(1)} collective-permute-done((f32[2,16,64,128]{3,2,1,0:T(8,128)S(1)}, f32[2,16,64,128]{3,2,1,0:T(8,128)S(1)}, u32[]{:S(2)}, u32[]{:S(2)}) %collective-permute-start) | collective-permute-done | bytes 1048608 | tf_op jit(solution)/shard_map/while/body/eval_jaxpr/ppermute | solution.py:15
  670.9 0.8 copy-done
  671.7 23.0 %collective-permute-start = (f32[2,16,64,128]{3,2,1,0:T(8,128)S(1)}, f32[2,16,64,128]{3,2,1,0:T(8,128)S(1)}, u32[]{:S(2)}, u32[]{:S(2)}) collective-permute-start(f32[2,16,64,128]{3,2,1,0:T(8,128)S(1)} %get-tuple-element.311), channel_id=1, source_target_pairs={{0,2},{2,4},{4,6},{6,8},{8,10},{10,12},{12,14},{14,16},{16,18},{18... | collective-permute-start | bytes 3145736 | tf_op jit(solution)/shard_map/while/body/eval_jaxpr/ppermute | solution.py:15
  694.8 19.0 %collective-permute-done = f32[2,16,64,128]{3,2,1,0:T(8,128)S(1)} collective-permute-done((f32[2,16,64,128]{3,2,1,0:T(8,128)S(1)}, f32[2,16,64,128]{3,2,1,0:T(8,128)S(1)}, u32[]{:S(2)}, u32[]{:S(2)}) %collective-permute-start) | collective-permute-done | bytes 1048608 | tf_op jit(solution)/shard_map/while/body/eval_jaxpr/ppermute | solution.py:15
  713.9 0.8 copy-done
  714.7 5.0 fusion.36
  720.2 13.1 %multiply_reduce_fusion = (f32[3,256,2]{1,2,0:T(2,128)S(1)}, f32[3,256,2,16,64]{1,4,3,2,0:T(8,128)}) fusion(f32[3,256,2,16,64]{1,4,3,2,0:T(8,128)} %copy.198, f32[3,2,256,16,64]{2,4,3,1,0:T(8,128)S(1)} %fusion.36, f32[3,256,2,16]{1,3,2,0:T(8,128)S(1)} %copy-done.11, bf16[3,256,2,16,64]{1,4,3,2,0:T(8,128)(2,1)S(1)} %copy-done.4, f32[2,16]{1,0:T(2,128)S(1)} %mul.262, ...), kind=kOutput, calls=%fused_computation.42 | convolution fusion | flops 865073664 | bytes 30480512 | tf_op jit(solution)/shard_map/cghqs,csghp->cqghp/dot_general | solution.py:20
  733.3 12.6 %copy.212 = f32[3,256,2,16,64]{4,3,2,1,0:T(8,128)} copy(f32[3,256,2,16,64]{1,4,3,2,0:T(8,128)} %get-tuple-element.158) | data formatting | bytes 12582912 | tf_op jit(solution)/shard_map/reshape | solution.py:237
  745.9 11.9 %reshape.324 = f32[768,2048]{1,0:T(8,128)} reshape(f32[3,256,2,16,64]{4,3,2,1,0:T(8,128)} %copy.212) | data formatting | bytes 12582912 | tf_op jit(solution)/shard_map/reshape | solution.py:237
  758.0 1.7 mul.282
  759.8 5.7 copy.224
  765.5 24.8 %fusion.30 = f32[768,4096]{1,0:T(8,128)} fusion(bf16[2048,4096]{1,0:T(8,128)(2,1)} %all-gather.8.cloned.1.call-done, f32[768,2048]{1,0:T(8,128)} %bitcast.144, f32[768,2048]{1,0:T(8,128)} %reshape.324, f32[2048]{0:T(1024)S(1)} %copy-done.20, bf16[768,2,2048]{2,0,1:T(8,128)(2,1)} %copy-done.5), kind=kOutput, calls=%fused_computation.47 | convolution fusion | flops 12899057664 | bytes 45096960 | tf_op jit(solution)/shard_map/dot_general | solution.py:244
  790.4 94.3 %reduce-scatter.2.cloned.1.call-done = f32[384,4096]{1,0:T(8,128)} async-done(((f32[768,4096]{1,0:T(8,128)}), f32[384,4096]{1,0:T(8,128)}) %reduce-scatter.2.cloned.1.call-update) | async-done | bytes 6291472 | tf_op jit(solution)/shard_map/reduce_scatter | solution.py:249
  884.7 4.9 convert_element_type.116
  (142 shorter events, 11.2 us)
Async XLA Ops:
  6.5 7.2 copy-start.21
  6.5 7.2 copy-start.22
  6.5 11.0 %copy-start.14 = (bf16[256,32]{0,1:T(8,128)(2,1)S(1)}, bf16[256,32]{0,1:T(8,128)(2,1)}, u32[]{:S(2)}) copy-start(bf16[256,32]{0,1:T(8,128)(2,1)} %param.26) | copy-start | bytes 49156
  6.5 94.9 %all-gather.6.cloned.1.call-start = ((), (), s32[]{:S(2)}) async-start(), calls=%async_computation.2 | async-start | bytes 4456448 | tf_op jit(solution)/shard_map/all_gather | solution.py:162
  8.4 57.8 %copy-start.19 = (f32[4096]{0:T(1024)S(1)}, f32[4096]{0:T(1024)}, u32[]{:S(2)}) copy-start(f32[4096]{0:T(1024)} %param.23) | copy-start | bytes 49156
  8.4 57.8 %copy-start.23 = (f32[32]{0:T(128)S(1)}, f32[32]{0:T(128)}, u32[]{:S(2)}) copy-start(f32[32]{0:T(128)} %param.29) | copy-start | bytes 388
  8.4 444.7 %all-gather.4.cloned.1.call-start = ((), (), s32[]{:S(2)}) async-start(), calls=%async_computation.1 | async-start | bytes 35651584 | tf_op jit(solution)/shard_map/all_gather | solution.py:161
  12.3 753.2 %all-gather.8.cloned.1.call-start = ((), (), s32[]{:S(2)}) async-start(), calls=%async_computation.3 | async-start | bytes 17825792 | tf_op jit(solution)/shard_map/all_gather | solution.py:246
  13.0 871.7 %reduce-scatter.2.cloned.1.call-start = ((), (), s32[]{:S(2)}) async-start(), calls=%async_computation.4 | async-start | bytes 18874368 | tf_op jit(solution)/shard_map/reduce_scatter | solution.py:249
  66.2 5.1 copy-start.24
  66.2 15.3 %copy-start.18 = (bf16[3,2,256]{2,1,0:T(2,128)(2,1)S(1)}, bf16[3,2,256]{2,1,0:T(2,128)(2,1)}, u32[]{:S(2)}) copy-start(bf16[3,2,256]{2,1,0:T(2,128)(2,1)} %param.39) | copy-start | bytes 9220
  66.2 15.3 %copy-start.15 = (bf16[3,2048]{1,0:T(4,128)(2,1)S(1)}, bf16[3,2048]{1,0:T(4,128)(2,1)}, u32[]{:S(2)}) copy-start(bf16[3,2048]{1,0:T(4,128)(2,1)} %param.38) | copy-start | bytes 36868
  66.2 15.4 %copy-start.17 = (bf16[4,2,256]{2,1,0:T(2,128)(2,1)S(1)}, bf16[4,2,256]{2,1,0:T(2,128)(2,1)}, u32[]{:S(2)}) copy-start(bf16[4,2,256]{2,1,0:T(2,128)(2,1)} %param.28) | copy-start | bytes 12292
  66.2 15.4 %copy-start.16 = (bf16[4,2048]{1,0:T(4,128)(2,1)S(1)}, bf16[4,2048]{1,0:T(4,128)(2,1)}, u32[]{:S(2)}) copy-start(bf16[4,2048]{1,0:T(4,128)(2,1)} %param.27) | copy-start | bytes 49156
  485.2 4.6 copy-start.5
  489.8 1.8 copy-start.1
  489.8 8.4 copy-start.25
  491.9 28.9 %collective-permute-start.1 = (bf16[3,2560]{1,0:T(4,128)(2,1)S(1)}, bf16[3,2560]{1,0:T(4,128)(2,1)S(1)}, u32[]{:S(2)}, u32[]{:S(2)}) collective-permute-start(bf16[3,2560]{1,0:T(4,128)(2,1)S(1)} %slice.135), channel_id=1, source_target_pairs={{0,2},{2,4},{4,6},{6,8},{8,10},{10,12},{12,14},{14,16},{16,18},{18... | collective-permute-start | bytes 46088 | tf_op jit(solution)/shard_map/ppermute | solution.py:15
  520.8 3.3 copy-start.2
  565.2 8.2 copy-start.3
  588.5 5.3 copy-start.8
  593.8 25.2 %collective-permute-start = (f32[2,16,64,128]{3,2,1,0:T(8,128)S(1)}, f32[2,16,64,128]{3,2,1,0:T(8,128)S(1)}, u32[]{:S(2)}, u32[]{:S(2)}) collective-permute-start(f32[2,16,64,128]{3,2,1,0:T(8,128)S(1)} %get-tuple-element.311), channel_id=1, source_target_pairs={{0,2},{2,4},{4,6},{6,8},{8,10},{10,12},{12,14},{14,16},{16,18},{18... | collective-permute-start | bytes 3145736 | tf_op jit(solution)/shard_map/while/body/eval_jaxpr/ppermute | solution.py:15
  619.0 1.0 copy-start
  620.0 25.3 %collective-permute-start = (f32[2,16,64,128]{3,2,1,0:T(8,128)S(1)}, f32[2,16,64,128]{3,2,1,0:T(8,128)S(1)}, u32[]{:S(2)}, u32[]{:S(2)}) collective-permute-start(f32[2,16,64,128]{3,2,1,0:T(8,128)S(1)} %get-tuple-element.311), channel_id=1, source_target_pairs={{0,2},{2,4},{4,6},{6,8},{8,10},{10,12},{12,14},{14,16},{16,18},{18... | collective-permute-start | bytes 3145736 | tf_op jit(solution)/shard_map/while/body/eval_jaxpr/ppermute | solution.py:15
  645.3 1.0 copy-start
  646.3 24.5 %collective-permute-start = (f32[2,16,64,128]{3,2,1,0:T(8,128)S(1)}, f32[2,16,64,128]{3,2,1,0:T(8,128)S(1)}, u32[]{:S(2)}, u32[]{:S(2)}) collective-permute-start(f32[2,16,64,128]{3,2,1,0:T(8,128)S(1)} %get-tuple-element.311), channel_id=1, source_target_pairs={{0,2},{2,4},{4,6},{6,8},{8,10},{10,12},{12,14},{14,16},{16,18},{18... | collective-permute-start | bytes 3145736 | tf_op jit(solution)/shard_map/while/body/eval_jaxpr/ppermute | solution.py:15
  670.7 1.0 copy-start
  671.7 42.0 %collective-permute-start = (f32[2,16,64,128]{3,2,1,0:T(8,128)S(1)}, f32[2,16,64,128]{3,2,1,0:T(8,128)S(1)}, u32[]{:S(2)}, u32[]{:S(2)}) collective-permute-start(f32[2,16,64,128]{3,2,1,0:T(8,128)S(1)} %get-tuple-element.311), channel_id=1, source_target_pairs={{0,2},{2,4},{4,6},{6,8},{8,10},{10,12},{12,14},{14,16},{16,18},{18... | collective-permute-start | bytes 3145736 | tf_op jit(solution)/shard_map/while/body/eval_jaxpr/ppermute | solution.py:15
  713.7 1.0 copy-start
  714.7 5.0 copy-start.4
  714.7 5.1 copy-start.6
  714.7 5.4 copy-start.7
  714.7 5.4 copy-start.9
  714.7 5.4 copy-start.10
  714.7 5.4 copy-start.11
  714.7 5.4 copy-start.12
  714.7 5.4 copy-start.13
  759.7 5.8 copy-start.20
Sparse Core Ops, SparseCore 0:
  10.1 91.2 all-gather.5
  104.2 348.9 all-gather.3
  455.9 233.4 all-gather.7
  790.5 94.1 reduce-scatter.1
where the time goes:
time: 902 us; the launch traced here: 896 us
  waiting for transfers between devices  538 us (60%)
  matrix products  98.9 us (11%)
  local copies, waits for them, and re-layouts  91.8 us (10%)
  other arithmetic  69.9 us (8%)
  blocking collectives  44.2 us (5%)
  starting transfers between devices  38.9 us (4%)
  between operations  14.6 us (2%)
    all_gather x1, waiting for transfers between devices, body(): lax.all_gather(w_zx, 'seq', axis=0, tiled=True)  344 us
    reduce_scatter x1, waiting for transfers between devices, body(): lax.psum_scatter(partial_out, 'fsdp', scatter_dimension=0, tiled=True)  94.3 us
    ppermute x5, waiting for transfers between devices, from_behind(): lax.ppermute(value, axis, [(source, source + steps) for source in range(l...  81.5 us
    all_gather x1, blocking collectives, body(): lax.all_gather(w_dt, 'seq', axis=0, tiled=True)  44.2 us
    ppermute x5, starting transfers between devices, from_behind(): lax.ppermute(value, axis, [(source, source + steps) for source in range(l...  38.7 us
    dot_general x1, matrix products, body(): jnp.einsum('td,dkc->tkc', normed, pieces[0], preferred_element_type=jnp.f...  32 us
    convert_element_type x1, other arithmetic, conv_rows(): return jax.nn.silu(summed).astype(jnp.bfloat16)  28.6 us
    dot_general x1, matrix products, body(): jnp.dot(normed_y, lax.all_gather(w_out, 'seq', axis=1, tiled=True), prefe...  24.8 us
  transfers between devices with their start and end apart: 9, of which 7 were waited for; matrix products, arithmetic and copies ran while one was open for 25% of the time, Pallas kernels for 0%

commit v1 on v0

--- a/solution.py
+++ b/solution.py
@@ -157,18 +157,20 @@
         prompt_lengths, pack_order, resume_prompt, position
     )
     normed = norm_rows(tokens, norm_gain)
-    pieces = (
-        lax.all_gather(w_zx, "seq", axis=0, tiled=True),
-        lax.all_gather(w_bc, "seq", axis=0, tiled=True),
-        lax.all_gather(w_dt, "seq", axis=0, tiled=True),
-    )
-    proj_zx = jnp.einsum("td,dkc->tkc", normed, pieces[0], preferred_element_type=jnp.float32)
-    proj_bc = jnp.einsum("td,dkc->tkc", normed, pieces[1], preferred_element_type=jnp.float32)
-    proj_dt = jnp.dot(normed, pieces[2], preferred_element_type=jnp.float32)
-    proj_zx = proj_zx.astype(jnp.bfloat16)
-    proj_bc = proj_bc.astype(jnp.bfloat16)
-    proj_dt = proj_dt.astype(jnp.bfloat16)
-    conv_in = jnp.concatenate([proj_zx[:, 1], proj_bc[:, 0], proj_bc[:, 1]], axis=1)
+    first_local = jnp.concatenate(
+        [w_zx[:, 1], w_bc.reshape(w_bc.shape[0], 2 * state_cols), w_dt], axis=1
+    )
+    first_full = lax.all_gather(first_local, "seq", axis=0, tiled=True)
+    proj_first = jnp.dot(normed, first_full, preferred_element_type=jnp.float32).astype(
+        jnp.bfloat16
+    )
+    conv_width = inner_local + 2 * state_cols
+    conv_in = proj_first[:, :conv_width]
+    proj_dt = proj_first[:, conv_width:]
+    z_local, out_local, _ = lax.optimization_barrier((w_zx[:, 0], w_out, proj_first))
+    z_full = lax.all_gather(z_local, "seq", axis=0, tiled=True)
+    out_full = lax.all_gather(out_local, "seq", axis=1, tiled=True)
+    proj_z = jnp.dot(normed, z_full, preferred_element_type=jnp.float32).astype(jnp.bfloat16)
     prior_rows = from_behind(conv_in[row_count - edge_rows :], "seq", 1)
     weight = jnp.concatenate([conv_x, conv_bc[:, 0], conv_bc[:, 1]], axis=1)
     carry_rows = jnp.concatenate([carry_conv_x, carry_conv_bc[:, 0], carry_conv_bc[:, 1]], axis=1)
@@ -226,29 +228,34 @@
         fold_span, (empty_state, unit_decay), (update, span_decay)
     )
     hop_count = lax.axis_size("seq") // 4
-
-    def hop_once(turn_id, carried):
-        received = from_behind(carried[1], "seq", 1)
-        return (received, local_decay[..., None, None] * received + local_state)
-
-    incoming = lax.fori_loop(0, hop_count, hop_once, (empty_state, local_state))[0]
+    incoming = jnp.zeros_like(local_state)
+    reach = jnp.ones_like(local_decay)
+    for steps in range(1, hop_count + 1):
+        state_back, decay_back = from_behind((local_state, local_decay), "seq", steps)
+        incoming = incoming + reach[..., None, None] * state_back
+        reach = reach * decay_back
     entering = prefix_decay[..., None, None] * incoming[None] + prefix_state
     from_state = product_of("cghpn,cqgn->cqghp", entering, c_conv)
     ssd_out = (direct + state_gain[..., None] * from_state).reshape(row_count, inner_local)
-    gate_act = jax.nn.silu(proj_zx[:, 0].astype(jnp.float32))
+    gate_act = jax.nn.silu(proj_z.astype(jnp.float32))
     gated = (ssd_out * gate_act).reshape(row_count, group_local, inner_local // group_local)
     factor = lax.rsqrt(jnp.mean(gated * gated, axis=-1, keepdims=True) + EPS)
     normed_y = ((gated * factor).reshape(row_count, inner_local) * gated_gain[None, :]).astype(
         jnp.bfloat16
     )
-    partial_out = jnp.dot(
-        normed_y,
-        lax.all_gather(w_out, "seq", axis=1, tiled=True),
-        preferred_element_type=jnp.float32,
-    )
-    return lax.psum_scatter(partial_out, "fsdp", scatter_dimension=0, tiled=True).astype(
-        jnp.bfloat16
-    )
+    core_count = lax.axis_size("fsdp")
+    piece = row_count // core_count
+    core = lax.axis_index("fsdp")
+    total = None
+    for shift in list(range(1, core_count)) + [0]:
+        rows = lax.dynamic_slice_in_dim(normed_y, (core + shift) % core_count * piece, piece, 0)
+        part = jnp.dot(rows, out_full, preferred_element_type=jnp.float32)
+        if shift:
+            part = lax.ppermute(
+                part, "fsdp", [(j, (j + shift) % core_count) for j in range(core_count)]
+            )
+        total = part if total is None else total + part
+    return total.astype(jnp.bfloat16)
 
 
 def solution(mesh):

time: 902 us -> 843 us (0.935)
  blocking collectives: 44.2 us -> 0 us
  local copies, waits for them, and re-layouts: 91.8 us -> 70.9 us
  waiting for transfers between devices: 538 us -> 558 us
  starting transfers between devices: 38.9 us -> 25.6 us
    all_gather x3, waiting for transfers between devices: 361 us -> 492 us  [the longest x1 238 us: body(): first_full = lax.all_gather(first_local, 'seq', axis=0, tiled=True)]
    reduce_scatter x1 -> x0, waiting for transfers between devices: 94.3 us -> none  [body(): lax.psum_scatter(partial_out, 'fsdp', scatter_dimension=0, tiled=True)]
    all_gather x1 -> x0, blocking collectives: 44.2 us -> none  [body(): lax.all_gather(w_dt, 'seq', axis=0, tiled=True)]
    ppermute x5 -> x8, waiting for transfers between devices: 81.5 us -> 54.9 us  [from_behind(): lax.ppermute(value, axis, [(source, source + steps) for source in range(l...]
    convert_element_type x2 -> x0, local copies, waits for them, and re-layouts: 22.6 us -> none  [body(): gate_act = jax.nn.silu(proj_zx[:, 0].astype(jnp.float32))]
    ppermute x5 -> x8, starting transfers between devices: 38.7 us -> 25 us  [from_behind(): lax.ppermute(value, axis, [(source, source + steps) for source in range(l...]
    slice x2 -> x6, local copies, waits for them, and re-layouts: 0.23 us -> 12.2 us  [the longest x1 5.61 us: body(): w_zx[:, 1]]
    ppermute x0 -> x1, waiting for transfers between devices: none -> 10.5 us  [body(): lax.ppermute(part, 'fsdp', [(j, (j + shift) % core_count) for j in range(...]
  transfers between devices with their start and end apart: 9 -> 12, of which waited for: 7 -> 5; matrix products, arithmetic and copies ran while one was open for 25% -> 21% of each run, Pallas kernels for 0% -> 0%
where the time goes in v1:
time: 843 us; the launch traced here: 833 us
  waiting for transfers between devices  558 us (66%)
  matrix products  101 us (12%)
  local copies, waits for them, and re-layouts  70.9 us (8%)
  other arithmetic  62.7 us (7%)
  starting transfers between devices  25.6 us (3%)
  between operations  15 us (2%)
    all_gather x1, waiting for transfers between devices, body(): first_full = lax.all_gather(first_local, 'seq', axis=0, tiled=True)  238 us
    all_gather x1, waiting for transfers between devices, body(): out_full = lax.all_gather(out_local, 'seq', axis=1, tiled=True)  231 us
    ppermute x8, waiting for transfers between devices, from_behind(): lax.ppermute(value, axis, [(source, source + steps) for source in range(l...  54.9 us
    dot_general x2, matrix products, body(): part = jnp.dot(rows, out_full, preferred_element_type=jnp.float32)  25.3 us
    dot_general x1, matrix products, body(): jnp.dot(normed, first_full, preferred_element_type=jnp.float32)  25.1 us
    ppermute x8, starting transfers between devices, from_behind(): lax.ppermute(value, axis, [(source, source + steps) for source in range(l...  25 us
    reshape x2, local copies, waits for them, and re-layouts, body(): (direct + state_gain[..., None] * from_state).reshape(row_count, inner_lo...  24.6 us
    dot_general x1, matrix products, body(): jnp.dot(normed, z_full, preferred_element_type=jnp.float32)  23.1 us
  transfers between devices with their start and end apart: 12, of which 5 were waited for; matrix products, arithmetic and copies ran while one was open for 21% of the time, Pallas kernels for 0%

profile of v1, /device:TPU:0, one launch (start us, length us, event | category | flops | bytes accessed | tf_op | source)
XLA Modules:
  0.0 833.2 jit_solution(15518981495876531560)
XLA Ops:
  6.5 5.6 fusion.98
  12.2 0.6 copy.288
  13.0 1.2 pad_maximum_fusion.1
  14.2 1.6 copy.287
  15.8 4.1 fusion.3
  20.0 238.4 %all-gather.4.cloned.1.call-done = bf16[4096,2592]{1,0:T(8,128)(2,1)} async-done(((bf16[256,2592]{1,0:T(8,128)(2,1)}), bf16[4096,2592]{1,0:T(8,128)(2,1)}) %all-gather.4.cloned.1.call-update) | async-done | bytes 21233680 | tf_op jit(solution)/shard_map/all_gather | solution.py:163
  258.4 25.1 %convolution_convert_fusion = bf16[768,2592]{0,1:T(8,128)(2,1)} fusion(bf16[4096,2592]{1,0:T(8,128)(2,1)} %all-gather.4.cloned.1.call-done, bf16[768,4096]{1,0:T(8,128)(2,1)} %param.20, f32[4096]{0:T(1024)S(1)} %copy-done.12, f32[768]{0:T(1024)S(1)} %add_rsqrt_fusion.1), kind=kOutput, calls=%fused_computation.39 | convolution fusion | flops 16322027520 | bytes 31525888 | tf_op jit(solution)/shard_map/dot_general | solution.py:164
  285.3 0.6 fusion.88
  285.9 1.2 fusion.89
  287.3 0.9 reduce-window.30
  288.8 0.8 fusion.67
  289.5 0.7 fusion.72
  290.2 0.7 fusion.74
  290.9 0.7 fusion.77
  291.6 0.7 fusion.80
  292.2 0.7 fusion.82
  292.9 0.7 fusion.85
  294.2 0.6 broadcast_compare_fusion
  295.4 0.9 compare_and_fusion
  296.3 1.3 slice.134
  297.9 3.4 collective-permute-start
  301.3 0.9 compare_select_fusion
  302.5 3.4 reduce-window.21
  306.2 0.7 copy_bitcast_fusion.3
  307.9 4.2 slice.129
  312.4 0.7 copy.203
  313.5 20.7 %multiply_convert_fusion.2 = bf16[768,2560]{0,1:T(8,128)(2,1)S(1)} fusion(bf16[768,2560]{0,1:T(8,128)(2,1)} %slice.129, bf16[3,2560]{0,1:T(8,128)(2,1)S(1)} %copy.193, f32[2560]{0:T(1024)S(1)} %get-tuple-element.81, f32[2560]{0:T(1024)S(1)} %get-tuple-element.82, f32[2560]{0:T(1024)S(1)} %get-tuple-element.83, f32[2560]{0:T(1024)S(1)} %get-tuple-element.80, ...), kind=kLoop, calls=%fused_computation.24 | loop fusion | flops 104202240 | bytes 7964416 | tf_op jit(solution)/shard_map/convert_element_type | solution.py:68
  334.2 1.8 copy-done.2
  336.0 1.9 slice.142
  337.9 9.5 %reshape.289 = bf16[3,256,2,16,64]{1,0,4,3,2:T(4,128)(2,1)} reshape(bf16[768,2048]{0,1:T(8,128)(2,1)} %slice.142) | data formatting | bytes 6291456 | tf_op jit(solution)/shard_map/reshape | solution.py:188
  347.3 1.9 fusion.97
  349.5 4.9 multiply_add_fusion
  354.4 7.8 while.18
  354.4 1.1 bitcast_dynamic-update-slice_fusion.6
  355.6 1.5 bitcast_add_fusion.3
  357.1 1.1 bitcast_dynamic-update-slice_fusion.6
  358.2 1.4 bitcast_add_fusion.3
  359.7 1.1 bitcast_dynamic-update-slice_fusion.6
  360.8 1.4 bitcast_add_fusion.3
  362.2 3.3 collective-permute-start.2
  365.5 1.5 collective-permute-start.4
  367.1 4.4 collective-permute-start.1
  371.5 2.5 collective-permute-start.3
  374.0 6.2 collective-permute-start.5
  380.8 1.4 collective-permute-start.7
  382.2 11.0 %fusion.2 = f32[3,2,16,64,256]{4,3,2,1,0:T(8,128)S(1)} fusion(f32[3,2,16,256]{3,2,1,0:T(8,128)} %copy.203, f32[3,2,16,256]{3,2,1,0:T(8,128)} %get-tuple-element.113, f32[3,2,256,256]{3,2,1,0:T(8,128)S(1)} %fusion.46, pred[3,256,256]{2,1,0:T(8,128)(4,1)} %compare_and_fusion, bf16[3,256,2,16,64]{1,0,4,3,2:T(4,128)(2,1)} %reshape.289), kind=kOutput, calls=%fused_computation.10 | convolution fusion | flops 843055104 | bytes 11403264 | tf_op jit(solution)/shard_map/cghqs,csghp->cqghp/dot_general | solution.py:20
  393.3 2.3 collective-permute-start.6
  395.6 2.7 fusion.50
  398.3 54.9 %collective-permute-done.6 = f32[2,16]{1,0:T(2,128)S(1)} collective-permute-done((f32[2,16]{1,0:T(2,128)S(1)}, f32[2,16]{1,0:T(2,128)S(1)}, u32[]{:S(2)}, u32[]{:S(2)}) %collective-permute-start.6) | collective-permute-done | bytes 160 | tf_op jit(solution)/shard_map/ppermute | solution.py:15
  453.2 2.2 multiply_add_fusion.1
  455.4 8.9 %fusion.13 = f32[3,256,2,16,64]{1,4,3,2,0:T(8,128)} fusion(f32[2,3,256,16,64]{2,4,3,0,1:T(8,128)S(1)} %fusion.50, f32[3,2,16,64,256]{4,3,2,1,0:T(8,128)S(1)} %fusion.2, f32[3,256,2,16]{1,3,2,0:T(8,128)S(1)} %copy.211, f32[2,16]{1,0:T(2,128)S(1)} %mul.282, f32[3,256,2,16]{1,3,2,0:T(8,128)S(1)} %copy.206, f32[3,2,16,64,128]{4,3,2,1,0:T(8,128)} %get-tuple-element.50, ...), kind=kOutput, calls=%fused_computation.26 | convolution fusion | flops 2428502016 | bytes 26804736 | tf_op jit(solution)/shard_map/cghpn,cqgn->cqghp/dot_general | solution.py:21
  464.4 12.8 %copy.234 = f32[3,256,2,16,64]{4,3,2,1,0:T(8,128)} copy(f32[3,256,2,16,64]{1,4,3,2,0:T(8,128)} %fusion.13) | data formatting | bytes 12582912 | tf_op jit(solution)/shard_map/reshape | solution.py:239
  477.2 11.8 %reshape.310 = f32[768,2048]{1,0:T(8,128)} reshape(f32[3,256,2,16,64]{4,3,2,1,0:T(8,128)} %copy.234) | data formatting | bytes 12582912 | tf_op jit(solution)/shard_map/reshape | solution.py:239
  489.0 23.0 %all-gather.6.cloned.1.call-done = bf16[4096,2048]{1,0:T(8,128)(2,1)} async-done(((bf16[256,2048]{1,0:T(8,128)(2,1)}), bf16[4096,2048]{1,0:T(8,128)(2,1)}) %all-gather.6.cloned.1.call-update) | async-done | bytes 16777232 | tf_op jit(solution)/shard_map/all_gather | solution.py:171
  511.9 23.1 %fusion.101 = (f32[768,2048]{1,0:T(8,128)}, f32[768,2048]{1,0:T(8,128)}) fusion(f32[768,2048]{1,0:T(8,128)} %reshape.310, bf16[4096,2048]{1,0:T(8,128)(2,1)} %all-gather.6.cloned.1.call-done, bf16[768,4096]{1,0:T(8,128)(2,1)} %param.20, f32[4096]{0:T(1024)S(1)} %copy-done.12, f32[768]{0:T(1024)S(1)} %add_rsqrt_fusion.1), kind=kOutput, calls=%fused_computation.170 | convolution fusion | flops 12910067712 | bytes 41962496 | tf_op jit(solution)/shard_map/dot_general | solution.py:173
  535.0 9.4 %mul.308 = f32[768,2,1024]{2,1,0:T(2,128)} reshape(f32[768,2048]{1,0:T(8,128)} %get-tuple-element.124) | data formatting | bytes 12582912 | tf_op jit(solution)/shard_map/mul | solution.py:242
  544.4 4.5 reduce_sum.69
  549.0 1.7 mul.309
  550.7 3.0 copy.245
  553.7 6.0 multiply_convert_fusion.3
  559.7 230.7 %all-gather.8.cloned.1.call-done = bf16[2048,4096]{1,0:T(8,128)(2,1)} async-done(((bf16[2048,256]{1,0:T(8,128)(2,1)}), bf16[2048,4096]{1,0:T(8,128)(2,1)}) %all-gather.8.cloned.1.call-update) | async-done | bytes 16777232 | tf_op jit(solution)/shard_map/all_gather | solution.py:172
  790.5 12.3 %fusion.35 = f32[384,4096]{1,0:T(8,128)} fusion(bf16[2048,4096]{1,0:T(8,128)(2,1)} %all-gather.8.cloned.1.call-done, bf16[768,2048]{1,0:T(8,128)(2,1)} %multiply_convert_fusion.3, s32[]{:T(128)S(6)} %select_n.164), kind=kOutput, calls=%fused_computation.53 | convolution fusion | flops 6442450944 | bytes 24641540 | tf_op jit(solution)/shard_map/dot_general | solution.py:252
  802.7 10.5 %collective-permute-done.8 = f32[384,4096]{1,0:T(8,128)} collective-permute-done((f32[384,4096]{1,0:T(8,128)}, f32[384,4096]{1,0:T(8,128)}, u32[]{:S(2)}, u32[]{:S(2)}) %collective-permute-start.8) | collective-permute-done | bytes 6291488 | tf_op jit(solution)/shard_map/ppermute | solution.py:254
  813.2 13.0 %add_convert_fusion = bf16[384,4096]{1,0:T(8,128)(2,1)} fusion(f32[384,4096]{1,0:T(8,128)} %collective-permute-done.8, bf16[2048,4096]{1,0:T(8,128)(2,1)} %all-gather.8.cloned.1.call-done, bf16[768,2048]{1,0:T(8,128)(2,1)} %multiply_convert_fusion.3, s32[]{:T(128)S(6)} %select_n.166), kind=kOutput, calls=%fused_computation.35 | convolution fusion | flops 6445596672 | bytes 27787268 | tf_op jit(solution)/shard_map/dot_general | solution.py:252
  (120 shorter events, 6.7 us)
Async XLA Ops:
  6.5 6.3 copy-start.5
  6.5 251.9 %all-gather.4.cloned.1.call-start = ((), (), s32[]{:S(2)}) async-start(), calls=%async_computation | async-start | bytes 23396352 | tf_op jit(solution)/shard_map/all_gather | solution.py:163
  6.5 6.2 copy-start.4
  12.9 245.5 %copy-start.12 = (f32[4096]{0:T(1024)S(1)}, f32[4096]{0:T(1024)}, u32[]{:S(2)}) copy-start(f32[4096]{0:T(1024)} %param.21) | copy-start | bytes 49156
  14.2 497.8 %all-gather.6.cloned.1.call-start = ((), (), s32[]{:S(2)}) async-start(), calls=%async_computation.1 | async-start | bytes 17825792 | tf_op jit(solution)/shard_map/all_gather | solution.py:171
  19.9 265.0 %copy-start.13 = (s32[8]{0:T(128)S(1)}, s32[8]{0:T(128)}, u32[]{:S(2)}) copy-start(s32[8]{0:T(128)} %param.32) | copy-start | bytes 100
  19.9 265.0 %copy-start.14 = (s32[8]{0:T(128)S(1)}, s32[8]{0:T(128)}, u32[]{:S(2)}) copy-start(s32[8]{0:T(128)} %param.33) | copy-start | bytes 100
  19.9 268.7 %copy-start.15 = (f32[32]{0:T(128)S(1)}, f32[32]{0:T(128)}, u32[]{:S(2)}) copy-start(f32[32]{0:T(128)} %param.28) | copy-start | bytes 388
  19.9 268.8 %copy-start.16 = (f32[32]{0:T(128)S(1)}, f32[32]{0:T(128)}, u32[]{:S(2)}) copy-start(f32[32]{0:T(128)} %param.29) | copy-start | bytes 388
  19.9 273.9 %copy-start.9 = (bf16[3,2,256]{2,1,0:T(2,128)(2,1)S(1)}, bf16[3,2,256]{2,1,0:T(2,128)(2,1)}, u32[]{:S(2)}) copy-start(bf16[3,2,256]{2,1,0:T(2,128)(2,1)} %param.37) | copy-start | bytes 9220
  19.9 274.0 %copy-start.6 = (bf16[3,2048]{1,0:T(4,128)(2,1)S(1)}, bf16[3,2048]{1,0:T(4,128)(2,1)}, u32[]{:S(2)}) copy-start(bf16[3,2048]{1,0:T(4,128)(2,1)} %param.36) | copy-start | bytes 36868
  20.0 274.1 %copy-start.8 = (bf16[4,2,256]{2,1,0:T(2,128)(2,1)S(1)}, bf16[4,2,256]{2,1,0:T(2,128)(2,1)}, u32[]{:S(2)}) copy-start(bf16[4,2,256]{2,1,0:T(2,128)(2,1)} %param.26) | copy-start | bytes 12292
  20.0 274.1 %copy-start.7 = (bf16[4,2048]{1,0:T(4,128)(2,1)S(1)}, bf16[4,2048]{1,0:T(4,128)(2,1)}, u32[]{:S(2)}) copy-start(bf16[4,2048]{1,0:T(4,128)(2,1)} %param.25) | copy-start | bytes 49156
  20.0 281.3 %copy-start.11 = (f32[32]{0:T(128)S(1)}, f32[32]{0:T(128)}, u32[]{:S(2)}) copy-start(f32[32]{0:T(128)} %param.27) | copy-start | bytes 388
  283.5 507.0 %all-gather.8.cloned.1.call-start = ((), (), s32[]{:S(2)}) async-start(), calls=%async_computation.2 | async-start | bytes 17825792 | tf_op jit(solution)/shard_map/all_gather | solution.py:172
  297.9 15.2 %collective-permute-start = (bf16[3,2560]{1,0:T(4,128)(2,1)S(1)}, bf16[3,2560]{1,0:T(4,128)(2,1)S(1)}, u32[]{:S(2)}, u32[]{:S(2)}) collective-permute-start(bf16[3,2560]{1,0:T(4,128)(2,1)S(1)} %copy.192), channel_id=1, source_target_pairs={{0,2},{2,4},{4,6},{6,8},{8,10},{10,12},{12,14},{14,16},{16,18},{18... | collective-permute-start | bytes 46088 | tf_op jit(solution)/shard_map/ppermute | solution.py:15
  334.2 1.8 copy-start.2
  337.9 11.7 %copy-start.1 = (f32[32,64,128]{2,1,0:T(8,128)S(1)}, f32[32,64,128]{2,1,0:T(8,128)}, u32[]{:S(2)}) copy-start(f32[32,64,128]{2,1,0:T(8,128)} %param.35) | copy-start | bytes 3145732
  354.4 25.7 %copy-start.3 = (bf16[768,256]{0,1:T(8,128)(2,1)S(1)}, bf16[768,256]{0,1:T(8,128)(2,1)}, u32[]{:S(2)}) copy-start(bf16[768,256]{0,1:T(8,128)(2,1)} %get-tuple-element.107) | copy-start | bytes 1179652
  362.2 18.6 %collective-permute-start.2 = (f32[2,16]{1,0:T(2,128)S(1)}, f32[2,16]{1,0:T(2,128)S(1)}, u32[]{:S(2)}, u32[]{:S(2)}) collective-permute-start(f32[2,16]{1,0:T(2,128)S(1)} %get-tuple-element.49), channel_id=1, source_target_pairs={{0,2},{2,4},{4,6},{6,8},{8,10},{10,12},{12,14},{14,16},{16,18},{18... | collective-permute-start | bytes 392 | tf_op jit(solution)/shard_map/ppermute | solution.py:15
  365.5 27.8 %collective-permute-start.4 = (f32[2,16]{1,0:T(2,128)S(1)}, f32[2,16]{1,0:T(2,128)S(1)}, u32[]{:S(2)}, u32[]{:S(2)}) collective-permute-start(f32[2,16]{1,0:T(2,128)S(1)} %get-tuple-element.49), channel_id=1, source_target_pairs={{0,4},{2,6},{4,8},{6,10},{8,12},{10,14},{12,16},{14,18},{16,20},{1... | collective-permute-start | bytes 392 | tf_op jit(solution)/shard_map/ppermute | solution.py:15
  367.1 86.1 %collective-permute-start.1 = (f32[2,16,64,128]{3,2,1,0:T(8,128)S(1)}, f32[2,16,64,128]{3,2,1,0:T(8,128)}, u32[]{:S(2)}, u32[]{:S(2)}) collective-permute-start(f32[2,16,64,128]{3,2,1,0:T(8,128)S(1)} %get-tuple-element.48), channel_id=1, source_target_pairs={{0,2},{2,4},{4,6},{6,8},{8,10},{10,12},{12,14},{14,16},{16,18},{18... | collective-permute-start | bytes 3145736 | tf_op jit(solution)/shard_map/ppermute | solution.py:15
  371.5 81.7 %collective-permute-start.3 = (f32[2,16,64,128]{3,2,1,0:T(8,128)S(1)}, f32[2,16,64,128]{3,2,1,0:T(8,128)}, u32[]{:S(2)}, u32[]{:S(2)}) collective-permute-start(f32[2,16,64,128]{3,2,1,0:T(8,128)S(1)} %get-tuple-element.48), channel_id=1, source_target_pairs={{0,4},{2,6},{4,8},{6,10},{8,12},{10,14},{12,16},{14,18},{16,20},{1... | collective-permute-start | bytes 3145736 | tf_op jit(solution)/shard_map/ppermute | solution.py:15
  374.0 79.2 %collective-permute-start.5 = (f32[2,16,64,128]{3,2,1,0:T(8,128)S(1)}, f32[2,16,64,128]{3,2,1,0:T(8,128)}, u32[]{:S(2)}, u32[]{:S(2)}) collective-permute-start(f32[2,16,64,128]{3,2,1,0:T(8,128)S(1)} %get-tuple-element.48), channel_id=1, source_target_pairs={{0,6},{2,8},{4,10},{6,12},{8,14},{10,16},{12,18},{14,20},{16,22},{... | collective-permute-start | bytes 3145736 | tf_op jit(solution)/shard_map/ppermute | solution.py:15
  380.8 72.4 %collective-permute-start.7 = (f32[2,16,64,128]{3,2,1,0:T(8,128)S(1)}, f32[2,16,64,128]{3,2,1,0:T(8,128)S(1)}, u32[]{:S(2)}, u32[]{:S(2)}) collective-permute-start(f32[2,16,64,128]{3,2,1,0:T(8,128)S(1)} %get-tuple-element.48), channel_id=1, source_target_pairs={{0,8},{2,10},{4,12},{6,14},{8,16},{10,18},{12,20},{14,22},{16,24},... | collective-permute-start | bytes 3145736 | tf_op jit(solution)/shard_map/ppermute | solution.py:15
  393.3 59.9 %collective-permute-start.6 = (f32[2,16]{1,0:T(2,128)S(1)}, f32[2,16]{1,0:T(2,128)S(1)}, u32[]{:S(2)}, u32[]{:S(2)}) collective-permute-start(f32[2,16]{1,0:T(2,128)S(1)} %get-tuple-element.49), channel_id=1, source_target_pairs={{0,6},{2,8},{4,10},{6,12},{8,14},{10,16},{12,18},{14,20},{16,22},{... | collective-permute-start | bytes 392 | tf_op jit(solution)/shard_map/ppermute | solution.py:15
  395.6 59.9 %copy-start = (bf16[3,256,2,16,64]{1,0,4,3,2:T(4,128)(2,1)S(1)}, bf16[3,256,2,16,64]{1,0,4,3,2:T(4,128)(2,1)}, u32[]{:S(2)}) copy-start(bf16[3,256,2,16,64]{1,0,4,3,2:T(4,128)(2,1)} %reshape.289) | copy-start | bytes 9437188
  550.6 3.1 copy-start.10
  802.7 10.5 %collective-permute-start.8 = (f32[384,4096]{1,0:T(8,128)}, f32[384,4096]{1,0:T(8,128)}, u32[]{:S(2)}, u32[]{:S(2)}) collective-permute-start(f32[384,4096]{1,0:T(8,128)} %fusion.35), channel_id=1, source_target_pairs={{0,1},{1,0},{2,3},{3,2},{4,5},{5,4},{6,7},{7,6},{8,9},{9,8},{10,11... | collective-permute-start | bytes 18874376 | tf_op jit(solution)/shard_map/ppermute | solution.py:254
Sparse Core Ops, SparseCore 0:
  14.3 244.0 all-gather.3
  283.6 228.2 all-gather.5
  514.7 275.7 all-gather.7

commit v2 on v1

--- a/solution.py
+++ b/solution.py
@@ -13,6 +13,37 @@
     count = lax.axis_size(axis)
     leading, last = (max(0, -steps), min(count, count - steps))
     return lax.ppermute(value, axis, [(source, source + steps) for source in range(leading, last)])
+
+
+def ring_order(count):
+    return list(range(0, count, 2)) + list(range(count - 1, 0, -2))
+
+
+def ring_gather(local, axis, order):
+    count = len(order)
+    forward = [(order[k], order[(k + 1) % count]) for k in range(count)]
+    backward = [(order[k], order[(k - 1) % count]) for k in range(count)]
+    chunks = [local] + [None] * (count - 1)
+    ahead, behind = local, local
+    for steps in range(1, count // 2 + 1):
+        ahead = lax.ppermute(ahead, axis, forward)
+        chunks[steps] = ahead
+        if steps < count - steps:
+            behind = lax.ppermute(behind, axis, backward)
+            chunks[count - steps] = behind
+    return chunks
+
+
+def ring_columns(values, axis, order, width):
+    count = len(order)
+    table = jnp.asarray(order, jnp.int32)
+    places = jnp.asarray([order.index(k) for k in range(count)], jnp.int32)
+    place = places[lax.axis_index(axis)]
+    blocks = [
+        lax.dynamic_slice_in_dim(values, table[(place - offset) % count] * width, width, 1)
+        for offset in range(count)
+    ]
+    return jnp.concatenate(blocks, axis=1)
 
 
 def product_of(form, left, right):
@@ -160,17 +191,21 @@
     first_local = jnp.concatenate(
         [w_zx[:, 1], w_bc.reshape(w_bc.shape[0], 2 * state_cols), w_dt], axis=1
     )
-    first_full = lax.all_gather(first_local, "seq", axis=0, tiled=True)
-    proj_first = jnp.dot(normed, first_full, preferred_element_type=jnp.float32).astype(
-        jnp.bfloat16
-    )
+    order = ring_order(lax.axis_size("seq"))
+    out_full = lax.all_gather(w_out, "seq", axis=1, tiled=True)
+    first_chunks = ring_gather(first_local, "seq", order)
+    normed_ring = ring_columns(normed, "seq", order, first_local.shape[0])
+    proj_first = jnp.dot(
+        normed_ring, jnp.concatenate(first_chunks, axis=0), preferred_element_type=jnp.float32
+    ).astype(jnp.bfloat16)
     conv_width = inner_local + 2 * state_cols
     conv_in = proj_first[:, :conv_width]
     proj_dt = proj_first[:, conv_width:]
-    z_local, out_local, _ = lax.optimization_barrier((w_zx[:, 0], w_out, proj_first))
-    z_full = lax.all_gather(z_local, "seq", axis=0, tiled=True)
-    out_full = lax.all_gather(out_local, "seq", axis=1, tiled=True)
-    proj_z = jnp.dot(normed, z_full, preferred_element_type=jnp.float32).astype(jnp.bfloat16)
+    z_local, _ = lax.optimization_barrier((w_zx[:, 0], first_chunks))
+    z_chunks = ring_gather(z_local, "seq", order)
+    proj_z = jnp.dot(
+        normed_ring, jnp.concatenate(z_chunks, axis=0), preferred_element_type=jnp.float32
+    ).astype(jnp.bfloat16)
     prior_rows = from_behind(conv_in[row_count - edge_rows :], "seq", 1)
     weight = jnp.concatenate([conv_x, conv_bc[:, 0], conv_bc[:, 1]], axis=1)
     carry_rows = jnp.concatenate([carry_conv_x, carry_conv_bc[:, 0], carry_conv_bc[:, 1]], axis=1)

time: 843 us -> 1130 us (1.34)
  starting transfers between devices: 25.6 us -> 230 us
  local copies, waits for them, and re-layouts: 70.9 us -> 207 us
  waiting for transfers between devices: 558 us -> 468 us
  between operations: 15 us -> 37.6 us
    all_gather x3 -> x1, waiting for transfers between devices: 492 us -> 0.01 us  [body(): out_full = lax.all_gather(w_out, 'seq', axis=1, tiled=True)]
    ppermute x0 -> x30, waiting for transfers between devices: none -> 447 us  [the longest x16 377 us: ring_gather(): ahead = lax.ppermute(ahead, axis, forward)]
    ppermute x0 -> x30, starting transfers between devices: none -> 210 us  [the longest x14 144 us: ring_gather(): behind = lax.ppermute(behind, axis, backward)]
    unnamed x42 -> x180, local copies, waits for them, and re-layouts: 7.3 us -> 89.6 us
    ppermute x8, waiting for transfers between devices: 54.9 us -> 10.2 us  [from_behind(): lax.ppermute(value, axis, [(source, source + steps) for source in range(l...]
    ppermute x0 -> x15, local copies, waits for them, and re-layouts: none -> 36.8 us  [the longest x8 20 us: ring_gather(): ahead = lax.ppermute(ahead, axis, forward)]
  transfers between devices with their start and end apart: 12 -> 40, of which waited for: 5 -> 18; matrix products, arithmetic and copies ran while one was open for 21% -> 31% of each run, Pallas kernels for 0% -> 0%
where the time goes in v2:
time: 1130 us; the launch traced here: 1120 us
  waiting for transfers between devices  468 us (41%)
  starting transfers between devices  230 us (20%)
  local copies, waits for them, and re-layouts  207 us (18%)
  matrix products  103 us (9%)
  other arithmetic  72.3 us (6%)
  between operations  37.6 us (3%)
    ppermute x16, waiting for transfers between devices, ring_gather(): ahead = lax.ppermute(ahead, axis, forward)  377 us
    ppermute x14, starting transfers between devices, ring_gather(): behind = lax.ppermute(behind, axis, backward)  144 us
    unnamed x180, local copies, waits for them, and re-layouts  89.6 us
    ppermute x14, waiting for transfers between devices, ring_gather(): behind = lax.ppermute(behind, axis, backward)  69.9 us
    ppermute x16, starting transfers between devices, ring_gather(): ahead = lax.ppermute(ahead, axis, forward)  66.1 us
    dot_general x2, matrix products, body(): part = jnp.dot(rows, out_full, preferred_element_type=jnp.float32)  27 us
    reshape x2, local copies, waits for them, and re-layouts, body(): (direct + state_gain[..., None] * from_state).reshape(row_count, inner_lo...  24.4 us
    dot_general x1, matrix products, body(): jnp.dot(normed_ring, jnp.concatenate(first_chunks, axis=0), preferred_ele...  23.9 us
  transfers between devices with their start and end apart: 40, of which 18 were waited for; matrix products, arithmetic and copies ran while one was open for 31% of the time, Pallas kernels for 0%

profile of v2, /device:TPU:0, one launch (start us, length us, event | category | flops | bytes accessed | tf_op | source)
XLA Modules:
  0.0 1117.4 jit_solution(14449577054209210427)
XLA Ops:
  6.5 5.6 fusion.96
  14.8 2.5 copy.245
  17.4 3.0 collective-permute-start
  23.6 59.6 %collective-permute-done = bf16[256,2592]{0,1:T(8,128)(2,1)} collective-permute-done((bf16[256,2592]{0,1:T(8,128)(2,1)}, bf16[256,2592]{0,1:T(8,128)(2,1)}, u32[]{:S(2)}, u32[]{:S(2)}) %collective-permute-start) | collective-permute-done | bytes 1327136 | tf_op jit(solution)/shard_map/ppermute | solution.py:29
  101.2 4.1 fusion.3
  106.5 57.2 %collective-permute-done.1 = bf16[256,2592]{0,1:T(8,128)(2,1)} collective-permute-done((bf16[256,2592]{0,1:T(8,128)(2,1)}, bf16[256,2592]{0,1:T(8,128)(2,1)}, u32[]{:S(2)}, u32[]{:S(2)}) %collective-permute-start.1) | collective-permute-done | bytes 1327136 | tf_op jit(solution)/shard_map/ppermute | solution.py:29
  168.9 72.6 %collective-permute-done.2 = bf16[256,2592]{0,1:T(8,128)(2,1)S(1)} collective-permute-done((bf16[256,2592]{0,1:T(8,128)(2,1)}, bf16[256,2592]{0,1:T(8,128)(2,1)S(1)}, u32[]{:S(2)}, u32[]{:S(2)}) %collective-permute-start.2) | collective-permute-done | bytes 1327136 | tf_op jit(solution)/shard_map/ppermute | solution.py:29
  243.9 5.3 fusion.5
  252.9 70.3 %collective-permute-done.3 = bf16[256,2592]{0,1:T(8,128)(2,1)} collective-permute-done((bf16[256,2592]{0,1:T(8,128)(2,1)S(1)}, bf16[256,2592]{0,1:T(8,128)(2,1)}, u32[]{:S(2)}, u32[]{:S(2)}) %collective-permute-start.3) | collective-permute-done | bytes 1327136 | tf_op jit(solution)/shard_map/ppermute | solution.py:29
  323.1 2.9 collective-permute-start.4
  348.0 10.1 collective-permute-done.4
  358.1 25.2 %collective-permute-start.5 = (bf16[256,2592]{0,1:T(8,128)(2,1)}, bf16[256,2592]{0,1:T(8,128)(2,1)}, u32[]{:S(2)}, u32[]{:S(2)}) collective-permute-start(bf16[256,2592]{0,1:T(8,128)(2,1)} %collective-permute-done.4), channel_id=1, source_target_pairs={{0,4},{4,8},{8,12},{12,16},{16,20},{20,24},{24,28},{28,30},{30,26}... | collective-permute-start | bytes 3981320 | tf_op jit(solution)/shard_map/ppermute | solution.py:29
  405.9 42.9 %collective-permute-done.5 = bf16[256,2592]{0,1:T(8,128)(2,1)} collective-permute-done((bf16[256,2592]{0,1:T(8,128)(2,1)}, bf16[256,2592]{0,1:T(8,128)(2,1)}, u32[]{:S(2)}, u32[]{:S(2)}) %collective-permute-start.5) | collective-permute-done | bytes 1327136 | tf_op jit(solution)/shard_map/ppermute | solution.py:29
  448.8 2.7 collective-permute-start.6
  457.1 2.5 constant_dynamic-update-slice_fusion.14
  462.1 2.5 copy.260
  464.7 2.5 constant_dynamic-update-slice_fusion.13
  472.2 22.0 %collective-permute-start.14 = (bf16[256,2592]{0,1:T(8,128)(2,1)}, bf16[256,2592]{0,1:T(8,128)(2,1)}, u32[]{:S(2)}, u32[]{:S(2)}) collective-permute-start(bf16[256,2592]{0,1:T(8,128)(2,1)} %collective-permute-done.13), channel_id=1, source_target_pairs={{0,2},{4,0},{8,4},{12,8},{16,12},{20,16},{24,20},{28,24},{30,28},{... | collective-permute-start | bytes 3981320 | tf_op jit(solution)/shard_map/ppermute | solution.py:32
  494.2 2.6 constant_dynamic-update-slice_fusion.12
  509.3 2.6 constant_dynamic-update-slice_fusion.10
  514.4 2.6 copy.256
  516.9 2.5 constant_dynamic-update-slice_fusion.9
  525.6 2.5 constant_dynamic-update-slice_fusion.8
  528.1 8.9 collective-permute-done.7
  539.5 19.6 %collective-permute-start.31 = (bf16[256,2048]{1,0:T(8,128)(2,1)S(1)}, bf16[256,2048]{1,0:T(8,128)(2,1)}, u32[]{:S(2)}, u32[]{:S(2)}) collective-permute-start(bf16[256,2048]{1,0:T(8,128)(2,1)S(1)} %bitcast.140), channel_id=1, source_target_pairs={{0,2},{4,0},{8,4},{12,8},{16,12},{20,16},{24,20},{28,24},{30,28},{... | collective-permute-start | bytes 3145736 | tf_op jit(solution)/shard_map/ppermute | solution.py:32
  561.6 2.7 constant_dynamic-update-slice_fusion.7
  564.4 2.6 constant_dynamic-update-slice_fusion.6
  574.2 23.9 %convolution_convert_fusion = bf16[768,2592]{0,1:T(8,128)(2,1)} fusion(bf16[768,4096]{1,0:T(8,128)(2,1)} %dynamic-slice_dynamic-update-slice_fusion, bf16[4096,2592]{1,0:T(8,128)(2,1)} %constant_dynamic-update-slice_fusion), kind=kOutput, calls=%fused_computation.39 | convolution fusion | flops 16309444608 | bytes 31506432 | tf_op jit(solution)/shard_map/dot_general | solution.py:198
  600.9 3.4 reduce-window.21
  606.0 4.4 collective-permute-start.15
  611.7 4.4 slice.129
  616.7 11.6 %collective-permute-start.24 = (bf16[256,2048]{1,0:T(8,128)(2,1)}, bf16[256,2048]{1,0:T(8,128)(2,1)}, u32[]{:S(2)}, u32[]{:S(2)}) collective-permute-start(bf16[256,2048]{1,0:T(8,128)(2,1)} %collective-permute-done.23), channel_id=1, source_target_pairs={{0,4},{4,8},{8,12},{12,16},{16,20},{20,24},{24,28},{28,30},{30,26}... | collective-permute-start | bytes 3145736 | tf_op jit(solution)/shard_map/ppermute | solution.py:29
  628.4 20.6 %multiply_convert_fusion.2 = bf16[768,2560]{0,1:T(8,128)(2,1)S(1)} fusion(bf16[768,2560]{0,1:T(8,128)(2,1)} %slice.129, bf16[3,2560]{0,1:T(8,128)(2,1)S(1)} %copy.263, f32[2560]{0:T(1024)S(1)} %get-tuple-element.79, f32[2560]{0:T(1024)S(1)} %get-tuple-element.80, f32[2560]{0:T(1024)S(1)} %get-tuple-element.81, f32[2560]{0:T(1024)S(1)} %get-tuple-element.78, ...), kind=kLoop, calls=%fused_computation.24 | loop fusion | flops 104202240 | bytes 7964416 | tf_op jit(solution)/shard_map/convert_element_type | solution.py:99
  652.8 9.5 reshape.321
  668.1 4.9 multiply_add_fusion
  675.1 7.5 while.18
  682.6 2.9 collective-permute-start.16
  685.6 11.4 %collective-permute-done.32 = bf16[256,2048]{1,0:T(8,128)(2,1)} collective-permute-done((bf16[256,2048]{1,0:T(8,128)(2,1)}, bf16[256,2048]{1,0:T(8,128)(2,1)}, u32[]{:S(2)}, u32[]{:S(2)}) %collective-permute-start.32) | collective-permute-done | bytes 1048608 | tf_op jit(solution)/shard_map/ppermute | solution.py:32
  697.0 20.1 %collective-permute-start.33 = (bf16[256,2048]{1,0:T(8,128)(2,1)}, bf16[256,2048]{1,0:T(8,128)(2,1)}, u32[]{:S(2)}, u32[]{:S(2)}) collective-permute-start(bf16[256,2048]{1,0:T(8,128)(2,1)} %collective-permute-done.32), channel_id=1, source_target_pairs={{0,2},{4,0},{8,4},{12,8},{16,12},{20,16},{24,20},{28,24},{30,28},{... | collective-permute-start | bytes 3145736 | tf_op jit(solution)/shard_map/ppermute | solution.py:32
  717.1 45.5 %collective-permute-done.25 = bf16[256,2048]{1,0:T(8,128)(2,1)} collective-permute-done((bf16[256,2048]{1,0:T(8,128)(2,1)}, bf16[256,2048]{1,0:T(8,128)(2,1)}, u32[]{:S(2)}, u32[]{:S(2)}) %collective-permute-start.25) | collective-permute-done | bytes 1048608 | tf_op jit(solution)/shard_map/ppermute | solution.py:29
  777.8 10.2 collective-permute-done.19
  788.1 4.6 collective-permute-start.18
  796.1 3.0 collective-permute-start.34
  799.5 13.0 %fusion.2 = f32[3,2,16,64,256]{4,3,2,1,0:T(8,128)} fusion(f32[3,2,16,256]{3,2,1,0:T(8,128)} %copy.273, f32[3,2,16,256]{3,2,1,0:T(8,128)} %get-tuple-element.113, f32[3,2,256,256]{3,2,1,0:T(8,128)S(1)} %fusion.44, pred[3,256,256]{2,1,0:T(8,128)(4,1)} %compare_and_fusion, bf16[3,256,2,16,64]{1,0,4,3,2:T(4,128)(2,1)} %reshape.321), kind=kOutput, calls=%fused_computation.10 | convolution fusion | flops 843055104 | bytes 11403264 | tf_op jit(solution)/shard_map/cghqs,csghp->cqghp/dot_general | solution.py:51
  812.5 40.3 %collective-permute-done.34 = bf16[256,2048]{1,0:T(8,128)(2,1)S(1)} collective-permute-done((bf16[256,2048]{1,0:T(8,128)(2,1)}, bf16[256,2048]{1,0:T(8,128)(2,1)S(1)}, u32[]{:S(2)}, u32[]{:S(2)}) %collective-permute-start.34) | collective-permute-done | bytes 1048608 | tf_op jit(solution)/shard_map/ppermute | solution.py:32
  852.8 26.9 %collective-permute-start.35 = (bf16[256,2048]{1,0:T(8,128)(2,1)S(1)}, bf16[256,2048]{1,0:T(8,128)(2,1)}, u32[]{:S(2)}, u32[]{:S(2)}) collective-permute-start(bf16[256,2048]{1,0:T(8,128)(2,1)S(1)} %collective-permute-done.34), channel_id=1, source_target_pairs={{0,2},{4,0},{8,4},{12,8},{16,12},{20,16},{24,20},{28,24},{30,28},{... | collective-permute-start | bytes 3145736 | tf_op jit(solution)/shard_map/ppermute | solution.py:32
  884.1 2.7 fusion.48
  890.8 10.0 collective-permute-done.35
  900.8 24.8 %collective-permute-start.36 = (bf16[256,2048]{1,0:T(8,128)(2,1)}, bf16[256,2048]{1,0:T(8,128)(2,1)S(1)}, u32[]{:S(2)}, u32[]{:S(2)}) collective-permute-start(bf16[256,2048]{1,0:T(8,128)(2,1)} %collective-permute-done.35), channel_id=1, source_target_pairs={{0,2},{4,0},{8,4},{12,8},{16,12},{20,16},{24,20},{28,24},{30,28},{... | collective-permute-start | bytes 3145736 | tf_op jit(solution)/shard_map/ppermute | solution.py:32
  927.2 3.0 collective-permute-start.29
  930.2 7.9 fusion.13
  938.1 12.7 %copy.304 = f32[3,256,2,16,64]{4,3,2,1,0:T(8,128)} copy(f32[3,256,2,16,64]{1,4,3,2,0:T(8,128)} %fusion.13) | data formatting | bytes 12582912 | tf_op jit(solution)/shard_map/reshape | solution.py:274
  950.8 11.8 %reshape.342 = f32[768,2048]{1,0:T(8,128)} reshape(f32[3,256,2,16,64]{4,3,2,1,0:T(8,128)} %copy.304) | data formatting | bytes 12582912 | tf_op jit(solution)/shard_map/reshape | solution.py:274
  968.0 27.1 %collective-permute-start.37 = (bf16[256,2048]{1,0:T(8,128)(2,1)S(1)}, bf16[256,2048]{1,0:T(8,128)(2,1)S(1)}, u32[]{:S(2)}, u32[]{:S(2)}) collective-permute-start(bf16[256,2048]{1,0:T(8,128)(2,1)S(1)} %collective-permute-done.36), channel_id=1, source_target_pairs={{0,2},{4,0},{8,4},{12,8},{16,12},{20,16},{24,20},{28,24},{30,28},{... | collective-permute-start | bytes 3145736 | tf_op jit(solution)/shard_map/ppermute | solution.py:32
  1001.9 6.4 collective-permute-done.30
  1009.3 7.0 collective-permute-done.37
  1028.7 22.1 %fusion.100 = (f32[768,2048]{1,0:T(8,128)}, f32[768,2048]{1,0:T(8,128)}) fusion(f32[768,2048]{1,0:T(8,128)S(1)} %bitcast.138, bf16[768,4096]{1,0:T(8,128)(2,1)} %dynamic-slice_dynamic-update-slice_fusion, bf16[4096,2048]{1,0:T(8,128)(2,1)} %constant_dynamic-update-slice_fusion.16), kind=kOutput, calls=%fused_computation.219 | convolution fusion | flops 12897484800 | bytes 41943040 | tf_op jit(solution)/shard_map/dot_general | solution.py:206
  1050.8 9.3 mul.436
  1060.2 4.5 reduce_sum.69
  1066.5 3.1 copy.315
  1069.6 3.3 multiply_convert_fusion.3
  1072.9 12.5 %fusion.33 = f32[384,4096]{1,0:T(8,128)} fusion(bf16[2048,4096]{1,0:T(8,128)(2,1)} %all-gather.2.cloned.1.call-done, bf16[768,2048]{1,0:T(8,128)(2,1)} %multiply_convert_fusion.3, s32[]{:T(128)S(6)} %select_n.376), kind=kOutput, calls=%fused_computation.53 | convolution fusion | flops 6442450944 | bytes 24641540 | tf_op jit(solution)/shard_map/dot_general | solution.py:287
  1085.4 10.5 collective-permute-done.38
  1095.9 14.5 %add_convert_fusion = bf16[384,4096]{1,0:T(8,128)(2,1)} fusion(f32[384,4096]{1,0:T(8,128)} %collective-permute-done.38, bf16[2048,4096]{1,0:T(8,128)(2,1)} %all-gather.2.cloned.1.call-done, bf16[768,2048]{1,0:T(8,128)(2,1)S(1)} %copy-done.10, s32[]{:T(128)S(6)} %select_n.378), kind=kOutput, calls=%fused_computation.35 | convolution fusion | flops 6445596672 | bytes 27787268 | tf_op jit(solution)/shard_map/dot_general | solution.py:287
  (336 shorter events, 185.7 us)
Async XLA Ops:
  6.5 1066.4 %all-gather.2.cloned.1.call-start = ((), (), s32[]{:S(2)}) async-start(), calls=%async_computation | async-start | bytes 17825792 | tf_op jit(solution)/shard_map/all_gather | solution.py:195
  12.2 73.5 %copy-start.59 = (s32[16]{0:T(128)S(1)}, s32[16]{0:T(128)}, u32[]{:S(2)}) copy-start(s32[16]{0:T(128)} %constant.234.clone) | copy-start | bytes 196
  12.2 86.1 %copy-start.21 = (s32[16]{0:T(128)S(1)}, s32[16]{0:T(128)}, u32[]{:S(2)}) copy-start(s32[16]{0:T(128)} %constant.233.clone) | copy-start | bytes 196
  12.3 88.9 %copy-start.25 = (bf16[4,2048]{1,0:T(4,128)(2,1)S(1)}, bf16[4,2048]{1,0:T(4,128)(2,1)}, u32[]{:S(2)}) copy-start(bf16[4,2048]{1,0:T(4,128)(2,1)} %param.27) | copy-start | bytes 49156
  14.8 152.7 %copy-start.28 = (bf16[3,2,256]{2,1,0:T(2,128)(2,1)S(1)}, bf16[3,2,256]{2,1,0:T(2,128)(2,1)}, u32[]{:S(2)}) copy-start(bf16[3,2,256]{2,1,0:T(2,128)(2,1)} %param.39) | copy-start | bytes 9220
  14.8 152.7 %copy-start.26 = (bf16[3,2048]{1,0:T(4,128)(2,1)S(1)}, bf16[3,2048]{1,0:T(4,128)(2,1)}, u32[]{:S(2)}) copy-start(bf16[3,2048]{1,0:T(4,128)(2,1)} %param.38) | copy-start | bytes 36868
  14.8 229.1 %copy-start.23 = (f32[4096]{0:T(1024)S(1)}, f32[4096]{0:T(1024)}, u32[]{:S(2)}) copy-start(f32[4096]{0:T(1024)} %param.23) | copy-start | bytes 49156
  17.4 65.7 %collective-permute-start = (bf16[256,2592]{0,1:T(8,128)(2,1)}, bf16[256,2592]{0,1:T(8,128)(2,1)}, u32[]{:S(2)}, u32[]{:S(2)}) collective-permute-start(bf16[256,2592]{0,1:T(8,128)(2,1)} %copy.245), channel_id=1, source_target_pairs={{0,4},{4,8},{8,12},{12,16},{16,20},{20,24},{24,28},{28,30},{30,26}... | collective-permute-start | bytes 3981320 | tf_op jit(solution)/shard_map/ppermute | solution.py:29
  20.4 84.9 %collective-permute-start.8 = (bf16[256,2592]{0,1:T(8,128)(2,1)}, bf16[256,2592]{0,1:T(8,128)(2,1)}, u32[]{:S(2)}, u32[]{:S(2)}) collective-permute-start(bf16[256,2592]{0,1:T(8,128)(2,1)} %copy.245), channel_id=1, source_target_pairs={{0,2},{4,0},{8,4},{12,8},{16,12},{20,16},{24,20},{28,24},{30,28},{... | collective-permute-start | bytes 3981320 | tf_op jit(solution)/shard_map/ppermute | solution.py:32
  83.1 80.6 %collective-permute-start.1 = (bf16[256,2592]{0,1:T(8,128)(2,1)}, bf16[256,2592]{0,1:T(8,128)(2,1)}, u32[]{:S(2)}, u32[]{:S(2)}) collective-permute-start(bf16[256,2592]{0,1:T(8,128)(2,1)} %collective-permute-done), channel_id=1, source_target_pairs={{0,4},{4,8},{8,12},{12,16},{16,20},{20,24},{24,28},{28,30},{30,26}... | collective-permute-start | bytes 3981320 | tf_op jit(solution)/shard_map/ppermute | solution.py:29
  105.3 62.4 %collective-permute-start.9 = (bf16[256,2592]{0,1:T(8,128)(2,1)}, bf16[256,2592]{0,1:T(8,128)(2,1)S(1)}, u32[]{:S(2)}, u32[]{:S(2)}) collective-permute-start(bf16[256,2592]{0,1:T(8,128)(2,1)} %collective-permute-done.8), channel_id=1, source_target_pairs={{0,2},{4,0},{8,4},{12,8},{16,12},{20,16},{24,20},{28,24},{30,28},{... | collective-permute-start | bytes 3981320 | tf_op jit(solution)/shard_map/ppermute | solution.py:32
  163.7 77.8 %collective-permute-start.2 = (bf16[256,2592]{0,1:T(8,128)(2,1)}, bf16[256,2592]{0,1:T(8,128)(2,1)S(1)}, u32[]{:S(2)}, u32[]{:S(2)}) collective-permute-start(bf16[256,2592]{0,1:T(8,128)(2,1)} %collective-permute-done.1), channel_id=1, source_target_pairs={{0,4},{4,8},{8,12},{12,16},{16,20},{20,24},{24,28},{28,30},{30,26}... | collective-permute-start | bytes 3981320 | tf_op jit(solution)/shard_map/ppermute | solution.py:29
  167.6 81.6 %copy-start.12 = (bf16[256,2592]{0,1:T(8,128)(2,1)}, bf16[256,2592]{0,1:T(8,128)(2,1)S(1)}, u32[]{:S(2)}) copy-start(bf16[256,2592]{0,1:T(8,128)(2,1)S(1)} %collective-permute-done.9) | copy-start | bytes 3981316
  167.6 81.7 %collective-permute-start.10 = (bf16[256,2592]{0,1:T(8,128)(2,1)S(1)}, bf16[256,2592]{0,1:T(8,128)(2,1)}, u32[]{:S(2)}, u32[]{:S(2)}) collective-permute-start(bf16[256,2592]{0,1:T(8,128)(2,1)S(1)} %collective-permute-done.9), channel_id=1, source_target_pairs={{0,2},{4,0},{8,4},{12,8},{16,12},{20,16},{24,20},{28,24},{30,28},{... | collective-permute-start | bytes 3981320 | tf_op jit(solution)/shard_map/ppermute | solution.py:32
  241.6 81.6 %collective-permute-start.3 = (bf16[256,2592]{0,1:T(8,128)(2,1)S(1)}, bf16[256,2592]{0,1:T(8,128)(2,1)}, u32[]{:S(2)}, u32[]{:S(2)}) collective-permute-start(bf16[256,2592]{0,1:T(8,128)(2,1)S(1)} %collective-permute-done.2), channel_id=1, source_target_pairs={{0,4},{4,8},{8,12},{12,16},{16,20},{20,24},{24,28},{28,30},{30,26}... | collective-permute-start | bytes 3981320 | tf_op jit(solution)/shard_map/ppermute | solution.py:29
  249.3 95.0 %collective-permute-start.11 = (bf16[256,2592]{0,1:T(8,128)(2,1)}, bf16[256,2592]{0,1:T(8,128)(2,1)}, u32[]{:S(2)}, u32[]{:S(2)}) collective-permute-start(bf16[256,2592]{0,1:T(8,128)(2,1)} %collective-permute-done.10), channel_id=1, source_target_pairs={{0,2},{4,0},{8,4},{12,8},{16,12},{20,16},{24,20},{28,24},{30,28},{... | collective-permute-start | bytes 3981320 | tf_op jit(solution)/shard_map/ppermute | solution.py:32
  323.1 35.0 %collective-permute-start.4 = (bf16[256,2592]{0,1:T(8,128)(2,1)}, bf16[256,2592]{0,1:T(8,128)(2,1)}, u32[]{:S(2)}, u32[]{:S(2)}) collective-permute-start(bf16[256,2592]{0,1:T(8,128)(2,1)} %collective-permute-done.3), channel_id=1, source_target_pairs={{0,4},{4,8},{8,12},{12,16},{16,20},{20,24},{24,28},{28,30},{30,26}... | collective-permute-start | bytes 3981320 | tf_op jit(solution)/shard_map/ppermute | solution.py:29
  333.5 68.2 %copy-start.57 = (f32[32]{0:T(128)S(1)}, f32[32]{0:T(128)}, u32[]{:S(2)}) copy-start(f32[32]{0:T(128)} %param.30) | copy-start | bytes 388
  344.3 53.7 %collective-permute-start.12 = (bf16[256,2592]{0,1:T(8,128)(2,1)}, bf16[256,2592]{0,1:T(8,128)(2,1)}, u32[]{:S(2)}, u32[]{:S(2)}) collective-permute-start(bf16[256,2592]{0,1:T(8,128)(2,1)} %collective-permute-done.11), channel_id=1, source_target_pairs={{0,2},{4,0},{8,4},{12,8},{16,12},{20,16},{24,20},{28,24},{30,28},{... | collective-permute-start | bytes 3981320 | tf_op jit(solution)/shard_map/ppermute | solution.py:32
  358.1 90.7 %collective-permute-start.5 = (bf16[256,2592]{0,1:T(8,128)(2,1)}, bf16[256,2592]{0,1:T(8,128)(2,1)}, u32[]{:S(2)}, u32[]{:S(2)}) collective-permute-start(bf16[256,2592]{0,1:T(8,128)(2,1)} %collective-permute-done.4), channel_id=1, source_target_pairs={{0,4},{4,8},{8,12},{12,16},{16,20},{20,24},{24,28},{28,30},{30,26}... | collective-permute-start | bytes 3981320 | tf_op jit(solution)/shard_map/ppermute | solution.py:29
  398.0 74.2 %collective-permute-start.13 = (bf16[256,2592]{0,1:T(8,128)(2,1)}, bf16[256,2592]{0,1:T(8,128)(2,1)}, u32[]{:S(2)}, u32[]{:S(2)}) collective-permute-start(bf16[256,2592]{0,1:T(8,128)(2,1)} %collective-permute-done.12), channel_id=1, source_target_pairs={{0,2},{4,0},{8,4},{12,8},{16,12},{20,16},{24,20},{28,24},{30,28},{... | collective-permute-start | bytes 3981320 | tf_op jit(solution)/shard_map/ppermute | solution.py:32
  448.8 50.5 %collective-permute-start.6 = (bf16[256,2592]{0,1:T(8,128)(2,1)}, bf16[256,2592]{0,1:T(8,128)(2,1)}, u32[]{:S(2)}, u32[]{:S(2)}) collective-permute-start(bf16[256,2592]{0,1:T(8,128)(2,1)} %collective-permute-done.5), channel_id=1, source_target_pairs={{0,4},{4,8},{8,12},{12,16},{16,20},{20,24},{24,28},{28,30},{30,26}... | collective-permute-start | bytes 3981320 | tf_op jit(solution)/shard_map/ppermute | solution.py:29
  472.2 50.9 %collective-permute-start.14 = (bf16[256,2592]{0,1:T(8,128)(2,1)}, bf16[256,2592]{0,1:T(8,128)(2,1)}, u32[]{:S(2)}, u32[]{:S(2)}) collective-permute-start(bf16[256,2592]{0,1:T(8,128)(2,1)} %collective-permute-done.13), channel_id=1, source_target_pairs={{0,2},{4,0},{8,4},{12,8},{16,12},{20,16},{24,20},{28,24},{30,28},{... | collective-permute-start | bytes 3981320 | tf_op jit(solution)/shard_map/ppermute | solution.py:32
  499.3 37.7 %collective-permute-start.7 = (bf16[256,2592]{0,1:T(8,128)(2,1)}, bf16[256,2592]{0,1:T(8,128)(2,1)}, u32[]{:S(2)}, u32[]{:S(2)}) collective-permute-start(bf16[256,2592]{0,1:T(8,128)(2,1)} %collective-permute-done.6), channel_id=1, source_target_pairs={{0,4},{4,8},{8,12},{12,16},{16,20},{20,24},{24,28},{28,30},{30,26}... | collective-permute-start | bytes 3981320 | tf_op jit(solution)/shard_map/ppermute | solution.py:29
  537.0 79.7 %collective-permute-start.23 = (bf16[256,2048]{1,0:T(8,128)(2,1)S(1)}, bf16[256,2048]{1,0:T(8,128)(2,1)}, u32[]{:S(2)}, u32[]{:S(2)}) collective-permute-start(bf16[256,2048]{1,0:T(8,128)(2,1)S(1)} %bitcast.139), channel_id=1, source_target_pairs={{0,4},{4,8},{8,12},{12,16},{16,20},{20,24},{24,28},{28,30},{30,26}... | collective-permute-start | bytes 3145736 | tf_op jit(solution)/shard_map/ppermute | solution.py:29
  539.5 133.5 %collective-permute-start.31 = (bf16[256,2048]{1,0:T(8,128)(2,1)S(1)}, bf16[256,2048]{1,0:T(8,128)(2,1)}, u32[]{:S(2)}, u32[]{:S(2)}) collective-permute-start(bf16[256,2048]{1,0:T(8,128)(2,1)S(1)} %bitcast.140), channel_id=1, source_target_pairs={{0,2},{4,0},{8,4},{12,8},{16,12},{20,16},{24,20},{28,24},{30,28},{... | collective-permute-start | bytes 3145736 | tf_op jit(solution)/shard_map/ppermute | solution.py:32
  574.2 36.2 %copy-start.52 = (pred[3,256]{1,0:T(4,128)(4,1)S(1)}, pred[3,256]{1,0:T(4,128)(4,1)}, u32[]{:S(2)}) copy-start(pred[3,256]{1,0:T(4,128)(4,1)} %get-tuple-element.115) | copy-start | bytes 2308
  574.2 36.2 %copy-start.53 = (pred[3,256]{1,0:T(4,128)(4,1)S(1)}, pred[3,256]{1,0:T(4,128)(4,1)}, u32[]{:S(2)}) copy-start(pred[3,256]{1,0:T(4,128)(4,1)} %get-tuple-element.150) | copy-start | bytes 2308
  574.2 36.6 %copy-start.47 = (pred[3,256]{1,0:T(4,128)(4,1)S(1)}, pred[3,256]{1,0:T(4,128)(4,1)}, u32[]{:S(2)}) copy-start(pred[3,256]{1,0:T(4,128)(4,1)} %get-tuple-element.114) | copy-start | bytes 2308
  574.2 36.6 %copy-start.48 = (pred[1,3,2,128]{3,1,2,0:T(4,128)(4,1)S(1)}, pred[1,3,2,128]{3,1,2,0:T(4,128)(4,1)}, u32[]{:S(2)}) copy-start(pred[1,3,2,128]{3,1,2,0:T(4,128)(4,1)} %copy.360) | copy-start | bytes 2308
  574.2 37.4 %copy-start.50 = (pred[3]{0:T(512)(128)(4,1)S(1)}, pred[3]{0:T(512)(128)(4,1)}, u32[]{:S(2)}) copy-start(pred[3]{0:T(512)(128)(4,1)} %fusion.87) | copy-start | bytes 13
  600.7 27.6 %copy-start.22 = (f32[2560]{0:T(1024)S(1)}, f32[2560]{0:T(1024)}, u32[]{:S(2)}) copy-start(f32[2560]{0:T(1024)} %get-tuple-element.77) | copy-start | bytes 30724
  600.7 27.6 %copy-start.30 = (pred[768]{0:T(1024)(128)(4,1)S(1)}, pred[768]{0:T(1024)(128)(4,1)}, u32[]{:S(2)}) copy-start(pred[768]{0:T(1024)(128)(4,1)} %get-tuple-element.116) | copy-start | bytes 2308
  600.7 27.5 %copy-start.31 = (pred[768]{0:T(1024)(128)(4,1)S(1)}, pred[768]{0:T(1024)(128)(4,1)}, u32[]{:S(2)}) copy-start(pred[768]{0:T(1024)(128)(4,1)} %get-tuple-element.117) | copy-start | bytes 2308
  600.8 27.5 %copy-start.32 = (pred[768]{0:T(1024)(128)(4,1)S(1)}, pred[768]{0:T(1024)(128)(4,1)}, u32[]{:S(2)}) copy-start(pred[768]{0:T(1024)(128)(4,1)} %get-tuple-element.118) | copy-start | bytes 2308
  606.0 10.3 collective-permute-start.15
  616.7 56.3 %collective-permute-start.24 = (bf16[256,2048]{1,0:T(8,128)(2,1)}, bf16[256,2048]{1,0:T(8,128)(2,1)}, u32[]{:S(2)}, u32[]{:S(2)}) collective-permute-start(bf16[256,2048]{1,0:T(8,128)(2,1)} %collective-permute-done.23), channel_id=1, source_target_pairs={{0,4},{4,8},{8,12},{12,16},{16,20},{20,24},{24,28},{28,30},{30,26}... | collective-permute-start | bytes 3145736 | tf_op jit(solution)/shard_map/ppermute | solution.py:29
  673.0 23.9 %collective-permute-start.32 = (bf16[256,2048]{1,0:T(8,128)(2,1)}, bf16[256,2048]{1,0:T(8,128)(2,1)}, u32[]{:S(2)}, u32[]{:S(2)}) collective-permute-start(bf16[256,2048]{1,0:T(8,128)(2,1)} %collective-permute-done.31), channel_id=1, source_target_pairs={{0,2},{4,0},{8,4},{12,8},{16,12},{20,16},{24,20},{28,24},{30,28},{... | collective-permute-start | bytes 3145736 | tf_op jit(solution)/shard_map/ppermute | solution.py:32
  673.1 89.6 %collective-permute-start.25 = (bf16[256,2048]{1,0:T(8,128)(2,1)}, bf16[256,2048]{1,0:T(8,128)(2,1)}, u32[]{:S(2)}, u32[]{:S(2)}) collective-permute-start(bf16[256,2048]{1,0:T(8,128)(2,1)} %collective-permute-done.24), channel_id=1, source_target_pairs={{0,4},{4,8},{8,12},{12,16},{16,20},{20,24},{24,28},{28,30},{30,26}... | collective-permute-start | bytes 3145736 | tf_op jit(solution)/shard_map/ppermute | solution.py:29
  675.1 90.0 %copy-start.58 = (f32[32]{0:T(128)S(1)}, f32[32]{0:T(128)}, u32[]{:S(2)}) copy-start(f32[32]{0:T(128)} %param.31) | copy-start | bytes 388
  675.1 92.6 %copy-start.16 = (f32[3,256,2,16]{1,0,3,2:T(4,128)S(1)}, f32[3,256,2,16]{1,0,3,2:T(4,128)}, u32[]{:S(2)}) copy-start(f32[3,256,2,16]{1,0,3,2:T(4,128)} %get-tuple-element.111) | copy-start | bytes 294916
  682.6 111.4 %collective-permute-start.16 = (f32[2,16,64,128]{3,2,1,0:T(8,128)S(1)}, f32[2,16,64,128]{3,2,1,0:T(8,128)}, u32[]{:S(2)}, u32[]{:S(2)}) collective-permute-start(f32[2,16,64,128]{3,2,1,0:T(8,128)S(1)} %get-tuple-element.47), channel_id=1, source_target_pairs={{0,2},{2,4},{4,6},{6,8},{8,10},{10,12},{12,14},{14,16},{16,18},{18... | collective-permute-start | bytes 3145736 | tf_op jit(solution)/shard_map/ppermute | solution.py:15
  697.0 99.1 %collective-permute-start.33 = (bf16[256,2048]{1,0:T(8,128)(2,1)}, bf16[256,2048]{1,0:T(8,128)(2,1)}, u32[]{:S(2)}, u32[]{:S(2)}) collective-permute-start(bf16[256,2048]{1,0:T(8,128)(2,1)} %collective-permute-done.32), channel_id=1, source_target_pairs={{0,2},{4,0},{8,4},{12,8},{16,12},{20,16},{24,20},{28,24},{30,28},{... | collective-permute-start | bytes 3145736 | tf_op jit(solution)/shard_map/ppermute | solution.py:32
  762.6 36.5 %collective-permute-start.26 = (bf16[256,2048]{1,0:T(8,128)(2,1)}, bf16[256,2048]{1,0:T(8,128)(2,1)}, u32[]{:S(2)}, u32[]{:S(2)}) collective-permute-start(bf16[256,2048]{1,0:T(8,128)(2,1)} %collective-permute-done.25), channel_id=1, source_target_pairs={{0,4},{4,8},{8,12},{12,16},{16,20},{20,24},{24,28},{28,30},{30,26}... | collective-permute-start | bytes 3145736 | tf_op jit(solution)/shard_map/ppermute | solution.py:29
  770.1 6.5 collective-permute-start.17
  771.5 16.6 %collective-permute-start.19 = (f32[2,16]{1,0:T(2,128)S(1)}, f32[2,16]{1,0:T(2,128)S(1)}, u32[]{:S(2)}, u32[]{:S(2)}) collective-permute-start(f32[2,16]{1,0:T(2,128)S(1)} %get-tuple-element.48), channel_id=1, source_target_pairs={{0,4},{2,6},{4,8},{6,10},{8,12},{10,14},{12,16},{14,18},{16,20},{1... | collective-permute-start | bytes 392 | tf_op jit(solution)/shard_map/ppermute | solution.py:15
  776.5 16.1 %collective-permute-start.21 = (f32[2,16]{1,0:T(2,128)S(1)}, f32[2,16]{1,0:T(2,128)S(1)}, u32[]{:S(2)}, u32[]{:S(2)}) collective-permute-start(f32[2,16]{1,0:T(2,128)S(1)} %get-tuple-element.48), channel_id=1, source_target_pairs={{0,6},{2,8},{4,10},{6,12},{8,14},{10,16},{12,18},{14,20},{16,22},{... | collective-permute-start | bytes 392 | tf_op jit(solution)/shard_map/ppermute | solution.py:15
  788.1 101.1 %collective-permute-start.18 = (f32[2,16,64,128]{3,2,1,0:T(8,128)S(1)}, f32[2,16,64,128]{3,2,1,0:T(8,128)S(1)}, u32[]{:S(2)}, u32[]{:S(2)}) collective-permute-start(f32[2,16,64,128]{3,2,1,0:T(8,128)S(1)} %get-tuple-element.47), channel_id=1, source_target_pairs={{0,4},{2,6},{4,8},{6,10},{8,12},{10,14},{12,16},{14,18},{16,20},{1... | collective-permute-start | bytes 3145736 | tf_op jit(solution)/shard_map/ppermute | solution.py:15
  792.7 96.5 %collective-permute-start.20 = (f32[2,16,64,128]{3,2,1,0:T(8,128)S(1)}, f32[2,16,64,128]{3,2,1,0:T(8,128)S(1)}, u32[]{:S(2)}, u32[]{:S(2)}) collective-permute-start(f32[2,16,64,128]{3,2,1,0:T(8,128)S(1)} %get-tuple-element.47), channel_id=1, source_target_pairs={{0,6},{2,8},{4,10},{6,12},{8,14},{10,16},{12,18},{14,20},{16,22},{... | collective-permute-start | bytes 3145736 | tf_op jit(solution)/shard_map/ppermute | solution.py:15
  794.1 95.1 %collective-permute-start.22 = (f32[2,16,64,128]{3,2,1,0:T(8,128)S(1)}, f32[2,16,64,128]{3,2,1,0:T(8,128)S(1)}, u32[]{:S(2)}, u32[]{:S(2)}) collective-permute-start(f32[2,16,64,128]{3,2,1,0:T(8,128)S(1)} %get-tuple-element.47), channel_id=1, source_target_pairs={{0,8},{2,10},{4,12},{6,14},{8,16},{10,18},{12,20},{14,22},{16,24},... | collective-permute-start | bytes 3145736 | tf_op jit(solution)/shard_map/ppermute | solution.py:15
  796.1 56.7 %collective-permute-start.34 = (bf16[256,2048]{1,0:T(8,128)(2,1)}, bf16[256,2048]{1,0:T(8,128)(2,1)S(1)}, u32[]{:S(2)}, u32[]{:S(2)}) collective-permute-start(bf16[256,2048]{1,0:T(8,128)(2,1)} %collective-permute-done.33), channel_id=1, source_target_pairs={{0,2},{4,0},{8,4},{12,8},{16,12},{20,16},{24,20},{28,24},{30,28},{... | collective-permute-start | bytes 3145736 | tf_op jit(solution)/shard_map/ppermute | solution.py:32
  799.1 82.6 %collective-permute-start.27 = (bf16[256,2048]{1,0:T(8,128)(2,1)}, bf16[256,2048]{1,0:T(8,128)(2,1)S(1)}, u32[]{:S(2)}, u32[]{:S(2)}) collective-permute-start(bf16[256,2048]{1,0:T(8,128)(2,1)} %collective-permute-done.26), channel_id=1, source_target_pairs={{0,4},{4,8},{8,12},{12,16},{16,20},{20,24},{24,28},{28,30},{30,26}... | collective-permute-start | bytes 3145736 | tf_op jit(solution)/shard_map/ppermute | solution.py:29
  852.8 48.0 %collective-permute-start.35 = (bf16[256,2048]{1,0:T(8,128)(2,1)S(1)}, bf16[256,2048]{1,0:T(8,128)(2,1)}, u32[]{:S(2)}, u32[]{:S(2)}) collective-permute-start(bf16[256,2048]{1,0:T(8,128)(2,1)S(1)} %collective-permute-done.34), channel_id=1, source_target_pairs={{0,2},{4,0},{8,4},{12,8},{16,12},{20,16},{24,20},{28,24},{30,28},{... | collective-permute-start | bytes 3145736 | tf_op jit(solution)/shard_map/ppermute | solution.py:32
  881.7 45.5 %collective-permute-start.28 = (bf16[256,2048]{1,0:T(8,128)(2,1)S(1)}, bf16[256,2048]{1,0:T(8,128)(2,1)}, u32[]{:S(2)}, u32[]{:S(2)}) collective-permute-start(bf16[256,2048]{1,0:T(8,128)(2,1)S(1)} %collective-permute-done.27), channel_id=1, source_target_pairs={{0,4},{4,8},{8,12},{12,16},{16,20},{20,24},{24,28},{28,30},{30,26}... | collective-permute-start | bytes 3145736 | tf_op jit(solution)/shard_map/ppermute | solution.py:29
  884.1 46.1 %copy-start = (bf16[3,256,2,16,64]{1,0,4,3,2:T(4,128)(2,1)S(1)}, bf16[3,256,2,16,64]{1,0,4,3,2:T(4,128)(2,1)}, u32[]{:S(2)}) copy-start(bf16[3,256,2,16,64]{1,0,4,3,2:T(4,128)(2,1)} %reshape.321) | copy-start | bytes 9437188
  884.1 46.1 %copy-start.11 = (f32[3,2,16,64,128]{4,3,2,1,0:T(8,128)S(1)}, f32[3,2,16,64,128]{4,3,2,1,0:T(8,128)}, u32[]{:S(2)}) copy-start(f32[3,2,16,64,128]{4,3,2,1,0:T(8,128)} %get-tuple-element.49) | copy-start | bytes 9437188
  884.1 46.1 %copy-start.17 = (f32[3,256,2,16]{1,3,2,0:T(8,128)S(1)}, f32[3,256,2,16]{1,3,2,0:T(8,128)}, u32[]{:S(2)}) copy-start(f32[3,256,2,16]{1,3,2,0:T(8,128)} %copy.276) | copy-start | bytes 294916
  884.1 46.1 %copy-start.18 = (f32[3,256,2,16]{1,3,2,0:T(8,128)S(1)}, f32[3,256,2,16]{1,3,2,0:T(8,128)}, u32[]{:S(2)}) copy-start(f32[3,256,2,16]{1,3,2,0:T(8,128)} %copy.281) | copy-start | bytes 294916
  900.8 67.2 %collective-permute-start.36 = (bf16[256,2048]{1,0:T(8,128)(2,1)}, bf16[256,2048]{1,0:T(8,128)(2,1)S(1)}, u32[]{:S(2)}, u32[]{:S(2)}) collective-permute-start(bf16[256,2048]{1,0:T(8,128)(2,1)} %collective-permute-done.35), channel_id=1, source_target_pairs={{0,2},{4,0},{8,4},{12,8},{16,12},{20,16},{24,20},{28,24},{30,28},{... | collective-permute-start | bytes 3145736 | tf_op jit(solution)/shard_map/ppermute | solution.py:32
  927.2 37.8 %collective-permute-start.29 = (bf16[256,2048]{1,0:T(8,128)(2,1)}, bf16[256,2048]{1,0:T(8,128)(2,1)S(1)}, u32[]{:S(2)}, u32[]{:S(2)}) collective-permute-start(bf16[256,2048]{1,0:T(8,128)(2,1)} %collective-permute-done.28), channel_id=1, source_target_pairs={{0,4},{4,8},{8,12},{12,16},{16,20},{20,24},{24,28},{28,30},{30,26}... | collective-permute-start | bytes 3145736 | tf_op jit(solution)/shard_map/ppermute | solution.py:29
  962.6 34.8 %copy-start.15 = (bf16[256,2048]{1,0:T(8,128)(2,1)S(1)}, bf16[256,2048]{1,0:T(8,128)(2,1)}, u32[]{:S(2)}) copy-start(bf16[256,2048]{1,0:T(8,128)(2,1)} %copy-done.14) | copy-start | bytes 3145732
  965.0 43.3 %collective-permute-start.30 = (bf16[256,2048]{1,0:T(8,128)(2,1)S(1)}, bf16[256,2048]{1,0:T(8,128)(2,1)S(1)}, u32[]{:S(2)}, u32[]{:S(2)}) collective-permute-start(bf16[256,2048]{1,0:T(8,128)(2,1)S(1)} %collective-permute-done.29), channel_id=1, source_target_pairs={{0,4},{4,8},{8,12},{12,16},{16,20},{20,24},{24,28},{28,30},{30,26}... | collective-permute-start | bytes 3145736 | tf_op jit(solution)/shard_map/ppermute | solution.py:29
  968.0 48.3 %collective-permute-start.37 = (bf16[256,2048]{1,0:T(8,128)(2,1)S(1)}, bf16[256,2048]{1,0:T(8,128)(2,1)S(1)}, u32[]{:S(2)}, u32[]{:S(2)}) collective-permute-start(bf16[256,2048]{1,0:T(8,128)(2,1)S(1)} %collective-permute-done.36), channel_id=1, source_target_pairs={{0,2},{4,0},{8,4},{12,8},{16,12},{20,16},{24,20},{28,24},{30,28},{... | collective-permute-start | bytes 3145736 | tf_op jit(solution)/shard_map/ppermute | solution.py:32
  1085.4 10.5 collective-permute-start.38
  (40 other events, 647.2 us)
Sparse Core Ops, SparseCore 0:
  20.5 375.6 all-gather.1

commit v3 on v1

--- a/solution.py
+++ b/solution.py
@@ -122,6 +122,19 @@
     return (direct, state_gain, update, span_decay)
 
 
+def swap_half(value):
+    count = lax.axis_size("half")
+    return lax.ppermute(value, "half", [(k, count - 1 - k) for k in range(count)])
+
+
+def ordered_pair(own, other, half, axis):
+    return jnp.where(
+        half == 0,
+        jnp.concatenate([own, other], axis=axis),
+        jnp.concatenate([other, own], axis=axis),
+    )
+
+
 def body(
     tokens,
     norm_gain,
@@ -142,38 +155,98 @@
     carry_conv_x,
     carry_conv_bc,
 ):
-    row_count = tokens.shape[0]
+    own_rows = tokens.shape[0]
+    row_count = 2 * own_rows
     edge_rows = conv_x.shape[0] - 1
-    inner_local = w_zx.shape[2]
-    state_cols = w_bc.shape[2]
-    head_local = w_dt.shape[1]
     head_width = carry_state.shape[1]
     state_width = carry_state.shape[2]
-    group_local = state_cols // state_width
-    per_group = head_local // group_local
+    head_fsdp = w_dt.shape[1]
+    group_fsdp = w_bc.shape[2] // state_width
+    per_group = head_fsdp // group_fsdp
+    head_local = head_fsdp // 2
+    group_local = max(1, head_local // per_group)
+    per_local = min(per_group, head_local)
+    inner_local = head_local * head_width
+    state_cols = group_local * state_width
     span_count = row_count // SPAN
-    position = lax.axis_index("seq") * row_count + jnp.arange(row_count, dtype=jnp.int32)
-    segment, seg_start, resume_slot, resume_start = layout(
-        prompt_lengths, pack_order, resume_prompt, position
-    )
-    normed = norm_rows(tokens, norm_gain)
-    first_local = jnp.concatenate(
-        [w_zx[:, 1], w_bc.reshape(w_bc.shape[0], 2 * state_cols), w_dt], axis=1
-    )
-    first_full = lax.all_gather(first_local, "seq", axis=0, tiled=True)
+    half = lax.axis_index("half")
+    core = lax.axis_index("fsdp")
+    core_count = lax.axis_size("fsdp")
+    x_off = half * inner_local
+    bc_off = (half * head_local) // per_group * state_width
+    h_off = half * head_local
+
+    def cut(value, axis, offset, width):
+        return lax.dynamic_slice_in_dim(value, offset, width, axis)
+
+    normed_own = norm_rows(tokens, norm_gain)
+    share = own_rows // core_count
+    fetched = swap_half(cut(normed_own, 0, core * share, share))
+    normed_other = lax.all_gather(fetched, "fsdp", axis=0, tiled=True)
+    normed = ordered_pair(normed_own, normed_other, half, 0)
+
+    def first_cols(offset_x, offset_bc, offset_h):
+        return jnp.concatenate(
+            [
+                cut(w_zx[:, 1], 1, offset_x, inner_local),
+                cut(w_bc[:, 0], 1, offset_bc, state_cols),
+                cut(w_bc[:, 1], 1, offset_bc, state_cols),
+                cut(w_dt, 1, offset_h, head_local),
+            ],
+            axis=1,
+        )
+
+    other = 1 - half
+    first_mine = first_cols(x_off, bc_off, h_off)
+    first_theirs = swap_half(
+        first_cols(other * inner_local, (other * head_local) // per_group * state_width, other * head_local)
+    )
+    first_local = ordered_pair(first_mine, first_theirs, half, 0)
+    first_full = lax.all_gather(first_local, "pair", axis=0, tiled=True)
     proj_first = jnp.dot(normed, first_full, preferred_element_type=jnp.float32).astype(
         jnp.bfloat16
     )
     conv_width = inner_local + 2 * state_cols
     conv_in = proj_first[:, :conv_width]
     proj_dt = proj_first[:, conv_width:]
-    z_local, out_local, _ = lax.optimization_barrier((w_zx[:, 0], w_out, proj_first))
-    z_full = lax.all_gather(z_local, "seq", axis=0, tiled=True)
-    out_full = lax.all_gather(out_local, "seq", axis=1, tiled=True)
+    w_z_all, w_out_all, _ = lax.optimization_barrier((w_zx[:, 0], w_out, proj_first))
+    z_local = ordered_pair(
+        cut(w_z_all, 1, x_off, inner_local),
+        swap_half(cut(w_z_all, 1, other * inner_local, inner_local)),
+        half,
+        0,
+    )
+    out_local = ordered_pair(
+        cut(w_out_all, 0, x_off, inner_local),
+        swap_half(cut(w_out_all, 0, other * inner_local, inner_local)),
+        half,
+        1,
+    )
+    z_full = lax.all_gather(z_local, "pair", axis=0, tiled=True)
+    out_full = lax.all_gather(out_local, "pair", axis=1, tiled=True)
     proj_z = jnp.dot(normed, z_full, preferred_element_type=jnp.float32).astype(jnp.bfloat16)
-    prior_rows = from_behind(conv_in[row_count - edge_rows :], "seq", 1)
-    weight = jnp.concatenate([conv_x, conv_bc[:, 0], conv_bc[:, 1]], axis=1)
-    carry_rows = jnp.concatenate([carry_conv_x, carry_conv_bc[:, 0], carry_conv_bc[:, 1]], axis=1)
+
+    position = lax.axis_index("pair") * row_count + jnp.arange(row_count, dtype=jnp.int32)
+    segment, seg_start, resume_slot, resume_start = layout(
+        prompt_lengths, pack_order, resume_prompt, position
+    )
+    prior_rows = from_behind(conv_in[row_count - edge_rows :], "pair", 1)
+    weight = jnp.concatenate(
+        [
+            cut(conv_x, 1, x_off, inner_local),
+            cut(conv_bc[:, 0], 1, bc_off, state_cols),
+            cut(conv_bc[:, 1], 1, bc_off, state_cols),
+        ],
+        axis=1,
+    )
+    carry_rows = jnp.concatenate(
+        [
+            cut(carry_conv_x, 1, x_off, inner_local),
+            cut(carry_conv_bc[:, 0], 1, bc_off, state_cols),
+            cut(carry_conv_bc[:, 1], 1, bc_off, state_cols),
+        ],
+        axis=1,
+    )
     conv_out = conv_rows(
         conv_in,
         prior_rows,
@@ -185,23 +258,25 @@
         resume_slot,
         resume_start,
     )
-    x_conv = conv_out[:, :inner_local].reshape(span_count, SPAN, group_local, per_group, head_width)
+    x_conv = conv_out[:, :inner_local].reshape(span_count, SPAN, group_local, per_local, head_width)
     b_conv = conv_out[:, inner_local : inner_local + state_cols].reshape(
         span_count, SPAN, group_local, state_width
     )
     c_conv = conv_out[:, inner_local + state_cols :].reshape(
         span_count, SPAN, group_local, state_width
     )
-    dt_full = jax.nn.softplus(proj_dt.astype(jnp.float32) + dt_bias[None, :]).reshape(
-        span_count, SPAN, group_local, per_group
-    )
+    dt_full = jax.nn.softplus(
+        proj_dt.astype(jnp.float32) + cut(dt_bias, 0, h_off, head_local)[None, :]
+    ).reshape(span_count, SPAN, group_local, per_local)
     seg_blocks = segment.reshape(span_count, SPAN)
     starting = (position == seg_start).reshape(span_count, SPAN)
     resumed = (segment == resume_slot).reshape(span_count, SPAN)
     resume_hit = (position == resume_start).reshape(span_count, SPAN)
-    head_rate = decay_rate.reshape(group_local, per_group)
-    skip_gain = d_skip.reshape(group_local, per_group)
-    carry_init = carry_state.reshape(group_local, per_group, head_width, state_width)
+    head_rate = cut(decay_rate, 0, h_off, head_local).reshape(group_local, per_local)
+    skip_gain = cut(d_skip, 0, h_off, head_local).reshape(group_local, per_local)
+    carry_init = cut(carry_state, 0, h_off, head_local).reshape(
+        group_local, per_local, head_width, state_width
+    )
     direct, state_gain, update, span_decay = span_pieces(
         x_conv,
         b_conv,
@@ -222,16 +297,16 @@
             carried,
         )
 
-    empty_state = jnp.zeros((group_local, per_group, head_width, state_width), jnp.float32)
-    unit_decay = jnp.ones((group_local, per_group), jnp.float32)
+    empty_state = jnp.zeros((group_local, per_local, head_width, state_width), jnp.float32)
+    unit_decay = jnp.ones((group_local, per_local), jnp.float32)
     (local_state, local_decay), (prefix_state, prefix_decay) = lax.scan(
         fold_span, (empty_state, unit_decay), (update, span_decay)
     )
-    hop_count = lax.axis_size("seq") // 4
+    hop_count = max(1, lax.axis_size("pair") // 4)
     incoming = jnp.zeros_like(local_state)
     reach = jnp.ones_like(local_decay)
     for steps in range(1, hop_count + 1):
-        state_back, decay_back = from_behind((local_state, local_decay), "seq", steps)
+        state_back, decay_back = from_behind((local_state, local_decay), "pair", steps)
         incoming = incoming + reach[..., None, None] * state_back
         reach = reach * decay_back
     entering = prefix_decay[..., None, None] * incoming[None] + prefix_state
@@ -239,42 +314,50 @@
     ssd_out = (direct + state_gain[..., None] * from_state).reshape(row_count, inner_local)
     gate_act = jax.nn.silu(proj_z.astype(jnp.float32))
     gated = (ssd_out * gate_act).reshape(row_count, group_local, inner_local // group_local)
-    factor = lax.rsqrt(jnp.mean(gated * gated, axis=-1, keepdims=True) + EPS)
-    normed_y = ((gated * factor).reshape(row_count, inner_local) * gated_gain[None, :]).astype(
-        jnp.bfloat16
-    )
-    core_count = lax.axis_size("fsdp")
-    piece = row_count // core_count
-    core = lax.axis_index("fsdp")
+    squares = jnp.sum(gated * gated, axis=-1, keepdims=True)
+    if head_local < per_group:
+        squares = lax.psum(squares, "half")
+    factor = lax.rsqrt(squares / (per_group * head_width) + EPS)
+    normed_y = (
+        (gated * factor).reshape(row_count, inner_local) * cut(gated_gain, 0, x_off, inner_local)[None, :]
+    ).astype(jnp.bfloat16)
+    piece = own_rows // core_count
+    by_owner = normed_y.reshape(2, core_count, piece, inner_local)
     total = None
     for shift in list(range(1, core_count)) + [0]:
-        rows = lax.dynamic_slice_in_dim(normed_y, (core + shift) % core_count * piece, piece, 0)
-        part = jnp.dot(rows, out_full, preferred_element_type=jnp.float32)
+        rows = lax.dynamic_index_in_dim(by_owner, (core + shift) % core_count, 1, keepdims=False)
+        part = jnp.einsum("hrc,cd->hrd", rows, out_full, preferred_element_type=jnp.float32)
         if shift:
             part = lax.ppermute(
                 part, "fsdp", [(j, (j + shift) % core_count) for j in range(core_count)]
             )
         total = part if total is None else total + part
-    return total.astype(jnp.bfloat16)
+    mine = lax.dynamic_index_in_dim(total, half, 0, keepdims=False)
+    theirs = swap_half(lax.dynamic_index_in_dim(total, 1 - half, 0, keepdims=False))
+    return (mine + theirs).astype(jnp.bfloat16)
 
 
 def solution(mesh):
+    seq_count = mesh.shape["seq"]
+    devices = mesh.devices.reshape(seq_count // 2, 2, mesh.shape["fsdp"])
+    paired = jax.sharding.Mesh(devices, ("pair", "half", "fsdp"))
+    seq = ("pair", "half")
     return jax.shard_map(
         body,
-        mesh=mesh,
+        mesh=paired,
         in_specs=(
-            P("seq", None),
+            P(seq, None),
             P(),
-            P("seq", None, "fsdp"),
-            P("seq", None, "fsdp"),
-            P("seq", "fsdp"),
+            P(seq, None, "fsdp"),
+            P(seq, None, "fsdp"),
+            P(seq, "fsdp"),
             P(None, "fsdp"),
             P(None, None, "fsdp"),
             P("fsdp"),
             P("fsdp"),
             P("fsdp"),
             P("fsdp"),
-            P("fsdp", "seq"),
+            P("fsdp", seq),
             P(),
             P(),
             P(),
@@ -282,6 +365,6 @@
             P(None, "fsdp"),
             P(None, None, "fsdp"),
         ),
-        out_specs=P(("seq", "fsdp"), None),
+        out_specs=P(("pair", "half", "fsdp"), None),
         check_vma=False,
     )

time: 843 us -> 809 us (0.960)
  waiting for transfers between devices: 558 us -> 473 us
  other arithmetic: 62.7 us -> 97 us
  starting transfers between devices: 25.6 us -> 37 us
    all_gather x3 -> x4, waiting for transfers between devices: 492 us -> 231 us  [the longest x1 155 us: body(): first_full = lax.all_gather(first_local, 'pair', axis=0, tiled=True)]
    ppermute x0 -> x5, waiting for transfers between devices: none -> 222 us  [swap_half(): lax.ppermute(value, 'half', [(k, count - 1 - k) for k in range(count)])]
    ppermute x8 -> x4, waiting for transfers between devices: 54.9 us -> 0.01 us  [from_behind(): lax.ppermute(value, axis, [(source, source + steps) for source in range(l...]
    convert_element_type x1 -> x4, other arithmetic: 6.02 us -> 18.3 us  [the longest x1 7.1 us: body(): return (mine + theirs).astype(jnp.bfloat16)]
    mul x5 -> x8, local copies, waits for them, and re-layouts: 11.2 us -> 0.74 us  [the longest x1 0.67 us: span_pieces(): weights = (scores[:, :, None] * decays * dt_source).astype(jnp.bfloat16)]
    reshape x4 -> x1, local copies, waits for them, and re-layouts: 9.7 us -> 0.03 us  [body(): dt_full = jax.nn.softplus(proj_dt.astype(jnp.float32) + cut(dt_bias, 0, h...]
    ppermute x0 -> x5, starting transfers between devices: none -> 9.27 us  [swap_half(): lax.ppermute(value, 'half', [(k, count - 1 - k) for k in range(count)])]
    ppermute x1, waiting for transfers between devices: 10.5 us -> 19.5 us  [body(): lax.ppermute(part, 'fsdp', [(j, (j + shift) % core_count) for j in range(...]
  transfers between devices with their start and end apart: 12 -> 14, of which waited for: 5 -> 7; matrix products, arithmetic and copies ran while one was open for 21% -> 25% of each run, Pallas kernels for 0% -> 0%
where the time goes in v3:
time: 809 us; the launch traced here: 803 us
  waiting for transfers between devices  473 us (58%)
  matrix products  106 us (13%)
  other arithmetic  97 us (12%)
  local copies, waits for them, and re-layouts  75.8 us (9%)
  starting transfers between devices  37 us (5%)
  between operations  15 us (2%)
    ppermute x5, waiting for transfers between devices, swap_half(): lax.ppermute(value, 'half', [(k, count - 1 - k) for k in range(count)])  222 us
    all_gather x1, waiting for transfers between devices, body(): first_full = lax.all_gather(first_local, 'pair', axis=0, tiled=True)  155 us
    all_gather x1, waiting for transfers between devices, body(): out_full = lax.all_gather(out_local, 'pair', axis=1, tiled=True)  75.4 us
    dot_general x1, matrix products, body(): jnp.dot(normed, z_full, preferred_element_type=jnp.float32)  27 us
    ppermute x4, starting transfers between devices, from_behind(): lax.ppermute(value, axis, [(source, source + steps) for source in range(l...  26.8 us
    dot_general x1, matrix products, body(): jnp.dot(normed, first_full, preferred_element_type=jnp.float32)  23.8 us
    dot_general x2, matrix products, body(): jnp.einsum('hrc,cd->hrd', rows, out_full, preferred_element_type=jnp.floa...  23.5 us
    reshape x2, local copies, waits for them, and re-layouts, body(): (direct + state_gain[..., None] * from_state).reshape(row_count, inner_lo...  23.1 us
  transfers between devices with their start and end apart: 14, of which 7 were waited for; matrix products, arithmetic and copies ran while one was open for 25% of the time, Pallas kernels for 0%

profile of v3, /device:TPU:0, one launch (start us, length us, event | category | flops | bytes accessed | tf_op | source)
XLA Modules:
  0.0 803.5 jit_solution(13390834283542198737)
XLA Ops:
  6.5 4.2 fusion.3
  10.7 5.3 fusion.5
  16.1 2.6 copy-done.4
  19.1 3.0 collective-permute-start
  22.1 68.2 %collective-permute-done = bf16[384,4096]{1,0:T(8,128)(2,1)} collective-permute-done((bf16[384,4096]{1,0:T(8,128)(2,1)S(1)}, bf16[384,4096]{1,0:T(8,128)(2,1)}, u32[]{:S(2)}, u32[]{:S(2)}) %collective-permute-start) | collective-permute-done | bytes 3145760 | tf_op jit(solution)/shard_map/ppermute | solution.py:127
  91.1 1.3 constant_dynamic-slice_fusion.17
  92.5 3.8 fusion.91
  96.3 2.2 constant_dynamic-slice_fusion.19
  99.1 1.8 collective-permute-start.1
  103.1 12.3 %collective-permute-done.1 = bf16[256,1296]{0,1:T(8,128)(2,1)} collective-permute-done((bf16[256,1296]{0,1:T(8,128)(2,1)S(1)}, bf16[256,1296]{0,1:T(8,128)(2,1)}, u32[]{:S(2)}, u32[]{:S(2)}) %collective-permute-start.1) | collective-permute-done | bytes 663584 | tf_op jit(solution)/shard_map/ppermute | solution.py:127
  115.3 1.4 copy.202
  116.8 5.3 maximum_select_fusion.3
  124.5 1.4 fusion.83
  126.2 1.8 reduce-window.30
  129.2 2.4 copy.282
  131.6 155.5 %all-gather.7.cloned.1.call-done = bf16[4096,1296]{1,0:T(8,128)(2,1)} async-done(((bf16[512,1296]{1,0:T(8,128)(2,1)}), bf16[4096,1296]{1,0:T(8,128)(2,1)}) %all-gather.7.cloned.1.call-update) | async-done | bytes 10616848 | tf_op jit(solution)/shard_map/all_gather | solution.py:205
  287.1 23.8 %convolution_convert_fusion = bf16[1536,1296]{0,1:T(8,128)(2,1)} fusion(bf16[4096,1296]{1,0:T(8,128)(2,1)} %all-gather.7.cloned.1.call-done, bf16[768,4096]{1,0:T(8,128)(2,1)} %all-gather.5.cloned.1.call-done, bf16[768,4096]{1,0:T(8,128)(2,1)} %copy-done.4, pred[]{:T(512)S(6)} %eq.200), kind=kOutput, calls=%fused_computation.30 | convolution fusion | flops 16366067712 | bytes 27181056 | tf_op jit(solution)/shard_map/dot_general | solution.py:206
  311.0 1.5 collective-permute-start.6
  312.5 1.3 fusion.59
  313.8 1.3 fusion.67
  315.1 1.3 fusion.57
  316.4 1.3 fusion.61
  317.7 1.3 fusion.65
  319.0 5.3 collective-permute-done.6
  324.3 1.5 maximum_select_fusion.4
  326.7 1.3 fusion.69
  328.6 1.2 broadcast_compare_fusion.1
  331.5 1.9 slice.145
  334.5 3.4 reduce-window.21
  338.6 2.6 collective-permute-start.2
  342.3 1.3 constant_dynamic-slice_fusion.2
  344.7 4.3 slice.140
  349.9 1.5 collective-permute-start.7
  352.0 21.4 %multiply_convert_fusion.3 = bf16[1536,1280]{0,1:T(8,128)(2,1)S(1)} fusion(bf16[1536,1280]{0,1:T(8,128)(2,1)} %slice.140, bf16[3,1280]{0,1:T(8,128)(2,1)S(1)} %collective-permute-done.2, f32[1280]{0:T(1024)S(1)} %get-tuple-element.132, f32[1280]{0:T(1024)S(1)} %get-tuple-element.133, f32[1280]{0:T(1024)S(1)} %get-tuple-element.134, ...), kind=kLoop, calls=%fused_computation.28 | loop fusion | flops 104202240 | bytes 7933952 | tf_op jit(solution)/shard_map/convert_element_type | solution.py:68
  373.5 4.9 fusion.89
  378.4 1.3 maximum_select_fusion.5
  379.7 1.2 fusion.90
  380.9 7.6 reshape.519
  388.7 3.2 multiply_convert_fusion.2
  391.9 2.7 add_bitcast_fusion
  394.6 12.5 %while.17 = (s32[]{:T(128)}, f32[1,16,64,128]{3,2,1,0:T(8,128)S(1)}, f32[1,16]{1,0:T(1,128)S(1)}, f32[6,1,16,64,128]{4,3,2,1,0:T(8,128)}, f32[6,1,16]{2,0,1:T(8,...) while((s32[]{:T(128)}, ...), condition=%wide.region_15.16_spmd.clone, body=%wide.region_14.15_spmd.clone.sunk | while | flops 524323 | bytes 2622649 | solution.py:302
  407.1 7.0 collective-permute-start.3
  414.0 11.5 %collective-permute-start.5 = (f32[1,16,64,128]{3,2,1,0:T(8,128)S(1)}, f32[1,16,64,128]{3,2,1,0:T(8,128)}, u32[]{:S(2)}, u32[]{:S(2)}) collective-permute-start(f32[1,16,64,128]{3,2,1,0:T(8,128)S(1)} %get-tuple-element.48), channel_id=1, source_target_pairs={{0,8},{4,12},{8,16},{12,20},{16,24},{20,28},{1,9},{5,13},{9,17},{1... | collective-permute-start | bytes 1572872 | tf_op jit(solution)/shard_map/ppermute | solution.py:15
  425.5 5.8 collective-permute-start.4
  431.5 1.5 fusion.95
  433.0 5.2 fusion.45
  438.3 8.8 %reshape.541 = f32[6,256,1,16,64]{1,0,4,3,2:T(8,128)} reshape(f32[1536,1024]{0,1:T(8,128)} %get-tuple-element.158) | data formatting | bytes 12582912 | tf_op jit(solution)/shard_map/convert_element_type | solution.py:119
  447.1 1.5 add_bitcast_fusion.1
  448.6 5.4 fusion.28
  454.0 16.6 %fusion.24 = f32[6,256,1,16,64]{1,4,3,0,2:T(8,128)} fusion(f32[6,256,1,16,64]{1,0,4,3,2:T(8,128)} %reshape.541, f32[6,256,16,64]{1,3,2,0:T(8,128)S(1)} %fusion.28, f32[6,256,16,64]{1,3,2,0:T(8,128)S(1)} %copy-done.7, f32[6,256,16]{1,2,0:T(8,128)S(1)} %copy-done.12, f32[16]{0:T(128)S(1)} %copy-done.31, f32[6,256,16]{1,2,0:T(8,128)S(1)} %copy-done.11, ...), kind=kOutput, calls=%fused_computation.37 | convolution fusion | flops 852492288 | bytes 30670912 | tf_op jit(solution)/shard_map/cghqs,csghp->cqghp/dot_general | solution.py:20
  470.7 11.3 %copy.227 = f32[6,256,1,16,64]{4,3,1,0,2:T(8,128)} copy(f32[6,256,1,16,64]{1,4,3,0,2:T(8,128)} %fusion.24) | data formatting | bytes 12582912 | tf_op jit(solution)/shard_map/reshape | solution.py:314
  481.9 11.8 %reshape.546 = f32[1536,1024]{1,0:T(8,128)} reshape(f32[6,256,1,16,64]{4,3,1,0,2:T(8,128)} %copy.227) | data formatting | bytes 12582912 | tf_op jit(solution)/shard_map/reshape | solution.py:314
  493.8 27.0 %multiply_reduce_fusion = (f32[1536]{0:T(1024)S(1)}, f32[1536,1024]{1,0:T(8,128)}) fusion(f32[1536,1024]{1,0:T(8,128)} %reshape.546, bf16[4096,1024]{1,0:T(8,128)(2,1)} %all-gather.9.cloned.1.call-done, bf16[768,4096]{1,0:T(8,128)(2,1)} %all-gather.5.cloned.1.call-done, bf16[768,4096]{1,0:T(8,128)(2,1)} %copy-done.4, pred[]{:T(512)S(6)} %eq.200), kind=kOutput, calls=%fused_computation.43 | convolution fusion | flops 12955678720 | bytes 33560576 | tf_op jit(solution)/shard_map/dot_general | solution.py:227
  520.8 3.3 broadcast_multiply_fusion
  524.1 2.6 multiply_convert_fusion.4
  526.7 75.4 %all-gather.11.cloned.1.call-done = bf16[1024,4096]{1,0:T(8,128)(2,1)} async-done(((bf16[1024,512]{1,0:T(8,128)(2,1)}), bf16[1024,4096]{1,0:T(8,128)(2,1)}) %all-gather.11.cloned.1.call-update) | async-done | bytes 8388624 | tf_op jit(solution)/shard_map/all_gather | solution.py:226
  602.2 12.2 %fusion.14 = f32[2,384,4096]{2,1,0:T(8,128)} fusion(bf16[1024,4096]{1,0:T(8,128)(2,1)} %all-gather.11.cloned.1.call-done, bf16[2,2,384,1024]{3,2,1,0:T(8,128)(2,1)} %multiply_convert_fusion.4, s32[]{:T(128)S(6)} %select_n.278), kind=kOutput, calls=%fused_computation.23 | convolution fusion | flops 6442450944 | bytes 22544388 | tf_op jit(solution)/shard_map/hrc,cd->hrd/dot_general | solution.py:329
  614.3 19.5 %collective-permute-done.8 = f32[2,384,4096]{2,1,0:T(8,128)} collective-permute-done((f32[2,384,4096]{2,1,0:T(8,128)}, f32[2,384,4096]{2,1,0:T(8,128)}, u32[]{:S(2)}, u32[]{:S(2)}) %collective-permute-start.8) | collective-permute-done | bytes 12582944 | tf_op jit(solution)/shard_map/ppermute | solution.py:331
  633.8 11.4 %fusion.16 = f32[2,384,4096]{2,1,0:T(8,128)S(1)} fusion(f32[2,384,4096]{2,1,0:T(8,128)} %collective-permute-done.8, bf16[1024,4096]{1,0:T(8,128)(2,1)} %all-gather.11.cloned.1.call-done, bf16[2,2,384,1024]{3,2,1,0:T(8,128)(2,1)} %multiply_convert_fusion.4, s32[]{:T(128)S(6)} %select_n.282), kind=kOutput, calls=%fused_computation.29 | convolution fusion | flops 6445596672 | bytes 35127300 | tf_op jit(solution)/shard_map/hrc,cd->hrd/dot_general | solution.py:329
  645.2 3.3 dynamic-slice_bitcast_fusion
  648.5 3.2 copy-done.5
  651.7 1.5 collective-permute-start.9
  653.2 136.4 %collective-permute-done.9 = f32[384,4096]{1,0:T(8,128)} collective-permute-done((f32[384,4096]{1,0:T(8,128)}, f32[384,4096]{1,0:T(8,128)}, u32[]{:S(2)}, u32[]{:S(2)}) %collective-permute-start.9) | collective-permute-done | bytes 6291488 | tf_op jit(solution)/shard_map/ppermute | solution.py:127
  789.6 7.1 fusion.25
  (199 shorter events, 28.4 us)
Async XLA Ops:
  6.5 322.0 %copy-start = (f32[32,64,128]{2,1,0:T(8,128)S(1)}, f32[32,64,128]{2,1,0:T(8,128)}, u32[]{:S(2)}) copy-start(f32[32,64,128]{2,1,0:T(8,128)} %param.35) | copy-start | bytes 3145732
  6.5 4.2 copy-start.14
  6.5 125.1 %all-gather.5.cloned.1.call-start = ((), (), s32[]{:S(2)}) async-start(), calls=%async_computation | async-start | bytes 9437184 | tf_op jit(solution)/shard_map/all_gather | solution.py:185
  16.1 2.7 copy-start.4
  18.7 72.0 %copy-start.9 = (bf16[256,2,256]{2,1,0:T(2,128)(2,1)S(1)}, bf16[256,2,256]{2,1,0:T(2,128)(2,1)}, u32[]{:S(2)}) copy-start(bf16[256,2,256]{2,1,0:T(2,128)(2,1)} %param.23) | copy-start | bytes 786436
  18.7 73.7 %copy-start.15 = (bf16[256,32]{0,1:T(8,128)(2,1)S(1)}, bf16[256,32]{0,1:T(8,128)(2,1)}, u32[]{:S(2)}) copy-start(bf16[256,32]{0,1:T(8,128)(2,1)} %param.24) | copy-start | bytes 49156
  18.7 73.8 %copy-start.6 = (bf16[256,2,2048]{2,1,0:T(2,128)(2,1)S(1)}, bf16[256,2,2048]{2,1,0:T(2,128)(2,1)}, u32[]{:S(2)}) copy-start(bf16[256,2,2048]{2,1,0:T(2,128)(2,1)} %param.22) | copy-start | bytes 6291460
  19.1 71.2 %collective-permute-start = (bf16[384,4096]{1,0:T(8,128)(2,1)S(1)}, bf16[384,4096]{1,0:T(8,128)(2,1)}, u32[]{:S(2)}, u32[]{:S(2)}) collective-permute-start(bf16[384,4096]{1,0:T(8,128)(2,1)S(1)} %constant_dynamic-slice_fusion.20), channel_id=1, source_target_pairs={{0,2},{2,0},{1,3},{3,1},{4,6},{6,4},{5,7},{7,5},{8,10},{10,8},{9,1... | collective-permute-start | bytes 9437192 | tf_op jit(solution)/shard_map/ppermute | solution.py:127
  90.3 196.8 %all-gather.7.cloned.1.call-start = ((), (), s32[]{:S(2)}) async-start(), calls=%async_computation.1 | async-start | bytes 12976128 | tf_op jit(solution)/shard_map/all_gather | solution.py:205
  98.5 24.9 %copy-start.26 = (s32[8]{0:T(128)S(1)}, s32[8]{0:T(128)}, u32[]{:S(2)}) copy-start(s32[8]{0:T(128)} %param.32) | copy-start | bytes 100
  98.5 24.9 %copy-start.27 = (s32[8]{0:T(128)S(1)}, s32[8]{0:T(128)}, u32[]{:S(2)}) copy-start(s32[8]{0:T(128)} %param.33) | copy-start | bytes 100
  98.5 27.5 %copy-start.28 = (f32[32]{0:T(128)S(1)}, f32[32]{0:T(128)}, u32[]{:S(2)}) copy-start(f32[32]{0:T(128)} %param.27) | copy-start | bytes 388
  98.5 27.6 %copy-start.29 = (f32[32]{0:T(128)S(1)}, f32[32]{0:T(128)}, u32[]{:S(2)}) copy-start(f32[32]{0:T(128)} %param.28) | copy-start | bytes 388
  98.5 30.0 %copy-start.16 = (bf16[4,2,256]{2,1,0:T(2,128)(2,1)S(1)}, bf16[4,2,256]{2,1,0:T(2,128)(2,1)}, u32[]{:S(2)}) copy-start(bf16[4,2,256]{2,1,0:T(2,128)(2,1)} %param.26) | copy-start | bytes 12292
  98.6 30.0 %copy-start.17 = (bf16[3,2,256]{2,1,0:T(2,128)(2,1)S(1)}, bf16[3,2,256]{2,1,0:T(2,128)(2,1)}, u32[]{:S(2)}) copy-start(bf16[3,2,256]{2,1,0:T(2,128)(2,1)} %param.37) | copy-start | bytes 9220
  98.6 30.1 %copy-start.30 = (f32[32]{0:T(128)S(1)}, f32[32]{0:T(128)}, u32[]{:S(2)}) copy-start(f32[32]{0:T(128)} %param.29) | copy-start | bytes 388
  99.1 16.3 %collective-permute-start.1 = (bf16[256,1296]{0,1:T(8,128)(2,1)S(1)}, bf16[256,1296]{0,1:T(8,128)(2,1)}, u32[]{:S(2)}, u32[]{:S(2)}) collective-permute-start(bf16[256,1296]{0,1:T(8,128)(2,1)S(1)} %copy.201), channel_id=1, source_target_pairs={{0,2},{2,0},{1,3},{3,1},{4,6},{6,4},{5,7},{7,5},{8,10},{10,8},{9,1... | collective-permute-start | bytes 1990664 | tf_op jit(solution)/shard_map/ppermute | solution.py:127
  122.1 371.6 %all-gather.9.cloned.1.call-start = ((), (), s32[]{:S(2)}) async-start(), calls=%async_computation.2 | async-start | bytes 9437184 | tf_op jit(solution)/shard_map/all_gather | solution.py:225
  131.6 196.6 %copy-start.24 = (bf16[4,2048]{1,0:T(4,128)(2,1)S(1)}, bf16[4,2048]{1,0:T(4,128)(2,1)}, u32[]{:S(2)}) copy-start(bf16[4,2048]{1,0:T(4,128)(2,1)} %param.25) | copy-start | bytes 49156
  131.6 196.6 %copy-start.25 = (bf16[3,2048]{1,0:T(4,128)(2,1)S(1)}, bf16[3,2048]{1,0:T(4,128)(2,1)}, u32[]{:S(2)}) copy-start(bf16[3,2048]{1,0:T(4,128)(2,1)} %param.36) | copy-start | bytes 36868
  311.0 13.3 %collective-permute-start.6 = (bf16[256,1024]{1,0:T(8,128)(2,1)S(1)}, bf16[256,1024]{1,0:T(8,128)(2,1)S(1)}, u32[]{:S(2)}, u32[]{:S(2)}) collective-permute-start(bf16[256,1024]{1,0:T(8,128)(2,1)S(1)} %get-tuple-element.166), channel_id=1, source_target_pairs={{0,2},{2,0},{1,3},{3,1},{4,6},{6,4},{5,7},{7,5},{8,10},{10,8},{9,1... | collective-permute-start | bytes 1572872 | tf_op jit(solution)/shard_map/ppermute | solution.py:127
  325.8 276.3 %all-gather.11.cloned.1.call-start = ((), (), s32[]{:S(2)}) async-start(), calls=%async_computation.3 | async-start | bytes 9437184 | tf_op jit(solution)/shard_map/all_gather | solution.py:226
  338.6 13.4 %collective-permute-start.2 = (bf16[3,1280]{0,1:T(8,128)(2,1)}, bf16[3,1280]{0,1:T(8,128)(2,1)S(1)}, u32[]{:S(2)}, u32[]{:S(2)}) collective-permute-start(bf16[3,1280]{0,1:T(8,128)(2,1)} %slice.145), channel_id=1, source_target_pairs={{0,4},{4,8},{8,12},{12,16},{16,20},{20,24},{24,28},{1,5},{5,9},{9,... | collective-permute-start | bytes 23048 | tf_op jit(solution)/shard_map/ppermute | solution.py:15
  341.2 10.8 %copy-start.18 = (pred[1536]{0:T(1024)(128)(4,1)S(1)}, pred[1536]{0:T(1024)(128)(4,1)}, u32[]{:S(2)}) copy-start(pred[1536]{0:T(1024)(128)(4,1)} %get-tuple-element.184) | copy-start | bytes 4612
  341.3 10.8 %copy-start.19 = (pred[1536]{0:T(1024)(128)(4,1)S(1)}, pred[1536]{0:T(1024)(128)(4,1)}, u32[]{:S(2)}) copy-start(pred[1536]{0:T(1024)(128)(4,1)} %get-tuple-element.191) | copy-start | bytes 4612
  341.3 10.8 %copy-start.20 = (pred[1536]{0:T(1024)(128)(4,1)S(1)}, pred[1536]{0:T(1024)(128)(4,1)}, u32[]{:S(2)}) copy-start(pred[1536]{0:T(1024)(128)(4,1)} %get-tuple-element.192) | copy-start | bytes 4612
  341.3 10.8 %copy-start.21 = (pred[1536]{0:T(1024)(128)(4,1)S(1)}, pred[1536]{0:T(1024)(128)(4,1)}, u32[]{:S(2)}) copy-start(pred[1536]{0:T(1024)(128)(4,1)} %get-tuple-element.193) | copy-start | bytes 4612
  341.3 10.8 %copy-start.22 = (pred[1536]{0:T(1024)(128)(4,1)S(1)}, pred[1536]{0:T(1024)(128)(4,1)}, u32[]{:S(2)}) copy-start(pred[1536]{0:T(1024)(128)(4,1)} %get-tuple-element.194) | copy-start | bytes 4612
  349.9 28.5 %collective-permute-start.7 = (bf16[1024,256]{1,0:T(8,128)(2,1)S(1)}, bf16[1024,256]{1,0:T(8,128)(2,1)S(1)}, u32[]{:S(2)}, u32[]{:S(2)}) collective-permute-start(bf16[1024,256]{1,0:T(8,128)(2,1)S(1)} %get-tuple-element.168), channel_id=1, source_target_pairs={{0,2},{2,0},{1,3},{3,1},{4,6},{6,4},{5,7},{7,5},{8,10},{10,8},{9,1... | collective-permute-start | bytes 1572872 | tf_op jit(solution)/shard_map/ppermute | solution.py:127
  373.5 4.9 copy-start.3
  391.9 2.7 copy-start.23
  407.1 40.0 %collective-permute-start.3 = (f32[1,16,64,128]{3,2,1,0:T(8,128)S(1)}, f32[1,16,64,128]{3,2,1,0:T(8,128)}, u32[]{:S(2)}, u32[]{:S(2)}) collective-permute-start(f32[1,16,64,128]{3,2,1,0:T(8,128)S(1)} %get-tuple-element.48), channel_id=1, source_target_pairs={{0,4},{4,8},{8,12},{12,16},{16,20},{20,24},{24,28},{1,5},{5,9},{9,... | collective-permute-start | bytes 1572872 | tf_op jit(solution)/shard_map/ppermute | solution.py:15
  414.0 33.0 %collective-permute-start.5 = (f32[1,16,64,128]{3,2,1,0:T(8,128)S(1)}, f32[1,16,64,128]{3,2,1,0:T(8,128)}, u32[]{:S(2)}, u32[]{:S(2)}) collective-permute-start(f32[1,16,64,128]{3,2,1,0:T(8,128)S(1)} %get-tuple-element.48), channel_id=1, source_target_pairs={{0,8},{4,12},{8,16},{12,20},{16,24},{20,28},{1,9},{5,13},{9,17},{1... | collective-permute-start | bytes 1572872 | tf_op jit(solution)/shard_map/ppermute | solution.py:15
  425.5 21.5 %collective-permute-start.4 = (f32[1,16]{1,0:T(1,128)S(1)}, f32[1,16]{1,0:T(1,128)S(1)}, u32[]{:S(2)}, u32[]{:S(2)}) collective-permute-start(f32[1,16]{1,0:T(1,128)S(1)} %get-tuple-element.49), channel_id=1, source_target_pairs={{0,4},{4,8},{8,12},{12,16},{16,20},{20,24},{24,28},{1,5},{5,9},{9,... | collective-permute-start | bytes 200 | tf_op jit(solution)/shard_map/ppermute | solution.py:15
  438.3 15.7 %copy-start.8 = (f32[6,256,256]{2,1,0:T(8,128)S(1)}, f32[6,256,256]{2,1,0:T(8,128)}, u32[]{:S(2)}) copy-start(f32[6,256,256]{2,1,0:T(8,128)} %fusion.95) | copy-start | bytes 4718596
  447.0 7.0 copy-start.2
  447.0 7.0 copy-start.7
  447.0 7.0 copy-start.10
  447.0 7.0 copy-start.11
  447.0 7.0 copy-start.12
  447.0 7.0 copy-start.13
  447.0 7.0 copy-start.31
  520.8 3.3 dynamic-slice-start
  614.3 19.5 %collective-permute-start.8 = (f32[2,384,4096]{2,1,0:T(8,128)}, f32[2,384,4096]{2,1,0:T(8,128)}, u32[]{:S(2)}, u32[]{:S(2)}) collective-permute-start(f32[2,384,4096]{2,1,0:T(8,128)} %fusion.14), channel_id=1, source_target_pairs={{0,1},{1,0},{2,3},{3,2},{4,5},{5,4},{6,7},{7,6},{8,9},{9,8},{10,11... | collective-permute-start | bytes 37748744 | tf_op jit(solution)/shard_map/ppermute | solution.py:331
  645.2 6.5 copy-start.5
  651.7 137.9 %collective-permute-start.9 = (f32[384,4096]{1,0:T(8,128)}, f32[384,4096]{1,0:T(8,128)}, u32[]{:S(2)}, u32[]{:S(2)}) collective-permute-start(f32[384,4096]{1,0:T(8,128)} %dynamic-slice_bitcast_fusion), channel_id=1, source_target_pairs={{0,2},{2,0},{1,3},{3,1},{4,6},{6,4},{5,7},{7,5},{8,10},{10,8},{9,1... | collective-permute-start | bytes 18874376 | tf_op jit(solution)/shard_map/ppermute | solution.py:127
  653.2 143.5 %copy-start.1 = (f32[32,64,128]{2,1,0:T(8,128)S(1)}, f32[32,64,128]{2,1,0:T(8,128)}, u32[]{:S(2)}) copy-start(f32[32,64,128]{2,1,0:T(8,128)} %param.35) | copy-start | bytes 3145732
Sparse Core Ops, SparseCore 0:
  90.4 18.2 all-gather.4
  122.3 164.8 all-gather.6
  325.9 139.8 all-gather.8
  467.7 134.3 all-gather.10

commit v4 on v3

--- a/solution.py
+++ b/solution.py
@@ -182,7 +182,13 @@
     normed_own = norm_rows(tokens, norm_gain)
     share = own_rows // core_count
     fetched = swap_half(cut(normed_own, 0, core * share, share))
-    normed_other = lax.all_gather(fetched, "fsdp", axis=0, tiled=True)
+    arrived = [fetched] + [
+        lax.ppermute(fetched, "fsdp", [(j, (j + shift) % core_count) for j in range(core_count)])
+        for shift in range(1, core_count)
+    ]
+    arrived = jnp.stack(arrived)
+    owners = (core - jnp.arange(core_count, dtype=jnp.int32)) % core_count
+    normed_other = jnp.take(arrived, owners, axis=0).reshape(own_rows, tokens.shape[1])
     normed = ordered_pair(normed_own, normed_other, half, 0)
 
     def first_cols(offset_x, offset_bc, offset_h):
@@ -323,18 +329,25 @@
     ).astype(jnp.bfloat16)
     piece = own_rows // core_count
     by_owner = normed_y.reshape(2, core_count, piece, inner_local)
-    total = None
-    for shift in list(range(1, core_count)) + [0]:
-        rows = lax.dynamic_index_in_dim(by_owner, (core + shift) % core_count, 1, keepdims=False)
-        part = jnp.einsum("hrc,cd->hrd", rows, out_full, preferred_element_type=jnp.float32)
-        if shift:
-            part = lax.ppermute(
-                part, "fsdp", [(j, (j + shift) % core_count) for j in range(core_count)]
-            )
-        total = part if total is None else total + part
-    mine = lax.dynamic_index_in_dim(total, half, 0, keepdims=False)
-    theirs = swap_half(lax.dynamic_index_in_dim(total, 1 - half, 0, keepdims=False))
-    return (mine + theirs).astype(jnp.bfloat16)
+    chunk_count = 2
+    chunk = out_full.shape[1] // chunk_count
+    results = []
+    for index in range(chunk_count):
+        columns = out_full[:, index * chunk : (index + 1) * chunk]
+        total = None
+        for shift in list(range(1, core_count)) + [0]:
+            rows = lax.dynamic_index_in_dim(by_owner, (core + shift) % core_count, 1, keepdims=False)
+            part = jnp.einsum("hrc,cd->hrd", rows, columns, preferred_element_type=jnp.float32)
+            if shift:
+                part = lax.ppermute(
+                    part, "fsdp", [(j, (j + shift) % core_count) for j in range(core_count)]
+                )
+            total = part if total is None else total + part
+        mine = lax.dynamic_index_in_dim(total, half, 0, keepdims=False)
+        theirs = lax.dynamic_index_in_dim(total, 1 - half, 0, keepdims=False)
+        theirs = swap_half(theirs.astype(jnp.bfloat16))
+        results.append((mine + theirs.astype(jnp.float32)).astype(jnp.bfloat16))
+    return jnp.concatenate(results, axis=1)
 
 
 def solution(mesh):

time: 809 us -> 645 us (0.80)
  waiting for transfers between devices: 473 us -> 269 us
  other arithmetic: 97 us -> 116 us
  local copies, waits for them, and re-layouts: 75.8 us -> 92.9 us
    all_gather x1, waiting for transfers between devices: 155 us -> 53.2 us  [body(): first_full = lax.all_gather(first_local, 'pair', axis=0, tiled=True)]
    ppermute x5 -> x6, waiting for transfers between devices: 222 us -> 141 us  [swap_half(): lax.ppermute(value, 'half', [(k, count - 1 - k) for k in range(count)])]
    ppermute x1 -> x2, waiting for transfers between devices: 19.5 us -> 4.39 us  [body(): lax.ppermute(part, 'fsdp', [(j, (j + shift) % core_count) for j in range(...]
    gather x0 -> x2, local copies, waits for them, and re-layouts: none -> 8.73 us  [body(): jnp.take(arrived, owners, axis=0).reshape(own_rows, tokens.shape[1])]
    dot_general x2 -> x4, matrix products: 23.5 us -> 29.4 us  [body(): jnp.einsum('hrc,cd->hrd', rows, columns, preferred_element_type=jnp.float32)]
  transfers between devices with their start and end apart: 14 -> 16, of which waited for: 7 -> 8; matrix products, arithmetic and copies ran while one was open for 25% -> 40% of each run, Pallas kernels for 0% -> 0%
where the time goes in v4:
time: 645 us; the launch traced here: 637 us
  waiting for transfers between devices  269 us (42%)
  other arithmetic  116 us (18%)
  matrix products  112 us (17%)
  local copies, waits for them, and re-layouts  92.9 us (14%)
  starting transfers between devices  32.1 us (5%)
  between operations  14.8 us (2%)
    ppermute x6, waiting for transfers between devices, swap_half(): lax.ppermute(value, 'half', [(k, count - 1 - k) for k in range(count)])  141 us
    all_gather x1, waiting for transfers between devices, body(): out_full = lax.all_gather(out_local, 'pair', axis=1, tiled=True)  70.3 us
    all_gather x1, waiting for transfers between devices, body(): first_full = lax.all_gather(first_local, 'pair', axis=0, tiled=True)  53.2 us
    dot_general x4, matrix products, body(): jnp.einsum('hrc,cd->hrd', rows, columns, preferred_element_type=jnp.float32)  29.4 us
    dot_general x1, matrix products, body(): jnp.dot(normed, z_full, preferred_element_type=jnp.float32)  27.1 us
    dot_general x1, matrix products, body(): jnp.dot(normed, first_full, preferred_element_type=jnp.float32)  23.8 us
    reshape x2, local copies, waits for them, and re-layouts, body(): (direct + state_gain[..., None] * from_state).reshape(row_count, inner_lo...  23 us
    convert_element_type x1, other arithmetic, conv_rows(): return jax.nn.silu(summed).astype(jnp.bfloat16)  22 us
  transfers between devices with their start and end apart: 16, of which 8 were waited for; matrix products, arithmetic and copies ran while one was open for 40% of the time, Pallas kernels for 0%

profile of v4, /device:TPU:0, one launch (start us, length us, event | category | flops | bytes accessed | tf_op | source)
XLA Modules:
  0.0 637.0 jit_solution(5091992194181022424)
XLA Ops:
  6.5 1.6 fusion.100
  11.4 6.9 %fusion.99 = (bf16[256,1,2048]{2,1,0:T(2,128)(2,1)}, bf16[256,1,2048]{2,1,0:T(2,128)(2,1)}) fusion(bf16[256,2,2048]{2,1,0:T(2,128)(2,1)} %param.22), kind=kLoop, calls=%fused_computation.228 | loop fusion | bytes 4194304 | tf_op jit(solution)/shard_map/slice | solution.py:197
  18.3 3.7 constant_dynamic-slice_fusion.19
  24.2 2.9 collective-permute-start.2
  29.0 13.3 %collective-permute-done.2 = bf16[256,1296]{0,1:T(8,128)(2,1)S(1)} collective-permute-done((bf16[256,1296]{0,1:T(8,128)(2,1)}, bf16[256,1296]{0,1:T(8,128)(2,1)S(1)}, u32[]{:S(2)}, u32[]{:S(2)}) %collective-permute-start.2) | collective-permute-done | bytes 663584 | tf_op jit(solution)/shard_map/ppermute | solution.py:127
  42.6 6.2 maximum_select_fusion.3
  49.0 4.1 fusion.3
  53.1 5.3 fusion.5
  58.4 2.9 copy-done.4
  61.6 1.8 collective-permute-start
  63.4 67.6 %collective-permute-done = bf16[384,4096]{1,0:T(8,128)(2,1)} collective-permute-done((bf16[384,4096]{1,0:T(8,128)(2,1)S(1)}, bf16[384,4096]{1,0:T(8,128)(2,1)}, u32[]{:S(2)}, u32[]{:S(2)}) %collective-permute-start) | collective-permute-done | bytes 3145760 | tf_op jit(solution)/shard_map/ppermute | solution.py:127
  132.8 1.3 fusion.88
  134.7 1.8 reduce-window.30
  137.6 2.2 copy.282
  139.8 5.0 fusion.22
  144.8 4.4 gather_fusion
  149.2 4.4 gather_fusion.1
  153.6 3.6 pad_maximum_fusion
  157.2 3.7 bitcast_select_fusion
  160.9 53.2 %all-gather.4.cloned.1.call-done = bf16[4096,1296]{1,0:T(8,128)(2,1)} async-done(((bf16[512,1296]{1,0:T(8,128)(2,1)}), bf16[4096,1296]{1,0:T(8,128)(2,1)}) %all-gather.4.cloned.1.call-update) | async-done | bytes 10616848 | tf_op jit(solution)/shard_map/all_gather | solution.py:211
  214.1 23.8 %convolution_convert_fusion = bf16[1536,1296]{0,1:T(8,128)(2,1)} fusion(bf16[4096,1296]{1,0:T(8,128)(2,1)} %all-gather.4.cloned.1.call-done, bf16[768,4096]{1,0:T(8,128)(2,1)} %bitcast_select_fusion, bf16[768,4096]{1,0:T(8,128)(2,1)} %copy-done.4, pred[]{:T(512)S(6)} %eq.204), kind=kOutput, calls=%fused_computation.27 | convolution fusion | flops 16366067712 | bytes 27181056 | tf_op jit(solution)/shard_map/dot_general | solution.py:212
  238.0 1.5 collective-permute-start.7
  245.6 5.7 collective-permute-done.7
  251.3 1.5 maximum_select_fusion.4
  259.4 1.9 slice.157
  261.3 2.4 collective-permute-start.3
  264.9 3.6 reduce-window.21
  273.8 4.3 slice.152
  278.4 1.5 collective-permute-start.8
  280.6 22.0 %multiply_convert_fusion.3 = bf16[1536,1280]{0,1:T(8,128)(2,1)S(1)} fusion(bf16[1536,1280]{0,1:T(8,128)(2,1)} %slice.152, bf16[3,1280]{0,1:T(8,128)(2,1)S(1)} %collective-permute-done.3, f32[1280]{0:T(1024)} %get-tuple-element.132, f32[1280]{0:T(1024)} %get-tuple-element.133, f32[1280]{0:T(1024)} %get-tuple-element.134, f32[1280]{0:T(1024)} %get-tuple-element.131, ...), kind=kLoop, calls=%fused_computation.26 | loop fusion | flops 104202240 | bytes 7933952 | tf_op jit(solution)/shard_map/convert_element_type | solution.py:68
  302.7 5.0 fusion.97
  310.4 7.7 %reshape.578 = bf16[6,256,16,64]{1,0,3,2:T(8,128)(2,1)} reshape(bf16[1536,1024]{0,1:T(8,128)(2,1)} %get-tuple-element.159) | data formatting | bytes 6291456 | tf_op jit(solution)/shard_map/reshape.48
  318.1 3.2 multiply_convert_fusion.2
  321.3 2.7 add_bitcast_fusion
  323.9 20.2 %while.17 = (s32[]{:T(128)}, f32[1,16,64,128]{3,2,1,0:T(8,128)S(1)}, f32[1,16]{1,0:T(1,128)S(1)}, f32[6,1,16,64,128]{4,3,2,1,0:T(8,128)}, f32[6,1,16]{2,0,1:T(8,...) while((s32[]{:T(128)}, ...), condition=%wide.region_15.16_spmd.clone, body=%wide.region_14.15_spmd.clone.sunk | while | flops 524323 | bytes 2622649 | solution.py:308
  344.2 3.1 collective-permute-start.4
  347.3 9.6 %collective-permute-start.6 = (f32[1,16,64,128]{3,2,1,0:T(8,128)S(1)}, f32[1,16,64,128]{3,2,1,0:T(8,128)}, u32[]{:S(2)}, u32[]{:S(2)}) collective-permute-start(f32[1,16,64,128]{3,2,1,0:T(8,128)S(1)} %get-tuple-element.48), channel_id=1, source_target_pairs={{0,8},{4,12},{8,16},{12,20},{16,24},{20,28},{1,9},{5,13},{9,17},{1... | collective-permute-start | bytes 1572872 | tf_op jit(solution)/shard_map/ppermute | solution.py:15
  357.1 5.2 collective-permute-start.5
  362.3 1.5 fusion.103
  363.8 5.3 fusion.48
  369.1 9.2 %reshape.600 = f32[6,256,1,16,64]{1,0,4,3,2:T(8,128)} reshape(f32[1536,1024]{0,1:T(8,128)} %get-tuple-element.160) | data formatting | bytes 12582912 | tf_op jit(solution)/shard_map/convert_element_type | solution.py:119
  378.3 1.5 add_bitcast_fusion.1
  379.8 5.4 fusion.25
  385.2 16.7 %fusion.17 = f32[6,256,1,16,64]{1,4,3,0,2:T(8,128)} fusion(f32[6,256,1,16,64]{1,0,4,3,2:T(8,128)} %reshape.600, f32[6,256,16,64]{1,3,2,0:T(8,128)S(1)} %fusion.25, f32[6,256,16,64]{1,3,2,0:T(8,128)S(1)} %copy-done.5, f32[6,256,16]{1,2,0:T(8,128)S(1)} %copy-done.13, f32[16]{0:T(128)S(1)} %copy-done.29, f32[6,256,16]{1,2,0:T(8,128)S(1)} %copy-done.12, ...), kind=kOutput, calls=%fused_computation.37 | convolution fusion | flops 852492288 | bytes 30670912 | tf_op jit(solution)/shard_map/cghqs,csghp->cqghp/dot_general | solution.py:20
  401.9 11.4 %copy.227 = f32[6,256,1,16,64]{4,3,1,0,2:T(8,128)} copy(f32[6,256,1,16,64]{1,4,3,0,2:T(8,128)} %fusion.17) | data formatting | bytes 12582912 | tf_op jit(solution)/shard_map/reshape | solution.py:320
  413.3 11.7 %reshape.622 = f32[1536,1024]{1,0:T(8,128)} reshape(f32[6,256,1,16,64]{4,3,1,0,2:T(8,128)} %copy.227) | data formatting | bytes 12582912 | tf_op jit(solution)/shard_map/reshape | solution.py:320
  424.9 27.1 %multiply_reduce_fusion = (f32[1536]{0:T(1024)S(1)}, f32[1536,1024]{1,0:T(8,128)}) fusion(f32[1536,1024]{1,0:T(8,128)} %reshape.622, bf16[4096,1024]{1,0:T(8,128)(2,1)} %all-gather.6.cloned.1.call-done, bf16[768,4096]{1,0:T(8,128)(2,1)} %bitcast_select_fusion, bf16[768,4096]{1,0:T(8,128)(2,1)} %copy-done.4, pred[]{:T(512)S(6)} %eq.204), kind=kOutput, calls=%fused_computation.41 | convolution fusion | flops 12955678720 | bytes 33560576 | tf_op jit(solution)/shard_map/dot_general | solution.py:233
  452.1 3.3 broadcast_multiply_fusion
  455.4 2.6 multiply_convert_fusion.4
  458.0 70.3 %all-gather.8.cloned.1.call-done = bf16[1024,4096]{1,0:T(8,128)(2,1)} async-done(((bf16[1024,512]{1,0:T(8,128)(2,1)}), bf16[1024,4096]{1,0:T(8,128)(2,1)}) %all-gather.8.cloned.1.call-update) | async-done | bytes 8388624 | tf_op jit(solution)/shard_map/all_gather | solution.py:232
  528.4 8.9 %fusion.20 = f32[2,384,2048]{2,1,0:T(8,128)} fusion(bf16[1024,4096]{1,0:T(8,128)(2,1)} %all-gather.8.cloned.1.call-done, bf16[2,2,384,1024]{3,2,1,0:T(8,128)(2,1)} %multiply_convert_fusion.4, s32[]{:T(128)S(6)} %select_n.329), kind=kOutput, calls=%fused_computation.52 | convolution fusion | flops 3221225472 | bytes 12058628 | tf_op jit(solution)/shard_map/hrc,cd->hrd/dot_general | solution.py:340
  537.2 5.5 fusion.21
  543.4 4.4 collective-permute-done.9
  547.7 7.9 %convolution_add_fusion.1 = f32[2,384,2048]{2,1,0:T(8,128)S(1)} fusion(f32[2,384,2048]{2,1,0:T(8,128)} %collective-permute-done.9, bf16[1024,4096]{1,0:T(8,128)(2,1)} %all-gather.8.cloned.1.call-done, bf16[2,2,384,1024]{3,2,1,0:T(8,128)(2,1)} %multiply_convert_fusion.4, s32[]{:T(128)S(6)} %select_n.333), kind=kOutput, calls=%fused_computation.51 | convolution fusion | flops 3222798336 | bytes 18350084 | tf_op jit(solution)/shard_map/hrc,cd->hrd/dot_general | solution.py:340
  555.9 1.5 collective-permute-start.10
  557.4 7.1 %convolution_add_fusion = f32[2,384,2048]{2,1,0:T(8,128)S(1)} fusion(f32[2,384,2048]{2,1,0:T(8,128)} %collective-permute-done.11, bf16[1024,4096]{1,0:T(8,128)(2,1)} %all-gather.8.cloned.1.call-done, bf16[2,2,384,1024]{3,2,1,0:T(8,128)(2,1)S(1)} %copy-done.10, s32[]{:T(128)S(6)} %select_n.333), kind=kOutput, calls=%fused_computation.50 | convolution fusion | flops 3222798336 | bytes 18350084 | tf_op jit(solution)/shard_map/hrc,cd->hrd/dot_general | solution.py:340
  564.6 1.5 fusion.37
  566.1 1.6 copy-done.7
  567.7 1.5 collective-permute-start.12
  569.3 23.9 %collective-permute-done.10 = bf16[384,2048]{1,0:T(8,128)(2,1)S(1)} collective-permute-done((bf16[384,2048]{1,0:T(8,128)(2,1)S(1)}, bf16[384,2048]{1,0:T(8,128)(2,1)S(1)}, u32[]{:S(2)}, u32[]{:S(2)}) %collective-permute-start.10) | collective-permute-done | bytes 1572896 | tf_op jit(solution)/shard_map/ppermute | solution.py:127
  593.2 2.5 fusion.24
  595.7 30.5 %collective-permute-done.12 = bf16[384,2048]{1,0:T(8,128)(2,1)} collective-permute-done((bf16[384,2048]{1,0:T(8,128)(2,1)}, bf16[384,2048]{1,0:T(8,128)(2,1)}, u32[]{:S(2)}, u32[]{:S(2)}) %collective-permute-start.12) | collective-permute-done | bytes 1572896 | tf_op jit(solution)/shard_map/ppermute | solution.py:127
  626.2 2.0 fusion.23
  628.2 2.0 pad_maximum_fusion.3
  (213 shorter events, 54.6 us)
Async XLA Ops:
  6.5 250.0 %copy-start = (f32[32,64,128]{2,1,0:T(8,128)S(1)}, f32[32,64,128]{2,1,0:T(8,128)}, u32[]{:S(2)}) copy-start(f32[32,64,128]{2,1,0:T(8,128)} %param.35) | copy-start | bytes 3145732
  6.5 207.5 %all-gather.4.cloned.1.call-start = ((), (), s32[]{:S(2)}) async-start(), calls=%async_computation | async-start | bytes 12976128 | tf_op jit(solution)/shard_map/all_gather | solution.py:211
  24.2 18.1 %collective-permute-start.2 = (bf16[256,1296]{0,1:T(8,128)(2,1)}, bf16[256,1296]{0,1:T(8,128)(2,1)S(1)}, u32[]{:S(2)}, u32[]{:S(2)}) collective-permute-start(bf16[256,1296]{0,1:T(8,128)(2,1)} %copy.201), channel_id=1, source_target_pairs={{0,2},{2,0},{1,3},{3,1},{4,6},{6,4},{5,7},{7,5},{8,10},{10,8},{9,1... | collective-permute-start | bytes 1990664 | tf_op jit(solution)/shard_map/ppermute | solution.py:127
  29.0 24.1 %copy-start.15 = (f32[4096]{0:T(1024)S(1)}, f32[4096]{0:T(1024)}, u32[]{:S(2)}) copy-start(f32[4096]{0:T(1024)} %param.21) | copy-start | bytes 49156
  48.8 376.2 %all-gather.6.cloned.1.call-start = ((), (), s32[]{:S(2)}) async-start(), calls=%async_computation.1 | async-start | bytes 9437184 | tf_op jit(solution)/shard_map/all_gather | solution.py:231
  58.4 2.9 copy-start.4
  61.3 70.4 %copy-start.24 = (s32[8]{0:T(128)S(1)}, s32[8]{0:T(128)}, u32[]{:S(2)}) copy-start(s32[8]{0:T(128)} %param.32) | copy-start | bytes 100
  61.3 70.4 %copy-start.25 = (s32[8]{0:T(128)S(1)}, s32[8]{0:T(128)}, u32[]{:S(2)}) copy-start(s32[8]{0:T(128)} %param.33) | copy-start | bytes 100
  61.3 73.1 %copy-start.16 = (bf16[4,2,256]{2,1,0:T(2,128)(2,1)S(1)}, bf16[4,2,256]{2,1,0:T(2,128)(2,1)}, u32[]{:S(2)}) copy-start(bf16[4,2,256]{2,1,0:T(2,128)(2,1)} %param.26) | copy-start | bytes 12292
  61.3 73.1 %copy-start.18 = (bf16[3,2,256]{2,1,0:T(2,128)(2,1)S(1)}, bf16[3,2,256]{2,1,0:T(2,128)(2,1)}, u32[]{:S(2)}) copy-start(bf16[3,2,256]{2,1,0:T(2,128)(2,1)} %param.37) | copy-start | bytes 9220
  61.3 73.2 %copy-start.26 = (f32[32]{0:T(128)S(1)}, f32[32]{0:T(128)}, u32[]{:S(2)}) copy-start(f32[32]{0:T(128)} %param.27) | copy-start | bytes 388
  61.3 73.3 %copy-start.27 = (f32[32]{0:T(128)S(1)}, f32[32]{0:T(128)}, u32[]{:S(2)}) copy-start(f32[32]{0:T(128)} %param.28) | copy-start | bytes 388
  61.4 75.6 %copy-start.28 = (f32[32]{0:T(128)S(1)}, f32[32]{0:T(128)}, u32[]{:S(2)}) copy-start(f32[32]{0:T(128)} %param.29) | copy-start | bytes 388
  61.6 69.5 %collective-permute-start = (bf16[384,4096]{1,0:T(8,128)(2,1)S(1)}, bf16[384,4096]{1,0:T(8,128)(2,1)}, u32[]{:S(2)}, u32[]{:S(2)}) collective-permute-start(bf16[384,4096]{1,0:T(8,128)(2,1)S(1)} %constant_dynamic-slice_fusion.20), channel_id=1, source_target_pairs={{0,2},{2,0},{1,3},{3,1},{4,6},{6,4},{5,7},{7,5},{8,10},{10,8},{9,1... | collective-permute-start | bytes 9437192 | tf_op jit(solution)/shard_map/ppermute | solution.py:127
  131.0 8.8 %collective-permute-start.1 = (bf16[384,4096]{1,0:T(8,128)(2,1)}, bf16[384,4096]{1,0:T(8,128)(2,1)}, u32[]{:S(2)}, u32[]{:S(2)}) collective-permute-start(bf16[384,4096]{1,0:T(8,128)(2,1)} %collective-permute-done), channel_id=1, source_target_pairs={{0,1},{1,0},{2,3},{3,2},{4,5},{5,4},{6,7},{7,6},{8,9},{9,8},{10,11... | collective-permute-start | bytes 9437192 | tf_op jit(solution)/shard_map/ppermute | solution.py:186
  160.9 94.1 %copy-start.20 = (bf16[4,2048]{1,0:T(4,128)(2,1)S(1)}, bf16[4,2048]{1,0:T(4,128)(2,1)}, u32[]{:S(2)}) copy-start(bf16[4,2048]{1,0:T(4,128)(2,1)} %param.25) | copy-start | bytes 49156
  160.9 94.1 %copy-start.21 = (bf16[3,2048]{1,0:T(4,128)(2,1)S(1)}, bf16[3,2048]{1,0:T(4,128)(2,1)}, u32[]{:S(2)}) copy-start(bf16[3,2048]{1,0:T(4,128)(2,1)} %param.36) | copy-start | bytes 36868
  238.0 13.3 %collective-permute-start.7 = (bf16[256,1024]{1,0:T(8,128)(2,1)S(1)}, bf16[256,1024]{1,0:T(8,128)(2,1)S(1)}, u32[]{:S(2)}, u32[]{:S(2)}) collective-permute-start(bf16[256,1024]{1,0:T(8,128)(2,1)S(1)} %get-tuple-element.168), channel_id=1, source_target_pairs={{0,2},{2,0},{1,3},{3,1},{4,6},{6,4},{5,7},{7,5},{8,10},{10,8},{9,1... | collective-permute-start | bytes 1572872 | tf_op jit(solution)/shard_map/ppermute | solution.py:127
  252.8 275.5 %all-gather.8.cloned.1.call-start = ((), (), s32[]{:S(2)}) async-start(), calls=%async_computation.2 | async-start | bytes 9437184 | tf_op jit(solution)/shard_map/all_gather | solution.py:232
  261.3 19.3 %collective-permute-start.3 = (bf16[3,1280]{0,1:T(8,128)(2,1)}, bf16[3,1280]{0,1:T(8,128)(2,1)S(1)}, u32[]{:S(2)}, u32[]{:S(2)}) collective-permute-start(bf16[3,1280]{0,1:T(8,128)(2,1)} %slice.157), channel_id=1, source_target_pairs={{0,4},{4,8},{8,12},{12,16},{16,20},{20,24},{24,28},{1,5},{5,9},{9,... | collective-permute-start | bytes 23048 | tf_op jit(solution)/shard_map/ppermute | solution.py:15
  278.4 29.3 %collective-permute-start.8 = (bf16[1024,256]{1,0:T(8,128)(2,1)S(1)}, bf16[1024,256]{1,0:T(8,128)(2,1)S(1)}, u32[]{:S(2)}, u32[]{:S(2)}) collective-permute-start(bf16[1024,256]{1,0:T(8,128)(2,1)S(1)} %get-tuple-element.170), channel_id=1, source_target_pairs={{0,2},{2,0},{1,3},{3,1},{4,6},{6,4},{5,7},{7,5},{8,10},{10,8},{9,1... | collective-permute-start | bytes 1572872 | tf_op jit(solution)/shard_map/ppermute | solution.py:127
  302.7 5.0 copy-start.3
  310.4 10.9 %copy-start.22 = (f32[6,16]{1,0:T(8,128)S(1)}, f32[6,16]{1,0:T(8,128)}, u32[]{:S(2)}) copy-start(f32[6,16]{1,0:T(8,128)} %slice_reduce_fusion.1) | copy-start | bytes 1156
  321.2 2.7 copy-start.17
  321.3 2.7 copy-start.19
  344.2 34.1 %collective-permute-start.4 = (f32[1,16,64,128]{3,2,1,0:T(8,128)S(1)}, f32[1,16,64,128]{3,2,1,0:T(8,128)}, u32[]{:S(2)}, u32[]{:S(2)}) collective-permute-start(f32[1,16,64,128]{3,2,1,0:T(8,128)S(1)} %get-tuple-element.48), channel_id=1, source_target_pairs={{0,4},{4,8},{8,12},{12,16},{16,20},{20,24},{24,28},{1,5},{5,9},{9,... | collective-permute-start | bytes 1572872 | tf_op jit(solution)/shard_map/ppermute | solution.py:15
  347.3 31.0 %collective-permute-start.6 = (f32[1,16,64,128]{3,2,1,0:T(8,128)S(1)}, f32[1,16,64,128]{3,2,1,0:T(8,128)}, u32[]{:S(2)}, u32[]{:S(2)}) collective-permute-start(f32[1,16,64,128]{3,2,1,0:T(8,128)S(1)} %get-tuple-element.48), channel_id=1, source_target_pairs={{0,8},{4,12},{8,16},{12,20},{16,24},{20,28},{1,9},{5,13},{9,17},{1... | collective-permute-start | bytes 1572872 | tf_op jit(solution)/shard_map/ppermute | solution.py:15
  357.1 21.1 %collective-permute-start.5 = (f32[1,16]{1,0:T(1,128)S(1)}, f32[1,16]{1,0:T(1,128)S(1)}, u32[]{:S(2)}, u32[]{:S(2)}) collective-permute-start(f32[1,16]{1,0:T(1,128)S(1)} %get-tuple-element.49), channel_id=1, source_target_pairs={{0,4},{4,8},{8,12},{12,16},{16,20},{20,24},{24,28},{1,5},{5,9},{9,... | collective-permute-start | bytes 200 | tf_op jit(solution)/shard_map/ppermute | solution.py:15
  369.1 16.1 %copy-start.11 = (f32[6,256,256]{2,1,0:T(8,128)S(1)}, f32[6,256,256]{2,1,0:T(8,128)}, u32[]{:S(2)}) copy-start(f32[6,256,256]{2,1,0:T(8,128)} %fusion.103) | copy-start | bytes 4718596
  378.2 6.9 %copy-start.2 = (bf16[6,256,16,64]{1,0,3,2:T(8,128)(2,1)S(1)}, bf16[6,256,16,64]{1,0,3,2:T(8,128)(2,1)}, u32[]{:S(2)}) copy-start(bf16[6,256,16,64]{1,0,3,2:T(8,128)(2,1)} %reshape.578) | copy-start | bytes 9437188
  378.2 6.9 %copy-start.5 = (f32[6,256,16,64]{1,3,2,0:T(8,128)S(1)}, f32[6,256,16,64]{1,3,2,0:T(8,128)}, u32[]{:S(2)}) copy-start(f32[6,256,16,64]{1,3,2,0:T(8,128)} %fusion.48) | copy-start | bytes 18874372
  378.2 7.0 %copy-start.12 = (f32[6,256,16]{1,2,0:T(8,128)S(1)}, f32[6,256,16]{1,2,0:T(8,128)}, u32[]{:S(2)}) copy-start(f32[6,256,16]{1,2,0:T(8,128)} %fusion.111) | copy-start | bytes 294916
  378.2 7.0 %copy-start.13 = (f32[6,256,16]{1,2,0:T(8,128)S(1)}, f32[6,256,16]{1,2,0:T(8,128)}, u32[]{:S(2)}) copy-start(f32[6,256,16]{1,2,0:T(8,128)} %get-tuple-element.151) | copy-start | bytes 294916
  378.2 7.0 %copy-start.14 = (f32[6,16,256]{2,1,0:T(8,128)S(1)}, f32[6,16,256]{2,1,0:T(8,128)}, u32[]{:S(2)}) copy-start(f32[6,16,256]{2,1,0:T(8,128)} %reduce_window_sum.55) | copy-start | bytes 294916
  378.3 7.0 %copy-start.29 = (f32[16]{0:T(128)S(1)}, f32[16]{0:T(128)}, u32[]{:S(2)}) copy-start(f32[16]{0:T(128)} %dynamic_slice.150) | copy-start | bytes 196
  452.1 3.3 dynamic-slice-start
  528.4 8.9 %copy-start.9 = (bf16[2,2,384,1024]{3,2,1,0:T(8,128)(2,1)S(1)}, bf16[2,2,384,1024]{3,2,1,0:T(8,128)(2,1)}, u32[]{:S(2)}) copy-start(bf16[2,2,384,1024]{3,2,1,0:T(8,128)(2,1)} %multiply_convert_fusion.4) | copy-start | bytes 9437188
  528.4 8.9 %copy-start.23 = (bf16[1024,4096]{1,0:T(8,128)(2,1)S(1)}, bf16[1024,4096]{1,0:T(8,128)(2,1)}, u32[]{:S(2)}) copy-start(bf16[1024,4096]{1,0:T(8,128)(2,1)} %all-gather.8.cloned.1.call-done) | copy-start | bytes 25165828
  537.2 10.5 %collective-permute-start.9 = (f32[2,384,2048]{2,1,0:T(8,128)}, f32[2,384,2048]{2,1,0:T(8,128)}, u32[]{:S(2)}, u32[]{:S(2)}) collective-permute-start(f32[2,384,2048]{2,1,0:T(8,128)} %fusion.20), channel_id=1, source_target_pairs={{0,1},{1,0},{2,3},{3,2},{4,5},{5,4},{6,7},{7,6},{8,9},{9,8},{10,11... | collective-permute-start | bytes 18874376 | tf_op jit(solution)/shard_map/ppermute | solution.py:342
  542.8 14.6 %collective-permute-start.11 = (f32[2,384,2048]{2,1,0:T(8,128)}, f32[2,384,2048]{2,1,0:T(8,128)}, u32[]{:S(2)}, u32[]{:S(2)}) collective-permute-start(f32[2,384,2048]{2,1,0:T(8,128)} %fusion.21), channel_id=1, source_target_pairs={{0,1},{1,0},{2,3},{3,2},{4,5},{5,4},{6,7},{7,6},{8,9},{9,8},{10,11... | collective-permute-start | bytes 18874376 | tf_op jit(solution)/shard_map/ppermute | solution.py:342
  543.3 14.1 %copy-start.10 = (bf16[2,2,384,1024]{3,2,1,0:T(8,128)(2,1)S(1)}, bf16[2,2,384,1024]{3,2,1,0:T(8,128)(2,1)}, u32[]{:S(2)}) copy-start(bf16[2,2,384,1024]{3,2,1,0:T(8,128)(2,1)} %multiply_convert_fusion.4) | copy-start | bytes 9437188
  555.7 8.9 %copy-start.6 = (f32[2,384,2048]{2,1,0:T(8,128)}, f32[2,384,2048]{2,1,0:T(8,128)S(1)}, u32[]{:S(2)}) copy-start(f32[2,384,2048]{2,1,0:T(8,128)S(1)} %convolution_add_fusion.1) | copy-start | bytes 18874372
  555.9 37.3 %collective-permute-start.10 = (bf16[384,2048]{1,0:T(8,128)(2,1)S(1)}, bf16[384,2048]{1,0:T(8,128)(2,1)S(1)}, u32[]{:S(2)}, u32[]{:S(2)}) collective-permute-start(bf16[384,2048]{1,0:T(8,128)(2,1)S(1)} %fusion.36), channel_id=1, source_target_pairs={{0,2},{2,0},{1,3},{3,1},{4,6},{6,4},{5,7},{7,5},{8,10},{10,8},{9,1... | collective-permute-start | bytes 4718600 | tf_op jit(solution)/shard_map/ppermute | solution.py:127
  564.6 3.2 copy-start.7
  567.7 58.5 %collective-permute-start.12 = (bf16[384,2048]{1,0:T(8,128)(2,1)}, bf16[384,2048]{1,0:T(8,128)(2,1)}, u32[]{:S(2)}, u32[]{:S(2)}) collective-permute-start(bf16[384,2048]{1,0:T(8,128)(2,1)} %fusion.37), channel_id=1, source_target_pairs={{0,2},{2,0},{1,3},{3,1},{4,6},{6,4},{5,7},{7,5},{8,10},{10,8},{9,1... | collective-permute-start | bytes 4718600 | tf_op jit(solution)/shard_map/ppermute | solution.py:127
  569.3 56.9 %copy-start.8 = (f32[2,384,2048]{2,1,0:T(8,128)S(1)}, f32[2,384,2048]{2,1,0:T(8,128)}, u32[]{:S(2)}) copy-start(f32[2,384,2048]{2,1,0:T(8,128)} %copy-done.7) | copy-start | bytes 18874372
  593.2 37.0 %copy-start.1 = (f32[32,64,128]{2,1,0:T(8,128)S(1)}, f32[32,64,128]{2,1,0:T(8,128)}, u32[]{:S(2)}) copy-start(f32[32,64,128]{2,1,0:T(8,128)} %param.35) | copy-start | bytes 3145732
Sparse Core Ops, SparseCore 0:
  48.9 165.1 all-gather.3
  252.9 137.3 all-gather.5
  392.4 135.9 all-gather.7

commit v5 on v4

--- a/solution.py
+++ b/solution.py
@@ -229,7 +229,11 @@
         1,
     )
     z_full = lax.all_gather(z_local, "pair", axis=0, tiled=True)
-    out_full = lax.all_gather(out_local, "pair", axis=1, tiled=True)
+    block = out_local.shape[1] // 2
+    out_first, _ = lax.optimization_barrier((out_local[:, :block], z_full))
+    out_first = lax.all_gather(out_first, "pair", axis=1, tiled=True)
+    out_second, _ = lax.optimization_barrier((out_local[:, block:], out_first))
+    out_second = lax.all_gather(out_second, "pair", axis=1, tiled=True)
     proj_z = jnp.dot(normed, z_full, preferred_element_type=jnp.float32).astype(jnp.bfloat16)
 
     position = lax.axis_index("pair") * row_count + jnp.arange(row_count, dtype=jnp.int32)
@@ -329,11 +333,8 @@
     ).astype(jnp.bfloat16)
     piece = own_rows // core_count
     by_owner = normed_y.reshape(2, core_count, piece, inner_local)
-    chunk_count = 2
-    chunk = out_full.shape[1] // chunk_count
     results = []
-    for index in range(chunk_count):
-        columns = out_full[:, index * chunk : (index + 1) * chunk]
+    for columns in (out_first, out_second):
         total = None
         for shift in list(range(1, core_count)) + [0]:
             rows = lax.dynamic_index_in_dim(by_owner, (core + shift) % core_count, 1, keepdims=False)
@@ -347,7 +348,9 @@
         theirs = lax.dynamic_index_in_dim(total, 1 - half, 0, keepdims=False)
         theirs = swap_half(theirs.astype(jnp.bfloat16))
         results.append((mine + theirs.astype(jnp.float32)).astype(jnp.bfloat16))
-    return jnp.concatenate(results, axis=1)
+    pair_count = lax.axis_size("pair")
+    joined = jnp.stack([r.reshape(piece, pair_count, block) for r in results], axis=2)
+    return joined.reshape(piece, 2 * pair_count * block)
 
 
 def solution(mesh):

time: 645 us -> 673 us (1.043)
  waiting for transfers between devices: 269 us -> 298 us
  local copies, waits for them, and re-layouts: 92.9 us -> 107 us
  starting transfers between devices: 32.1 us -> 22.5 us
  other arithmetic: 116 us -> 108 us
    all_gather x1, waiting for transfers between devices: 0.01 us -> 75.8 us  [body(): z_full = lax.all_gather(z_local, 'pair', axis=0, tiled=True)]
    all_gather x1 -> x2, waiting for transfers between devices: 70.3 us -> 24.3 us  [the longest x1 17.3 us: body(): out_first = lax.all_gather(out_first, 'pair', axis=1, tiled=True)]
    ppermute x4, starting transfers between devices: 20.3 us -> 11.8 us  [from_behind(): lax.ppermute(value, axis, [(source, source + steps) for source in range(l...]
    ppermute x6, waiting for transfers between devices: 141 us -> 148 us  [swap_half(): lax.ppermute(value, 'half', [(k, count - 1 - k) for k in range(count)])]
    another operation x15 -> x16, local copies, waits for them, and re-layouts: 8.62 us -> 15 us
  transfers between devices with their start and end apart: 16 -> 17, of which waited for: 8 -> 11; matrix products, arithmetic and copies ran while one was open for 40% -> 39% of each run, Pallas kernels for 0% -> 0%
where the time goes in v5:
time: 673 us; the launch traced here: 662 us
  waiting for transfers between devices  298 us (44%)
  matrix products  112 us (17%)
  other arithmetic  108 us (16%)
  local copies, waits for them, and re-layouts  107 us (16%)
  starting transfers between devices  22.5 us (3%)
  between operations  15.2 us (2%)
    ppermute x6, waiting for transfers between devices, swap_half(): lax.ppermute(value, 'half', [(k, count - 1 - k) for k in range(count)])  148 us
    all_gather x1, waiting for transfers between devices, body(): z_full = lax.all_gather(z_local, 'pair', axis=0, tiled=True)  75.8 us
    all_gather x1, waiting for transfers between devices, body(): first_full = lax.all_gather(first_local, 'pair', axis=0, tiled=True)  47.7 us
    dot_general x4, matrix products, body(): jnp.einsum('hrc,cd->hrd', rows, columns, preferred_element_type=jnp.float32)  28.2 us
    dot_general x1, matrix products, body(): jnp.dot(normed, z_full, preferred_element_type=jnp.float32)  27.1 us
    dot_general x1, matrix products, body(): jnp.dot(normed, first_full, preferred_element_type=jnp.float32)  23.7 us
    reshape x2, local copies, waits for them, and re-layouts, body(): (direct + state_gain[..., None] * from_state).reshape(row_count, inner_lo...  23 us
    convert_element_type x1, other arithmetic, conv_rows(): return jax.nn.silu(summed).astype(jnp.bfloat16)  21.3 us
  transfers between devices with their start and end apart: 17, of which 11 were waited for; matrix products, arithmetic and copies ran while one was open for 39% of the time, Pallas kernels for 0%

profile of v5, /device:TPU:0, one launch (start us, length us, event | category | flops | bytes accessed | tf_op | source)
XLA Modules:
  0.0 662.4 jit_solution(14529462510385809423)
XLA Ops:
  6.5 2.3 fusion.113
  8.9 2.2 constant_dynamic-slice_fusion.17
  12.0 4.2 fusion.111
  16.1 3.7 constant_dynamic-slice_fusion.19
  20.3 3.0 collective-permute-start.2
  25.5 12.9 %collective-permute-done.2 = bf16[256,1296]{0,1:T(8,128)(2,1)} collective-permute-done((bf16[256,1296]{0,1:T(8,128)(2,1)S(1)}, bf16[256,1296]{0,1:T(8,128)(2,1)}, u32[]{:S(2)}, u32[]{:S(2)}) %collective-permute-start.2) | collective-permute-done | bytes 663584 | tf_op jit(solution)/shard_map/ppermute | solution.py:127
  38.3 1.4 copy.208
  39.8 5.4 maximum_select_fusion.3
  45.4 4.1 fusion.3
  49.5 5.3 fusion.5
  54.9 2.9 copy-done.3
  58.1 1.8 collective-permute-start
  59.9 67.6 %collective-permute-done = bf16[384,4096]{1,0:T(8,128)(2,1)} collective-permute-done((bf16[384,4096]{1,0:T(8,128)(2,1)S(1)}, bf16[384,4096]{1,0:T(8,128)(2,1)}, u32[]{:S(2)}, u32[]{:S(2)}) %collective-permute-start) | collective-permute-done | bytes 3145760 | tf_op jit(solution)/shard_map/ppermute | solution.py:127
  130.7 1.8 reduce-window.30
  132.8 1.6 copy.291
  141.7 5.0 fusion.34
  146.7 4.4 gather_fusion
  151.1 4.3 gather_fusion.1
  155.4 3.6 pad_maximum_fusion
  159.0 3.7 bitcast_select_fusion
  162.7 47.7 %all-gather.5.cloned.1.call-done = bf16[4096,1296]{1,0:T(8,128)(2,1)} async-done(((bf16[512,1296]{1,0:T(8,128)(2,1)}), bf16[4096,1296]{1,0:T(8,128)(2,1)}) %all-gather.5.cloned.1.call-update) | async-done | bytes 10616848 | tf_op jit(solution)/shard_map/all_gather | solution.py:211
  210.5 23.7 %convolution_convert_fusion = bf16[1536,1296]{0,1:T(8,128)(2,1)} fusion(bf16[4096,1296]{1,0:T(8,128)(2,1)} %all-gather.5.cloned.1.call-done, bf16[768,4096]{1,0:T(8,128)(2,1)} %bitcast_select_fusion, bf16[768,4096]{1,0:T(8,128)(2,1)} %copy-done.3, pred[]{:T(512)S(6)} %eq.204), kind=kOutput, calls=%fused_computation.27 | convolution fusion | flops 16366067712 | bytes 27181056 | tf_op jit(solution)/shard_map/dot_general | solution.py:212
  234.3 1.5 collective-permute-start.7
  236.1 11.5 %collective-permute-done.7 = bf16[256,1024]{1,0:T(8,128)(2,1)S(1)} collective-permute-done((bf16[256,1024]{1,0:T(8,128)(2,1)S(1)}, bf16[256,1024]{1,0:T(8,128)(2,1)S(1)}, u32[]{:S(2)}, u32[]{:S(2)}) %collective-permute-start.7) | collective-permute-done | bytes 524320 | tf_op jit(solution)/shard_map/ppermute | solution.py:127
  247.6 1.5 maximum_select_fusion.4
  256.4 2.5 collective-permute-start.3
  260.0 3.8 reduce-window.21
  269.0 4.2 slice.152
  274.2 1.5 collective-permute-start.8
  276.3 21.3 %multiply_convert_fusion.3 = bf16[1536,1280]{0,1:T(8,128)(2,1)S(1)} fusion(bf16[1536,1280]{0,1:T(8,128)(2,1)} %slice.152, bf16[3,1280]{0,1:T(8,128)(2,1)S(1)} %collective-permute-done.3, f32[1280]{0:T(1024)S(1)} %get-tuple-element.136, f32[1280]{0:T(1024)S(1)} %get-tuple-element.137, f32[1280]{0:T(1024)} %get-tuple-element.138, ...), kind=kLoop, calls=%fused_computation.26 | loop fusion | flops 104202240 | bytes 7933952 | tf_op jit(solution)/shard_map/convert_element_type | solution.py:68
  297.6 4.9 fusion.109
  303.9 75.8 %all-gather.7.cloned.1.call-done = bf16[4096,1024]{1,0:T(8,128)(2,1)} async-done(((bf16[512,1024]{1,0:T(8,128)(2,1)}), bf16[4096,1024]{1,0:T(8,128)(2,1)}) %all-gather.7.cloned.1.call-update) | async-done | bytes 8388624 | tf_op jit(solution)/shard_map/all_gather | solution.py:231
  381.2 7.5 %reshape.581 = bf16[6,256,16,64]{1,0,3,2:T(8,128)(2,1)} reshape(bf16[1536,1024]{0,1:T(8,128)(2,1)} %get-tuple-element.163) | data formatting | bytes 6291456 | tf_op jit(solution)/shard_map/reshape.49
  388.8 3.3 multiply_convert_fusion.2
  392.1 2.7 add_bitcast_fusion
  394.7 19.8 %while.17 = (s32[]{:T(128)}, f32[1,16,64,128]{3,2,1,0:T(8,128)S(1)}, f32[1,16]{1,0:T(1,128)S(1)}, f32[6,1,16,64,128]{4,3,2,1,0:T(8,128)}, f32[6,1,16]{2,0,1:T(8,...) while((s32[]{:T(128)}, ...), condition=%wide.region_15.16_spmd.clone, body=%wide.region_14.15_spmd.clone.sunk | while | flops 524323 | bytes 2622649 | solution.py:312
  414.5 2.6 collective-permute-start.4
  417.1 1.4 collective-permute-start.6
  418.8 5.3 collective-permute-start.5
  424.1 1.5 fusion.116
  425.6 5.2 fusion.60
  430.8 8.9 %reshape.604 = f32[6,256,1,16,64]{1,0,4,3,2:T(8,128)} reshape(f32[1536,1024]{0,1:T(8,128)} %get-tuple-element.164) | data formatting | bytes 12582912 | tf_op jit(solution)/shard_map/convert_element_type | solution.py:119
  441.7 7.3 %fusion.37 = f32[6,256,16,64]{1,3,2,0:T(8,128)} fusion(bf16[6,256,128,1]{2,1,3,0:T(8,128)(2,1)S(1)} %bitcast.201, f32[6,1,16,64,128]{4,3,2,1,0:T(8,128)} %get-tuple-element.52, f32[16,64,128]{2,1,0:T(8,128)S(1)} %add_bitcast_fusion.1, f32[6,16]{1,0:T(8,128)S(1)} %bitcast.219), kind=kOutput, calls=%fused_computation.65 | convolution fusion | flops 2417491968 | bytes 10355072 | tf_op jit(solution)/shard_map/cghpn,cqgn->cqghp/dot_general | solution.py:21
  449.0 17.3 %all-gather.9.cloned.1.call-done = bf16[1024,2048]{1,0:T(8,128)(2,1)} async-done(((bf16[1024,256]{1,0:T(8,128)(2,1)}), bf16[1024,2048]{1,0:T(8,128)(2,1)}) %all-gather.9.cloned.1.call-update) | async-done | bytes 4194320 | tf_op jit(solution)/shard_map/all_gather | solution.py:234
  466.4 16.2 %fusion.17 = f32[6,256,1,16,64]{1,4,3,0,2:T(8,128)} fusion(f32[6,256,1,16,64]{1,0,4,3,2:T(8,128)} %reshape.604, f32[6,256,16,64]{1,3,2,0:T(8,128)} %fusion.37, f32[6,256,16,64]{1,3,2,0:T(8,128)} %fusion.60, f32[6,256,16]{1,2,0:T(8,128)S(1)} %copy-done.16, f32[16]{0:T(128)S(1)} %copy-done.33, f32[6,256,16]{1,2,0:T(8,128)S(1)} %copy-done.15, ...), kind=kOutput, calls=%fused_computation.37 | convolution fusion | flops 852492288 | bytes 30670912 | tf_op jit(solution)/shard_map/cghqs,csghp->cqghp/dot_general | solution.py:20
  482.6 11.4 %copy.234 = f32[6,256,1,16,64]{4,3,1,0,2:T(8,128)} copy(f32[6,256,1,16,64]{1,4,3,0,2:T(8,128)} %fusion.17) | data formatting | bytes 12582912 | tf_op jit(solution)/shard_map/reshape | solution.py:324
  493.9 11.6 %reshape.626 = f32[1536,1024]{1,0:T(8,128)} reshape(f32[6,256,1,16,64]{4,3,1,0,2:T(8,128)} %copy.234) | data formatting | bytes 12582912 | tf_op jit(solution)/shard_map/reshape | solution.py:324
  505.6 27.1 %multiply_reduce_fusion = (f32[1536]{0:T(1024)S(1)}, f32[1536,1024]{1,0:T(8,128)}) fusion(f32[1536,1024]{1,0:T(8,128)} %reshape.626, bf16[4096,1024]{1,0:T(8,128)(2,1)} %all-gather.7.cloned.1.call-done, bf16[768,4096]{1,0:T(8,128)(2,1)} %bitcast_select_fusion, bf16[768,4096]{1,0:T(8,128)(2,1)} %copy-done.3, pred[]{:T(512)S(6)} %eq.204), kind=kOutput, calls=%fused_computation.41 | convolution fusion | flops 12955678720 | bytes 33560576 | tf_op jit(solution)/shard_map/dot_general | solution.py:237
  532.7 3.3 broadcast_multiply_fusion
  538.2 5.5 fusion.24
  543.8 7.0 %all-gather.11.cloned.1.call-done = bf16[1024,2048]{1,0:T(8,128)(2,1)} async-done(((bf16[1024,256]{1,0:T(8,128)(2,1)}), bf16[1024,2048]{1,0:T(8,128)(2,1)}) %all-gather.11.cloned.1.call-update) | async-done | bytes 4194320 | tf_op jit(solution)/shard_map/all_gather | solution.py:236
  550.8 8.7 %fusion.20 = f32[2,384,2048]{2,1,0:T(8,128)} fusion(bf16[1024,2048]{1,0:T(8,128)(2,1)} %all-gather.11.cloned.1.call-done, bf16[2,2,384,1024]{3,2,1,0:T(8,128)(2,1)} %copy-done.10, s32[]{:T(128)S(6)} %select_n.329), kind=kOutput, calls=%fused_computation.46 | convolution fusion | flops 3221225472 | bytes 12058628 | tf_op jit(solution)/shard_map/hrc,cd->hrd/dot_general | solution.py:341
  559.5 8.1 %fusion.28 = f32[2,384,2048]{2,1,0:T(8,128)S(1)} fusion(f32[2,384,2048]{2,1,0:T(8,128)} %collective-permute-done.9, bf16[1024,2048]{1,0:T(8,128)(2,1)} %all-gather.9.cloned.1.call-done, bf16[2,2,384,1024]{3,2,1,0:T(8,128)(2,1)} %copy-done.10, s32[]{:T(128)S(6)} %select_n.333), kind=kOutput, calls=%fused_computation.56 | convolution fusion | flops 3222798336 | bytes 18350084 | tf_op jit(solution)/shard_map/hrc,cd->hrd/dot_general | solution.py:341
  567.6 1.5 fusion.48
  569.2 1.5 collective-permute-start.10
  570.6 6.0 fusion.31
  576.6 1.6 fusion.49
  578.2 1.6 copy-done.8
  580.8 25.8 %collective-permute-done.10 = bf16[384,2048]{1,0:T(8,128)(2,1)S(1)} collective-permute-done((bf16[384,2048]{1,0:T(8,128)(2,1)}, bf16[384,2048]{1,0:T(8,128)(2,1)S(1)}, u32[]{:S(2)}, u32[]{:S(2)}) %collective-permute-start.10) | collective-permute-done | bytes 1572896 | tf_op jit(solution)/shard_map/ppermute | solution.py:127
  606.6 2.4 fusion.36
  609.4 30.5 %collective-permute-done.12 = bf16[384,2048]{1,0:T(8,128)(2,1)} collective-permute-done((bf16[384,2048]{1,0:T(8,128)(2,1)}, bf16[384,2048]{1,0:T(8,128)(2,1)}, u32[]{:S(2)}, u32[]{:S(2)}) %collective-permute-start.12) | collective-permute-done | bytes 1572896 | tf_op jit(solution)/shard_map/ppermute | solution.py:127
  640.0 2.0 fusion.35
  642.7 6.5 copy.231
  649.2 6.1 reshape.596
  (229 shorter events, 58.8 us)
Async XLA Ops:
  6.5 245.2 %copy-start = (f32[32,64,128]{2,1,0:T(8,128)S(1)}, f32[32,64,128]{2,1,0:T(8,128)}, u32[]{:S(2)}) copy-start(f32[32,64,128]{2,1,0:T(8,128)} %param.35) | copy-start | bytes 3145732
  6.5 5.4 copy-start.4
  6.5 203.9 %all-gather.5.cloned.1.call-start = ((), (), s32[]{:S(2)}) async-start(), calls=%async_computation | async-start | bytes 12976128 | tf_op jit(solution)/shard_map/all_gather | solution.py:211
  20.3 18.0 %collective-permute-start.2 = (bf16[256,1296]{0,1:T(8,128)(2,1)S(1)}, bf16[256,1296]{0,1:T(8,128)(2,1)}, u32[]{:S(2)}, u32[]{:S(2)}) collective-permute-start(bf16[256,1296]{0,1:T(8,128)(2,1)S(1)} %copy.207), channel_id=1, source_target_pairs={{0,2},{2,0},{1,3},{3,1},{4,6},{6,4},{5,7},{7,5},{8,10},{10,8},{9,1... | collective-permute-start | bytes 1990664 | tf_op jit(solution)/shard_map/ppermute | solution.py:127
  45.1 4.4 copy-start.18
  45.2 334.6 %all-gather.7.cloned.1.call-start = ((), (), s32[]{:S(2)}) async-start(), calls=%async_computation.1 | async-start | bytes 9437184 | tf_op jit(solution)/shard_map/all_gather | solution.py:231
  54.9 2.9 copy-start.3
  57.7 70.6 %copy-start.28 = (s32[8]{0:T(128)S(1)}, s32[8]{0:T(128)}, u32[]{:S(2)}) copy-start(s32[8]{0:T(128)} %param.32) | copy-start | bytes 100
  57.7 70.6 %copy-start.29 = (s32[8]{0:T(128)S(1)}, s32[8]{0:T(128)}, u32[]{:S(2)}) copy-start(s32[8]{0:T(128)} %param.33) | copy-start | bytes 100
  57.7 75.1 %copy-start.5 = (bf16[256,1,2048]{2,1,0:T(2,128)(2,1)S(1)}, bf16[256,1,2048]{2,1,0:T(2,128)(2,1)}, u32[]{:S(2)}) copy-start(bf16[256,1,2048]{2,1,0:T(2,128)(2,1)} %get-tuple-element.170) | copy-start | bytes 3145732
  57.7 83.9 %copy-start.21 = (bf16[3,2,256]{2,1,0:T(2,128)(2,1)S(1)}, bf16[3,2,256]{2,1,0:T(2,128)(2,1)}, u32[]{:S(2)}) copy-start(bf16[3,2,256]{2,1,0:T(2,128)(2,1)} %param.37) | copy-start | bytes 9220
  57.7 84.0 %copy-start.19 = (bf16[4,2,256]{2,1,0:T(2,128)(2,1)S(1)}, bf16[4,2,256]{2,1,0:T(2,128)(2,1)}, u32[]{:S(2)}) copy-start(bf16[4,2,256]{2,1,0:T(2,128)(2,1)} %param.26) | copy-start | bytes 12292
  58.1 69.5 %collective-permute-start = (bf16[384,4096]{1,0:T(8,128)(2,1)S(1)}, bf16[384,4096]{1,0:T(8,128)(2,1)}, u32[]{:S(2)}, u32[]{:S(2)}) collective-permute-start(bf16[384,4096]{1,0:T(8,128)(2,1)S(1)} %constant_dynamic-slice_fusion.20), channel_id=1, source_target_pairs={{0,2},{2,0},{1,3},{3,1},{4,6},{6,4},{5,7},{7,5},{8,10},{10,8},{9,1... | collective-permute-start | bytes 9437192 | tf_op jit(solution)/shard_map/ppermute | solution.py:127
  127.6 14.1 %collective-permute-start.1 = (bf16[384,4096]{1,0:T(8,128)(2,1)}, bf16[384,4096]{1,0:T(8,128)(2,1)}, u32[]{:S(2)}, u32[]{:S(2)}) collective-permute-start(bf16[384,4096]{1,0:T(8,128)(2,1)} %collective-permute-done), channel_id=1, source_target_pairs={{0,1},{1,0},{2,3},{3,2},{4,5},{5,4},{6,7},{7,6},{8,9},{9,8},{10,11... | collective-permute-start | bytes 9437192 | tf_op jit(solution)/shard_map/ppermute | solution.py:186
  162.7 71.5 %copy-start.6 = (bf16[256,1,2048]{2,0,1:T(8,128)(2,1)S(1)}, bf16[256,1,2048]{2,0,1:T(8,128)(2,1)}, u32[]{:S(2)}) copy-start(bf16[256,1,2048]{2,0,1:T(8,128)(2,1)} %copy.291) | copy-start | bytes 3145732
  234.2 15.9 %copy-start.30 = (f32[32]{0:T(128)S(1)}, f32[32]{0:T(128)}, u32[]{:S(2)}) copy-start(f32[32]{0:T(128)} %param.27) | copy-start | bytes 388
  234.2 15.9 %copy-start.31 = (f32[32]{0:T(128)S(1)}, f32[32]{0:T(128)}, u32[]{:S(2)}) copy-start(f32[32]{0:T(128)} %param.28) | copy-start | bytes 388
  234.2 16.0 %copy-start.32 = (f32[32]{0:T(128)S(1)}, f32[32]{0:T(128)}, u32[]{:S(2)}) copy-start(f32[32]{0:T(128)} %param.29) | copy-start | bytes 388
  234.2 16.6 %copy-start.23 = (bf16[4,2048]{1,0:T(4,128)(2,1)S(1)}, bf16[4,2048]{1,0:T(4,128)(2,1)}, u32[]{:S(2)}) copy-start(bf16[4,2048]{1,0:T(4,128)(2,1)} %param.25) | copy-start | bytes 49156
  234.2 16.6 %copy-start.24 = (bf16[3,2048]{1,0:T(4,128)(2,1)S(1)}, bf16[3,2048]{1,0:T(4,128)(2,1)}, u32[]{:S(2)}) copy-start(bf16[3,2048]{1,0:T(4,128)(2,1)} %param.36) | copy-start | bytes 36868
  234.3 13.3 %collective-permute-start.7 = (bf16[256,1024]{1,0:T(8,128)(2,1)S(1)}, bf16[256,1024]{1,0:T(8,128)(2,1)S(1)}, u32[]{:S(2)}, u32[]{:S(2)}) collective-permute-start(bf16[256,1024]{1,0:T(8,128)(2,1)S(1)} %get-tuple-element.172), channel_id=1, source_target_pairs={{0,2},{2,0},{1,3},{3,1},{4,6},{6,4},{5,7},{7,5},{8,10},{10,8},{9,1... | collective-permute-start | bytes 1572872 | tf_op jit(solution)/shard_map/ppermute | solution.py:127
  249.1 217.1 %all-gather.9.cloned.1.call-start = ((), (), s32[]{:S(2)}) async-start(), calls=%async_computation.2 | async-start | bytes 4718592 | tf_op jit(solution)/shard_map/all_gather | solution.py:234
  256.4 20.0 %collective-permute-start.3 = (bf16[3,1280]{0,1:T(8,128)(2,1)S(1)}, bf16[3,1280]{0,1:T(8,128)(2,1)S(1)}, u32[]{:S(2)}, u32[]{:S(2)}) collective-permute-start(bf16[3,1280]{0,1:T(8,128)(2,1)S(1)} %slice.157), channel_id=1, source_target_pairs={{0,4},{4,8},{8,12},{12,16},{16,20},{20,24},{24,28},{1,5},{5,9},{9,... | collective-permute-start | bytes 23048 | tf_op jit(solution)/shard_map/ppermute | solution.py:15
  274.2 28.4 %collective-permute-start.8 = (bf16[1024,256]{1,0:T(8,128)(2,1)S(1)}, bf16[1024,256]{1,0:T(8,128)(2,1)S(1)}, u32[]{:S(2)}, u32[]{:S(2)}) collective-permute-start(bf16[1024,256]{1,0:T(8,128)(2,1)S(1)} %get-tuple-element.176), channel_id=1, source_target_pairs={{0,2},{2,0},{1,3},{3,1},{4,6},{6,4},{5,7},{7,5},{8,10},{10,8},{9,1... | collective-permute-start | bytes 1572872 | tf_op jit(solution)/shard_map/ppermute | solution.py:127
  297.6 4.9 copy-start.2
  379.8 171.1 %all-gather.11.cloned.1.call-start = ((), (), s32[]{:S(2)}) async-start(), calls=%async_computation.3 | async-start | bytes 4718592 | tf_op jit(solution)/shard_map/all_gather | solution.py:236
  388.8 3.3 copy-start.25
  392.1 2.7 copy-start.20
  392.1 2.7 copy-start.22
  414.5 25.6 %collective-permute-start.4 = (f32[1,16,64,128]{3,2,1,0:T(8,128)S(1)}, f32[1,16,64,128]{3,2,1,0:T(8,128)S(1)}, u32[]{:S(2)}, u32[]{:S(2)}) collective-permute-start(f32[1,16,64,128]{3,2,1,0:T(8,128)S(1)} %get-tuple-element.50), channel_id=1, source_target_pairs={{0,4},{4,8},{8,12},{12,16},{16,20},{20,24},{24,28},{1,5},{5,9},{9,... | collective-permute-start | bytes 1572872 | tf_op jit(solution)/shard_map/ppermute | solution.py:15
  417.1 24.4 %collective-permute-start.6 = (f32[1,16,64,128]{3,2,1,0:T(8,128)S(1)}, f32[1,16,64,128]{3,2,1,0:T(8,128)S(1)}, u32[]{:S(2)}, u32[]{:S(2)}) collective-permute-start(f32[1,16,64,128]{3,2,1,0:T(8,128)S(1)} %get-tuple-element.50), channel_id=1, source_target_pairs={{0,8},{4,12},{8,16},{12,20},{16,24},{20,28},{1,9},{5,13},{9,17},{1... | collective-permute-start | bytes 1572872 | tf_op jit(solution)/shard_map/ppermute | solution.py:15
  418.8 21.3 %collective-permute-start.5 = (f32[1,16]{1,0:T(1,128)S(1)}, f32[1,16]{1,0:T(1,128)S(1)}, u32[]{:S(2)}, u32[]{:S(2)}) collective-permute-start(f32[1,16]{1,0:T(1,128)S(1)} %get-tuple-element.51), channel_id=1, source_target_pairs={{0,4},{4,8},{8,12},{12,16},{16,20},{20,24},{24,28},{1,5},{5,9},{9,... | collective-permute-start | bytes 200 | tf_op jit(solution)/shard_map/ppermute | solution.py:15
  441.6 24.7 %copy-start.12 = (f32[6,256,256]{2,1,0:T(8,128)S(1)}, f32[6,256,256]{2,1,0:T(8,128)}, u32[]{:S(2)}) copy-start(f32[6,256,256]{2,1,0:T(8,128)} %fusion.116) | copy-start | bytes 4718596
  441.6 24.7 %copy-start.13 = (pred[6,256,256]{2,1,0:T(8,128)(4,1)S(1)}, pred[6,256,256]{2,1,0:T(8,128)(4,1)}, u32[]{:S(2)}) copy-start(pred[6,256,256]{2,1,0:T(8,128)(4,1)} %compare_and_fusion) | copy-start | bytes 1179652
  441.6 24.7 %copy-start.14 = (f32[6,16,256]{2,1,0:T(8,128)S(1)}, f32[6,16,256]{2,1,0:T(8,128)}, u32[]{:S(2)}) copy-start(f32[6,16,256]{2,1,0:T(8,128)} %copy.216) | copy-start | bytes 294916
  441.6 24.7 %copy-start.15 = (f32[6,256,16]{1,2,0:T(8,128)S(1)}, f32[6,256,16]{1,2,0:T(8,128)}, u32[]{:S(2)}) copy-start(f32[6,256,16]{1,2,0:T(8,128)} %fusion.124) | copy-start | bytes 294916
  441.6 24.7 %copy-start.16 = (f32[6,256,16]{1,2,0:T(8,128)S(1)}, f32[6,256,16]{1,2,0:T(8,128)}, u32[]{:S(2)}) copy-start(f32[6,256,16]{1,2,0:T(8,128)} %get-tuple-element.155) | copy-start | bytes 294916
  441.6 24.7 %copy-start.17 = (f32[6,16,256]{2,1,0:T(8,128)S(1)}, f32[6,16,256]{2,1,0:T(8,128)}, u32[]{:S(2)}) copy-start(f32[6,16,256]{2,1,0:T(8,128)} %reduce_window_sum.55) | copy-start | bytes 294916
  441.6 24.7 %copy-start.33 = (f32[16]{0:T(128)S(1)}, f32[16]{0:T(128)}, u32[]{:S(2)}) copy-start(f32[16]{0:T(128)} %dynamic_slice.150) | copy-start | bytes 196
  532.7 3.3 dynamic-slice-start
  536.0 2.2 copy-start.26
  538.2 5.6 copy-start.10
  543.7 15.8 %collective-permute-start.9 = (f32[2,384,2048]{2,1,0:T(8,128)}, f32[2,384,2048]{2,1,0:T(8,128)}, u32[]{:S(2)}, u32[]{:S(2)}) collective-permute-start(f32[2,384,2048]{2,1,0:T(8,128)} %fusion.24), channel_id=1, source_target_pairs={{0,1},{1,0},{2,3},{3,2},{4,5},{5,4},{6,7},{7,6},{8,9},{9,8},{10,11... | collective-permute-start | bytes 18874376 | tf_op jit(solution)/shard_map/ppermute | solution.py:343
  559.5 11.1 %collective-permute-start.11 = (f32[2,384,2048]{2,1,0:T(8,128)}, f32[2,384,2048]{2,1,0:T(8,128)}, u32[]{:S(2)}, u32[]{:S(2)}) collective-permute-start(f32[2,384,2048]{2,1,0:T(8,128)} %fusion.20), channel_id=1, source_target_pairs={{0,1},{1,0},{2,3},{3,2},{4,5},{5,4},{6,7},{7,6},{8,9},{9,8},{10,11... | collective-permute-start | bytes 18874376 | tf_op jit(solution)/shard_map/ppermute | solution.py:343
  559.5 11.1 %copy-start.11 = (bf16[2,2,384,1024]{3,2,1,0:T(8,128)(2,1)S(1)}, bf16[2,2,384,1024]{3,2,1,0:T(8,128)(2,1)}, u32[]{:S(2)}) copy-start(bf16[2,2,384,1024]{3,2,1,0:T(8,128)(2,1)} %copy-done.10) | copy-start | bytes 9437188
  559.5 11.1 %copy-start.27 = (bf16[1024,2048]{1,0:T(8,128)(2,1)S(1)}, bf16[1024,2048]{1,0:T(8,128)(2,1)}, u32[]{:S(2)}) copy-start(bf16[1024,2048]{1,0:T(8,128)(2,1)} %all-gather.11.cloned.1.call-done) | copy-start | bytes 12582916
  567.6 9.0 %copy-start.7 = (f32[2,384,2048]{2,1,0:T(8,128)}, f32[2,384,2048]{2,1,0:T(8,128)S(1)}, u32[]{:S(2)}) copy-start(f32[2,384,2048]{2,1,0:T(8,128)S(1)} %fusion.28) | copy-start | bytes 18874372
  569.2 37.4 %collective-permute-start.10 = (bf16[384,2048]{1,0:T(8,128)(2,1)}, bf16[384,2048]{1,0:T(8,128)(2,1)S(1)}, u32[]{:S(2)}, u32[]{:S(2)}) collective-permute-start(bf16[384,2048]{1,0:T(8,128)(2,1)} %fusion.48), channel_id=1, source_target_pairs={{0,2},{2,0},{1,3},{3,1},{4,6},{6,4},{5,7},{7,5},{8,10},{10,8},{9,1... | collective-permute-start | bytes 4718600 | tf_op jit(solution)/shard_map/ppermute | solution.py:127
  576.6 3.2 copy-start.8
  579.8 60.2 %collective-permute-start.12 = (bf16[384,2048]{1,0:T(8,128)(2,1)}, bf16[384,2048]{1,0:T(8,128)(2,1)}, u32[]{:S(2)}, u32[]{:S(2)}) collective-permute-start(bf16[384,2048]{1,0:T(8,128)(2,1)} %fusion.49), channel_id=1, source_target_pairs={{0,2},{2,0},{1,3},{3,1},{4,6},{6,4},{5,7},{7,5},{8,10},{10,8},{9,1... | collective-permute-start | bytes 4718600 | tf_op jit(solution)/shard_map/ppermute | solution.py:127
  580.8 59.2 %copy-start.9 = (f32[2,384,2048]{2,1,0:T(8,128)S(1)}, f32[2,384,2048]{2,1,0:T(8,128)}, u32[]{:S(2)}) copy-start(f32[2,384,2048]{2,1,0:T(8,128)} %copy-done.8) | copy-start | bytes 18874372
  642.7 12.6 %copy-start.1 = (f32[32,64,128]{2,1,0:T(8,128)S(1)}, f32[32,64,128]{2,1,0:T(8,128)}, u32[]{:S(2)}) copy-start(f32[32,64,128]{2,1,0:T(8,128)} %param.35) | copy-start | bytes 3145732
Sparse Core Ops, SparseCore 0:
  45.3 165.1 all-gather.4
  249.3 130.4 all-gather.6
  381.8 84.4 all-gather.8
  468.2 82.6 all-gather.10

commit v6 on v5

--- a/solution.py
+++ b/solution.py
@@ -230,10 +230,8 @@
     )
     z_full = lax.all_gather(z_local, "pair", axis=0, tiled=True)
     block = out_local.shape[1] // 2
-    out_first, _ = lax.optimization_barrier((out_local[:, :block], z_full))
-    out_first = lax.all_gather(out_first, "pair", axis=1, tiled=True)
-    out_second, _ = lax.optimization_barrier((out_local[:, block:], out_first))
-    out_second = lax.all_gather(out_second, "pair", axis=1, tiled=True)
+    out_first = lax.all_gather(out_local[:, :block], "pair", axis=1, tiled=True)
+    out_second = lax.all_gather(out_local[:, block:], "pair", axis=1, tiled=True)
     proj_z = jnp.dot(normed, z_full, preferred_element_type=jnp.float32).astype(jnp.bfloat16)
 
     position = lax.axis_index("pair") * row_count + jnp.arange(row_count, dtype=jnp.int32)

time: 673 us -> 670 us (level)
  starting transfers between devices: 22.5 us -> 40.2 us
  waiting for transfers between devices: 298 us -> 281 us
    all_gather x1, waiting for transfers between devices: 75.8 us -> 0.01 us  [body(): z_full = lax.all_gather(z_local, 'pair', axis=0, tiled=True)]
    all_gather x2, waiting for transfers between devices: 24.3 us -> 82.6 us  [the longest x1 66.5 us: body(): out_first = lax.all_gather(out_local[:, :block], 'pair', axis=1, tiled=True)]
    ppermute x4, starting transfers between devices: 11.8 us -> 29.1 us  [from_behind(): lax.ppermute(value, axis, [(source, source + steps) for source in range(l...]
  transfers between devices with their start and end apart: 17 -> 17, of which waited for: 11 -> 9; matrix products, arithmetic and copies ran while one was open for 39% -> 38% of each run, Pallas kernels for 0% -> 0%
where the time goes in v6:
time: 670 us; the launch traced here: 661 us
  waiting for transfers between devices  281 us (42%)
  matrix products  114 us (17%)
  local copies, waits for them, and re-layouts  106 us (16%)
  other arithmetic  106 us (16%)
  starting transfers between devices  40.2 us (6%)
  between operations  14.9 us (2%)
    ppermute x6, waiting for transfers between devices, swap_half(): lax.ppermute(value, 'half', [(k, count - 1 - k) for k in range(count)])  144 us
    all_gather x1, waiting for transfers between devices, body(): out_first = lax.all_gather(out_local[:, :block], 'pair', axis=1, tiled=True)  66.5 us
    all_gather x1, waiting for transfers between devices, body(): first_full = lax.all_gather(first_local, 'pair', axis=0, tiled=True)  53.4 us
    dot_general x4, matrix products, body(): jnp.einsum('hrc,cd->hrd', rows, columns, preferred_element_type=jnp.float32)  31.3 us
    ppermute x4, starting transfers between devices, from_behind(): lax.ppermute(value, axis, [(source, source + steps) for source in range(l...  29.1 us
    dot_general x1, matrix products, body(): jnp.dot(normed, z_full, preferred_element_type=jnp.float32)  27.2 us
    dot_general x1, matrix products, body(): jnp.dot(normed, first_full, preferred_element_type=jnp.float32)  23.7 us
    reshape x2, local copies, waits for them, and re-layouts, body(): (direct + state_gain[..., None] * from_state).reshape(row_count, inner_lo...  23 us
  transfers between devices with their start and end apart: 17, of which 9 were waited for; matrix products, arithmetic and copies ran while one was open for 38% of the time, Pallas kernels for 0%

profile of v6, /device:TPU:0, one launch (start us, length us, event | category | flops | bytes accessed | tf_op | source)
XLA Modules:
  0.0 661.2 jit_solution(15657321310560683049)
XLA Ops:
  6.6 6.9 %fusion.111 = (bf16[256,1,2048]{2,1,0:T(2,128)(2,1)}, bf16[256,1,2048]{2,1,0:T(2,128)(2,1)}) fusion(bf16[256,2,2048]{2,1,0:T(2,128)(2,1)} %param.22), kind=kLoop, calls=%fused_computation.232 | loop fusion | bytes 4194304 | tf_op jit(solution)/shard_map/slice | solution.py:197
  16.4 3.7 constant_dynamic-slice_fusion.19
  21.5 2.9 collective-permute-start.2
  26.9 12.7 %collective-permute-done.2 = bf16[256,1296]{0,1:T(8,128)(2,1)S(1)} collective-permute-done((bf16[256,1296]{0,1:T(8,128)(2,1)}, bf16[256,1296]{0,1:T(8,128)(2,1)S(1)}, u32[]{:S(2)}, u32[]{:S(2)}) %collective-permute-start.2) | collective-permute-done | bytes 663584 | tf_op jit(solution)/shard_map/ppermute | solution.py:127
  39.9 6.2 maximum_select_fusion.3
  46.5 4.1 fusion.3
  50.6 5.3 fusion.5
  56.0 2.8 copy-done.4
  59.0 1.8 collective-permute-start
  60.9 67.7 %collective-permute-done = bf16[384,4096]{1,0:T(8,128)(2,1)} collective-permute-done((bf16[384,4096]{1,0:T(8,128)(2,1)S(1)}, bf16[384,4096]{1,0:T(8,128)(2,1)}, u32[]{:S(2)}, u32[]{:S(2)}) %collective-permute-start) | collective-permute-done | bytes 3145760 | tf_op jit(solution)/shard_map/ppermute | solution.py:127
  131.7 2.2 copy.291
  134.2 2.4 reduce-window.30
  137.0 5.0 fusion.34
  142.0 4.4 gather_fusion.1
  146.3 4.3 gather_fusion
  150.7 3.6 pad_maximum_fusion
  154.3 3.7 bitcast_select_fusion
  158.0 53.4 %all-gather.5.cloned.1.call-done = bf16[4096,1296]{1,0:T(8,128)(2,1)} async-done(((bf16[512,1296]{1,0:T(8,128)(2,1)}), bf16[4096,1296]{1,0:T(8,128)(2,1)}) %all-gather.5.cloned.1.call-update) | async-done | bytes 10616848 | tf_op jit(solution)/shard_map/all_gather | solution.py:211
  211.5 23.7 %convolution_convert_fusion = bf16[1536,1296]{0,1:T(8,128)(2,1)} fusion(bf16[4096,1296]{1,0:T(8,128)(2,1)} %all-gather.5.cloned.1.call-done, bf16[768,4096]{1,0:T(8,128)(2,1)} %bitcast_select_fusion, bf16[768,4096]{1,0:T(8,128)(2,1)} %copy-done.4, pred[]{:T(512)S(6)} %eq.204), kind=kOutput, calls=%fused_computation.27 | convolution fusion | flops 16366067712 | bytes 27181056 | tf_op jit(solution)/shard_map/dot_general | solution.py:212
  236.1 1.5 collective-permute-start.7
  240.7 8.8 %collective-permute-done.7 = bf16[256,1024]{1,0:T(8,128)(2,1)S(1)} collective-permute-done((bf16[256,1024]{1,0:T(8,128)(2,1)}, bf16[256,1024]{1,0:T(8,128)(2,1)S(1)}, u32[]{:S(2)}, u32[]{:S(2)}) %collective-permute-start.7) | collective-permute-done | bytes 524320 | tf_op jit(solution)/shard_map/ppermute | solution.py:127
  249.5 1.5 maximum_select_fusion.4
  256.1 1.9 slice.157
  259.2 3.4 reduce-window.21
  263.4 2.1 constant_dynamic-slice_fusion.2
  266.9 2.5 collective-permute-start.3
  271.5 4.3 slice.152
  277.2 21.3 %multiply_convert_fusion.3 = bf16[1536,1280]{0,1:T(8,128)(2,1)S(1)} fusion(bf16[1536,1280]{0,1:T(8,128)(2,1)} %slice.152, bf16[3,1280]{0,1:T(8,128)(2,1)S(1)} %collective-permute-done.3, f32[1280]{0:T(1024)S(1)} %get-tuple-element.132, f32[1280]{0:T(1024)S(1)} %get-tuple-element.133, f32[1280]{0:T(1024)S(1)} %get-tuple-element.134, ...), kind=kLoop, calls=%fused_computation.26 | loop fusion | flops 104202240 | bytes 7933952 | tf_op jit(solution)/shard_map/convert_element_type | solution.py:68
  298.5 1.8 copy-done.3
  304.0 7.1 %fusion.109 = (bf16[1536,1024]{0,1:T(8,128)(2,1)}, f32[1536,1024]{0,1:T(8,128)}) fusion(bf16[1536,1280]{0,1:T(8,128)(2,1)} %copy-done.3), kind=kLoop, calls=%fused_computation.230 | loop fusion | flops 1572864 | bytes 12582912 | tf_op jit(solution)/shard_map/slice | solution.py:269
  311.1 7.5 %reshape.581 = bf16[6,256,16,64]{1,0,3,2:T(8,128)(2,1)} reshape(bf16[1536,1024]{0,1:T(8,128)(2,1)} %get-tuple-element.159) | data formatting | bytes 6291456 | tf_op jit(solution)/shard_map/reshape.49
  318.6 3.2 multiply_convert_fusion.2
  321.8 2.7 add_bitcast_fusion
  324.5 12.6 %while.17 = (s32[]{:T(128)}, f32[1,16,64,128]{3,2,1,0:T(8,128)S(1)}, f32[1,16]{1,0:T(1,128)S(1)}, f32[6,1,16,64,128]{4,3,2,1,0:T(8,128)}, f32[6,1,16]{2,0,1:T(8,...) while((s32[]{:T(128)}, ...), condition=%wide.region_15.16_spmd.clone, body=%wide.region_14.15_spmd.clone.sunk | while | flops 524323 | bytes 2622149 | solution.py:310
  337.1 8.8 %collective-permute-start.4 = (f32[1,16,64,128]{3,2,1,0:T(8,128)S(1)}, f32[1,16,64,128]{3,2,1,0:T(8,128)S(1)}, u32[]{:S(2)}, u32[]{:S(2)}) collective-permute-start(f32[1,16,64,128]{3,2,1,0:T(8,128)S(1)} %get-tuple-element.48), channel_id=1, source_target_pairs={{0,4},{4,8},{8,12},{12,16},{16,20},{20,24},{24,28},{1,5},{5,9},{9,... | collective-permute-start | bytes 1572872 | tf_op jit(solution)/shard_map/ppermute | solution.py:15
  345.9 12.3 %collective-permute-start.6 = (f32[1,16,64,128]{3,2,1,0:T(8,128)S(1)}, f32[1,16,64,128]{3,2,1,0:T(8,128)}, u32[]{:S(2)}, u32[]{:S(2)}) collective-permute-start(f32[1,16,64,128]{3,2,1,0:T(8,128)S(1)} %get-tuple-element.48), channel_id=1, source_target_pairs={{0,8},{4,12},{8,16},{12,20},{16,24},{20,28},{1,9},{5,13},{9,17},{1... | collective-permute-start | bytes 1572872 | tf_op jit(solution)/shard_map/ppermute | solution.py:15
  358.2 8.7 %reshape.604 = f32[6,256,1,16,64]{1,0,4,3,2:T(8,128)} reshape(f32[1536,1024]{0,1:T(8,128)} %get-tuple-element.160) | data formatting | bytes 12582912 | tf_op jit(solution)/shard_map/convert_element_type | solution.py:119
  367.1 5.5 collective-permute-start.5
  372.6 1.5 fusion.116
  374.2 5.2 fusion.60
  380.2 1.5 add_bitcast_fusion.1
  381.7 5.3 fusion.37
  387.1 16.9 %fusion.17 = f32[6,256,1,16,64]{1,4,3,0,2:T(8,128)} fusion(f32[6,256,1,16,64]{1,0,4,3,2:T(8,128)} %reshape.604, f32[6,256,16,64]{1,3,2,0:T(8,128)S(1)} %fusion.37, f32[6,256,16,64]{1,3,2,0:T(8,128)S(1)} %copy-done.5, f32[6,256,16]{1,2,0:T(8,128)S(1)} %copy-done.19, f32[16]{0:T(128)S(1)} %copy-done.33, f32[6,256,16]{1,2,0:T(8,128)S(1)} %copy-done.18, ...), kind=kOutput, calls=%fused_computation.37 | convolution fusion | flops 852492288 | bytes 30670912 | tf_op jit(solution)/shard_map/cghqs,csghp->cqghp/dot_general | solution.py:20
  404.0 11.4 %copy.234 = f32[6,256,1,16,64]{4,3,1,0,2:T(8,128)} copy(f32[6,256,1,16,64]{1,4,3,0,2:T(8,128)} %fusion.17) | data formatting | bytes 12582912 | tf_op jit(solution)/shard_map/reshape | solution.py:322
  415.4 11.6 %reshape.626 = f32[1536,1024]{1,0:T(8,128)} reshape(f32[6,256,1,16,64]{4,3,1,0,2:T(8,128)} %copy.234) | data formatting | bytes 12582912 | tf_op jit(solution)/shard_map/reshape | solution.py:322
  427.0 27.2 %multiply_reduce_fusion = (f32[1536]{0:T(1024)S(1)}, f32[1536,1024]{1,0:T(8,128)}) fusion(f32[1536,1024]{1,0:T(8,128)} %reshape.626, bf16[4096,1024]{1,0:T(8,128)(2,1)} %all-gather.7.cloned.1.call-done, bf16[768,4096]{1,0:T(8,128)(2,1)} %bitcast_select_fusion, bf16[768,4096]{1,0:T(8,128)(2,1)} %copy-done.4, pred[]{:T(512)S(6)} %eq.204), kind=kOutput, calls=%fused_computation.41 | convolution fusion | flops 12955678720 | bytes 33560576 | tf_op jit(solution)/shard_map/dot_general | solution.py:235
  454.2 3.3 broadcast_multiply_fusion
  457.5 2.6 multiply_convert_fusion.4
  460.1 16.1 %all-gather.11.cloned.1.call-done = bf16[1024,2048]{1,0:T(8,128)(2,1)} async-done(((bf16[1024,256]{1,0:T(8,128)(2,1)}), bf16[1024,2048]{1,0:T(8,128)(2,1)}) %all-gather.11.cloned.1.call-update) | async-done | bytes 4194320 | tf_op jit(solution)/shard_map/all_gather | solution.py:234
  476.3 8.7 %fusion.20 = f32[2,384,2048]{2,1,0:T(8,128)} fusion(bf16[1024,2048]{1,0:T(8,128)(2,1)} %all-gather.11.cloned.1.call-done, bf16[2,2,384,1024]{3,2,1,0:T(8,128)(2,1)} %multiply_convert_fusion.4, s32[]{:T(128)S(6)} %select_n.329), kind=kOutput, calls=%fused_computation.46 | convolution fusion | flops 3221225472 | bytes 12058628 | tf_op jit(solution)/shard_map/hrc,cd->hrd/dot_general | solution.py:339
  484.9 66.5 %all-gather.9.cloned.1.call-done = bf16[1024,2048]{1,0:T(8,128)(2,1)} async-done(((bf16[1024,256]{1,0:T(8,128)(2,1)}), bf16[1024,2048]{1,0:T(8,128)(2,1)}) %all-gather.9.cloned.1.call-update) | async-done | bytes 4194320 | tf_op jit(solution)/shard_map/all_gather | solution.py:233
  551.4 8.7 %fusion.24 = f32[2,384,2048]{2,1,0:T(8,128)} fusion(bf16[1024,2048]{1,0:T(8,128)(2,1)} %all-gather.9.cloned.1.call-done, bf16[2,2,384,1024]{3,2,1,0:T(8,128)(2,1)} %multiply_convert_fusion.4, s32[]{:T(128)S(6)} %select_n.329), kind=kOutput, calls=%fused_computation.50 | convolution fusion | flops 3221225472 | bytes 12058628 | tf_op jit(solution)/shard_map/hrc,cd->hrd/dot_general | solution.py:339
  560.1 8.1 %fusion.31 = f32[2,384,2048]{2,1,0:T(8,128)S(1)} fusion(f32[2,384,2048]{2,1,0:T(8,128)} %collective-permute-done.11, bf16[1024,2048]{1,0:T(8,128)(2,1)} %all-gather.11.cloned.1.call-done, bf16[2,2,384,1024]{3,2,1,0:T(8,128)(2,1)} %multiply_convert_fusion.4, s32[]{:T(128)S(6)} %select_n.333), kind=kOutput, calls=%fused_computation.57 | convolution fusion | flops 3222798336 | bytes 18350084 | tf_op jit(solution)/shard_map/hrc,cd->hrd/dot_general | solution.py:339
  568.4 1.5 collective-permute-start.12
  570.6 5.8 fusion.28
  576.5 1.6 fusion.48
  578.0 1.6 copy-done.7
  579.6 1.5 collective-permute-start.10
  581.1 24.6 %collective-permute-done.12 = bf16[384,2048]{1,0:T(8,128)(2,1)S(1)} collective-permute-done((bf16[384,2048]{1,0:T(8,128)(2,1)S(1)}, bf16[384,2048]{1,0:T(8,128)(2,1)S(1)}, u32[]{:S(2)}, u32[]{:S(2)}) %collective-permute-start.12) | collective-permute-done | bytes 1572896 | tf_op jit(solution)/shard_map/ppermute | solution.py:127
  605.7 2.4 fusion.35
  608.6 30.5 %collective-permute-done.10 = bf16[384,2048]{1,0:T(8,128)(2,1)} collective-permute-done((bf16[384,2048]{1,0:T(8,128)(2,1)}, bf16[384,2048]{1,0:T(8,128)(2,1)}, u32[]{:S(2)}, u32[]{:S(2)}) %collective-permute-start.10) | collective-permute-done | bytes 1572896 | tf_op jit(solution)/shard_map/ppermute | solution.py:127
  639.1 2.0 fusion.36
  641.9 6.5 copy.231
  648.4 6.1 reshape.596
  (229 shorter events, 45.8 us)
Async XLA Ops:
  6.5 247.0 %copy-start = (f32[32,64,128]{2,1,0:T(8,128)S(1)}, f32[32,64,128]{2,1,0:T(8,128)}, u32[]{:S(2)}) copy-start(f32[32,64,128]{2,1,0:T(8,128)} %param.35) | copy-start | bytes 3145732
  6.5 6.9 %copy-start.22 = (bf16[256,32]{0,1:T(8,128)(2,1)S(1)}, bf16[256,32]{0,1:T(8,128)(2,1)}, u32[]{:S(2)}) copy-start(bf16[256,32]{0,1:T(8,128)(2,1)} %param.24) | copy-start | bytes 49156
  6.5 204.9 %all-gather.5.cloned.1.call-start = ((), (), s32[]{:S(2)}) async-start(), calls=%async_computation | async-start | bytes 12976128 | tf_op jit(solution)/shard_map/all_gather | solution.py:211
  6.5 7.6 %copy-start.11 = (bf16[256,2,256]{2,1,0:T(2,128)(2,1)S(1)}, bf16[256,2,256]{2,1,0:T(2,128)(2,1)}, u32[]{:S(2)}) copy-start(bf16[256,2,256]{2,1,0:T(2,128)(2,1)} %param.23) | copy-start | bytes 786436
  16.4 3.9 copy-start.15
  16.4 3.9 copy-start.16
  21.5 18.1 %collective-permute-start.2 = (bf16[256,1296]{0,1:T(8,128)(2,1)}, bf16[256,1296]{0,1:T(8,128)(2,1)S(1)}, u32[]{:S(2)}, u32[]{:S(2)}) collective-permute-start(bf16[256,1296]{0,1:T(8,128)(2,1)} %copy.207), channel_id=1, source_target_pairs={{0,2},{2,0},{1,3},{3,1},{4,6},{6,4},{5,7},{7,5},{8,10},{10,8},{9,1... | collective-permute-start | bytes 1990664 | tf_op jit(solution)/shard_map/ppermute | solution.py:127
  46.1 4.5 copy-start.21
  46.2 380.8 %all-gather.7.cloned.1.call-start = ((), (), s32[]{:S(2)}) async-start(), calls=%async_computation.1 | async-start | bytes 9437184 | tf_op jit(solution)/shard_map/all_gather | solution.py:231
  55.9 2.8 copy-start.4
  58.8 70.4 %copy-start.28 = (s32[8]{0:T(128)S(1)}, s32[8]{0:T(128)}, u32[]{:S(2)}) copy-start(s32[8]{0:T(128)} %param.32) | copy-start | bytes 100
  58.8 70.4 %copy-start.29 = (s32[8]{0:T(128)S(1)}, s32[8]{0:T(128)}, u32[]{:S(2)}) copy-start(s32[8]{0:T(128)} %param.33) | copy-start | bytes 100
  58.8 75.3 %copy-start.23 = (bf16[4,2,256]{2,1,0:T(2,128)(2,1)S(1)}, bf16[4,2,256]{2,1,0:T(2,128)(2,1)}, u32[]{:S(2)}) copy-start(bf16[4,2,256]{2,1,0:T(2,128)(2,1)} %param.26) | copy-start | bytes 12292
  58.8 78.1 %copy-start.24 = (bf16[3,2,256]{2,1,0:T(2,128)(2,1)S(1)}, bf16[3,2,256]{2,1,0:T(2,128)(2,1)}, u32[]{:S(2)}) copy-start(bf16[3,2,256]{2,1,0:T(2,128)(2,1)} %param.37) | copy-start | bytes 9220
  59.0 69.5 %collective-permute-start = (bf16[384,4096]{1,0:T(8,128)(2,1)S(1)}, bf16[384,4096]{1,0:T(8,128)(2,1)}, u32[]{:S(2)}, u32[]{:S(2)}) collective-permute-start(bf16[384,4096]{1,0:T(8,128)(2,1)S(1)} %constant_dynamic-slice_fusion.20), channel_id=1, source_target_pairs={{0,2},{2,0},{1,3},{3,1},{4,6},{6,4},{5,7},{7,5},{8,10},{10,8},{9,1... | collective-permute-start | bytes 9437192 | tf_op jit(solution)/shard_map/ppermute | solution.py:127
  128.5 8.5 %collective-permute-start.1 = (bf16[384,4096]{1,0:T(8,128)(2,1)}, bf16[384,4096]{1,0:T(8,128)(2,1)}, u32[]{:S(2)}, u32[]{:S(2)}) collective-permute-start(bf16[384,4096]{1,0:T(8,128)(2,1)} %collective-permute-done), channel_id=1, source_target_pairs={{0,1},{1,0},{2,3},{3,2},{4,5},{5,4},{6,7},{7,6},{8,9},{9,8},{10,11... | collective-permute-start | bytes 9437192 | tf_op jit(solution)/shard_map/ppermute | solution.py:186
  158.0 79.6 %copy-start.30 = (f32[32]{0:T(128)S(1)}, f32[32]{0:T(128)}, u32[]{:S(2)}) copy-start(f32[32]{0:T(128)} %param.27) | copy-start | bytes 388
  158.0 79.7 %copy-start.31 = (f32[32]{0:T(128)S(1)}, f32[32]{0:T(128)}, u32[]{:S(2)}) copy-start(f32[32]{0:T(128)} %param.28) | copy-start | bytes 388
  158.0 79.7 %copy-start.32 = (f32[32]{0:T(128)S(1)}, f32[32]{0:T(128)}, u32[]{:S(2)}) copy-start(f32[32]{0:T(128)} %param.29) | copy-start | bytes 388
  235.2 17.9 %copy-start.25 = (bf16[4,2048]{1,0:T(4,128)(2,1)S(1)}, bf16[4,2048]{1,0:T(4,128)(2,1)}, u32[]{:S(2)}) copy-start(bf16[4,2048]{1,0:T(4,128)(2,1)} %param.25) | copy-start | bytes 49156
  235.2 18.0 %copy-start.26 = (bf16[3,2048]{1,0:T(4,128)(2,1)S(1)}, bf16[3,2048]{1,0:T(4,128)(2,1)}, u32[]{:S(2)}) copy-start(bf16[3,2048]{1,0:T(4,128)(2,1)} %param.36) | copy-start | bytes 36868
  236.1 13.5 %collective-permute-start.7 = (bf16[256,1024]{1,0:T(8,128)(2,1)}, bf16[256,1024]{1,0:T(8,128)(2,1)S(1)}, u32[]{:S(2)}, u32[]{:S(2)}) collective-permute-start(bf16[256,1024]{1,0:T(8,128)(2,1)} %get-tuple-element.170), channel_id=1, source_target_pairs={{0,2},{2,0},{1,3},{3,1},{4,6},{6,4},{5,7},{7,5},{8,10},{10,8},{9,1... | collective-permute-start | bytes 1572872 | tf_op jit(solution)/shard_map/ppermute | solution.py:127
  251.1 225.2 %all-gather.11.cloned.1.call-start = ((), (), s32[]{:S(2)}) async-start(), calls=%async_computation.3 | async-start | bytes 4718592 | tf_op jit(solution)/shard_map/all_gather | solution.py:234
  265.5 35.2 %collective-permute-start.8 = (bf16[1024,256]{1,0:T(8,128)(2,1)}, bf16[1024,256]{1,0:T(8,128)(2,1)S(1)}, u32[]{:S(2)}, u32[]{:S(2)}) collective-permute-start(bf16[1024,256]{1,0:T(8,128)(2,1)} %get-tuple-element.172), channel_id=1, source_target_pairs={{0,2},{2,0},{1,3},{3,1},{4,6},{6,4},{5,7},{7,5},{8,10},{10,8},{9,1... | collective-permute-start | bytes 1572872 | tf_op jit(solution)/shard_map/ppermute | solution.py:127
  266.9 10.3 %collective-permute-start.3 = (bf16[3,1280]{0,1:T(8,128)(2,1)}, bf16[3,1280]{0,1:T(8,128)(2,1)S(1)}, u32[]{:S(2)}, u32[]{:S(2)}) collective-permute-start(bf16[3,1280]{0,1:T(8,128)(2,1)} %slice.157), channel_id=1, source_target_pairs={{0,4},{4,8},{8,12},{12,16},{16,20},{20,24},{24,28},{1,5},{5,9},{9,... | collective-permute-start | bytes 23048 | tf_op jit(solution)/shard_map/ppermute | solution.py:15
  298.5 1.9 copy-start.3
  300.7 0.8 copy-start.12
  304.0 247.4 %all-gather.9.cloned.1.call-start = ((), (), s32[]{:S(2)}) async-start(), calls=%async_computation.2 | async-start | bytes 4718592 | tf_op jit(solution)/shard_map/all_gather | solution.py:233
  337.1 42.4 %collective-permute-start.4 = (f32[1,16,64,128]{3,2,1,0:T(8,128)S(1)}, f32[1,16,64,128]{3,2,1,0:T(8,128)S(1)}, u32[]{:S(2)}, u32[]{:S(2)}) collective-permute-start(f32[1,16,64,128]{3,2,1,0:T(8,128)S(1)} %get-tuple-element.48), channel_id=1, source_target_pairs={{0,4},{4,8},{8,12},{12,16},{16,20},{20,24},{24,28},{1,5},{5,9},{9,... | collective-permute-start | bytes 1572872 | tf_op jit(solution)/shard_map/ppermute | solution.py:15
  345.9 33.5 %collective-permute-start.6 = (f32[1,16,64,128]{3,2,1,0:T(8,128)S(1)}, f32[1,16,64,128]{3,2,1,0:T(8,128)}, u32[]{:S(2)}, u32[]{:S(2)}) collective-permute-start(f32[1,16,64,128]{3,2,1,0:T(8,128)S(1)} %get-tuple-element.48), channel_id=1, source_target_pairs={{0,8},{4,12},{8,16},{12,20},{16,24},{20,28},{1,9},{5,13},{9,17},{1... | collective-permute-start | bytes 1572872 | tf_op jit(solution)/shard_map/ppermute | solution.py:15
  367.1 12.3 %collective-permute-start.5 = (f32[1,16]{1,0:T(1,128)S(1)}, f32[1,16]{1,0:T(1,128)S(1)}, u32[]{:S(2)}, u32[]{:S(2)}) collective-permute-start(f32[1,16]{1,0:T(1,128)S(1)} %get-tuple-element.49), channel_id=1, source_target_pairs={{0,4},{4,8},{8,12},{12,16},{16,20},{20,24},{24,28},{1,5},{5,9},{9,... | collective-permute-start | bytes 200 | tf_op jit(solution)/shard_map/ppermute | solution.py:15
  374.2 12.9 %copy-start.17 = (f32[6,16,256]{2,1,0:T(8,128)S(1)}, f32[6,16,256]{2,1,0:T(8,128)}, u32[]{:S(2)}) copy-start(f32[6,16,256]{2,1,0:T(8,128)} %copy.216) | copy-start | bytes 294916
  374.2 12.9 %copy-start.18 = (f32[6,256,16]{1,2,0:T(8,128)S(1)}, f32[6,256,16]{1,2,0:T(8,128)}, u32[]{:S(2)}) copy-start(f32[6,256,16]{1,2,0:T(8,128)} %fusion.124) | copy-start | bytes 294916
  374.2 12.9 %copy-start.19 = (f32[6,256,16]{1,2,0:T(8,128)S(1)}, f32[6,256,16]{1,2,0:T(8,128)}, u32[]{:S(2)}) copy-start(f32[6,256,16]{1,2,0:T(8,128)} %get-tuple-element.151) | copy-start | bytes 294916
  374.2 12.9 %copy-start.20 = (f32[6,16,256]{2,1,0:T(8,128)S(1)}, f32[6,16,256]{2,1,0:T(8,128)}, u32[]{:S(2)}) copy-start(f32[6,16,256]{2,1,0:T(8,128)} %reduce_window_sum.55) | copy-start | bytes 294916
  379.4 7.7 %copy-start.10 = (f32[6,256,256]{2,1,0:T(8,128)S(1)}, f32[6,256,256]{2,1,0:T(8,128)}, u32[]{:S(2)}) copy-start(f32[6,256,256]{2,1,0:T(8,128)} %fusion.116) | copy-start | bytes 4718596
  379.4 0.8 copy-start.13
  380.2 6.9 %copy-start.5 = (f32[6,256,16,64]{1,3,2,0:T(8,128)S(1)}, f32[6,256,16,64]{1,3,2,0:T(8,128)}, u32[]{:S(2)}) copy-start(f32[6,256,16,64]{1,3,2,0:T(8,128)} %fusion.60) | copy-start | bytes 18874372
  381.7 5.4 copy-start.2
  381.7 5.4 copy-start.14
  381.7 5.4 copy-start.33
  454.2 3.3 dynamic-slice-start
  484.9 75.2 %collective-permute-start.11 = (f32[2,384,2048]{2,1,0:T(8,128)}, f32[2,384,2048]{2,1,0:T(8,128)}, u32[]{:S(2)}, u32[]{:S(2)}) collective-permute-start(f32[2,384,2048]{2,1,0:T(8,128)} %fusion.20), channel_id=1, source_target_pairs={{0,1},{1,0},{2,3},{3,2},{4,5},{5,4},{6,7},{7,6},{8,9},{9,8},{10,11... | collective-permute-start | bytes 18874376 | tf_op jit(solution)/shard_map/ppermute | solution.py:341
  560.1 10.5 %collective-permute-start.9 = (f32[2,384,2048]{2,1,0:T(8,128)}, f32[2,384,2048]{2,1,0:T(8,128)}, u32[]{:S(2)}, u32[]{:S(2)}) collective-permute-start(f32[2,384,2048]{2,1,0:T(8,128)} %fusion.24), channel_id=1, source_target_pairs={{0,1},{1,0},{2,3},{3,2},{4,5},{5,4},{6,7},{7,6},{8,9},{9,8},{10,11... | collective-permute-start | bytes 18874376 | tf_op jit(solution)/shard_map/ppermute | solution.py:341
  560.1 10.5 %copy-start.9 = (bf16[2,2,384,1024]{3,2,1,0:T(8,128)(2,1)S(1)}, bf16[2,2,384,1024]{3,2,1,0:T(8,128)(2,1)}, u32[]{:S(2)}) copy-start(bf16[2,2,384,1024]{3,2,1,0:T(8,128)(2,1)} %multiply_convert_fusion.4) | copy-start | bytes 9437188
  560.1 10.5 %copy-start.27 = (bf16[1024,2048]{1,0:T(8,128)(2,1)S(1)}, bf16[1024,2048]{1,0:T(8,128)(2,1)}, u32[]{:S(2)}) copy-start(bf16[1024,2048]{1,0:T(8,128)(2,1)} %all-gather.9.cloned.1.call-done) | copy-start | bytes 12582916
  568.2 8.3 %copy-start.6 = (f32[2,384,2048]{2,1,0:T(8,128)}, f32[2,384,2048]{2,1,0:T(8,128)S(1)}, u32[]{:S(2)}) copy-start(f32[2,384,2048]{2,1,0:T(8,128)S(1)} %fusion.31) | copy-start | bytes 18874372
  568.4 37.3 %collective-permute-start.12 = (bf16[384,2048]{1,0:T(8,128)(2,1)S(1)}, bf16[384,2048]{1,0:T(8,128)(2,1)S(1)}, u32[]{:S(2)}, u32[]{:S(2)}) collective-permute-start(bf16[384,2048]{1,0:T(8,128)(2,1)S(1)} %fusion.49), channel_id=1, source_target_pairs={{0,2},{2,0},{1,3},{3,1},{4,6},{6,4},{5,7},{7,5},{8,10},{10,8},{9,1... | collective-permute-start | bytes 4718600 | tf_op jit(solution)/shard_map/ppermute | solution.py:127
  576.5 3.2 copy-start.7
  579.6 59.5 %collective-permute-start.10 = (bf16[384,2048]{1,0:T(8,128)(2,1)}, bf16[384,2048]{1,0:T(8,128)(2,1)}, u32[]{:S(2)}, u32[]{:S(2)}) collective-permute-start(bf16[384,2048]{1,0:T(8,128)(2,1)} %fusion.48), channel_id=1, source_target_pairs={{0,2},{2,0},{1,3},{3,1},{4,6},{6,4},{5,7},{7,5},{8,10},{10,8},{9,1... | collective-permute-start | bytes 4718600 | tf_op jit(solution)/shard_map/ppermute | solution.py:127
  581.1 58.0 %copy-start.8 = (f32[2,384,2048]{2,1,0:T(8,128)S(1)}, f32[2,384,2048]{2,1,0:T(8,128)}, u32[]{:S(2)}) copy-start(f32[2,384,2048]{2,1,0:T(8,128)} %copy-done.7) | copy-start | bytes 18874372
  641.9 12.6 %copy-start.1 = (f32[32,64,128]{2,1,0:T(8,128)S(1)}, f32[32,64,128]{2,1,0:T(8,128)}, u32[]{:S(2)}) copy-start(f32[32,64,128]{2,1,0:T(8,128)} %param.35) | copy-start | bytes 3145732
Sparse Core Ops, SparseCore 0:
  46.3 165.1 all-gather.4
  251.2 136.0 all-gather.6
  389.3 86.8 all-gather.10
  478.2 73.1 all-gather.8

commit v7 on v6

--- a/solution.py
+++ b/solution.py
@@ -231,7 +231,6 @@
     z_full = lax.all_gather(z_local, "pair", axis=0, tiled=True)
     block = out_local.shape[1] // 2
     out_first = lax.all_gather(out_local[:, :block], "pair", axis=1, tiled=True)
-    out_second = lax.all_gather(out_local[:, block:], "pair", axis=1, tiled=True)
     proj_z = jnp.dot(normed, z_full, preferred_element_type=jnp.float32).astype(jnp.bfloat16)
 
     position = lax.axis_index("pair") * row_count + jnp.arange(row_count, dtype=jnp.int32)
@@ -332,11 +331,18 @@
     piece = own_rows // core_count
     by_owner = normed_y.reshape(2, core_count, piece, inner_local)
     results = []
-    for columns in (out_first, out_second):
+    second_local = out_local[:, block:]
+    for index in range(2):
+        columns = out_first
+        if index:
+            columns, results[0] = lax.optimization_barrier((out_second, results[0]))
         total = None
         for shift in list(range(1, core_count)) + [0]:
             rows = lax.dynamic_index_in_dim(by_owner, (core + shift) % core_count, 1, keepdims=False)
             part = jnp.einsum("hrc,cd->hrd", rows, columns, preferred_element_type=jnp.float32)
+            if index == 0 and total is None:
+                second_local, part = lax.optimization_barrier((second_local, part))
+                out_second = lax.all_gather(second_local, "pair", axis=1, tiled=True)
             if shift:
                 part = lax.ppermute(
                     part, "fsdp", [(j, (j + shift) % core_count) for j in range(core_count)]

time: 670 us -> 657 us (0.981)
  waiting for transfers between devices: 281 us -> 298 us
  starting transfers between devices: 40.2 us -> 23.8 us
  matrix products: 114 us -> 105 us
    ppermute x2, waiting for transfers between devices: 0.63 us -> 20.6 us  [body(): lax.ppermute(part, 'fsdp', [(j, (j + shift) % core_count) for j in range(...]
    ppermute x4, starting transfers between devices: 29.1 us -> 13.3 us  [from_behind(): lax.ppermute(value, axis, [(source, source + steps) for source in range(l...]
    all_gather x1, waiting for transfers between devices: 66.5 us -> 51.7 us  [body(): out_first = lax.all_gather(out_local[:, :block], 'pair', axis=1, tiled=True)]
    ppermute x6, waiting for transfers between devices: 144 us -> 156 us  [swap_half(): lax.ppermute(value, 'half', [(k, count - 1 - k) for k in range(count)])]
    unnamed x84 -> x88, local copies, waits for them, and re-layouts: 15.2 us -> 14.7 us
  transfers between devices with their start and end apart: 17 -> 17, of which waited for: 9 -> 11; matrix products, arithmetic and copies ran while one was open for 38% -> 34% of each run, Pallas kernels for 0% -> 0%
where the time goes in v7:
time: 657 us; the launch traced here: 649 us
  waiting for transfers between devices  298 us (45%)
  matrix products  105 us (16%)
  other arithmetic  104 us (16%)
  local copies, waits for them, and re-layouts  102 us (16%)
  starting transfers between devices  23.8 us (4%)
  between operations  15.2 us (2%)
    ppermute x6, waiting for transfers between devices, swap_half(): lax.ppermute(value, 'half', [(k, count - 1 - k) for k in range(count)])  156 us
    all_gather x1, waiting for transfers between devices, body(): first_full = lax.all_gather(first_local, 'pair', axis=0, tiled=True)  52.6 us
    all_gather x1, waiting for transfers between devices, body(): out_first = lax.all_gather(out_local[:, :block], 'pair', axis=1, tiled=True)  51.7 us
    dot_general x1, matrix products, body(): jnp.dot(normed, z_full, preferred_element_type=jnp.float32)  26.9 us
    dot_general x4, matrix products, body(): jnp.einsum('hrc,cd->hrd', rows, columns, preferred_element_type=jnp.float32)  26.1 us
    reshape x2, local copies, waits for them, and re-layouts, body(): (direct + state_gain[..., None] * from_state).reshape(row_count, inner_lo...  22.8 us
    dot_general x1, matrix products, body(): jnp.dot(normed, first_full, preferred_element_type=jnp.float32)  21.8 us
    convert_element_type x1, other arithmetic, conv_rows(): return jax.nn.silu(summed).astype(jnp.bfloat16)  21.6 us
  transfers between devices with their start and end apart: 17, of which 11 were waited for; matrix products, arithmetic and copies ran while one was open for 34% of the time, Pallas kernels for 0%

profile of v7, /device:TPU:0, one launch (start us, length us, event | category | flops | bytes accessed | tf_op | source)
XLA Modules:
  0.0 648.5 jit_solution(9195791667580933829)
XLA Ops:
  6.6 6.8 %fusion.111 = (bf16[256,1,2048]{2,1,0:T(2,128)(2,1)}, bf16[256,1,2048]{2,1,0:T(2,128)(2,1)}) fusion(bf16[256,2,2048]{2,1,0:T(2,128)(2,1)} %param.22), kind=kLoop, calls=%fused_computation.232 | loop fusion | bytes 4194304 | tf_op jit(solution)/shard_map/slice | solution.py:197
  16.4 3.7 constant_dynamic-slice_fusion.19
  21.4 2.9 collective-permute-start.2
  26.8 12.7 %collective-permute-done.2 = bf16[256,1296]{0,1:T(8,128)(2,1)S(1)} collective-permute-done((bf16[256,1296]{0,1:T(8,128)(2,1)}, bf16[256,1296]{0,1:T(8,128)(2,1)S(1)}, u32[]{:S(2)}, u32[]{:S(2)}) %collective-permute-start.2) | collective-permute-done | bytes 663584 | tf_op jit(solution)/shard_map/ppermute | solution.py:127
  39.8 6.2 maximum_select_fusion.3
  46.4 4.1 fusion.3
  50.5 5.3 fusion.5
  55.8 2.9 copy-done.4
  58.7 1.9 constant_dynamic-slice_fusion.20
  60.6 1.8 collective-permute-start
  65.4 2.2 copy.291
  67.9 2.1 reduce-window.30
  71.9 58.3 %collective-permute-done = bf16[384,4096]{1,0:T(8,128)(2,1)} collective-permute-done((bf16[384,4096]{1,0:T(8,128)(2,1)}, bf16[384,4096]{1,0:T(8,128)(2,1)}, u32[]{:S(2)}, u32[]{:S(2)}) %collective-permute-start) | collective-permute-done | bytes 3145760 | tf_op jit(solution)/shard_map/ppermute | solution.py:127
  138.2 4.5 fusion.34
  142.7 4.4 gather_fusion.1
  147.1 4.4 gather_fusion
  151.4 3.6 pad_maximum_fusion
  155.0 3.7 bitcast_select_fusion
  158.8 52.6 %all-gather.5.cloned.1.call-done = bf16[4096,1296]{1,0:T(8,128)(2,1)} async-done(((bf16[512,1296]{1,0:T(8,128)(2,1)}), bf16[4096,1296]{1,0:T(8,128)(2,1)}) %all-gather.5.cloned.1.call-update) | async-done | bytes 10616848 | tf_op jit(solution)/shard_map/all_gather | solution.py:211
  211.4 21.8 %convolution_convert_fusion = bf16[1536,1296]{0,1:T(8,128)(2,1)S(1)} fusion(bf16[4096,1296]{1,0:T(8,128)(2,1)} %all-gather.5.cloned.1.call-done, bf16[768,4096]{1,0:T(8,128)(2,1)} %bitcast_select_fusion, bf16[768,4096]{1,0:T(8,128)(2,1)} %copy-done.4, pred[]{:T(512)S(6)} %eq.201), kind=kOutput, calls=%fused_computation.27 | convolution fusion | flops 16366067712 | bytes 27181056 | tf_op jit(solution)/shard_map/dot_general | solution.py:212
  233.2 2.1 slice.153
  236.5 3.4 reduce-window.21
  240.8 2.1 constant_dynamic-slice_fusion.11
  242.9 1.5 collective-permute-start.3
  244.4 3.2 collective-permute-start.4
  252.5 15.1 %collective-permute-done.8 = bf16[256,1024]{1,0:T(8,128)(2,1)S(1)} collective-permute-done((bf16[256,1024]{1,0:T(8,128)(2,1)S(1)}, bf16[256,1024]{1,0:T(8,128)(2,1)S(1)}, u32[]{:S(2)}, u32[]{:S(2)}) %collective-permute-start.8) | collective-permute-done | bytes 524320 | tf_op jit(solution)/shard_map/ppermute | solution.py:127
  267.6 1.5 maximum_select_fusion.5
  269.2 21.6 %multiply_convert_fusion.3 = bf16[1536,1280]{0,1:T(8,128)(2,1)S(1)} fusion(bf16[1536,1280]{0,1:T(8,128)(2,1)} %slice.153, bf16[3,1280]{0,1:T(8,128)(2,1)} %collective-permute-done.4, f32[1280]{0:T(1024)S(1)} %get-tuple-element.140, f32[1280]{0:T(1024)S(1)} %get-tuple-element.141, f32[1280]{0:T(1024)S(1)} %get-tuple-element.142, ...), kind=kLoop, calls=%fused_computation.26 | loop fusion | flops 104202240 | bytes 7933952 | tf_op jit(solution)/shard_map/convert_element_type | solution.py:68
  290.9 1.9 copy-done.3
  293.0 6.6 %fusion.109 = (bf16[1536,1024]{0,1:T(8,128)(2,1)}, f32[1536,1024]{0,1:T(8,128)}) fusion(bf16[1536,1280]{0,1:T(8,128)(2,1)} %copy-done.3), kind=kLoop, calls=%fused_computation.230 | loop fusion | flops 1572864 | bytes 12582912 | tf_op jit(solution)/shard_map/slice | solution.py:268
  299.6 7.6 %reshape.581 = bf16[6,256,16,64]{1,0,3,2:T(8,128)(2,1)} reshape(bf16[1536,1024]{0,1:T(8,128)(2,1)} %get-tuple-element.167) | data formatting | bytes 6291456 | tf_op jit(solution)/shard_map/reshape.49
  307.1 3.2 multiply_convert_fusion.2
  310.3 2.7 add_bitcast_fusion
  313.0 12.5 %while.17 = (s32[]{:T(128)}, f32[1,16,64,128]{3,2,1,0:T(8,128)S(1)}, f32[1,16]{1,0:T(1,128)S(1)}, f32[6,1,16,64,128]{4,3,2,1,0:T(8,128)}, f32[6,1,16]{2,0,1:T(8,...) while((s32[]{:T(128)}, ...), condition=%wide.region_15.16_spmd.clone, body=%wide.region_14.15_spmd.clone.sunk | while | flops 524323 | bytes 2622149 | solution.py:309
  325.5 3.4 collective-permute-start.5
  329.0 2.1 collective-permute-start.7
  331.1 8.8 %reshape.604 = f32[6,256,1,16,64]{1,0,4,3,2:T(8,128)} reshape(f32[1536,1024]{0,1:T(8,128)} %get-tuple-element.168) | data formatting | bytes 12582912 | tf_op jit(solution)/shard_map/convert_element_type | solution.py:119
  340.0 4.6 collective-permute-start.6
  344.7 5.2 fusion.60
  353.1 1.5 add_bitcast_fusion.1
  354.6 5.4 fusion.37
  360.1 16.9 %fusion.17 = f32[6,256,1,16,64]{1,4,3,0,2:T(8,128)} fusion(f32[6,256,1,16,64]{1,0,4,3,2:T(8,128)} %reshape.604, f32[6,256,16,64]{1,3,2,0:T(8,128)S(1)} %fusion.37, f32[6,256,16,64]{1,3,2,0:T(8,128)S(1)} %copy-done.5, f32[6,256,16]{1,2,0:T(8,128)S(1)} %copy-done.15, f32[16]{0:T(128)S(1)} %copy-done.35, f32[6,256,16]{1,2,0:T(8,128)S(1)} %copy-done.14, ...), kind=kOutput, calls=%fused_computation.37 | convolution fusion | flops 852492288 | bytes 30670912 | tf_op jit(solution)/shard_map/cghqs,csghp->cqghp/dot_general | solution.py:20
  377.0 11.3 %copy.234 = f32[6,256,1,16,64]{4,3,1,0,2:T(8,128)} copy(f32[6,256,1,16,64]{1,4,3,0,2:T(8,128)} %fusion.17) | data formatting | bytes 12582912 | tf_op jit(solution)/shard_map/reshape | solution.py:321
  388.3 11.5 %reshape.626 = f32[1536,1024]{1,0:T(8,128)} reshape(f32[6,256,1,16,64]{4,3,1,0,2:T(8,128)} %copy.234) | data formatting | bytes 12582912 | tf_op jit(solution)/shard_map/reshape | solution.py:321
  399.8 4.4 all-gather.7.cloned.1.call-done
  404.2 26.9 %multiply_reduce_fusion = (f32[1536]{0:T(1024)S(1)}, f32[1536,1024]{1,0:T(8,128)}) fusion(f32[1536,1024]{1,0:T(8,128)} %reshape.626, bf16[4096,1024]{1,0:T(8,128)(2,1)} %all-gather.7.cloned.1.call-done, bf16[768,4096]{1,0:T(8,128)(2,1)} %bitcast_select_fusion, bf16[768,4096]{1,0:T(8,128)(2,1)} %copy-done.4, pred[]{:T(512)S(6)} %eq.201), kind=kOutput, calls=%fused_computation.41 | convolution fusion | flops 12955678720 | bytes 33560576 | tf_op jit(solution)/shard_map/dot_general | solution.py:234
  431.2 3.3 broadcast_multiply_fusion
  434.5 2.6 multiply_convert_fusion.4
  437.1 51.7 %all-gather.9.cloned.1.call-done = bf16[1024,2048]{1,0:T(8,128)(2,1)} async-done(((bf16[1024,256]{1,0:T(8,128)(2,1)}), bf16[1024,2048]{1,0:T(8,128)(2,1)}) %all-gather.9.cloned.1.call-update) | async-done | bytes 4194320 | tf_op jit(solution)/shard_map/all_gather | solution.py:233
  488.8 8.7 %fusion.24 = f32[2,384,2048]{2,1,0:T(8,128)} fusion(bf16[1024,2048]{1,0:T(8,128)(2,1)} %all-gather.9.cloned.1.call-done, bf16[2,2,384,1024]{3,2,1,0:T(8,128)(2,1)} %multiply_convert_fusion.4, s32[]{:T(128)S(6)} %select_n.331), kind=kOutput, calls=%fused_computation.50 | convolution fusion | flops 3221225472 | bytes 12058628 | tf_op jit(solution)/shard_map/hrc,cd->hrd/dot_general | solution.py:342
  497.5 10.5 %collective-permute-done.9 = f32[2,384,2048]{2,1,0:T(8,128)} collective-permute-done((f32[2,384,2048]{2,1,0:T(8,128)}, f32[2,384,2048]{2,1,0:T(8,128)}, u32[]{:S(2)}, u32[]{:S(2)}) %collective-permute-start.9) | collective-permute-done | bytes 6291488 | tf_op jit(solution)/shard_map/ppermute | solution.py:347
  508.0 7.9 %fusion.28 = f32[2,384,2048]{2,1,0:T(8,128)S(1)} fusion(f32[2,384,2048]{2,1,0:T(8,128)} %collective-permute-done.9, bf16[1024,2048]{1,0:T(8,128)(2,1)} %all-gather.9.cloned.1.call-done, bf16[2,2,384,1024]{3,2,1,0:T(8,128)(2,1)} %multiply_convert_fusion.4, s32[]{:T(128)S(6)} %select_n.333), kind=kOutput, calls=%fused_computation.56 | convolution fusion | flops 3222798336 | bytes 18350084 | tf_op jit(solution)/shard_map/hrc,cd->hrd/dot_general | solution.py:342
  515.9 2.7 copy-done.6
  518.8 1.5 collective-permute-start.10
  520.4 35.0 %collective-permute-done.10 = bf16[384,2048]{1,0:T(8,128)(2,1)S(1)} collective-permute-done((bf16[384,2048]{1,0:T(8,128)(2,1)S(1)}, bf16[384,2048]{1,0:T(8,128)(2,1)S(1)}, u32[]{:S(2)}, u32[]{:S(2)}) %collective-permute-start.10) | collective-permute-done | bytes 1572896 | tf_op jit(solution)/shard_map/ppermute | solution.py:127
  555.3 2.4 fusion.36
  557.7 13.3 %all-gather.11.cloned.1.call-done = bf16[1024,2048]{1,0:T(8,128)(2,1)} async-done(((bf16[1024,256]{1,0:T(8,128)(2,1)}), bf16[1024,2048]{1,0:T(8,128)(2,1)}) %all-gather.11.cloned.1.call-update) | async-done | bytes 4194320 | tf_op jit(solution)/shard_map/all_gather | solution.py:345
  571.0 6.1 fusion.20
  577.2 10.1 %collective-permute-done.11 = f32[2,384,2048]{2,1,0:T(8,128)S(1)} collective-permute-done((f32[2,384,2048]{2,1,0:T(8,128)S(1)}, f32[2,384,2048]{2,1,0:T(8,128)S(1)}, u32[]{:S(2)}, u32[]{:S(2)}) %collective-permute-start.11) | collective-permute-done | bytes 6291488 | tf_op jit(solution)/shard_map/ppermute | solution.py:347
  587.3 3.5 fusion.31
  591.0 1.5 collective-permute-start.12
  593.1 34.5 %collective-permute-done.12 = bf16[384,2048]{1,0:T(8,128)(2,1)S(1)} collective-permute-done((bf16[384,2048]{1,0:T(8,128)(2,1)S(1)}, bf16[384,2048]{1,0:T(8,128)(2,1)S(1)}, u32[]{:S(2)}, u32[]{:S(2)}) %collective-permute-start.12) | collective-permute-done | bytes 1572896 | tf_op jit(solution)/shard_map/ppermute | solution.py:127
  628.9 6.5 %copy.231 = bf16[384,8,2,256]{3,2,1,0:T(2,128)(2,1)} copy(bf16[384,8,2,256]{3,1,0,2:T(8,128)(2,1)S(1)} %pad_maximum_fusion.3) | data formatting | bytes 6291456 | tf_op jit(solution)/shard_map/stack | solution.py:356
  635.4 6.1 reshape.596
  (233 shorter events, 45.0 us)
Async XLA Ops:
  6.5 129.3 %copy-start = (f32[32,64,128]{2,1,0:T(8,128)S(1)}, f32[32,64,128]{2,1,0:T(8,128)}, u32[]{:S(2)}) copy-start(f32[32,64,128]{2,1,0:T(8,128)} %param.35) | copy-start | bytes 3145732
  6.5 6.8 %copy-start.18 = (bf16[256,32]{0,1:T(8,128)(2,1)S(1)}, bf16[256,32]{0,1:T(8,128)(2,1)}, u32[]{:S(2)}) copy-start(bf16[256,32]{0,1:T(8,128)(2,1)} %param.24) | copy-start | bytes 49156
  6.5 204.9 %all-gather.5.cloned.1.call-start = ((), (), s32[]{:S(2)}) async-start(), calls=%async_computation | async-start | bytes 12976128 | tf_op jit(solution)/shard_map/all_gather | solution.py:211
  6.5 7.6 %copy-start.8 = (bf16[256,2,256]{2,1,0:T(2,128)(2,1)S(1)}, bf16[256,2,256]{2,1,0:T(2,128)(2,1)}, u32[]{:S(2)}) copy-start(bf16[256,2,256]{2,1,0:T(2,128)(2,1)} %param.23) | copy-start | bytes 786436
  16.4 3.9 copy-start.11
  16.4 3.9 copy-start.12
  21.4 18.1 %collective-permute-start.2 = (bf16[256,1296]{0,1:T(8,128)(2,1)}, bf16[256,1296]{0,1:T(8,128)(2,1)S(1)}, u32[]{:S(2)}, u32[]{:S(2)}) collective-permute-start(bf16[256,1296]{0,1:T(8,128)(2,1)} %copy.208), channel_id=1, source_target_pairs={{0,2},{2,0},{1,3},{3,1},{4,6},{6,4},{5,7},{7,5},{8,10},{10,8},{9,1... | collective-permute-start | bytes 1990664 | tf_op jit(solution)/shard_map/ppermute | solution.py:127
  46.1 4.4 copy-start.17
  46.1 358.1 %all-gather.7.cloned.1.call-start = ((), (), s32[]{:S(2)}) async-start(), calls=%async_computation.1 | async-start | bytes 9437184 | tf_op jit(solution)/shard_map/all_gather | solution.py:231
  55.8 2.9 copy-start.4
  58.7 4.4 copy-start.30
  58.7 4.4 copy-start.31
  58.7 9.1 %copy-start.19 = (bf16[4,2,256]{2,1,0:T(2,128)(2,1)S(1)}, bf16[4,2,256]{2,1,0:T(2,128)(2,1)}, u32[]{:S(2)}) copy-start(bf16[4,2,256]{2,1,0:T(2,128)(2,1)} %param.26) | copy-start | bytes 12292
  58.7 9.1 %copy-start.20 = (bf16[3,2,256]{2,1,0:T(2,128)(2,1)S(1)}, bf16[3,2,256]{2,1,0:T(2,128)(2,1)}, u32[]{:S(2)}) copy-start(bf16[3,2,256]{2,1,0:T(2,128)(2,1)} %param.37) | copy-start | bytes 9220
  58.7 11.7 %copy-start.32 = (f32[32]{0:T(128)S(1)}, f32[32]{0:T(128)}, u32[]{:S(2)}) copy-start(f32[32]{0:T(128)} %param.27) | copy-start | bytes 388
  58.7 11.8 %copy-start.33 = (f32[32]{0:T(128)S(1)}, f32[32]{0:T(128)}, u32[]{:S(2)}) copy-start(f32[32]{0:T(128)} %param.28) | copy-start | bytes 388
  58.7 11.9 %copy-start.34 = (f32[32]{0:T(128)S(1)}, f32[32]{0:T(128)}, u32[]{:S(2)}) copy-start(f32[32]{0:T(128)} %param.29) | copy-start | bytes 388
  58.7 76.2 %copy-start.24 = (bf16[4,2048]{1,0:T(4,128)(2,1)S(1)}, bf16[4,2048]{1,0:T(4,128)(2,1)}, u32[]{:S(2)}) copy-start(bf16[4,2048]{1,0:T(4,128)(2,1)} %param.25) | copy-start | bytes 49156
  58.7 76.2 %copy-start.25 = (bf16[3,2048]{1,0:T(4,128)(2,1)S(1)}, bf16[3,2048]{1,0:T(4,128)(2,1)}, u32[]{:S(2)}) copy-start(bf16[3,2048]{1,0:T(4,128)(2,1)} %param.36) | copy-start | bytes 36868
  60.6 69.6 %collective-permute-start = (bf16[384,4096]{1,0:T(8,128)(2,1)}, bf16[384,4096]{1,0:T(8,128)(2,1)}, u32[]{:S(2)}, u32[]{:S(2)}) collective-permute-start(bf16[384,4096]{1,0:T(8,128)(2,1)} %constant_dynamic-slice_fusion.20), channel_id=1, source_target_pairs={{0,2},{2,0},{1,3},{3,1},{4,6},{6,4},{5,7},{7,5},{8,10},{10,8},{9,1... | collective-permute-start | bytes 9437192 | tf_op jit(solution)/shard_map/ppermute | solution.py:127
  70.6 165.8 %copy-start.26 = (f32[16]{0:T(128)}, f32[16]{0:T(128)S(1)}, u32[]{:S(2)}) copy-start(f32[16]{0:T(128)S(1)} %dynamic_slice.150) | copy-start | bytes 196
  130.2 8.0 %collective-permute-start.1 = (bf16[384,4096]{1,0:T(8,128)(2,1)}, bf16[384,4096]{1,0:T(8,128)(2,1)S(1)}, u32[]{:S(2)}, u32[]{:S(2)}) collective-permute-start(bf16[384,4096]{1,0:T(8,128)(2,1)} %collective-permute-done), channel_id=1, source_target_pairs={{0,1},{1,0},{2,3},{3,2},{4,5},{5,4},{6,7},{7,6},{8,9},{9,8},{10,11... | collective-permute-start | bytes 9437192 | tf_op jit(solution)/shard_map/ppermute | solution.py:186
  236.2 15.5 %copy-start.28 = (pred[6]{0:T(512)(128)(4,1)S(1)}, pred[6]{0:T(512)(128)(4,1)}, u32[]{:S(2)}) copy-start(pred[6]{0:T(512)(128)(4,1)} %fusion.87) | copy-start | bytes 22
  236.4 12.0 %copy-start.27 = (f32[16]{0:T(128)S(1)}, f32[16]{0:T(128)}, u32[]{:S(2)}) copy-start(f32[16]{0:T(128)} %copy-done.26) | copy-start | bytes 196
  242.9 26.3 %copy-start.21 = (pred[1536]{0:T(1024)(128)(4,1)S(1)}, pred[1536]{0:T(1024)(128)(4,1)}, u32[]{:S(2)}) copy-start(pred[1536]{0:T(1024)(128)(4,1)} %get-tuple-element.215) | copy-start | bytes 4612
  242.9 26.3 %copy-start.22 = (pred[1536]{0:T(1024)(128)(4,1)S(1)}, pred[1536]{0:T(1024)(128)(4,1)}, u32[]{:S(2)}) copy-start(pred[1536]{0:T(1024)(128)(4,1)} %get-tuple-element.216) | copy-start | bytes 4612
  242.9 107.4 %collective-permute-start.3 = (bf16[1024,256]{1,0:T(8,128)(2,1)}, bf16[1024,256]{1,0:T(8,128)(2,1)}, u32[]{:S(2)}, u32[]{:S(2)}) collective-permute-start(bf16[1024,256]{1,0:T(8,128)(2,1)} %get-tuple-element.180), channel_id=1, source_target_pairs={{0,2},{2,0},{1,3},{3,1},{4,6},{6,4},{5,7},{7,5},{8,10},{10,8},{9,1... | collective-permute-start | bytes 1572872 | tf_op jit(solution)/shard_map/ppermute | solution.py:127
  244.4 24.8 %collective-permute-start.4 = (bf16[3,1280]{0,1:T(8,128)(2,1)}, bf16[3,1280]{0,1:T(8,128)(2,1)}, u32[]{:S(2)}, u32[]{:S(2)}) collective-permute-start(bf16[3,1280]{0,1:T(8,128)(2,1)} %slice.158), channel_id=1, source_target_pairs={{0,4},{4,8},{8,12},{12,16},{16,20},{20,24},{24,28},{1,5},{5,9},{9,... | collective-permute-start | bytes 23048 | tf_op jit(solution)/shard_map/ppermute | solution.py:15
  250.2 17.5 %collective-permute-start.8 = (bf16[256,1024]{1,0:T(8,128)(2,1)S(1)}, bf16[256,1024]{1,0:T(8,128)(2,1)S(1)}, u32[]{:S(2)}, u32[]{:S(2)}) collective-permute-start(bf16[256,1024]{1,0:T(8,128)(2,1)S(1)} %get-tuple-element.176), channel_id=1, source_target_pairs={{0,2},{2,0},{1,3},{3,1},{4,6},{6,4},{5,7},{7,5},{8,10},{10,8},{9,1... | collective-permute-start | bytes 1572872 | tf_op jit(solution)/shard_map/ppermute | solution.py:127
  269.2 219.6 %all-gather.9.cloned.1.call-start = ((), (), s32[]{:S(2)}) async-start(), calls=%async_computation.2 | async-start | bytes 4718592 | tf_op jit(solution)/shard_map/all_gather | solution.py:233
  290.8 1.9 copy-start.3
  299.6 7.6 %copy-start.9 = (f32[6,256,16]{1,0,2:T(8,128)S(1)}, f32[6,256,16]{1,0,2:T(8,128)}, u32[]{:S(2)}) copy-start(f32[6,256,16]{1,0,2:T(8,128)} %copy.226) | copy-start | bytes 294916
  310.3 2.7 copy-start.23
  325.5 27.5 %collective-permute-start.5 = (f32[1,16,64,128]{3,2,1,0:T(8,128)S(1)}, f32[1,16,64,128]{3,2,1,0:T(8,128)}, u32[]{:S(2)}, u32[]{:S(2)}) collective-permute-start(f32[1,16,64,128]{3,2,1,0:T(8,128)S(1)} %get-tuple-element.53), channel_id=1, source_target_pairs={{0,4},{4,8},{8,12},{12,16},{16,20},{20,24},{24,28},{1,5},{5,9},{9,... | collective-permute-start | bytes 1572872 | tf_op jit(solution)/shard_map/ppermute | solution.py:15
  329.0 24.1 %collective-permute-start.7 = (f32[1,16,64,128]{3,2,1,0:T(8,128)S(1)}, f32[1,16,64,128]{3,2,1,0:T(8,128)}, u32[]{:S(2)}, u32[]{:S(2)}) collective-permute-start(f32[1,16,64,128]{3,2,1,0:T(8,128)S(1)} %get-tuple-element.53), channel_id=1, source_target_pairs={{0,8},{4,12},{8,16},{12,20},{16,24},{20,28},{1,9},{5,13},{9,17},{1... | collective-permute-start | bytes 1572872 | tf_op jit(solution)/shard_map/ppermute | solution.py:15
  340.0 13.0 %collective-permute-start.6 = (f32[1,16]{1,0:T(1,128)S(1)}, f32[1,16]{1,0:T(1,128)S(1)}, u32[]{:S(2)}, u32[]{:S(2)}) collective-permute-start(f32[1,16]{1,0:T(1,128)S(1)} %get-tuple-element.54), channel_id=1, source_target_pairs={{0,4},{4,8},{8,12},{12,16},{16,20},{20,24},{24,28},{1,5},{5,9},{9,... | collective-permute-start | bytes 200 | tf_op jit(solution)/shard_map/ppermute | solution.py:15
  352.8 218.2 %all-gather.11.cloned.1.call-start = ((), (), s32[]{:S(2)}) async-start(), calls=%async_computation.3 | async-start | bytes 4718592 | tf_op jit(solution)/shard_map/all_gather | solution.py:345
  353.1 6.9 %copy-start.5 = (f32[6,256,16,64]{1,3,2,0:T(8,128)S(1)}, f32[6,256,16,64]{1,3,2,0:T(8,128)}, u32[]{:S(2)}) copy-start(f32[6,256,16,64]{1,3,2,0:T(8,128)} %fusion.60) | copy-start | bytes 18874372
  354.5 5.5 copy-start.2
  354.6 5.5 copy-start.10
  354.6 5.5 copy-start.13
  354.6 5.5 copy-start.14
  354.6 5.5 copy-start.15
  354.6 5.5 copy-start.16
  354.6 5.5 copy-start.35
  431.1 3.3 dynamic-slice-start
  497.5 10.5 %collective-permute-start.9 = (f32[2,384,2048]{2,1,0:T(8,128)}, f32[2,384,2048]{2,1,0:T(8,128)}, u32[]{:S(2)}, u32[]{:S(2)}) collective-permute-start(f32[2,384,2048]{2,1,0:T(8,128)} %fusion.24), channel_id=1, source_target_pairs={{0,1},{1,0},{2,3},{3,2},{4,5},{5,4},{6,7},{7,6},{8,9},{9,8},{10,11... | collective-permute-start | bytes 18874376 | tf_op jit(solution)/shard_map/ppermute | solution.py:347
  515.9 2.7 copy-start.6
  518.8 36.5 %collective-permute-start.10 = (bf16[384,2048]{1,0:T(8,128)(2,1)S(1)}, bf16[384,2048]{1,0:T(8,128)(2,1)S(1)}, u32[]{:S(2)}, u32[]{:S(2)}) collective-permute-start(bf16[384,2048]{1,0:T(8,128)(2,1)S(1)} %fusion.48), channel_id=1, source_target_pairs={{0,2},{2,0},{1,3},{3,1},{4,6},{6,4},{5,7},{7,5},{8,10},{10,8},{9,1... | collective-permute-start | bytes 4718600 | tf_op jit(solution)/shard_map/ppermute | solution.py:127
  571.0 16.3 %copy-start.7 = (bf16[2,2,384,1024]{3,2,1,0:T(8,128)(2,1)S(1)}, bf16[2,2,384,1024]{3,2,1,0:T(8,128)(2,1)}, u32[]{:S(2)}) copy-start(bf16[2,2,384,1024]{3,2,1,0:T(8,128)(2,1)} %multiply_convert_fusion.4) | copy-start | bytes 9437188
  571.0 16.3 %copy-start.29 = (bf16[1024,2048]{1,0:T(8,128)(2,1)S(1)}, bf16[1024,2048]{1,0:T(8,128)(2,1)}, u32[]{:S(2)}) copy-start(bf16[1024,2048]{1,0:T(8,128)(2,1)} %all-gather.11.cloned.1.call-done) | copy-start | bytes 12582916
  577.1 10.2 %collective-permute-start.11 = (f32[2,384,2048]{2,1,0:T(8,128)S(1)}, f32[2,384,2048]{2,1,0:T(8,128)S(1)}, u32[]{:S(2)}, u32[]{:S(2)}) collective-permute-start(f32[2,384,2048]{2,1,0:T(8,128)S(1)} %fusion.20), channel_id=1, source_target_pairs={{0,1},{1,0},{2,3},{3,2},{4,5},{5,4},{6,7},{7,6},{8,9},{9,8},{10,11... | collective-permute-start | bytes 18874376 | tf_op jit(solution)/shard_map/ppermute | solution.py:347
  591.0 36.5 %collective-permute-start.12 = (bf16[384,2048]{1,0:T(8,128)(2,1)S(1)}, bf16[384,2048]{1,0:T(8,128)(2,1)S(1)}, u32[]{:S(2)}, u32[]{:S(2)}) collective-permute-start(bf16[384,2048]{1,0:T(8,128)(2,1)S(1)} %fusion.49), channel_id=1, source_target_pairs={{0,2},{2,0},{1,3},{3,1},{4,6},{6,4},{5,7},{7,5},{8,10},{10,8},{9,1... | collective-permute-start | bytes 4718600 | tf_op jit(solution)/shard_map/ppermute | solution.py:127
  628.9 12.6 %copy-start.1 = (f32[32,64,128]{2,1,0:T(8,128)S(1)}, f32[32,64,128]{2,1,0:T(8,128)}, u32[]{:S(2)}) copy-start(f32[32,64,128]{2,1,0:T(8,128)} %param.35) | copy-start | bytes 3145732
Sparse Core Ops, SparseCore 0:
  46.2 165.1 all-gather.4
  269.3 134.8 all-gather.6
  406.2 82.5 all-gather.8
  497.7 73.3 all-gather.10

commit v8 on v4

--- a/solution.py
+++ b/solution.py
@@ -340,8 +340,10 @@
             part = jnp.einsum("hrc,cd->hrd", rows, columns, preferred_element_type=jnp.float32)
             if shift:
                 part = lax.ppermute(
-                    part, "fsdp", [(j, (j + shift) % core_count) for j in range(core_count)]
-                )
+                    part.astype(jnp.bfloat16),
+                    "fsdp",
+                    [(j, (j + shift) % core_count) for j in range(core_count)],
+                ).astype(jnp.float32)
             total = part if total is None else total + part
         mine = lax.dynamic_index_in_dim(total, half, 0, keepdims=False)
         theirs = lax.dynamic_index_in_dim(total, 1 - half, 0, keepdims=False)

time: 645 us -> 639 us (level)
  no operation moved by 1% of the time
where the time goes in v8:
time: 639 us; the launch traced here: 631 us
  waiting for transfers between devices  265 us (41%)
  other arithmetic  116 us (18%)
  matrix products  110 us (17%)
  local copies, waits for them, and re-layouts  92.8 us (15%)
  starting transfers between devices  32.1 us (5%)
  between operations  14.8 us (2%)
    ppermute x6, waiting for transfers between devices, swap_half(): lax.ppermute(value, 'half', [(k, count - 1 - k) for k in range(count)])  141 us
    all_gather x1, waiting for transfers between devices, body(): out_full = lax.all_gather(out_local, 'pair', axis=1, tiled=True)  70.3 us
    all_gather x1, waiting for transfers between devices, body(): first_full = lax.all_gather(first_local, 'pair', axis=0, tiled=True)  53.2 us
    dot_general x1, matrix products, body(): jnp.dot(normed, z_full, preferred_element_type=jnp.float32)  27.1 us
    dot_general x4, matrix products, body(): jnp.einsum('hrc,cd->hrd', rows, columns, preferred_element_type=jnp.float32)  27 us
    dot_general x1, matrix products, body(): jnp.dot(normed, first_full, preferred_element_type=jnp.float32)  23.8 us
    reshape x2, local copies, waits for them, and re-layouts, body(): (direct + state_gain[..., None] * from_state).reshape(row_count, inner_lo...  23 us
    convert_element_type x1, other arithmetic, conv_rows(): return jax.nn.silu(summed).astype(jnp.bfloat16)  22 us
  transfers between devices with their start and end apart: 16, of which 8 were waited for; matrix products, arithmetic and copies ran while one was open for 40% of the time, Pallas kernels for 0%

profile of v8, /device:TPU:0, one launch (start us, length us, event | category | flops | bytes accessed | tf_op | source)
XLA Modules:
  0.0 630.8 jit_solution(7261183218806408477)
XLA Ops:
  6.5 1.6 fusion.100
  11.4 6.9 %fusion.99 = (bf16[256,1,2048]{2,1,0:T(2,128)(2,1)}, bf16[256,1,2048]{2,1,0:T(2,128)(2,1)}) fusion(bf16[256,2,2048]{2,1,0:T(2,128)(2,1)} %param.22), kind=kLoop, calls=%fused_computation.230 | loop fusion | bytes 4194304 | tf_op jit(solution)/shard_map/slice | solution.py:197
  18.3 3.7 constant_dynamic-slice_fusion.19
  24.2 2.9 collective-permute-start.2
  29.0 13.3 %collective-permute-done.2 = bf16[256,1296]{0,1:T(8,128)(2,1)S(1)} collective-permute-done((bf16[256,1296]{0,1:T(8,128)(2,1)}, bf16[256,1296]{0,1:T(8,128)(2,1)S(1)}, u32[]{:S(2)}, u32[]{:S(2)}) %collective-permute-start.2) | collective-permute-done | bytes 663584 | tf_op jit(solution)/shard_map/ppermute | solution.py:127
  42.6 6.2 maximum_select_fusion.3
  49.0 4.1 fusion.3
  53.1 5.3 fusion.5
  58.4 2.9 copy-done.4
  61.6 1.8 collective-permute-start
  63.4 67.6 %collective-permute-done = bf16[384,4096]{1,0:T(8,128)(2,1)} collective-permute-done((bf16[384,4096]{1,0:T(8,128)(2,1)S(1)}, bf16[384,4096]{1,0:T(8,128)(2,1)}, u32[]{:S(2)}, u32[]{:S(2)}) %collective-permute-start) | collective-permute-done | bytes 3145760 | tf_op jit(solution)/shard_map/ppermute | solution.py:127
  132.8 1.3 fusion.88
  134.7 1.8 reduce-window.30
  137.6 2.2 copy.282
  139.8 5.0 fusion.22
  144.8 4.4 gather_fusion
  149.2 4.4 gather_fusion.1
  153.6 3.6 pad_maximum_fusion
  157.2 3.7 bitcast_select_fusion
  160.9 53.2 %all-gather.4.cloned.1.call-done = bf16[4096,1296]{1,0:T(8,128)(2,1)} async-done(((bf16[512,1296]{1,0:T(8,128)(2,1)}), bf16[4096,1296]{1,0:T(8,128)(2,1)}) %all-gather.4.cloned.1.call-update) | async-done | bytes 10616848 | tf_op jit(solution)/shard_map/all_gather | solution.py:211
  214.1 23.8 %convolution_convert_fusion = bf16[1536,1296]{0,1:T(8,128)(2,1)} fusion(bf16[4096,1296]{1,0:T(8,128)(2,1)} %all-gather.4.cloned.1.call-done, bf16[768,4096]{1,0:T(8,128)(2,1)} %bitcast_select_fusion, bf16[768,4096]{1,0:T(8,128)(2,1)} %copy-done.4, pred[]{:T(512)S(6)} %eq.204), kind=kOutput, calls=%fused_computation.27 | convolution fusion | flops 16366067712 | bytes 27181056 | tf_op jit(solution)/shard_map/dot_general | solution.py:212
  238.0 1.5 collective-permute-start.7
  245.6 5.7 collective-permute-done.7
  251.3 1.5 maximum_select_fusion.4
  259.4 1.9 slice.157
  261.3 2.4 collective-permute-start.3
  264.9 3.6 reduce-window.21
  270.2 1.3 constant_dynamic-slice_fusion.2
  273.8 4.3 slice.152
  278.4 1.5 collective-permute-start.8
  280.6 22.0 %multiply_convert_fusion.3 = bf16[1536,1280]{0,1:T(8,128)(2,1)S(1)} fusion(bf16[1536,1280]{0,1:T(8,128)(2,1)} %slice.152, bf16[3,1280]{0,1:T(8,128)(2,1)S(1)} %collective-permute-done.3, f32[1280]{0:T(1024)} %get-tuple-element.132, f32[1280]{0:T(1024)} %get-tuple-element.133, f32[1280]{0:T(1024)} %get-tuple-element.134, f32[1280]{0:T(1024)} %get-tuple-element.131, ...), kind=kLoop, calls=%fused_computation.26 | loop fusion | flops 104202240 | bytes 7933952 | tf_op jit(solution)/shard_map/convert_element_type | solution.py:68
  302.7 5.0 fusion.97
  310.4 7.7 %reshape.578 = bf16[6,256,16,64]{1,0,3,2:T(8,128)(2,1)} reshape(bf16[1536,1024]{0,1:T(8,128)(2,1)} %get-tuple-element.159) | data formatting | bytes 6291456 | tf_op jit(solution)/shard_map/reshape.48
  318.1 3.2 multiply_convert_fusion.2
  321.3 2.7 add_bitcast_fusion
  323.9 20.2 %while.17 = (s32[]{:T(128)}, f32[1,16,64,128]{3,2,1,0:T(8,128)S(1)}, f32[1,16]{1,0:T(1,128)S(1)}, f32[6,1,16,64,128]{4,3,2,1,0:T(8,128)}, f32[6,1,16]{2,0,1:T(8,...) while((s32[]{:T(128)}, ...), condition=%wide.region_15.16_spmd.clone, body=%wide.region_14.15_spmd.clone.sunk | while | flops 524323 | bytes 2622649 | solution.py:308
  344.2 3.1 collective-permute-start.4
  347.3 9.6 %collective-permute-start.6 = (f32[1,16,64,128]{3,2,1,0:T(8,128)S(1)}, f32[1,16,64,128]{3,2,1,0:T(8,128)}, u32[]{:S(2)}, u32[]{:S(2)}) collective-permute-start(f32[1,16,64,128]{3,2,1,0:T(8,128)S(1)} %get-tuple-element.48), channel_id=1, source_target_pairs={{0,8},{4,12},{8,16},{12,20},{16,24},{20,28},{1,9},{5,13},{9,17},{1... | collective-permute-start | bytes 1572872 | tf_op jit(solution)/shard_map/ppermute | solution.py:15
  357.1 5.2 collective-permute-start.5
  362.3 1.5 fusion.103
  363.8 5.3 fusion.48
  369.1 9.2 %reshape.600 = f32[6,256,1,16,64]{1,0,4,3,2:T(8,128)} reshape(f32[1536,1024]{0,1:T(8,128)} %get-tuple-element.160) | data formatting | bytes 12582912 | tf_op jit(solution)/shard_map/convert_element_type | solution.py:119
  378.3 1.5 add_bitcast_fusion.1
  379.8 5.4 fusion.25
  385.2 16.7 %fusion.17 = f32[6,256,1,16,64]{1,4,3,0,2:T(8,128)} fusion(f32[6,256,1,16,64]{1,0,4,3,2:T(8,128)} %reshape.600, f32[6,256,16,64]{1,3,2,0:T(8,128)S(1)} %fusion.25, f32[6,256,16,64]{1,3,2,0:T(8,128)S(1)} %copy-done.5, f32[6,256,16]{1,2,0:T(8,128)S(1)} %copy-done.13, f32[16]{0:T(128)S(1)} %copy-done.29, f32[6,256,16]{1,2,0:T(8,128)S(1)} %copy-done.12, ...), kind=kOutput, calls=%fused_computation.37 | convolution fusion | flops 852492288 | bytes 30670912 | tf_op jit(solution)/shard_map/cghqs,csghp->cqghp/dot_general | solution.py:20
  401.9 11.4 %copy.227 = f32[6,256,1,16,64]{4,3,1,0,2:T(8,128)} copy(f32[6,256,1,16,64]{1,4,3,0,2:T(8,128)} %fusion.17) | data formatting | bytes 12582912 | tf_op jit(solution)/shard_map/reshape | solution.py:320
  413.3 11.7 %reshape.622 = f32[1536,1024]{1,0:T(8,128)} reshape(f32[6,256,1,16,64]{4,3,1,0,2:T(8,128)} %copy.227) | data formatting | bytes 12582912 | tf_op jit(solution)/shard_map/reshape | solution.py:320
  424.9 27.1 %multiply_reduce_fusion = (f32[1536]{0:T(1024)S(1)}, f32[1536,1024]{1,0:T(8,128)}) fusion(f32[1536,1024]{1,0:T(8,128)} %reshape.622, bf16[4096,1024]{1,0:T(8,128)(2,1)} %all-gather.6.cloned.1.call-done, bf16[768,4096]{1,0:T(8,128)(2,1)} %bitcast_select_fusion, bf16[768,4096]{1,0:T(8,128)(2,1)} %copy-done.4, pred[]{:T(512)S(6)} %eq.204), kind=kOutput, calls=%fused_computation.43 | convolution fusion | flops 12955678720 | bytes 33560576 | tf_op jit(solution)/shard_map/dot_general | solution.py:233
  452.1 3.3 broadcast_multiply_fusion
  455.4 2.6 multiply_convert_fusion.4
  458.0 70.3 %all-gather.8.cloned.1.call-done = bf16[1024,4096]{1,0:T(8,128)(2,1)} async-done(((bf16[1024,512]{1,0:T(8,128)(2,1)}), bf16[1024,4096]{1,0:T(8,128)(2,1)}) %all-gather.8.cloned.1.call-update) | async-done | bytes 8388624 | tf_op jit(solution)/shard_map/all_gather | solution.py:232
  528.4 7.9 %convolution_convert_fusion.3 = bf16[2,384,2048]{2,1,0:T(8,128)(2,1)} fusion(bf16[1024,4096]{1,0:T(8,128)(2,1)} %all-gather.8.cloned.1.call-done, bf16[2,2,384,1024]{3,2,1,0:T(8,128)(2,1)} %multiply_convert_fusion.4, s32[]{:T(128)S(6)} %select_n.329), kind=kOutput, calls=%fused_computation.53 | convolution fusion | flops 3222798336 | bytes 8912900 | tf_op jit(solution)/shard_map/hrc,cd->hrd/dot_general | solution.py:340
  536.3 5.1 convolution_convert_fusion.2
  542.3 7.2 %convert_add_fusion.1 = f32[2,384,2048]{2,1,0:T(8,128)S(1)} fusion(bf16[2,384,2048]{2,1,0:T(8,128)(2,1)} %collective-permute-done.9, bf16[1024,4096]{1,0:T(8,128)(2,1)} %all-gather.8.cloned.1.call-done, bf16[2,2,384,1024]{3,2,1,0:T(8,128)(2,1)} %multiply_convert_fusion.4, s32[]{:T(128)S(6)} %select_n.333), kind=kOutput, calls=%fused_computation.41 | convolution fusion | flops 3224371200 | bytes 15204356 | tf_op jit(solution)/shard_map/hrc,cd->hrd/dot_general | solution.py:340
  549.7 1.5 collective-permute-start.10
  551.2 6.9 %convert_add_fusion = f32[2,384,2048]{2,1,0:T(8,128)S(1)} fusion(bf16[2,384,2048]{2,1,0:T(8,128)(2,1)} %collective-permute-done.11, bf16[1024,4096]{1,0:T(8,128)(2,1)} %all-gather.8.cloned.1.call-done, bf16[2,2,384,1024]{3,2,1,0:T(8,128)(2,1)S(1)} %copy-done.10, s32[]{:T(128)S(6)} %select_n.333), kind=kOutput, calls=%fused_computation.40 | convolution fusion | flops 3224371200 | bytes 15204356 | tf_op jit(solution)/shard_map/hrc,cd->hrd/dot_general | solution.py:340
  558.2 1.5 fusion.37
  559.7 1.6 copy-done.7
  561.3 1.6 collective-permute-start.12
  562.8 24.2 %collective-permute-done.10 = bf16[384,2048]{1,0:T(8,128)(2,1)S(1)} collective-permute-done((bf16[384,2048]{1,0:T(8,128)(2,1)S(1)}, bf16[384,2048]{1,0:T(8,128)(2,1)S(1)}, u32[]{:S(2)}, u32[]{:S(2)}) %collective-permute-start.10) | collective-permute-done | bytes 1572896 | tf_op jit(solution)/shard_map/ppermute | solution.py:127
  587.0 2.5 fusion.24
  589.5 30.6 %collective-permute-done.12 = bf16[384,2048]{1,0:T(8,128)(2,1)} collective-permute-done((bf16[384,2048]{1,0:T(8,128)(2,1)}, bf16[384,2048]{1,0:T(8,128)(2,1)}, u32[]{:S(2)}, u32[]{:S(2)}) %collective-permute-start.12) | collective-permute-done | bytes 1572896 | tf_op jit(solution)/shard_map/ppermute | solution.py:127
  620.1 2.0 fusion.23
  622.0 2.0 pad_maximum_fusion.3
  (213 shorter events, 53.7 us)
Async XLA Ops:
  6.5 250.0 %copy-start = (f32[32,64,128]{2,1,0:T(8,128)S(1)}, f32[32,64,128]{2,1,0:T(8,128)}, u32[]{:S(2)}) copy-start(f32[32,64,128]{2,1,0:T(8,128)} %param.35) | copy-start | bytes 3145732
  6.5 207.5 %all-gather.4.cloned.1.call-start = ((), (), s32[]{:S(2)}) async-start(), calls=%async_computation | async-start | bytes 12976128 | tf_op jit(solution)/shard_map/all_gather | solution.py:211
  24.2 18.1 %collective-permute-start.2 = (bf16[256,1296]{0,1:T(8,128)(2,1)}, bf16[256,1296]{0,1:T(8,128)(2,1)S(1)}, u32[]{:S(2)}, u32[]{:S(2)}) collective-permute-start(bf16[256,1296]{0,1:T(8,128)(2,1)} %copy.201), channel_id=1, source_target_pairs={{0,2},{2,0},{1,3},{3,1},{4,6},{6,4},{5,7},{7,5},{8,10},{10,8},{9,1... | collective-permute-start | bytes 1990664 | tf_op jit(solution)/shard_map/ppermute | solution.py:127
  29.0 24.1 %copy-start.15 = (f32[4096]{0:T(1024)S(1)}, f32[4096]{0:T(1024)}, u32[]{:S(2)}) copy-start(f32[4096]{0:T(1024)} %param.21) | copy-start | bytes 49156
  48.8 376.2 %all-gather.6.cloned.1.call-start = ((), (), s32[]{:S(2)}) async-start(), calls=%async_computation.1 | async-start | bytes 9437184 | tf_op jit(solution)/shard_map/all_gather | solution.py:231
  58.4 2.9 copy-start.4
  61.3 70.4 %copy-start.24 = (s32[8]{0:T(128)S(1)}, s32[8]{0:T(128)}, u32[]{:S(2)}) copy-start(s32[8]{0:T(128)} %param.32) | copy-start | bytes 100
  61.3 70.4 %copy-start.25 = (s32[8]{0:T(128)S(1)}, s32[8]{0:T(128)}, u32[]{:S(2)}) copy-start(s32[8]{0:T(128)} %param.33) | copy-start | bytes 100
  61.3 73.1 %copy-start.16 = (bf16[4,2,256]{2,1,0:T(2,128)(2,1)S(1)}, bf16[4,2,256]{2,1,0:T(2,128)(2,1)}, u32[]{:S(2)}) copy-start(bf16[4,2,256]{2,1,0:T(2,128)(2,1)} %param.26) | copy-start | bytes 12292
  61.3 73.1 %copy-start.18 = (bf16[3,2,256]{2,1,0:T(2,128)(2,1)S(1)}, bf16[3,2,256]{2,1,0:T(2,128)(2,1)}, u32[]{:S(2)}) copy-start(bf16[3,2,256]{2,1,0:T(2,128)(2,1)} %param.37) | copy-start | bytes 9220
  61.3 73.2 %copy-start.26 = (f32[32]{0:T(128)S(1)}, f32[32]{0:T(128)}, u32[]{:S(2)}) copy-start(f32[32]{0:T(128)} %param.27) | copy-start | bytes 388
  61.3 73.3 %copy-start.27 = (f32[32]{0:T(128)S(1)}, f32[32]{0:T(128)}, u32[]{:S(2)}) copy-start(f32[32]{0:T(128)} %param.28) | copy-start | bytes 388
  61.4 75.6 %copy-start.28 = (f32[32]{0:T(128)S(1)}, f32[32]{0:T(128)}, u32[]{:S(2)}) copy-start(f32[32]{0:T(128)} %param.29) | copy-start | bytes 388
  61.6 69.5 %collective-permute-start = (bf16[384,4096]{1,0:T(8,128)(2,1)S(1)}, bf16[384,4096]{1,0:T(8,128)(2,1)}, u32[]{:S(2)}, u32[]{:S(2)}) collective-permute-start(bf16[384,4096]{1,0:T(8,128)(2,1)S(1)} %constant_dynamic-slice_fusion.20), channel_id=1, source_target_pairs={{0,2},{2,0},{1,3},{3,1},{4,6},{6,4},{5,7},{7,5},{8,10},{10,8},{9,1... | collective-permute-start | bytes 9437192 | tf_op jit(solution)/shard_map/ppermute | solution.py:127
  131.0 8.8 %collective-permute-start.1 = (bf16[384,4096]{1,0:T(8,128)(2,1)}, bf16[384,4096]{1,0:T(8,128)(2,1)}, u32[]{:S(2)}, u32[]{:S(2)}) collective-permute-start(bf16[384,4096]{1,0:T(8,128)(2,1)} %collective-permute-done), channel_id=1, source_target_pairs={{0,1},{1,0},{2,3},{3,2},{4,5},{5,4},{6,7},{7,6},{8,9},{9,8},{10,11... | collective-permute-start | bytes 9437192 | tf_op jit(solution)/shard_map/ppermute | solution.py:186
  160.9 94.1 %copy-start.20 = (bf16[4,2048]{1,0:T(4,128)(2,1)S(1)}, bf16[4,2048]{1,0:T(4,128)(2,1)}, u32[]{:S(2)}) copy-start(bf16[4,2048]{1,0:T(4,128)(2,1)} %param.25) | copy-start | bytes 49156
  160.9 94.1 %copy-start.21 = (bf16[3,2048]{1,0:T(4,128)(2,1)S(1)}, bf16[3,2048]{1,0:T(4,128)(2,1)}, u32[]{:S(2)}) copy-start(bf16[3,2048]{1,0:T(4,128)(2,1)} %param.36) | copy-start | bytes 36868
  238.0 13.3 %collective-permute-start.7 = (bf16[256,1024]{1,0:T(8,128)(2,1)S(1)}, bf16[256,1024]{1,0:T(8,128)(2,1)S(1)}, u32[]{:S(2)}, u32[]{:S(2)}) collective-permute-start(bf16[256,1024]{1,0:T(8,128)(2,1)S(1)} %get-tuple-element.168), channel_id=1, source_target_pairs={{0,2},{2,0},{1,3},{3,1},{4,6},{6,4},{5,7},{7,5},{8,10},{10,8},{9,1... | collective-permute-start | bytes 1572872 | tf_op jit(solution)/shard_map/ppermute | solution.py:127
  252.8 275.5 %all-gather.8.cloned.1.call-start = ((), (), s32[]{:S(2)}) async-start(), calls=%async_computation.2 | async-start | bytes 9437184 | tf_op jit(solution)/shard_map/all_gather | solution.py:232
  261.3 19.3 %collective-permute-start.3 = (bf16[3,1280]{0,1:T(8,128)(2,1)}, bf16[3,1280]{0,1:T(8,128)(2,1)S(1)}, u32[]{:S(2)}, u32[]{:S(2)}) collective-permute-start(bf16[3,1280]{0,1:T(8,128)(2,1)} %slice.157), channel_id=1, source_target_pairs={{0,4},{4,8},{8,12},{12,16},{16,20},{20,24},{24,28},{1,5},{5,9},{9,... | collective-permute-start | bytes 23048 | tf_op jit(solution)/shard_map/ppermute | solution.py:15
  278.4 29.3 %collective-permute-start.8 = (bf16[1024,256]{1,0:T(8,128)(2,1)S(1)}, bf16[1024,256]{1,0:T(8,128)(2,1)S(1)}, u32[]{:S(2)}, u32[]{:S(2)}) collective-permute-start(bf16[1024,256]{1,0:T(8,128)(2,1)S(1)} %get-tuple-element.170), channel_id=1, source_target_pairs={{0,2},{2,0},{1,3},{3,1},{4,6},{6,4},{5,7},{7,5},{8,10},{10,8},{9,1... | collective-permute-start | bytes 1572872 | tf_op jit(solution)/shard_map/ppermute | solution.py:127
  302.7 5.0 copy-start.3
  310.4 10.9 %copy-start.22 = (f32[6,16]{1,0:T(8,128)S(1)}, f32[6,16]{1,0:T(8,128)}, u32[]{:S(2)}) copy-start(f32[6,16]{1,0:T(8,128)} %slice_reduce_fusion.1) | copy-start | bytes 1156
  321.2 2.7 copy-start.17
  321.3 2.7 copy-start.19
  344.2 34.1 %collective-permute-start.4 = (f32[1,16,64,128]{3,2,1,0:T(8,128)S(1)}, f32[1,16,64,128]{3,2,1,0:T(8,128)}, u32[]{:S(2)}, u32[]{:S(2)}) collective-permute-start(f32[1,16,64,128]{3,2,1,0:T(8,128)S(1)} %get-tuple-element.48), channel_id=1, source_target_pairs={{0,4},{4,8},{8,12},{12,16},{16,20},{20,24},{24,28},{1,5},{5,9},{9,... | collective-permute-start | bytes 1572872 | tf_op jit(solution)/shard_map/ppermute | solution.py:15
  347.3 31.0 %collective-permute-start.6 = (f32[1,16,64,128]{3,2,1,0:T(8,128)S(1)}, f32[1,16,64,128]{3,2,1,0:T(8,128)}, u32[]{:S(2)}, u32[]{:S(2)}) collective-permute-start(f32[1,16,64,128]{3,2,1,0:T(8,128)S(1)} %get-tuple-element.48), channel_id=1, source_target_pairs={{0,8},{4,12},{8,16},{12,20},{16,24},{20,28},{1,9},{5,13},{9,17},{1... | collective-permute-start | bytes 1572872 | tf_op jit(solution)/shard_map/ppermute | solution.py:15
  357.1 21.1 %collective-permute-start.5 = (f32[1,16]{1,0:T(1,128)S(1)}, f32[1,16]{1,0:T(1,128)S(1)}, u32[]{:S(2)}, u32[]{:S(2)}) collective-permute-start(f32[1,16]{1,0:T(1,128)S(1)} %get-tuple-element.49), channel_id=1, source_target_pairs={{0,4},{4,8},{8,12},{12,16},{16,20},{20,24},{24,28},{1,5},{5,9},{9,... | collective-permute-start | bytes 200 | tf_op jit(solution)/shard_map/ppermute | solution.py:15
  369.1 16.1 %copy-start.11 = (f32[6,256,256]{2,1,0:T(8,128)S(1)}, f32[6,256,256]{2,1,0:T(8,128)}, u32[]{:S(2)}) copy-start(f32[6,256,256]{2,1,0:T(8,128)} %fusion.103) | copy-start | bytes 4718596
  378.2 6.9 %copy-start.2 = (bf16[6,256,16,64]{1,0,3,2:T(8,128)(2,1)S(1)}, bf16[6,256,16,64]{1,0,3,2:T(8,128)(2,1)}, u32[]{:S(2)}) copy-start(bf16[6,256,16,64]{1,0,3,2:T(8,128)(2,1)} %reshape.578) | copy-start | bytes 9437188
  378.2 6.9 %copy-start.5 = (f32[6,256,16,64]{1,3,2,0:T(8,128)S(1)}, f32[6,256,16,64]{1,3,2,0:T(8,128)}, u32[]{:S(2)}) copy-start(f32[6,256,16,64]{1,3,2,0:T(8,128)} %fusion.48) | copy-start | bytes 18874372
  378.2 7.0 %copy-start.12 = (f32[6,256,16]{1,2,0:T(8,128)S(1)}, f32[6,256,16]{1,2,0:T(8,128)}, u32[]{:S(2)}) copy-start(f32[6,256,16]{1,2,0:T(8,128)} %fusion.111) | copy-start | bytes 294916
  378.2 7.0 %copy-start.13 = (f32[6,256,16]{1,2,0:T(8,128)S(1)}, f32[6,256,16]{1,2,0:T(8,128)}, u32[]{:S(2)}) copy-start(f32[6,256,16]{1,2,0:T(8,128)} %get-tuple-element.151) | copy-start | bytes 294916
  378.2 7.0 %copy-start.14 = (f32[6,16,256]{2,1,0:T(8,128)S(1)}, f32[6,16,256]{2,1,0:T(8,128)}, u32[]{:S(2)}) copy-start(f32[6,16,256]{2,1,0:T(8,128)} %reduce_window_sum.55) | copy-start | bytes 294916
  378.3 7.0 %copy-start.29 = (f32[16]{0:T(128)S(1)}, f32[16]{0:T(128)}, u32[]{:S(2)}) copy-start(f32[16]{0:T(128)} %dynamic_slice.150) | copy-start | bytes 196
  452.1 3.3 dynamic-slice-start
  528.4 7.9 %copy-start.9 = (bf16[2,2,384,1024]{3,2,1,0:T(8,128)(2,1)S(1)}, bf16[2,2,384,1024]{3,2,1,0:T(8,128)(2,1)}, u32[]{:S(2)}) copy-start(bf16[2,2,384,1024]{3,2,1,0:T(8,128)(2,1)} %multiply_convert_fusion.4) | copy-start | bytes 9437188
  528.4 7.9 %copy-start.23 = (bf16[1024,4096]{1,0:T(8,128)(2,1)S(1)}, bf16[1024,4096]{1,0:T(8,128)(2,1)}, u32[]{:S(2)}) copy-start(bf16[1024,4096]{1,0:T(8,128)(2,1)} %all-gather.8.cloned.1.call-done) | copy-start | bytes 25165828
  536.3 6.0 collective-permute-start.9
  541.3 9.9 %collective-permute-start.11 = (bf16[2,384,2048]{2,1,0:T(8,128)(2,1)}, bf16[2,384,2048]{2,1,0:T(8,128)(2,1)}, u32[]{:S(2)}, u32[]{:S(2)}) collective-permute-start(bf16[2,384,2048]{2,1,0:T(8,128)(2,1)} %convolution_convert_fusion.2), channel_id=1, source_target_pairs={{0,1},{1,0},{2,3},{3,2},{4,5},{5,4},{6,7},{7,6},{8,9},{9,8},{10,11... | collective-permute-start | bytes 9437192 | tf_op jit(solution)/shard_map/ppermute | solution.py:342
  541.9 9.4 %copy-start.10 = (bf16[2,2,384,1024]{3,2,1,0:T(8,128)(2,1)S(1)}, bf16[2,2,384,1024]{3,2,1,0:T(8,128)(2,1)}, u32[]{:S(2)}) copy-start(bf16[2,2,384,1024]{3,2,1,0:T(8,128)(2,1)} %multiply_convert_fusion.4) | copy-start | bytes 9437188
  549.5 8.7 %copy-start.6 = (f32[2,384,2048]{2,1,0:T(8,128)}, f32[2,384,2048]{2,1,0:T(8,128)S(1)}, u32[]{:S(2)}) copy-start(f32[2,384,2048]{2,1,0:T(8,128)S(1)} %convert_add_fusion.1) | copy-start | bytes 18874372
  549.7 37.3 %collective-permute-start.10 = (bf16[384,2048]{1,0:T(8,128)(2,1)S(1)}, bf16[384,2048]{1,0:T(8,128)(2,1)S(1)}, u32[]{:S(2)}, u32[]{:S(2)}) collective-permute-start(bf16[384,2048]{1,0:T(8,128)(2,1)S(1)} %fusion.36), channel_id=1, source_target_pairs={{0,2},{2,0},{1,3},{3,1},{4,6},{6,4},{5,7},{7,5},{8,10},{10,8},{9,1... | collective-permute-start | bytes 4718600 | tf_op jit(solution)/shard_map/ppermute | solution.py:127
  558.2 3.1 copy-start.7
  561.3 58.8 %collective-permute-start.12 = (bf16[384,2048]{1,0:T(8,128)(2,1)}, bf16[384,2048]{1,0:T(8,128)(2,1)}, u32[]{:S(2)}, u32[]{:S(2)}) collective-permute-start(bf16[384,2048]{1,0:T(8,128)(2,1)} %fusion.37), channel_id=1, source_target_pairs={{0,2},{2,0},{1,3},{3,1},{4,6},{6,4},{5,7},{7,5},{8,10},{10,8},{9,1... | collective-permute-start | bytes 4718600 | tf_op jit(solution)/shard_map/ppermute | solution.py:127
  562.8 57.2 %copy-start.8 = (f32[2,384,2048]{2,1,0:T(8,128)S(1)}, f32[2,384,2048]{2,1,0:T(8,128)}, u32[]{:S(2)}) copy-start(f32[2,384,2048]{2,1,0:T(8,128)} %copy-done.7) | copy-start | bytes 18874372
  587.0 37.0 %copy-start.1 = (f32[32,64,128]{2,1,0:T(8,128)S(1)}, f32[32,64,128]{2,1,0:T(8,128)}, u32[]{:S(2)}) copy-start(f32[32,64,128]{2,1,0:T(8,128)} %param.35) | copy-start | bytes 3145732
Sparse Core Ops, SparseCore 0:
  48.9 165.1 all-gather.3
  252.9 137.3 all-gather.5
  392.4 135.9 all-gather.7

commit v9 on v8

--- a/solution.py
+++ b/solution.py
@@ -329,7 +329,7 @@
     ).astype(jnp.bfloat16)
     piece = own_rows // core_count
     by_owner = normed_y.reshape(2, core_count, piece, inner_local)
-    chunk_count = 2
+    chunk_count = 4
     chunk = out_full.shape[1] // chunk_count
     results = []
     for index in range(chunk_count):

time: 639 us -> 638 us (level)
  waiting for transfers between devices: 265 us -> 276 us
    all_gather x1, waiting for transfers between devices: 70.3 us -> 78.6 us  [body(): out_full = lax.all_gather(out_local, 'pair', axis=1, tiled=True)]
    ppermute x6 -> x8, waiting for transfers between devices: 141 us -> 145 us  [swap_half(): lax.ppermute(value, 'half', [(k, count - 1 - k) for k in range(count)])]
    dot_general x4 -> x8, matrix products: 27 us -> 24.5 us  [body(): jnp.einsum('hrc,cd->hrd', rows, columns, preferred_element_type=jnp.float32)]
  transfers between devices with their start and end apart: 16 -> 20, of which waited for: 8 -> 9; matrix products, arithmetic and copies ran while one was open for 40% -> 39% of each run, Pallas kernels for 0% -> 0%
where the time goes in v9:
time: 638 us; the launch traced here: 629 us
  waiting for transfers between devices  276 us (43%)
  other arithmetic  114 us (18%)
  matrix products  107 us (17%)
  local copies, waits for them, and re-layouts  86.5 us (14%)
  starting transfers between devices  31.2 us (5%)
  between operations  15.3 us (2%)
    ppermute x8, waiting for transfers between devices, swap_half(): lax.ppermute(value, 'half', [(k, count - 1 - k) for k in range(count)])  145 us
    all_gather x1, waiting for transfers between devices, body(): out_full = lax.all_gather(out_local, 'pair', axis=1, tiled=True)  78.6 us
    all_gather x1, waiting for transfers between devices, body(): first_full = lax.all_gather(first_local, 'pair', axis=0, tiled=True)  51.8 us
    dot_general x1, matrix products, body(): jnp.dot(normed, z_full, preferred_element_type=jnp.float32)  27 us
    dot_general x8, matrix products, body(): jnp.einsum('hrc,cd->hrd', rows, columns, preferred_element_type=jnp.float32)  24.5 us
    dot_general x1, matrix products, body(): jnp.dot(normed, first_full, preferred_element_type=jnp.float32)  23.8 us
    reshape x2, local copies, waits for them, and re-layouts, body(): (direct + state_gain[..., None] * from_state).reshape(row_count, inner_lo...  22.9 us
    convert_element_type x1, other arithmetic, conv_rows(): return jax.nn.silu(summed).astype(jnp.bfloat16)  21.4 us
  transfers between devices with their start and end apart: 20, of which 9 were waited for; matrix products, arithmetic and copies ran while one was open for 39% of the time, Pallas kernels for 0%

profile of v9, /device:TPU:0, one launch (start us, length us, event | category | flops | bytes accessed | tf_op | source)
XLA Modules:
  0.0 629.4 jit_solution(5641792374067063064)
XLA Ops:
  6.5 1.6 fusion.118
  11.4 6.9 %fusion.117 = (bf16[256,1,2048]{2,1,0:T(2,128)(2,1)}, bf16[256,1,2048]{2,1,0:T(2,128)(2,1)}) fusion(bf16[256,2,2048]{2,1,0:T(2,128)(2,1)} %param.22), kind=kLoop, calls=%fused_computation.258 | loop fusion | bytes 4194304 | tf_op jit(solution)/shard_map/slice | solution.py:197
  18.3 3.7 constant_dynamic-slice_fusion.19
  24.2 2.9 collective-permute-start.2
  29.0 13.3 %collective-permute-done.2 = bf16[256,1296]{0,1:T(8,128)(2,1)S(1)} collective-permute-done((bf16[256,1296]{0,1:T(8,128)(2,1)}, bf16[256,1296]{0,1:T(8,128)(2,1)S(1)}, u32[]{:S(2)}, u32[]{:S(2)}) %collective-permute-start.2) | collective-permute-done | bytes 663584 | tf_op jit(solution)/shard_map/ppermute | solution.py:127
  42.6 6.2 maximum_select_fusion.3
  49.0 4.1 fusion.3
  53.1 5.3 fusion.5
  58.4 2.9 copy-done.4
  61.6 1.8 collective-permute-start
  63.4 67.6 %collective-permute-done = bf16[384,4096]{1,0:T(8,128)(2,1)} collective-permute-done((bf16[384,4096]{1,0:T(8,128)(2,1)S(1)}, bf16[384,4096]{1,0:T(8,128)(2,1)}, u32[]{:S(2)}, u32[]{:S(2)}) %collective-permute-start) | collective-permute-done | bytes 3145760 | tf_op jit(solution)/shard_map/ppermute | solution.py:127
  135.6 1.8 reduce-window.30
  139.1 2.2 copy.282
  141.3 5.0 fusion.20
  146.3 4.3 gather_fusion
  150.6 4.3 gather_fusion.1
  154.9 3.6 pad_maximum_fusion
  158.6 3.7 bitcast_select_fusion
  162.3 51.8 %all-gather.4.cloned.1.call-done = bf16[4096,1296]{1,0:T(8,128)(2,1)} async-done(((bf16[512,1296]{1,0:T(8,128)(2,1)}), bf16[4096,1296]{1,0:T(8,128)(2,1)}) %all-gather.4.cloned.1.call-update) | async-done | bytes 10616848 | tf_op jit(solution)/shard_map/all_gather | solution.py:211
  214.1 23.8 %convolution_convert_fusion = bf16[1536,1296]{0,1:T(8,128)(2,1)} fusion(bf16[4096,1296]{1,0:T(8,128)(2,1)} %all-gather.4.cloned.1.call-done, bf16[768,4096]{1,0:T(8,128)(2,1)} %bitcast_select_fusion, bf16[768,4096]{1,0:T(8,128)(2,1)} %copy-done.4, pred[]{:T(512)S(6)} %eq.208), kind=kOutput, calls=%fused_computation.27 | convolution fusion | flops 16366067712 | bytes 27181056 | tf_op jit(solution)/shard_map/dot_general | solution.py:212
  238.0 1.5 collective-permute-start.7
  245.9 5.4 collective-permute-done.7
  251.3 1.5 maximum_select_fusion.4
  261.1 1.9 slice.165
  263.0 3.2 collective-permute-start.3
  267.9 3.8 reduce-window.21
  278.9 4.4 slice.160
  283.6 1.5 collective-permute-start.8
  286.0 21.4 %multiply_convert_fusion.3 = bf16[1536,1280]{0,1:T(8,128)(2,1)S(1)} fusion(bf16[1536,1280]{0,1:T(8,128)(2,1)} %slice.160, bf16[3,1280]{0,1:T(8,128)(2,1)} %collective-permute-done.3, f32[1280]{0:T(1024)S(1)} %copy-done.17, f32[1280]{0:T(1024)S(1)} %copy-done.18, f32[1280]{0:T(1024)S(1)} %copy-done.19, f32[1280]{0:T(1024)S(1)} %copy-done.16, ...), kind=kLoop, calls=%fused_computation.26 | loop fusion | flops 104202240 | bytes 7933952 | tf_op jit(solution)/shard_map/convert_element_type | solution.py:68
  307.4 5.3 fusion.115
  315.4 7.5 %reshape.580 = bf16[6,256,16,64]{1,0,3,2:T(8,128)(2,1)} reshape(bf16[1536,1024]{0,1:T(8,128)(2,1)} %get-tuple-element.159) | data formatting | bytes 6291456 | tf_op jit(solution)/shard_map/reshape.48
  322.9 3.2 multiply_convert_fusion.2
  326.2 2.7 add_bitcast_fusion
  328.8 12.6 %while.17 = (s32[]{:T(128)}, f32[1,16,64,128]{3,2,1,0:T(8,128)S(1)}, f32[1,16]{1,0:T(1,128)S(1)}, f32[6,1,16,64,128]{4,3,2,1,0:T(8,128)}, f32[6,1,16]{2,0,1:T(8,...) while((s32[]{:T(128)}, ...), condition=%wide.region_15.16_spmd.clone, body=%wide.region_14.15_spmd.clone.sunk | while | flops 524323 | bytes 2622649 | solution.py:308
  341.4 2.3 collective-permute-start.4
  343.7 6.8 %collective-permute-start.6 = (f32[1,16,64,128]{3,2,1,0:T(8,128)S(1)}, f32[1,16,64,128]{3,2,1,0:T(8,128)}, u32[]{:S(2)}, u32[]{:S(2)}) collective-permute-start(f32[1,16,64,128]{3,2,1,0:T(8,128)S(1)} %get-tuple-element.48), channel_id=1, source_target_pairs={{0,8},{4,12},{8,16},{12,20},{16,24},{20,28},{1,9},{5,13},{9,17},{1... | collective-permute-start | bytes 1572872 | tf_op jit(solution)/shard_map/ppermute | solution.py:15
  350.7 5.3 collective-permute-start.5
  356.1 1.5 fusion.121
  357.6 5.3 fusion.62
  362.9 9.0 %reshape.602 = f32[6,256,1,16,64]{1,0,4,3,2:T(8,128)} reshape(f32[1536,1024]{0,1:T(8,128)} %get-tuple-element.160) | data formatting | bytes 12582912 | tf_op jit(solution)/shard_map/convert_element_type | solution.py:119
  371.9 1.5 add_bitcast_fusion.1
  373.4 5.3 fusion.21
  378.8 16.6 %fusion.17 = f32[6,256,1,16,64]{1,4,3,0,2:T(8,128)} fusion(f32[6,256,1,16,64]{1,0,4,3,2:T(8,128)} %reshape.602, f32[6,256,16,64]{1,3,2,0:T(8,128)S(1)} %fusion.21, f32[6,256,16,64]{1,3,2,0:T(8,128)S(1)} %copy-done.5, f32[6,256,16]{1,2,0:T(8,128)S(1)} %copy-done.12, f32[16]{0:T(128)S(1)} %copy-done.49, f32[6,256,16]{1,2,0:T(8,128)S(1)} %copy-done.11, ...), kind=kOutput, calls=%fused_computation.37 | convolution fusion | flops 852492288 | bytes 30670912 | tf_op jit(solution)/shard_map/cghqs,csghp->cqghp/dot_general | solution.py:20
  395.5 11.3 %copy.227 = f32[6,256,1,16,64]{4,3,1,0,2:T(8,128)} copy(f32[6,256,1,16,64]{1,4,3,0,2:T(8,128)} %fusion.17) | data formatting | bytes 12582912 | tf_op jit(solution)/shard_map/reshape | solution.py:320
  406.8 11.6 %reshape.626 = f32[1536,1024]{1,0:T(8,128)} reshape(f32[6,256,1,16,64]{4,3,1,0,2:T(8,128)} %copy.227) | data formatting | bytes 12582912 | tf_op jit(solution)/shard_map/reshape | solution.py:320
  418.4 27.0 %multiply_reduce_fusion = (f32[1536]{0:T(1024)S(1)}, f32[1536,1024]{1,0:T(8,128)}) fusion(f32[1536,1024]{1,0:T(8,128)} %reshape.626, bf16[4096,1024]{1,0:T(8,128)(2,1)} %all-gather.6.cloned.1.call-done, bf16[768,4096]{1,0:T(8,128)(2,1)} %bitcast_select_fusion, bf16[768,4096]{1,0:T(8,128)(2,1)} %copy-done.4, pred[]{:T(512)S(6)} %eq.208), kind=kOutput, calls=%fused_computation.41 | convolution fusion | flops 12955678720 | bytes 33560576 | tf_op jit(solution)/shard_map/dot_general | solution.py:233
  445.4 3.3 broadcast_multiply_fusion
  448.7 2.6 multiply_convert_fusion.4
  451.4 78.6 %all-gather.8.cloned.1.call-done = bf16[1024,4096]{1,0:T(8,128)(2,1)} async-done(((bf16[1024,512]{1,0:T(8,128)(2,1)}), bf16[1024,4096]{1,0:T(8,128)(2,1)}) %all-gather.8.cloned.1.call-update) | async-done | bytes 8388624 | tf_op jit(solution)/shard_map/all_gather | solution.py:232
  529.9 5.2 convolution_convert_fusion.5
  535.1 4.6 convolution_convert_fusion.4
  540.2 4.0 convolution_convert_fusion.3
  544.3 3.5 convolution_convert_fusion.2
  548.5 1.8 convert_add_fusion.3
  550.4 1.5 collective-permute-start.10
  552.0 1.8 convert_add_fusion.2
  554.5 1.8 convert_add_fusion.1
  556.5 1.5 collective-permute-start.14
  558.0 1.8 convert_add_fusion
  560.6 10.3 %collective-permute-done.10 = bf16[384,1024]{1,0:T(8,128)(2,1)S(1)} collective-permute-done((bf16[384,1024]{1,0:T(8,128)(2,1)S(1)}, bf16[384,1024]{1,0:T(8,128)(2,1)S(1)}, u32[]{:S(2)}, u32[]{:S(2)}) %collective-permute-start.10) | collective-permute-done | bytes 786464 | tf_op jit(solution)/shard_map/ppermute | solution.py:127
  571.2 16.6 %collective-permute-done.12 = bf16[384,1024]{1,0:T(8,128)(2,1)S(1)} collective-permute-done((bf16[384,1024]{1,0:T(8,128)(2,1)S(1)}, bf16[384,1024]{1,0:T(8,128)(2,1)S(1)}, u32[]{:S(2)}, u32[]{:S(2)}) %collective-permute-start.12) | collective-permute-done | bytes 786464 | tf_op jit(solution)/shard_map/ppermute | solution.py:127
  588.0 16.6 %collective-permute-done.14 = bf16[384,1024]{1,0:T(8,128)(2,1)S(1)} collective-permute-done((bf16[384,1024]{1,0:T(8,128)(2,1)S(1)}, bf16[384,1024]{1,0:T(8,128)(2,1)S(1)}, u32[]{:S(2)}, u32[]{:S(2)}) %collective-permute-start.14) | collective-permute-done | bytes 786464 | tf_op jit(solution)/shard_map/ppermute | solution.py:127
  604.9 15.7 %collective-permute-done.16 = bf16[384,1024]{1,0:T(8,128)(2,1)S(1)} collective-permute-done((bf16[384,1024]{1,0:T(8,128)(2,1)S(1)}, bf16[384,1024]{1,0:T(8,128)(2,1)S(1)}, u32[]{:S(2)}, u32[]{:S(2)}) %collective-permute-start.16) | collective-permute-done | bytes 786464 | tf_op jit(solution)/shard_map/ppermute | solution.py:127
  620.8 1.8 pad_maximum_fusion.3
  (274 shorter events, 57.2 us)
Async XLA Ops:
  6.5 251.2 %copy-start = (f32[32,64,128]{2,1,0:T(8,128)S(1)}, f32[32,64,128]{2,1,0:T(8,128)}, u32[]{:S(2)}) copy-start(f32[32,64,128]{2,1,0:T(8,128)} %param.35) | copy-start | bytes 3145732
  6.5 207.5 %all-gather.4.cloned.1.call-start = ((), (), s32[]{:S(2)}) async-start(), calls=%async_computation | async-start | bytes 12976128 | tf_op jit(solution)/shard_map/all_gather | solution.py:211
  24.2 18.1 %collective-permute-start.2 = (bf16[256,1296]{0,1:T(8,128)(2,1)}, bf16[256,1296]{0,1:T(8,128)(2,1)S(1)}, u32[]{:S(2)}, u32[]{:S(2)}) collective-permute-start(bf16[256,1296]{0,1:T(8,128)(2,1)} %copy.201), channel_id=1, source_target_pairs={{0,2},{2,0},{1,3},{3,1},{4,6},{6,4},{5,7},{7,5},{8,10},{10,8},{9,1... | collective-permute-start | bytes 1990664 | tf_op jit(solution)/shard_map/ppermute | solution.py:127
  48.8 369.6 %all-gather.6.cloned.1.call-start = ((), (), s32[]{:S(2)}) async-start(), calls=%async_computation.1 | async-start | bytes 9437184 | tf_op jit(solution)/shard_map/all_gather | solution.py:231
  61.3 70.4 %copy-start.44 = (s32[8]{0:T(128)S(1)}, s32[8]{0:T(128)}, u32[]{:S(2)}) copy-start(s32[8]{0:T(128)} %param.32) | copy-start | bytes 100
  61.3 70.4 %copy-start.45 = (s32[8]{0:T(128)S(1)}, s32[8]{0:T(128)}, u32[]{:S(2)}) copy-start(s32[8]{0:T(128)} %param.33) | copy-start | bytes 100
  61.3 72.9 %copy-start.21 = (bf16[4,2,256]{2,1,0:T(2,128)(2,1)S(1)}, bf16[4,2,256]{2,1,0:T(2,128)(2,1)}, u32[]{:S(2)}) copy-start(bf16[4,2,256]{2,1,0:T(2,128)(2,1)} %param.26) | copy-start | bytes 12292
  61.3 73.0 %copy-start.23 = (bf16[3,2,256]{2,1,0:T(2,128)(2,1)S(1)}, bf16[3,2,256]{2,1,0:T(2,128)(2,1)}, u32[]{:S(2)}) copy-start(bf16[3,2,256]{2,1,0:T(2,128)(2,1)} %param.37) | copy-start | bytes 9220
  61.3 73.0 %copy-start.46 = (f32[32]{0:T(128)S(1)}, f32[32]{0:T(128)}, u32[]{:S(2)}) copy-start(f32[32]{0:T(128)} %param.27) | copy-start | bytes 388
  61.3 73.7 %copy-start.47 = (f32[32]{0:T(128)S(1)}, f32[32]{0:T(128)}, u32[]{:S(2)}) copy-start(f32[32]{0:T(128)} %param.28) | copy-start | bytes 388
  61.4 77.1 %copy-start.48 = (f32[32]{0:T(128)S(1)}, f32[32]{0:T(128)}, u32[]{:S(2)}) copy-start(f32[32]{0:T(128)} %param.29) | copy-start | bytes 388
  61.6 69.5 %collective-permute-start = (bf16[384,4096]{1,0:T(8,128)(2,1)S(1)}, bf16[384,4096]{1,0:T(8,128)(2,1)}, u32[]{:S(2)}, u32[]{:S(2)}) collective-permute-start(bf16[384,4096]{1,0:T(8,128)(2,1)S(1)} %constant_dynamic-slice_fusion.20), channel_id=1, source_target_pairs={{0,2},{2,0},{1,3},{3,1},{4,6},{6,4},{5,7},{7,5},{8,10},{10,8},{9,1... | collective-permute-start | bytes 9437192 | tf_op jit(solution)/shard_map/ppermute | solution.py:127
  131.0 10.3 %collective-permute-start.1 = (bf16[384,4096]{1,0:T(8,128)(2,1)}, bf16[384,4096]{1,0:T(8,128)(2,1)}, u32[]{:S(2)}, u32[]{:S(2)}) collective-permute-start(bf16[384,4096]{1,0:T(8,128)(2,1)} %collective-permute-done), channel_id=1, source_target_pairs={{0,1},{1,0},{2,3},{3,2},{4,5},{5,4},{6,7},{7,6},{8,9},{9,8},{10,11... | collective-permute-start | bytes 9437192 | tf_op jit(solution)/shard_map/ppermute | solution.py:186
  237.9 17.8 %copy-start.42 = (bf16[4,2048]{1,0:T(4,128)(2,1)S(1)}, bf16[4,2048]{1,0:T(4,128)(2,1)}, u32[]{:S(2)}) copy-start(bf16[4,2048]{1,0:T(4,128)(2,1)} %param.25) | copy-start | bytes 49156
  237.9 17.9 %copy-start.43 = (bf16[3,2048]{1,0:T(4,128)(2,1)S(1)}, bf16[3,2048]{1,0:T(4,128)(2,1)}, u32[]{:S(2)}) copy-start(bf16[3,2048]{1,0:T(4,128)(2,1)} %param.36) | copy-start | bytes 36868
  238.0 13.3 %collective-permute-start.7 = (bf16[256,1024]{1,0:T(8,128)(2,1)S(1)}, bf16[256,1024]{1,0:T(8,128)(2,1)S(1)}, u32[]{:S(2)}, u32[]{:S(2)}) collective-permute-start(bf16[256,1024]{1,0:T(8,128)(2,1)S(1)} %get-tuple-element.168), channel_id=1, source_target_pairs={{0,2},{2,0},{1,3},{3,1},{4,6},{6,4},{5,7},{7,5},{8,10},{10,8},{9,1... | collective-permute-start | bytes 1572872 | tf_op jit(solution)/shard_map/ppermute | solution.py:127
  251.3 23.5 %copy-start.9 = (bf16[2048,256]{1,0:T(8,128)(2,1)S(1)}, bf16[2048,256]{1,0:T(8,128)(2,1)}, u32[]{:S(2)}) copy-start(bf16[2048,256]{1,0:T(8,128)(2,1)} %param.31) | copy-start | bytes 3145732
  252.8 277.1 %all-gather.8.cloned.1.call-start = ((), (), s32[]{:S(2)}) async-start(), calls=%async_computation.2 | async-start | bytes 9437184 | tf_op jit(solution)/shard_map/all_gather | solution.py:232
  263.0 22.8 %collective-permute-start.3 = (bf16[3,1280]{0,1:T(8,128)(2,1)}, bf16[3,1280]{0,1:T(8,128)(2,1)}, u32[]{:S(2)}, u32[]{:S(2)}) collective-permute-start(bf16[3,1280]{0,1:T(8,128)(2,1)} %slice.165), channel_id=1, source_target_pairs={{0,4},{4,8},{8,12},{12,16},{16,20},{20,24},{24,28},{1,5},{5,9},{9,... | collective-permute-start | bytes 23048 | tf_op jit(solution)/shard_map/ppermute | solution.py:15
  278.7 7.1 %copy-start.14 = (f32[1280]{0:T(1024)S(1)}, f32[1280]{0:T(1024)}, u32[]{:S(2)}) copy-start(f32[1280]{0:T(1024)} %get-tuple-element.129) | copy-start | bytes 15364
  278.7 7.1 %copy-start.15 = (f32[1280]{0:T(1024)S(1)}, f32[1280]{0:T(1024)}, u32[]{:S(2)}) copy-start(f32[1280]{0:T(1024)} %get-tuple-element.130) | copy-start | bytes 15364
  278.7 7.1 %copy-start.16 = (f32[1280]{0:T(1024)S(1)}, f32[1280]{0:T(1024)}, u32[]{:S(2)}) copy-start(f32[1280]{0:T(1024)} %get-tuple-element.131) | copy-start | bytes 15364
  278.7 7.1 %copy-start.17 = (f32[1280]{0:T(1024)S(1)}, f32[1280]{0:T(1024)}, u32[]{:S(2)}) copy-start(f32[1280]{0:T(1024)} %get-tuple-element.132) | copy-start | bytes 15364
  278.7 7.1 %copy-start.18 = (f32[1280]{0:T(1024)S(1)}, f32[1280]{0:T(1024)}, u32[]{:S(2)}) copy-start(f32[1280]{0:T(1024)} %get-tuple-element.133) | copy-start | bytes 15364
  278.7 7.1 %copy-start.19 = (f32[1280]{0:T(1024)S(1)}, f32[1280]{0:T(1024)}, u32[]{:S(2)}) copy-start(f32[1280]{0:T(1024)} %get-tuple-element.134) | copy-start | bytes 15364
  278.7 7.1 %copy-start.24 = (pred[1536]{0:T(1024)(128)(4,1)S(1)}, pred[1536]{0:T(1024)(128)(4,1)}, u32[]{:S(2)}) copy-start(pred[1536]{0:T(1024)(128)(4,1)} %get-tuple-element.183) | copy-start | bytes 4612
  278.8 7.1 %copy-start.25 = (pred[1536]{0:T(1024)(128)(4,1)S(1)}, pred[1536]{0:T(1024)(128)(4,1)}, u32[]{:S(2)}) copy-start(pred[1536]{0:T(1024)(128)(4,1)} %get-tuple-element.184) | copy-start | bytes 4612
  278.8 7.1 %copy-start.26 = (pred[1536]{0:T(1024)(128)(4,1)S(1)}, pred[1536]{0:T(1024)(128)(4,1)}, u32[]{:S(2)}) copy-start(pred[1536]{0:T(1024)(128)(4,1)} %get-tuple-element.185) | copy-start | bytes 4612
  278.8 7.1 %copy-start.27 = (pred[1536]{0:T(1024)(128)(4,1)S(1)}, pred[1536]{0:T(1024)(128)(4,1)}, u32[]{:S(2)}) copy-start(pred[1536]{0:T(1024)(128)(4,1)} %get-tuple-element.186) | copy-start | bytes 4612
  278.8 7.1 %copy-start.28 = (pred[1536]{0:T(1024)(128)(4,1)S(1)}, pred[1536]{0:T(1024)(128)(4,1)}, u32[]{:S(2)}) copy-start(pred[1536]{0:T(1024)(128)(4,1)} %get-tuple-element.193) | copy-start | bytes 4612
  278.8 7.1 %copy-start.29 = (pred[1536]{0:T(1024)(128)(4,1)S(1)}, pred[1536]{0:T(1024)(128)(4,1)}, u32[]{:S(2)}) copy-start(pred[1536]{0:T(1024)(128)(4,1)} %get-tuple-element.194) | copy-start | bytes 4612
  278.8 7.1 %copy-start.30 = (pred[1536]{0:T(1024)(128)(4,1)S(1)}, pred[1536]{0:T(1024)(128)(4,1)}, u32[]{:S(2)}) copy-start(pred[1536]{0:T(1024)(128)(4,1)} %get-tuple-element.195) | copy-start | bytes 4612
  278.8 7.1 %copy-start.31 = (pred[1536]{0:T(1024)(128)(4,1)S(1)}, pred[1536]{0:T(1024)(128)(4,1)}, u32[]{:S(2)}) copy-start(pred[1536]{0:T(1024)(128)(4,1)} %get-tuple-element.196) | copy-start | bytes 4612
  278.8 7.1 %copy-start.32 = (pred[1536]{0:T(1024)(128)(4,1)S(1)}, pred[1536]{0:T(1024)(128)(4,1)}, u32[]{:S(2)}) copy-start(pred[1536]{0:T(1024)(128)(4,1)} %get-tuple-element.205) | copy-start | bytes 4612
  278.8 7.1 %copy-start.33 = (pred[1536]{0:T(1024)(128)(4,1)S(1)}, pred[1536]{0:T(1024)(128)(4,1)}, u32[]{:S(2)}) copy-start(pred[1536]{0:T(1024)(128)(4,1)} %get-tuple-element.206) | copy-start | bytes 4612
  278.8 7.1 %copy-start.34 = (pred[1536]{0:T(1024)(128)(4,1)S(1)}, pred[1536]{0:T(1024)(128)(4,1)}, u32[]{:S(2)}) copy-start(pred[1536]{0:T(1024)(128)(4,1)} %get-tuple-element.207) | copy-start | bytes 4612
  278.9 7.1 %copy-start.35 = (pred[1536]{0:T(1024)(128)(4,1)S(1)}, pred[1536]{0:T(1024)(128)(4,1)}, u32[]{:S(2)}) copy-start(pred[1536]{0:T(1024)(128)(4,1)} %get-tuple-element.208) | copy-start | bytes 4612
  278.9 7.1 %copy-start.36 = (pred[1536]{0:T(1024)(128)(4,1)S(1)}, pred[1536]{0:T(1024)(128)(4,1)}, u32[]{:S(2)}) copy-start(pred[1536]{0:T(1024)(128)(4,1)} %get-tuple-element.209) | copy-start | bytes 4612
  278.9 7.1 %copy-start.37 = (pred[1536]{0:T(1024)(128)(4,1)S(1)}, pred[1536]{0:T(1024)(128)(4,1)}, u32[]{:S(2)}) copy-start(pred[1536]{0:T(1024)(128)(4,1)} %get-tuple-element.210) | copy-start | bytes 4612
  278.9 7.1 %copy-start.38 = (pred[1536]{0:T(1024)(128)(4,1)S(1)}, pred[1536]{0:T(1024)(128)(4,1)}, u32[]{:S(2)}) copy-start(pred[1536]{0:T(1024)(128)(4,1)} %get-tuple-element.211) | copy-start | bytes 4612
  278.9 7.1 %copy-start.39 = (pred[1536]{0:T(1024)(128)(4,1)S(1)}, pred[1536]{0:T(1024)(128)(4,1)}, u32[]{:S(2)}) copy-start(pred[1536]{0:T(1024)(128)(4,1)} %get-tuple-element.212) | copy-start | bytes 4612
  278.9 7.1 %copy-start.40 = (pred[1536]{0:T(1024)(128)(4,1)S(1)}, pred[1536]{0:T(1024)(128)(4,1)}, u32[]{:S(2)}) copy-start(pred[1536]{0:T(1024)(128)(4,1)} %broadcast_compare_fusion.1) | copy-start | bytes 4612
  283.6 29.1 %collective-permute-start.8 = (bf16[1024,256]{1,0:T(8,128)(2,1)S(1)}, bf16[1024,256]{1,0:T(8,128)(2,1)S(1)}, u32[]{:S(2)}, u32[]{:S(2)}) collective-permute-start(bf16[1024,256]{1,0:T(8,128)(2,1)S(1)} %copy-done.10), channel_id=1, source_target_pairs={{0,2},{2,0},{1,3},{3,1},{4,6},{6,4},{5,7},{7,5},{8,10},{10,8},{9,1... | collective-permute-start | bytes 1572872 | tf_op jit(solution)/shard_map/ppermute | solution.py:127
  307.4 5.3 copy-start.3
  341.4 30.4 %collective-permute-start.4 = (f32[1,16,64,128]{3,2,1,0:T(8,128)S(1)}, f32[1,16,64,128]{3,2,1,0:T(8,128)}, u32[]{:S(2)}, u32[]{:S(2)}) collective-permute-start(f32[1,16,64,128]{3,2,1,0:T(8,128)S(1)} %get-tuple-element.48), channel_id=1, source_target_pairs={{0,4},{4,8},{8,12},{12,16},{16,20},{20,24},{24,28},{1,5},{5,9},{9,... | collective-permute-start | bytes 1572872 | tf_op jit(solution)/shard_map/ppermute | solution.py:15
  343.7 28.2 %collective-permute-start.6 = (f32[1,16,64,128]{3,2,1,0:T(8,128)S(1)}, f32[1,16,64,128]{3,2,1,0:T(8,128)}, u32[]{:S(2)}, u32[]{:S(2)}) collective-permute-start(f32[1,16,64,128]{3,2,1,0:T(8,128)S(1)} %get-tuple-element.48), channel_id=1, source_target_pairs={{0,8},{4,12},{8,16},{12,20},{16,24},{20,28},{1,9},{5,13},{9,17},{1... | collective-permute-start | bytes 1572872 | tf_op jit(solution)/shard_map/ppermute | solution.py:15
  350.7 21.1 %collective-permute-start.5 = (f32[1,16]{1,0:T(1,128)S(1)}, f32[1,16]{1,0:T(1,128)S(1)}, u32[]{:S(2)}, u32[]{:S(2)}) collective-permute-start(f32[1,16]{1,0:T(1,128)S(1)} %get-tuple-element.49), channel_id=1, source_target_pairs={{0,4},{4,8},{8,12},{12,16},{16,20},{20,24},{24,28},{1,5},{5,9},{9,... | collective-permute-start | bytes 200 | tf_op jit(solution)/shard_map/ppermute | solution.py:15
  362.9 15.9 %copy-start.8 = (f32[6,256,256]{2,1,0:T(8,128)S(1)}, f32[6,256,256]{2,1,0:T(8,128)}, u32[]{:S(2)}) copy-start(f32[6,256,256]{2,1,0:T(8,128)} %fusion.121) | copy-start | bytes 4718596
  371.9 6.9 %copy-start.5 = (f32[6,256,16,64]{1,3,2,0:T(8,128)S(1)}, f32[6,256,16,64]{1,3,2,0:T(8,128)}, u32[]{:S(2)}) copy-start(f32[6,256,16,64]{1,3,2,0:T(8,128)} %fusion.62) | copy-start | bytes 18874372
  373.3 5.4 copy-start.2
  373.4 5.4 copy-start.11
  373.4 5.4 copy-start.12
  373.4 5.4 copy-start.13
  373.4 5.4 copy-start.49
  529.9 5.2 copy-start.6
  535.1 13.4 %collective-permute-start.9 = (bf16[2,384,1024]{2,1,0:T(8,128)(2,1)}, bf16[2,384,1024]{2,1,0:T(8,128)(2,1)S(1)}, u32[]{:S(2)}, u32[]{:S(2)}) collective-permute-start(bf16[2,384,1024]{2,1,0:T(8,128)(2,1)} %convolution_convert_fusion.5), channel_id=1, source_target_pairs={{0,1},{1,0},{2,3},{3,2},{4,5},{5,4},{6,7},{7,6},{8,9},{9,8},{10,11... | collective-permute-start | bytes 4718600 | tf_op jit(solution)/shard_map/ppermute | solution.py:342
  539.6 12.3 %collective-permute-start.11 = (bf16[2,384,1024]{2,1,0:T(8,128)(2,1)}, bf16[2,384,1024]{2,1,0:T(8,128)(2,1)S(1)}, u32[]{:S(2)}, u32[]{:S(2)}) collective-permute-start(bf16[2,384,1024]{2,1,0:T(8,128)(2,1)} %convolution_convert_fusion.4), channel_id=1, source_target_pairs={{0,1},{1,0},{2,3},{3,2},{4,5},{5,4},{6,7},{7,6},{8,9},{9,8},{10,11... | collective-permute-start | bytes 4718600 | tf_op jit(solution)/shard_map/ppermute | solution.py:342
  540.2 8.3 %slice-start = ((s8[8388608]{0:T(1024)(128)(4,1)}), s8[4194304]{0:T(1024)(128)(4,1)S(1)}, s32[]{:S(2)}) async-start(s8[8388608]{0:T(1024)(128)(4,1)} %bitcast.245), calls=%async_computation.4 | async-start | bytes 8388608
  544.2 10.4 %collective-permute-start.13 = (bf16[2,384,1024]{2,1,0:T(8,128)(2,1)S(1)}, bf16[2,384,1024]{2,1,0:T(8,128)(2,1)S(1)}, u32[]{:S(2)}, u32[]{:S(2)}) collective-permute-start(bf16[2,384,1024]{2,1,0:T(8,128)(2,1)S(1)} %convolution_convert_fusion.3), channel_id=1, source_target_pairs={{0,1},{1,0},{2,3},{3,2},{4,5},{5,4},{6,7},{7,6},{8,9},{9,8},{10,11... | collective-permute-start | bytes 4718600 | tf_op jit(solution)/shard_map/ppermute | solution.py:342
  547.8 10.2 %collective-permute-start.15 = (bf16[2,384,1024]{2,1,0:T(8,128)(2,1)S(1)}, bf16[2,384,1024]{2,1,0:T(8,128)(2,1)S(1)}, u32[]{:S(2)}, u32[]{:S(2)}) collective-permute-start(bf16[2,384,1024]{2,1,0:T(8,128)(2,1)S(1)} %convolution_convert_fusion.2), channel_id=1, source_target_pairs={{0,1},{1,0},{2,3},{3,2},{4,5},{5,4},{6,7},{7,6},{8,9},{9,8},{10,11... | collective-permute-start | bytes 4718600 | tf_op jit(solution)/shard_map/ppermute | solution.py:342
  550.4 20.5 %collective-permute-start.10 = (bf16[384,1024]{1,0:T(8,128)(2,1)S(1)}, bf16[384,1024]{1,0:T(8,128)(2,1)S(1)}, u32[]{:S(2)}, u32[]{:S(2)}) collective-permute-start(bf16[384,1024]{1,0:T(8,128)(2,1)S(1)} %fusion.58), channel_id=1, source_target_pairs={{0,2},{2,0},{1,3},{3,1},{4,6},{6,4},{5,7},{7,5},{8,10},{10,8},{9,1... | collective-permute-start | bytes 2359304 | tf_op jit(solution)/shard_map/ppermute | solution.py:127
  553.9 33.8 %collective-permute-start.12 = (bf16[384,1024]{1,0:T(8,128)(2,1)S(1)}, bf16[384,1024]{1,0:T(8,128)(2,1)S(1)}, u32[]{:S(2)}, u32[]{:S(2)}) collective-permute-start(bf16[384,1024]{1,0:T(8,128)(2,1)S(1)} %fusion.59), channel_id=1, source_target_pairs={{0,2},{2,0},{1,3},{3,1},{4,6},{6,4},{5,7},{7,5},{8,10},{10,8},{9,1... | collective-permute-start | bytes 2359304 | tf_op jit(solution)/shard_map/ppermute | solution.py:127
  556.5 48.1 %collective-permute-start.14 = (bf16[384,1024]{1,0:T(8,128)(2,1)S(1)}, bf16[384,1024]{1,0:T(8,128)(2,1)S(1)}, u32[]{:S(2)}, u32[]{:S(2)}) collective-permute-start(bf16[384,1024]{1,0:T(8,128)(2,1)S(1)} %fusion.60), channel_id=1, source_target_pairs={{0,2},{2,0},{1,3},{3,1},{4,6},{6,4},{5,7},{7,5},{8,10},{10,8},{9,1... | collective-permute-start | bytes 2359304 | tf_op jit(solution)/shard_map/ppermute | solution.py:127
  559.9 60.6 %collective-permute-start.16 = (bf16[384,1024]{1,0:T(8,128)(2,1)S(1)}, bf16[384,1024]{1,0:T(8,128)(2,1)S(1)}, u32[]{:S(2)}, u32[]{:S(2)}) collective-permute-start(bf16[384,1024]{1,0:T(8,128)(2,1)S(1)} %fusion.61), channel_id=1, source_target_pairs={{0,2},{2,0},{1,3},{3,1},{4,6},{6,4},{5,7},{7,5},{8,10},{10,8},{9,1... | collective-permute-start | bytes 2359304 | tf_op jit(solution)/shard_map/ppermute | solution.py:127
  (9 other events, 31.3 us)
Sparse Core Ops, SparseCore 0:
  48.9 165.1 all-gather.3
  253.0 139.6 all-gather.5
  394.7 135.1 all-gather.7

commit v10 on v9

--- a/solution.py
+++ b/solution.py
@@ -13,6 +13,37 @@
     count = lax.axis_size(axis)
     leading, last = (max(0, -steps), min(count, count - steps))
     return lax.ppermute(value, axis, [(source, source + steps) for source in range(leading, last)])
+
+
+def ring_order(count):
+    return list(range(0, count, 2)) + list(range(count - 1, 0, -2))
+
+
+def ring_gather(local, axis, order):
+    count = len(order)
+    forward = [(order[k], order[(k + 1) % count]) for k in range(count)]
+    backward = [(order[k], order[(k - 1) % count]) for k in range(count)]
+    chunks = [local] + [None] * (count - 1)
+    ahead, behind = local, local
+    for steps in range(1, count // 2 + 1):
+        ahead = lax.ppermute(ahead, axis, forward)
+        chunks[steps] = ahead
+        if steps < count - steps:
+            behind = lax.ppermute(behind, axis, backward)
+            chunks[count - steps] = behind
+    return chunks
+
+
+def ring_columns(values, axis, order, width):
+    count = len(order)
+    table = jnp.asarray(order, jnp.int32)
+    places = jnp.asarray([order.index(k) for k in range(count)], jnp.int32)
+    place = places[lax.axis_index(axis)]
+    blocks = [
+        lax.dynamic_slice_in_dim(values, table[(place - offset) % count] * width, width, 1)
+        for offset in range(count)
+    ]
+    return jnp.concatenate(blocks, axis=1)
 
 
 def product_of(form, left, right):
@@ -228,9 +259,23 @@
         half,
         1,
     )
-    z_full = lax.all_gather(z_local, "pair", axis=0, tiled=True)
     out_full = lax.all_gather(out_local, "pair", axis=1, tiled=True)
-    proj_z = jnp.dot(normed, z_full, preferred_element_type=jnp.float32).astype(jnp.bfloat16)
+    z_split = z_local.shape[1] // 2
+    z_full = lax.all_gather(z_local[:, :z_split], "pair", axis=0, tiled=True)
+    order = ring_order(lax.axis_size("pair"))
+    z_chunks = ring_gather(z_local[:, z_split:], "pair", order)
+    normed_ring = ring_columns(normed, "pair", order, z_local.shape[0])
+    proj_z = jnp.concatenate(
+        [
+            jnp.dot(normed, z_full, preferred_element_type=jnp.float32),
+            jnp.dot(
+                normed_ring,
+                jnp.concatenate(z_chunks, axis=0),
+                preferred_element_type=jnp.float32,
+            ),
+        ],
+        axis=1,
+    ).astype(jnp.bfloat16)
 
     position = lax.axis_index("pair") * row_count + jnp.arange(row_count, dtype=jnp.int32)
     segment, seg_start, resume_slot, resume_start = layout(

time: 638 us -> 725 us (1.14)
  the two profiles are of different devices: /device:TPU:0 before, /device:TPU:14 now
where the time goes in v10:
time: 725 us; the launch traced here: 716 us
  waiting for transfers between devices  252 us (35%)
  local copies, waits for them, and re-layouts  159 us (22%)
  other arithmetic  143 us (20%)
  matrix products  103 us (14%)
  starting transfers between devices  32.6 us (4%)
  between operations  26.6 us (4%)
    ppermute x8, waiting for transfers between devices, swap_half(): lax.ppermute(value, 'half', [(k, count - 1 - k) for k in range(count)])  133 us
    ppermute x4, waiting for transfers between devices, ring_gather(): ahead = lax.ppermute(ahead, axis, forward)  53.1 us
    dot_general x1, matrix products, body(): jnp.dot(normed, first_full, preferred_element_type=jnp.float32)  24.3 us
    convert_element_type x1, other arithmetic, body(): normed_y = ((gated * factor).reshape(row_count, inner_local) * cut(gated_...  23.4 us
    dot_general x3, matrix products, product_of(): return jnp.einsum(form, left, right, preferred_element_type=jnp.float32)  23.2 us
    dynamic_slice x3, local copies, waits for them, and re-layouts, body(): lax.dynamic_index_in_dim(by_owner, (core + shift) % core_count, 1, keepdi...  22.9 us
    unnamed x115, local copies, waits for them, and re-layouts  22.9 us
    all_gather x1, waiting for transfers between devices, body(): first_full = lax.all_gather(first_local, 'pair', axis=0, tiled=True)  22.4 us
  transfers between devices with their start and end apart: 27, of which 12 were waited for; matrix products, arithmetic and copies ran while one was open for 47% of the time, Pallas kernels for 0%

profile of v10, /device:TPU:14, one launch (start us, length us, event | category | flops | bytes accessed | tf_op | source)
XLA Modules:
  0.0 716.3 jit_solution(6250550523876448124)
XLA Ops:
  6.5 6.5 fusion.98
  14.3 2.4 constant_dynamic-slice_fusion.19
  16.7 3.1 constant_dynamic-slice_fusion.21
  23.1 14.1 %collective-permute-done.2 = bf16[256,1296]{0,1:T(8,128)(2,1)} collective-permute-done((bf16[256,1296]{0,1:T(8,128)(2,1)S(1)}, bf16[256,1296]{0,1:T(8,128)(2,1)}, u32[]{:S(2)}, u32[]{:S(2)}) %collective-permute-start.2) | collective-permute-done | bytes 663584 | tf_op jit(solution)/shard_map/ppermute | solution.py:158
  38.6 5.3 maximum_select_fusion.1
  44.5 4.1 fusion.3
  48.6 5.3 fusion.5
  53.9 2.8 copy-done.3
  75.3 2.2 copy.322
  81.8 46.3 %collective-permute-done = bf16[384,4096]{1,0:T(8,128)(2,1)} collective-permute-done((bf16[384,4096]{1,0:T(8,128)(2,1)}, bf16[384,4096]{1,0:T(8,128)(2,1)}, u32[]{:S(2)}, u32[]{:S(2)}) %collective-permute-start) | collective-permute-done | bytes 3145760 | tf_op jit(solution)/shard_map/ppermute | solution.py:158
  140.8 4.5 fusion.19
  145.3 4.4 gather_fusion.1
  149.7 4.3 gather_fusion
  154.0 3.8 pad_maximum_fusion
  157.8 3.7 bitcast_select_fusion
  161.5 9.3 %maximum_select_fusion = bf16[1536,4096]{1,0:T(8,128)(2,1)S(1)} fusion(bf16[768,4096]{1,0:T(8,128)(2,1)} %bitcast_select_fusion, bf16[768,4096]{1,0:T(8,128)(2,1)S(1)} %bitcast.237, pred[]{:T(512)S(6)} %eq.216), kind=kLoop, calls=%fused_computation.16 | loop fusion | flops 56623104 | bytes 25165824 | tf_op jit(solution)/shard_map/jit(_where)/select_n | solution.py:162
  183.7 22.4 %all-gather.4.cloned.1.call-done = bf16[4096,1296]{1,0:T(8,128)(2,1)} async-done(((bf16[512,1296]{1,0:T(8,128)(2,1)}), bf16[4096,1296]{1,0:T(8,128)(2,1)}) %all-gather.4.cloned.1.call-update) | async-done | bytes 10616848 | tf_op jit(solution)/shard_map/all_gather | solution.py:242
  206.1 24.3 %convolution_convert_fusion = bf16[1536,1296]{0,1:T(8,128)(2,1)} fusion(bf16[1536,4096]{1,0:T(8,128)(2,1)} %copy-done.2, bf16[4096,1296]{1,0:T(8,128)(2,1)} %all-gather.4.cloned.1.call-done), kind=kOutput, calls=%fused_computation.27 | convolution fusion | flops 16309444608 | bytes 27181056 | tf_op jit(solution)/shard_map/dot_general | solution.py:243
  230.4 4.3 slice.168
  237.7 3.4 reduce-window.21
  241.9 2.2 constant_dynamic-slice_fusion.3
  247.2 5.2 collective-permute-start.3
  255.3 13.5 %collective-permute-done.7 = bf16[256,1024]{1,0:T(8,128)(2,1)S(1)} collective-permute-done((bf16[256,1024]{1,0:T(8,128)(2,1)S(1)}, bf16[256,1024]{1,0:T(8,128)(2,1)S(1)}, u32[]{:S(2)}, u32[]{:S(2)}) %collective-permute-start.7) | collective-permute-done | bytes 524320 | tf_op jit(solution)/shard_map/ppermute | solution.py:158
  271.8 21.7 %multiply_convert_fusion.3 = bf16[1536,1280]{0,1:T(8,128)(2,1)S(1)} fusion(bf16[1536,1280]{0,1:T(8,128)(2,1)} %slice.168, bf16[3,1280]{0,1:T(8,128)(2,1)S(1)} %collective-permute-done.3, f32[1280]{0:T(1024)S(1)} %copy-done.17, f32[1280]{0:T(1024)S(1)} %copy-done.18, f32[1280]{0:T(1024)S(1)} %copy-done.19, f32[1280]{0:T(1024)S(1)} %copy-done.16, ...), kind=kLoop, calls=%fused_computation.26 | loop fusion | flops 104202240 | bytes 7933952 | tf_op jit(solution)/shard_map/convert_element_type | solution.py:99
  293.5 5.0 fusion.96
  298.5 7.5 %reshape.659 = bf16[6,256,16,64]{1,0,3,2:T(8,128)(2,1)} reshape(bf16[1536,1024]{0,1:T(8,128)(2,1)} %get-tuple-element.159) | data formatting | bytes 6291456 | tf_op jit(solution)/shard_map/reshape.48
  307.2 5.2 multiply_convert_fusion.2
  312.6 2.3 collective-permute-start.8
  314.9 4.9 add_bitcast_fusion
  320.1 2.5 maximum_select_fusion.3
  322.6 28.5 %collective-permute-done.8 = bf16[512,512]{1,0:T(8,128)(2,1)} collective-permute-done((bf16[512,512]{1,0:T(8,128)(2,1)S(1)}, bf16[512,512]{1,0:T(8,128)(2,1)}, u32[]{:S(2)}, u32[]{:S(2)}) %collective-permute-start.8) | collective-permute-done | bytes 524320 | tf_op jit(solution)/shard_map/ppermute | solution.py:29
  351.1 2.6 collective-permute-start.9
  353.7 19.8 %while.17 = (s32[]{:T(128)}, f32[1,16,64,128]{3,2,1,0:T(8,128)S(1)}, f32[1,16]{1,0:T(1,128)S(1)}, f32[6,1,16,64,128]{4,3,2,1,0:T(8,128)}, f32[6,1,16]{2,0,1:T(8,...) while((s32[]{:T(128)}, ...), condition=%wide.region_15.16_spmd.clone, body=%wide.region_14.15_spmd.clone.sunk | while | flops 524323 | bytes 2622149 | solution.py:353
  373.5 3.4 collective-permute-start.4
  379.1 2.3 collective-permute-start.5
  381.5 5.3 fusion.53
  386.8 2.9 collective-permute-start.10
  391.2 8.7 %reshape.680 = f32[6,256,1,16,64]{1,0,4,3,2:T(8,128)} reshape(f32[1536,1024]{0,1:T(8,128)} %get-tuple-element.160) | data formatting | bytes 12582912 | tf_op jit(solution)/shard_map/convert_element_type | solution.py:150
  399.9 22.3 %collective-permute-done.5 = f32[1,16]{1,0:T(1,128)S(1)} collective-permute-done((f32[1,16]{1,0:T(1,128)S(1)}, f32[1,16]{1,0:T(1,128)S(1)}, u32[]{:S(2)}, u32[]{:S(2)}) %collective-permute-start.5) | collective-permute-done | bytes 96 | tf_op jit(solution)/shard_map/ppermute | solution.py:15
  423.5 20.2 %collective-permute-done.13 = bf16[512,512]{1,0:T(8,128)(2,1)S(1)} collective-permute-done((bf16[512,512]{1,0:T(8,128)(2,1)}, bf16[512,512]{1,0:T(8,128)(2,1)S(1)}, u32[]{:S(2)}, u32[]{:S(2)}) %collective-permute-start.13) | collective-permute-done | bytes 524320 | tf_op jit(solution)/shard_map/ppermute | solution.py:32
  443.7 2.4 collective-permute-start.14
  446.1 7.4 %fusion.20 = f32[6,256,16,64]{1,3,2,0:T(8,128)} fusion(bf16[6,256,128,1]{2,1,3,0:T(8,128)(2,1)S(1)} %bitcast.240, f32[6,1,16,64,128]{4,3,2,1,0:T(8,128)} %get-tuple-element.50, f32[16,64,128]{2,1,0:T(8,128)S(1)} %add_bitcast_fusion.1, f32[6,16]{1,0:T(8,128)S(1)} %bitcast.259), kind=kOutput, calls=%fused_computation.50 | convolution fusion | flops 2417491968 | bytes 10355072 | tf_op jit(solution)/shard_map/cghpn,cqgn->cqghp/dot_general | solution.py:52
  455.7 24.5 %collective-permute-done.11 = bf16[512,512]{1,0:T(8,128)(2,1)S(1)} collective-permute-done((bf16[512,512]{1,0:T(8,128)(2,1)S(1)}, bf16[512,512]{1,0:T(8,128)(2,1)S(1)}, u32[]{:S(2)}, u32[]{:S(2)}) %collective-permute-start.11) | collective-permute-done | bytes 524320 | tf_op jit(solution)/shard_map/ppermute | solution.py:29
  481.5 10.7 %convolution_convert_fusion.1 = bf16[1536,512]{1,0:T(8,128)(2,1)} fusion(bf16[1536,4096]{1,0:T(8,128)(2,1)} %dynamic-slice_dynamic-update-slice_fusion, bf16[4096,512]{1,0:T(8,128)(2,1)S(1)} %constant_dynamic-update-slice_fusion), kind=kOutput, calls=%fused_computation.62 | convolution fusion | flops 6443237376 | bytes 18350080 | tf_op jit(solution)/shard_map/dot_general | solution.py:271
  492.2 4.3 copy.257
  496.6 11.0 %convolution_convert_fusion.2 = bf16[1536,512]{1,0:T(8,128)(2,1)S(1)} fusion(bf16[1536,4096]{1,0:T(8,128)(2,1)} %copy-done.2, bf16[4096,512]{1,0:T(8,128)(2,1)} %all-gather.6.cloned.1.call-done), kind=kOutput, calls=%fused_computation.63 | convolution fusion | flops 6443237376 | bytes 18350080 | tf_op jit(solution)/shard_map/dot_general | solution.py:270
  508.8 3.5 maximum_convert_fusion
  512.3 10.5 %reshape.705 = f32[6,256,1,16,64]{4,3,1,0,2:T(8,128)} reshape(f32[1536,1,1024]{2,0,1:T(8,128)} %maximum_convert_fusion) | data formatting | bytes 12582912 | tf_op jit(solution)/shard_map/convert_element_type | solution.py:366
  522.8 10.8 %copy.260 = f32[6,256,1,16,64]{1,4,3,0,2:T(8,128)} copy(f32[6,256,1,16,64]{4,3,1,0,2:T(8,128)} %reshape.705) | data formatting | bytes 12582912 | tf_op jit(solution)/shard_map/convert_element_type | solution.py:366
  533.6 16.8 %multiply_reduce_fusion = (f32[6,256]{1,0:T(8,128)S(1)}, f32[6,256,1,16,64]{1,4,3,0,2:T(8,128)S(1)}) fusion(f32[6,256,1,16,64]{1,4,3,0,2:T(8,128)} %copy.260, f32[6,256,16,64]{1,3,2,0:T(8,128)} %fusion.20, f32[6,256,16]{1,2,0:T(8,128)S(1)} %get-tuple-element.151, f32[6,256,1,16,64]{1,0,4,3,2:T(8,128)} %reshape.680, f32[16]{0:T(128)S(1)} %copy-done.40, ...), kind=kOutput, calls=%fused_computation.40 | convolution fusion | flops 863500800 | bytes 36968512 | tf_op jit(solution)/shard_map/cghqs,csghp->cqghp/dot_general | solution.py:51
  550.4 7.8 %copy.254 = f32[6,256,1,16,64]{1,0,4,3,2:T(8,128)} copy(f32[6,256,1,16,64]{1,4,3,0,2:T(8,128)S(1)} %get-tuple-element.205) | data formatting | bytes 12582912 | tf_op jit(solution)/shard_map/add | solution.py:365
  558.2 9.7 %reshape.672 = f32[2,2,384,1024]{2,1,0,3:T(2,128)} reshape(f32[6,256,1,16,64]{1,0,4,3,2:T(8,128)} %copy.254) | data formatting | bytes 12582912 | tf_op jit(solution)/shard_map/reshape | solution.py:365
  567.9 4.9 copy.256
  572.9 23.4 %multiply_convert_fusion.4 = bf16[2,2,384,1024]{2,1,0,3:T(2,128)(2,1)S(1)} fusion(f32[2,2,384,1024]{2,1,0,3:T(2,128)} %reshape.672, f32[1024]{0:T(1024)S(1)} %dynamic-slice-done, bf16[2,2,384,512]{2,1,0,3:T(2,128)(2,1)S(1)} %copy.257, bf16[2,2,384,512]{2,1,0,3:T(2,128)(2,1)} %copy.256, f32[2,2,384]{2,1,0:T(2,128)S(1)} %rsqrt.21), kind=kLoop, calls=%fused_computation.39 | loop fusion | flops 15728640 | bytes 12593152 | tf_op jit(solution)/shard_map/convert_element_type | solution.py:374
  596.2 9.1 %constant_dynamic-slice_fusion.1 = (bf16[2,1,384,1024]{2,1,0,3:T(2,128)(2,1)}, bf16[2,1,384,1024]{2,1,0,3:T(2,128)(2,1)}) fusion(bf16[2,2,384,1024]{2,1,0,3:T(2,128)(2,1)S(1)} %multiply_convert_fusion.4, s32[]{:T(128)S(6)} %select_n.457, s32[]{:T(128)S(6)} %select_n.453), kind=kLoop, calls=%fused_computation.155 | loop fusion | bytes 6291464 | tf_op jit(solution)/shard_map/jit(dynamic_index_in_dim)/dynamic_slice | solution.py:384
  605.4 6.8 copy.261
  612.2 5.1 convolution_convert_fusion.3
  617.3 7.0 copy.262
  624.3 4.0 convolution_convert_fusion.4
  633.6 3.2 convert_add_fusion
  647.1 10.2 %collective-permute-done.23 = bf16[384,1024]{1,0:T(8,128)(2,1)S(1)} collective-permute-done((bf16[384,1024]{1,0:T(8,128)(2,1)S(1)}, bf16[384,1024]{1,0:T(8,128)(2,1)S(1)}, u32[]{:S(2)}, u32[]{:S(2)}) %collective-permute-start.23) | collective-permute-done | bytes 786464 | tf_op jit(solution)/shard_map/ppermute | solution.py:158
  657.6 16.6 %collective-permute-done.21 = bf16[384,1024]{1,0:T(8,128)(2,1)S(1)} collective-permute-done((bf16[384,1024]{1,0:T(8,128)(2,1)S(1)}, bf16[384,1024]{1,0:T(8,128)(2,1)S(1)}, u32[]{:S(2)}, u32[]{:S(2)}) %collective-permute-start.21) | collective-permute-done | bytes 786464 | tf_op jit(solution)/shard_map/ppermute | solution.py:158
  674.5 16.6 %collective-permute-done.19 = bf16[384,1024]{1,0:T(8,128)(2,1)S(1)} collective-permute-done((bf16[384,1024]{1,0:T(8,128)(2,1)S(1)}, bf16[384,1024]{1,0:T(8,128)(2,1)S(1)}, u32[]{:S(2)}, u32[]{:S(2)}) %collective-permute-start.19) | collective-permute-done | bytes 786464 | tf_op jit(solution)/shard_map/ppermute | solution.py:158
  691.3 16.2 %collective-permute-done.17 = bf16[384,1024]{1,0:T(8,128)(2,1)S(1)} collective-permute-done((bf16[384,1024]{1,0:T(8,128)(2,1)S(1)}, bf16[384,1024]{1,0:T(8,128)(2,1)S(1)}, u32[]{:S(2)}, u32[]{:S(2)}) %collective-permute-start.17) | collective-permute-done | bytes 786464 | tf_op jit(solution)/shard_map/ppermute | solution.py:158
  (300 shorter events, 104.3 us)
Async XLA Ops:
  6.5 130.6 %copy-start = (f32[32,64,128]{2,1,0:T(8,128)S(1)}, f32[32,64,128]{2,1,0:T(8,128)}, u32[]{:S(2)}) copy-start(f32[32,64,128]{2,1,0:T(8,128)} %param.37) | copy-start | bytes 3145732
  6.5 199.6 %all-gather.4.cloned.1.call-start = ((), (), s32[]{:S(2)}) async-start(), calls=%async_computation | async-start | bytes 12976128 | tf_op jit(solution)/shard_map/all_gather | solution.py:242
  6.5 6.5 copy-start.22
  6.5 6.7 copy-start.11
  20.4 16.8 %collective-permute-start.2 = (bf16[256,1296]{0,1:T(8,128)(2,1)S(1)}, bf16[256,1296]{0,1:T(8,128)(2,1)}, u32[]{:S(2)}, u32[]{:S(2)}) collective-permute-start(bf16[256,1296]{0,1:T(8,128)(2,1)S(1)} %copy.233), channel_id=1, source_target_pairs={{0,2},{2,0},{1,3},{3,1},{4,6},{6,4},{5,7},{7,5},{8,10},{10,8},{9,1... | collective-permute-start | bytes 1990664 | tf_op jit(solution)/shard_map/ppermute | solution.py:158
  44.0 452.6 %all-gather.6.cloned.1.call-start = ((), (), s32[]{:S(2)}) async-start(), calls=%async_computation.1 | async-start | bytes 4718592 | tf_op jit(solution)/shard_map/all_gather | solution.py:264
  56.7 9.6 %copy-start.14 = (s32[8]{0:T(128)S(1)}, s32[8]{0:T(128)}, u32[]{:S(2)}) copy-start(s32[8]{0:T(128)} %constant.286.clone) | copy-start | bytes 100
  56.7 16.1 %copy-start.35 = (s32[8]{0:T(128)S(1)}, s32[8]{0:T(128)}, u32[]{:S(2)}) copy-start(s32[8]{0:T(128)} %param.34) | copy-start | bytes 100
  56.7 16.1 %copy-start.36 = (s32[8]{0:T(128)S(1)}, s32[8]{0:T(128)}, u32[]{:S(2)}) copy-start(s32[8]{0:T(128)} %param.35) | copy-start | bytes 100
  56.7 20.9 %copy-start.23 = (bf16[4,2,256]{2,1,0:T(2,128)(2,1)S(1)}, bf16[4,2,256]{2,1,0:T(2,128)(2,1)}, u32[]{:S(2)}) copy-start(bf16[4,2,256]{2,1,0:T(2,128)(2,1)} %param.28) | copy-start | bytes 12292
  56.7 21.0 %copy-start.25 = (bf16[3,2,256]{2,1,0:T(2,128)(2,1)S(1)}, bf16[3,2,256]{2,1,0:T(2,128)(2,1)}, u32[]{:S(2)}) copy-start(bf16[3,2,256]{2,1,0:T(2,128)(2,1)} %param.39) | copy-start | bytes 9220
  56.7 23.4 %copy-start.37 = (f32[32]{0:T(128)S(1)}, f32[32]{0:T(128)}, u32[]{:S(2)}) copy-start(f32[32]{0:T(128)} %param.29) | copy-start | bytes 388
  56.7 23.5 %copy-start.38 = (f32[32]{0:T(128)S(1)}, f32[32]{0:T(128)}, u32[]{:S(2)}) copy-start(f32[32]{0:T(128)} %param.30) | copy-start | bytes 388
  56.8 23.6 %copy-start.39 = (f32[32]{0:T(128)S(1)}, f32[32]{0:T(128)}, u32[]{:S(2)}) copy-start(f32[32]{0:T(128)} %param.31) | copy-start | bytes 388
  56.8 78.9 %copy-start.31 = (bf16[4,2048]{1,0:T(4,128)(2,1)S(1)}, bf16[4,2048]{1,0:T(4,128)(2,1)}, u32[]{:S(2)}) copy-start(bf16[4,2048]{1,0:T(4,128)(2,1)} %param.27) | copy-start | bytes 49156
  56.8 78.9 %copy-start.32 = (bf16[3,2048]{1,0:T(4,128)(2,1)S(1)}, bf16[3,2048]{1,0:T(4,128)(2,1)}, u32[]{:S(2)}) copy-start(bf16[3,2048]{1,0:T(4,128)(2,1)} %param.38) | copy-start | bytes 36868
  58.7 69.4 %collective-permute-start = (bf16[384,4096]{1,0:T(8,128)(2,1)}, bf16[384,4096]{1,0:T(8,128)(2,1)}, u32[]{:S(2)}, u32[]{:S(2)}) collective-permute-start(bf16[384,4096]{1,0:T(8,128)(2,1)} %constant_dynamic-slice_fusion.22), channel_id=1, source_target_pairs={{0,2},{2,0},{1,3},{3,1},{4,6},{6,4},{5,7},{7,5},{8,10},{10,8},{9,1... | collective-permute-start | bytes 9437192 | tf_op jit(solution)/shard_map/ppermute | solution.py:158
  128.1 12.8 %collective-permute-start.1 = (bf16[384,4096]{1,0:T(8,128)(2,1)}, bf16[384,4096]{1,0:T(8,128)(2,1)S(1)}, u32[]{:S(2)}, u32[]{:S(2)}) collective-permute-start(bf16[384,4096]{1,0:T(8,128)(2,1)} %collective-permute-done), channel_id=1, source_target_pairs={{0,1},{1,0},{2,3},{3,2},{4,5},{5,4},{6,7},{7,6},{8,9},{9,8},{10,11... | collective-permute-start | bytes 9437192 | tf_op jit(solution)/shard_map/ppermute | solution.py:217
  139.1 113.9 %copy-start.20 = (pred[6,256]{1,0:T(8,128)(4,1)}, pred[6,256]{1,0:T(8,128)(4,1)S(1)}, u32[]{:S(2)}) copy-start(pred[6,256]{1,0:T(8,128)(4,1)S(1)} %get-tuple-element.186) | copy-start | bytes 4612
  154.0 7.5 %slice-start = ((s8[6291456]{0:T(1024)(128)(4,1)}), s8[2097152]{0:T(1024)(128)(4,1)S(1)}, s32[]{:S(2)}) async-start(s8[6291456]{0:T(1024)(128)(4,1)} %bitcast.236), calls=%async_computation.3 | async-start | bytes 4194304
  170.8 11.4 %copy-start.2 = (bf16[1536,4096]{1,0:T(8,128)(2,1)}, bf16[1536,4096]{1,0:T(8,128)(2,1)S(1)}, u32[]{:S(2)}) copy-start(bf16[1536,4096]{1,0:T(8,128)(2,1)S(1)} %maximum_select_fusion) | copy-start | bytes 37748740
  244.1 75.9 %collective-permute-start.15 = (bf16[1024,256]{1,0:T(8,128)(2,1)}, bf16[1024,256]{1,0:T(8,128)(2,1)}, u32[]{:S(2)}, u32[]{:S(2)}) collective-permute-start(bf16[1024,256]{1,0:T(8,128)(2,1)} %get-tuple-element.175), channel_id=1, source_target_pairs={{0,2},{2,0},{1,3},{3,1},{4,6},{6,4},{5,7},{7,5},{8,10},{10,8},{9,1... | collective-permute-start | bytes 1572872 | tf_op jit(solution)/shard_map/ppermute | solution.py:158
  245.5 26.2 %copy-start.15 = (f32[1280]{0:T(1024)S(1)}, f32[1280]{0:T(1024)}, u32[]{:S(2)}) copy-start(f32[1280]{0:T(1024)} %get-tuple-element.130) | copy-start | bytes 15364
  245.5 26.2 %copy-start.16 = (f32[1280]{0:T(1024)S(1)}, f32[1280]{0:T(1024)}, u32[]{:S(2)}) copy-start(f32[1280]{0:T(1024)} %get-tuple-element.131) | copy-start | bytes 15364
  245.5 26.2 %copy-start.17 = (f32[1280]{0:T(1024)S(1)}, f32[1280]{0:T(1024)}, u32[]{:S(2)}) copy-start(f32[1280]{0:T(1024)} %get-tuple-element.132) | copy-start | bytes 15364
  245.5 26.2 %copy-start.18 = (f32[1280]{0:T(1024)S(1)}, f32[1280]{0:T(1024)}, u32[]{:S(2)}) copy-start(f32[1280]{0:T(1024)} %get-tuple-element.133) | copy-start | bytes 15364
  245.5 26.2 %copy-start.19 = (f32[1280]{0:T(1024)S(1)}, f32[1280]{0:T(1024)}, u32[]{:S(2)}) copy-start(f32[1280]{0:T(1024)} %get-tuple-element.134) | copy-start | bytes 15364
  245.5 26.2 %copy-start.26 = (pred[1536]{0:T(1024)(128)(4,1)S(1)}, pred[1536]{0:T(1024)(128)(4,1)}, u32[]{:S(2)}) copy-start(pred[1536]{0:T(1024)(128)(4,1)} %get-tuple-element.188) | copy-start | bytes 4612
  245.5 26.2 %copy-start.27 = (pred[1536]{0:T(1024)(128)(4,1)S(1)}, pred[1536]{0:T(1024)(128)(4,1)}, u32[]{:S(2)}) copy-start(pred[1536]{0:T(1024)(128)(4,1)} %get-tuple-element.189) | copy-start | bytes 4612
  245.5 26.2 %copy-start.28 = (pred[1536]{0:T(1024)(128)(4,1)S(1)}, pred[1536]{0:T(1024)(128)(4,1)}, u32[]{:S(2)}) copy-start(pred[1536]{0:T(1024)(128)(4,1)} %get-tuple-element.190) | copy-start | bytes 4612
  245.5 26.2 %copy-start.29 = (pred[1536]{0:T(1024)(128)(4,1)S(1)}, pred[1536]{0:T(1024)(128)(4,1)}, u32[]{:S(2)}) copy-start(pred[1536]{0:T(1024)(128)(4,1)} %get-tuple-element.191) | copy-start | bytes 4612
  245.5 23.3 %collective-permute-start.7 = (bf16[256,1024]{1,0:T(8,128)(2,1)S(1)}, bf16[256,1024]{1,0:T(8,128)(2,1)S(1)}, u32[]{:S(2)}, u32[]{:S(2)}) collective-permute-start(bf16[256,1024]{1,0:T(8,128)(2,1)S(1)} %get-tuple-element.173), channel_id=1, source_target_pairs={{0,2},{2,0},{1,3},{3,1},{4,6},{6,4},{5,7},{7,5},{8,10},{10,8},{9,1... | collective-permute-start | bytes 1572872 | tf_op jit(solution)/shard_map/ppermute | solution.py:158
  247.2 24.5 %collective-permute-start.3 = (bf16[3,1280]{0,1:T(8,128)(2,1)}, bf16[3,1280]{0,1:T(8,128)(2,1)S(1)}, u32[]{:S(2)}, u32[]{:S(2)}) collective-permute-start(bf16[3,1280]{0,1:T(8,128)(2,1)} %slice.173), channel_id=1, source_target_pairs={{0,4},{4,8},{8,12},{12,16},{16,20},{20,24},{24,28},{1,5},{5,9},{9,... | collective-permute-start | bytes 23048 | tf_op jit(solution)/shard_map/ppermute | solution.py:15
  271.6 340.6 %all-gather.8.cloned.1.call-start = ((), (), s32[]{:S(2)}) async-start(), calls=%async_computation.2 | async-start | bytes 9437184 | tf_op jit(solution)/shard_map/all_gather | solution.py:262
  293.5 5.0 copy-start.4
  307.2 7.7 %copy-start.33 = (f32[6,16]{1,0:T(8,128)S(1)}, f32[6,16]{1,0:T(8,128)}, u32[]{:S(2)}) copy-start(f32[6,16]{1,0:T(8,128)} %slice_reduce_fusion.1) | copy-start | bytes 1156
  312.6 38.5 %collective-permute-start.8 = (bf16[512,512]{1,0:T(8,128)(2,1)S(1)}, bf16[512,512]{1,0:T(8,128)(2,1)}, u32[]{:S(2)}, u32[]{:S(2)}) collective-permute-start(bf16[512,512]{1,0:T(8,128)(2,1)S(1)} %get-tuple-element.171), channel_id=1, source_target_pairs={{0,8},{8,16},{16,24},{24,28},{28,20},{20,12},{12,4},{4,0},{1,9},{9... | collective-permute-start | bytes 1572872 | tf_op jit(solution)/shard_map/ppermute | solution.py:29
  314.9 5.2 copy-start.8
  314.9 38.8 %copy-start.24 = (f32[1,16]{1,0:T(1,128)S(1)}, f32[1,16]{1,0:T(1,128)}, u32[]{:S(2)}) copy-start(f32[1,16]{1,0:T(1,128)} %custom-call.1) | copy-start | bytes 196
  314.9 38.8 %copy-start.30 = (f32[6,1,16]{2,0,1:T(8,128)S(1)}, f32[6,1,16]{2,0,1:T(8,128)}, u32[]{:S(2)}) copy-start(f32[6,1,16]{2,0,1:T(8,128)} %custom-call.9) | copy-start | bytes 1156
  319.8 66.9 %collective-permute-start.12 = (bf16[512,512]{1,0:T(8,128)(2,1)S(1)}, bf16[512,512]{1,0:T(8,128)(2,1)}, u32[]{:S(2)}, u32[]{:S(2)}) collective-permute-start(bf16[512,512]{1,0:T(8,128)(2,1)S(1)} %get-tuple-element.171), channel_id=1, source_target_pairs={{0,4},{8,0},{16,8},{24,16},{28,24},{20,28},{12,20},{4,12},{1,5},{9... | collective-permute-start | bytes 1572872 | tf_op jit(solution)/shard_map/ppermute | solution.py:32
  351.1 35.7 %collective-permute-start.9 = (bf16[512,512]{1,0:T(8,128)(2,1)}, bf16[512,512]{1,0:T(8,128)(2,1)}, u32[]{:S(2)}, u32[]{:S(2)}) collective-permute-start(bf16[512,512]{1,0:T(8,128)(2,1)} %collective-permute-done.8), channel_id=1, source_target_pairs={{0,8},{8,16},{16,24},{24,28},{28,20},{20,12},{12,4},{4,0},{1,9},{9... | collective-permute-start | bytes 1572872 | tf_op jit(solution)/shard_map/ppermute | solution.py:29
  373.5 48.7 %collective-permute-start.4 = (f32[1,16,64,128]{3,2,1,0:T(8,128)S(1)}, f32[1,16,64,128]{3,2,1,0:T(8,128)}, u32[]{:S(2)}, u32[]{:S(2)}) collective-permute-start(f32[1,16,64,128]{3,2,1,0:T(8,128)S(1)} %get-tuple-element.48), channel_id=1, source_target_pairs={{0,4},{4,8},{8,12},{12,16},{16,20},{20,24},{24,28},{1,5},{5,9},{9,... | collective-permute-start | bytes 1572872 | tf_op jit(solution)/shard_map/ppermute | solution.py:15
  377.0 45.2 %collective-permute-start.6 = (f32[1,16,64,128]{3,2,1,0:T(8,128)S(1)}, f32[1,16,64,128]{3,2,1,0:T(8,128)}, u32[]{:S(2)}, u32[]{:S(2)}) collective-permute-start(f32[1,16,64,128]{3,2,1,0:T(8,128)S(1)} %get-tuple-element.48), channel_id=1, source_target_pairs={{0,8},{4,12},{8,16},{12,20},{16,24},{20,28},{1,9},{5,13},{9,17},{1... | collective-permute-start | bytes 1572872 | tf_op jit(solution)/shard_map/ppermute | solution.py:15
  379.1 43.0 %collective-permute-start.5 = (f32[1,16]{1,0:T(1,128)S(1)}, f32[1,16]{1,0:T(1,128)S(1)}, u32[]{:S(2)}, u32[]{:S(2)}) collective-permute-start(f32[1,16]{1,0:T(1,128)S(1)} %get-tuple-element.49), channel_id=1, source_target_pairs={{0,4},{4,8},{8,12},{12,16},{16,20},{20,24},{24,28},{1,5},{5,9},{9,... | collective-permute-start | bytes 200 | tf_op jit(solution)/shard_map/ppermute | solution.py:15
  386.8 56.9 %collective-permute-start.13 = (bf16[512,512]{1,0:T(8,128)(2,1)}, bf16[512,512]{1,0:T(8,128)(2,1)S(1)}, u32[]{:S(2)}, u32[]{:S(2)}) collective-permute-start(bf16[512,512]{1,0:T(8,128)(2,1)} %collective-permute-done.12), channel_id=1, source_target_pairs={{0,4},{8,0},{16,8},{24,16},{28,24},{20,28},{12,20},{4,12},{1,5},{9... | collective-permute-start | bytes 1572872 | tf_op jit(solution)/shard_map/ppermute | solution.py:32
  386.8 59.3 %collective-permute-start.10 = (bf16[512,512]{1,0:T(8,128)(2,1)}, bf16[512,512]{1,0:T(8,128)(2,1)S(1)}, u32[]{:S(2)}, u32[]{:S(2)}) collective-permute-start(bf16[512,512]{1,0:T(8,128)(2,1)} %collective-permute-done.9), channel_id=1, source_target_pairs={{0,8},{8,16},{16,24},{24,28},{28,20},{20,12},{12,4},{4,0},{1,9},{9... | collective-permute-start | bytes 1572872 | tf_op jit(solution)/shard_map/ppermute | solution.py:29
  443.7 36.6 %collective-permute-start.14 = (bf16[512,512]{1,0:T(8,128)(2,1)S(1)}, bf16[512,512]{1,0:T(8,128)(2,1)S(1)}, u32[]{:S(2)}, u32[]{:S(2)}) collective-permute-start(bf16[512,512]{1,0:T(8,128)(2,1)S(1)} %collective-permute-done.13), channel_id=1, source_target_pairs={{0,4},{8,0},{16,8},{24,16},{28,24},{20,28},{12,20},{4,12},{1,5},{9... | collective-permute-start | bytes 1572872 | tf_op jit(solution)/shard_map/ppermute | solution.py:32
  446.1 34.2 %collective-permute-start.11 = (bf16[512,512]{1,0:T(8,128)(2,1)S(1)}, bf16[512,512]{1,0:T(8,128)(2,1)S(1)}, u32[]{:S(2)}, u32[]{:S(2)}) collective-permute-start(bf16[512,512]{1,0:T(8,128)(2,1)S(1)} %collective-permute-done.10), channel_id=1, source_target_pairs={{0,8},{8,16},{16,24},{24,28},{28,20},{20,12},{12,4},{4,0},{1,9},{9... | collective-permute-start | bytes 1572872 | tf_op jit(solution)/shard_map/ppermute | solution.py:29
  446.1 7.4 %copy-start.13 = (bf16[4096,512]{1,0:T(8,128)(2,1)S(1)}, bf16[4096,512]{1,0:T(8,128)(2,1)}, u32[]{:S(2)}) copy-start(bf16[4096,512]{1,0:T(8,128)(2,1)} %get-tuple-element.170) | copy-start | bytes 12582916
  496.5 12.2 %copy-start.6 = (bf16[1536,512]{1,0:T(8,128)(2,1)S(1)}, bf16[1536,512]{1,0:T(8,128)(2,1)}, u32[]{:S(2)}) copy-start(bf16[1536,512]{1,0:T(8,128)(2,1)} %convolution_convert_fusion.1) | copy-start | bytes 4718596
  522.8 10.8 %copy-start.12 = (pred[6,256,256]{2,1,0:T(8,128)(4,1)S(1)}, pred[6,256,256]{2,1,0:T(8,128)(4,1)}, u32[]{:S(2)}) copy-start(pred[6,256,256]{2,1,0:T(8,128)(4,1)} %compare_and_fusion) | copy-start | bytes 1179652
  522.8 10.8 %copy-start.40 = (f32[16]{0:T(128)S(1)}, f32[16]{0:T(128)}, u32[]{:S(2)}) copy-start(f32[16]{0:T(128)} %dynamic_slice.217) | copy-start | bytes 196
  558.2 14.7 %dynamic-slice-start = ((f32[2048]{0:T(1024)}, s32[]{:T(128)}), f32[1024]{0:T(1024)S(1)}, s32[]{:S(2)}) async-start(f32[2048]{0:T(1024)} %param.32, s32[]{:T(128)} %select_n.384), calls=%async_computation.5 | async-start | bytes 8704 | tf_op jit(solution)/shard_map/dynamic_slice | solution.py:211
  612.2 5.1 copy-start.9
  617.3 16.3 %collective-permute-start.22 = (bf16[2,384,1024]{2,1,0:T(8,128)(2,1)}, bf16[2,384,1024]{2,1,0:T(8,128)(2,1)}, u32[]{:S(2)}, u32[]{:S(2)}) collective-permute-start(bf16[2,384,1024]{2,1,0:T(8,128)(2,1)} %convolution_convert_fusion.3), channel_id=1, source_target_pairs={{0,1},{1,0},{2,3},{3,2},{4,5},{5,4},{6,7},{7,6},{8,9},{9,8},{10,11... | collective-permute-start | bytes 4718600 | tf_op jit(solution)/shard_map/ppermute | solution.py:387
  628.3 8.7 %collective-permute-start.20 = (bf16[2,384,1024]{2,1,0:T(8,128)(2,1)S(1)}, bf16[2,384,1024]{2,1,0:T(8,128)(2,1)S(1)}, u32[]{:S(2)}, u32[]{:S(2)}) collective-permute-start(bf16[2,384,1024]{2,1,0:T(8,128)(2,1)S(1)} %convolution_convert_fusion.4), channel_id=1, source_target_pairs={{0,1},{1,0},{2,3},{3,2},{4,5},{5,4},{6,7},{7,6},{8,9},{9,8},{10,11... | collective-permute-start | bytes 4718600 | tf_op jit(solution)/shard_map/ppermute | solution.py:387
  631.1 10.0 %collective-permute-start.18 = (bf16[2,384,1024]{2,1,0:T(8,128)(2,1)S(1)}, bf16[2,384,1024]{2,1,0:T(8,128)(2,1)S(1)}, u32[]{:S(2)}, u32[]{:S(2)}) collective-permute-start(bf16[2,384,1024]{2,1,0:T(8,128)(2,1)S(1)} %convolution_convert_fusion.5), channel_id=1, source_target_pairs={{0,1},{1,0},{2,3},{3,2},{4,5},{5,4},{6,7},{7,6},{8,9},{9,8},{10,11... | collective-permute-start | bytes 4718600 | tf_op jit(solution)/shard_map/ppermute | solution.py:387
  633.5 9.6 %collective-permute-start.16 = (bf16[2,384,1024]{2,1,0:T(8,128)(2,1)S(1)}, bf16[2,384,1024]{2,1,0:T(8,128)(2,1)S(1)}, u32[]{:S(2)}, u32[]{:S(2)}) collective-permute-start(bf16[2,384,1024]{2,1,0:T(8,128)(2,1)S(1)} %convolution_convert_fusion.6), channel_id=1, source_target_pairs={{0,1},{1,0},{2,3},{3,2},{4,5},{5,4},{6,7},{7,6},{8,9},{9,8},{10,11... | collective-permute-start | bytes 4718600 | tf_op jit(solution)/shard_map/ppermute | solution.py:387
  636.9 20.4 %collective-permute-start.23 = (bf16[384,1024]{1,0:T(8,128)(2,1)S(1)}, bf16[384,1024]{1,0:T(8,128)(2,1)S(1)}, u32[]{:S(2)}, u32[]{:S(2)}) collective-permute-start(bf16[384,1024]{1,0:T(8,128)(2,1)S(1)} %fusion.52), channel_id=1, source_target_pairs={{0,2},{2,0},{1,3},{3,1},{4,6},{6,4},{5,7},{7,5},{8,10},{10,8},{9,1... | collective-permute-start | bytes 2359304 | tf_op jit(solution)/shard_map/ppermute | solution.py:158
  639.0 35.2 %collective-permute-start.21 = (bf16[384,1024]{1,0:T(8,128)(2,1)S(1)}, bf16[384,1024]{1,0:T(8,128)(2,1)S(1)}, u32[]{:S(2)}, u32[]{:S(2)}) collective-permute-start(bf16[384,1024]{1,0:T(8,128)(2,1)S(1)} %fusion.51), channel_id=1, source_target_pairs={{0,2},{2,0},{1,3},{3,1},{4,6},{6,4},{5,7},{7,5},{8,10},{10,8},{9,1... | collective-permute-start | bytes 2359304 | tf_op jit(solution)/shard_map/ppermute | solution.py:158
  643.0 48.0 %collective-permute-start.19 = (bf16[384,1024]{1,0:T(8,128)(2,1)S(1)}, bf16[384,1024]{1,0:T(8,128)(2,1)S(1)}, u32[]{:S(2)}, u32[]{:S(2)}) collective-permute-start(bf16[384,1024]{1,0:T(8,128)(2,1)S(1)} %fusion.50), channel_id=1, source_target_pairs={{0,2},{2,0},{1,3},{3,1},{4,6},{6,4},{5,7},{7,5},{8,10},{10,8},{9,1... | collective-permute-start | bytes 2359304 | tf_op jit(solution)/shard_map/ppermute | solution.py:158
  645.1 62.4 %collective-permute-start.17 = (bf16[384,1024]{1,0:T(8,128)(2,1)S(1)}, bf16[384,1024]{1,0:T(8,128)(2,1)S(1)}, u32[]{:S(2)}, u32[]{:S(2)}) collective-permute-start(bf16[384,1024]{1,0:T(8,128)(2,1)S(1)} %fusion.49), channel_id=1, source_target_pairs={{0,2},{2,0},{1,3},{3,1},{4,6},{6,4},{5,7},{7,5},{8,10},{10,8},{9,1... | collective-permute-start | bytes 2359304 | tf_op jit(solution)/shard_map/ppermute | solution.py:158
  691.0 18.6 %copy-start.1 = (f32[32,64,128]{2,1,0:T(8,128)S(1)}, f32[32,64,128]{2,1,0:T(8,128)}, u32[]{:S(2)}) copy-start(f32[32,64,128]{2,1,0:T(8,128)} %param.37) | copy-start | bytes 3145732
  (8 other events, 27.5 us)
Sparse Core Ops, SparseCore 0:
  44.1 161.9 all-gather.3
  271.8 92.2 all-gather.5
  366.1 163.1 all-gather.7

commit v11 on v9

--- a/solution.py
+++ b/solution.py
@@ -228,8 +228,11 @@
         half,
         1,
     )
-    z_full = lax.all_gather(z_local, "pair", axis=0, tiled=True)
-    out_full = lax.all_gather(out_local, "pair", axis=1, tiled=True)
+    late_full = lax.all_gather(
+        jnp.concatenate([z_local, out_local.T], axis=1), "pair", axis=0, tiled=True
+    )
+    z_full = late_full[:, :inner_local]
+    out_rows = late_full[:, inner_local:]
     proj_z = jnp.dot(normed, z_full, preferred_element_type=jnp.float32).astype(jnp.bfloat16)
 
     position = lax.axis_index("pair") * row_count + jnp.arange(row_count, dtype=jnp.int32)
@@ -330,14 +333,14 @@
     piece = own_rows // core_count
     by_owner = normed_y.reshape(2, core_count, piece, inner_local)
     chunk_count = 4
-    chunk = out_full.shape[1] // chunk_count
+    chunk = out_rows.shape[0] // chunk_count
     results = []
     for index in range(chunk_count):
-        columns = out_full[:, index * chunk : (index + 1) * chunk]
+        columns = out_rows[index * chunk : (index + 1) * chunk]
         total = None
         for shift in list(range(1, core_count)) + [0]:
             rows = lax.dynamic_index_in_dim(by_owner, (core + shift) % core_count, 1, keepdims=False)
-            part = jnp.einsum("hrc,cd->hrd", rows, columns, preferred_element_type=jnp.float32)
+            part = jnp.einsum("hrc,dc->hrd", rows, columns, preferred_element_type=jnp.float32)
             if shift:
                 part = lax.ppermute(
                     part.astype(jnp.bfloat16),

time: 638 us -> 653 us (1.024)
  the two profiles are of different devices: /device:TPU:0 before, /device:TPU:28 now
where the time goes in v11:
time: 653 us; the launch traced here: 645 us
  waiting for transfers between devices  314 us (48%)
  matrix products  114 us (17%)
  other arithmetic  100 us (15%)
  local copies, waits for them, and re-layouts  84 us (13%)
  starting transfers between devices  16 us (2%)
  between operations  15.3 us (2%)
    ppermute x8, waiting for transfers between devices, swap_half(): lax.ppermute(value, 'half', [(k, count - 1 - k) for k in range(count)])  156 us
    ppermute x4, waiting for transfers between devices, from_behind(): lax.ppermute(value, axis, [(source, source + steps) for source in range(l...  63.2 us
    all_gather x1, waiting for transfers between devices, body(): first_full = lax.all_gather(first_local, 'pair', axis=0, tiled=True)  52.6 us
    all_gather x1, waiting for transfers between devices, body(): lax.all_gather(jnp.concatenate([z_local, out_local.T], axis=1), 'pair', a...  38.5 us
    dot_general x8, matrix products, body(): jnp.einsum('hrc,dc->hrd', rows, columns, preferred_element_type=jnp.float32)  32.5 us
    dot_general x1, matrix products, body(): jnp.dot(normed, z_full, preferred_element_type=jnp.float32)  26.2 us
    dot_general x1, matrix products, body(): jnp.dot(normed, first_full, preferred_element_type=jnp.float32)  24 us
    reshape x2, local copies, waits for them, and re-layouts, body(): (direct + state_gain[..., None] * from_state).reshape(row_count, inner_lo...  22.9 us
  transfers between devices with their start and end apart: 19, of which 14 were waited for; matrix products, arithmetic and copies ran while one was open for 32% of the time, Pallas kernels for 0%

profile of v11, /device:TPU:28, one launch (start us, length us, event | category | flops | bytes accessed | tf_op | source)
XLA Modules:
  0.0 644.5 jit_solution(2867044717189112055)
XLA Ops:
  6.5 2.3 fusion.126
  8.9 2.2 constant_dynamic-slice_fusion.17
  12.0 4.2 fusion.125
  16.1 3.7 constant_dynamic-slice_fusion.19
  20.3 1.6 collective-permute-start.2
  24.0 13.1 %collective-permute-done.2 = bf16[256,1296]{0,1:T(8,128)(2,1)} collective-permute-done((bf16[256,1296]{0,1:T(8,128)(2,1)S(1)}, bf16[256,1296]{0,1:T(8,128)(2,1)}, u32[]{:S(2)}, u32[]{:S(2)}) %collective-permute-start.2) | collective-permute-done | bytes 663584 | tf_op jit(solution)/shard_map/ppermute | solution.py:127
  38.6 5.4 maximum_select_fusion.3
  44.2 4.1 fusion.3
  48.3 5.3 fusion.5
  53.6 2.8 copy-done.4
  56.8 1.6 collective-permute-start
  58.3 67.6 %collective-permute-done = bf16[384,4096]{1,0:T(8,128)(2,1)} collective-permute-done((bf16[384,4096]{1,0:T(8,128)(2,1)S(1)}, bf16[384,4096]{1,0:T(8,128)(2,1)}, u32[]{:S(2)}, u32[]{:S(2)}) %collective-permute-start) | collective-permute-done | bytes 3145760 | tf_op jit(solution)/shard_map/ppermute | solution.py:127
  126.1 1.6 copy.297
  127.7 4.3 collective-permute-done.1
  132.0 5.2 fusion.27
  137.2 4.4 gather_fusion
  141.5 4.3 gather_fusion.1
  145.8 3.6 pad_maximum_fusion
  149.5 3.7 bitcast_select_fusion
  153.2 52.6 %all-gather.3.cloned.1.call-done = bf16[4096,1296]{1,0:T(8,128)(2,1)} async-done(((bf16[512,1296]{1,0:T(8,128)(2,1)}), bf16[4096,1296]{1,0:T(8,128)(2,1)}) %all-gather.3.cloned.1.call-update) | async-done | bytes 10616848 | tf_op jit(solution)/shard_map/all_gather | solution.py:211
  205.8 24.0 %convolution_convert_fusion = bf16[1536,1296]{0,1:T(8,128)(2,1)} fusion(bf16[4096,1296]{1,0:T(8,128)(2,1)} %all-gather.3.cloned.1.call-done, bf16[768,4096]{1,0:T(8,128)(2,1)} %bitcast_select_fusion, bf16[768,4096]{1,0:T(8,128)(2,1)} %copy-done.4, pred[]{:T(512)S(6)} %eq.208), kind=kOutput, calls=%fused_computation.29 | convolution fusion | flops 16366067712 | bytes 27181056 | tf_op jit(solution)/shard_map/dot_general | solution.py:212
  230.6 1.5 collective-permute-start.7
  232.2 1.5 copy.237
  234.3 11.3 %collective-permute-done.7 = bf16[256,1024]{1,0:T(8,128)(2,1)S(1)} collective-permute-done((bf16[256,1024]{1,0:T(8,128)(2,1)}, bf16[256,1024]{1,0:T(8,128)(2,1)S(1)}, u32[]{:S(2)}, u32[]{:S(2)}) %collective-permute-start.7) | collective-permute-done | bytes 524320 | tf_op jit(solution)/shard_map/ppermute | solution.py:127
  246.1 9.9 %collective-permute-done.8 = bf16[1024,256]{0,1:T(8,128)(2,1)S(1)} collective-permute-done((bf16[1024,256]{0,1:T(8,128)(2,1)S(1)}, bf16[1024,256]{0,1:T(8,128)(2,1)S(1)}, u32[]{:S(2)}, u32[]{:S(2)}) %collective-permute-start.8) | collective-permute-done | bytes 524320 | tf_op jit(solution)/shard_map/ppermute | solution.py:127
  256.5 1.6 pad_maximum_fusion.4
  261.6 1.8 reduce-window.30
  274.8 3.8 reduce-window.21
  281.4 4.3 slice.169
  287.2 4.0 collective-permute-done.3
  291.2 21.6 %multiply_convert_fusion.3 = bf16[1536,1280]{0,1:T(8,128)(2,1)S(1)} fusion(bf16[1536,1280]{0,1:T(8,128)(2,1)} %slice.169, bf16[3,1280]{0,1:T(8,128)(2,1)S(1)} %collective-permute-done.3, f32[1280]{0:T(1024)S(1)} %get-tuple-element.132, f32[1280]{0:T(1024)S(1)} %get-tuple-element.133, f32[1280]{0:T(1024)S(1)} %get-tuple-element.134, ...), kind=kLoop, calls=%fused_computation.28 | loop fusion | flops 104202240 | bytes 7933952 | tf_op jit(solution)/shard_map/convert_element_type | solution.py:68
  312.8 1.9 copy-done.3
  315.0 6.6 %fusion.123 = (bf16[1536,1024]{0,1:T(8,128)(2,1)}, f32[1536,1024]{0,1:T(8,128)}) fusion(bf16[1536,1280]{0,1:T(8,128)(2,1)} %copy-done.3), kind=kLoop, calls=%fused_computation.260 | loop fusion | flops 1572864 | bytes 12582912 | tf_op jit(solution)/shard_map/slice | solution.py:270
  321.6 7.5 %reshape.580 = bf16[6,256,16,64]{1,0,3,2:T(8,128)(2,1)} reshape(bf16[1536,1024]{0,1:T(8,128)(2,1)} %get-tuple-element.159) | data formatting | bytes 6291456 | tf_op jit(solution)/shard_map/reshape.48
  329.1 3.2 multiply_convert_fusion.2
  332.3 2.7 add_bitcast_fusion
  335.0 12.5 %while.17 = (s32[]{:T(128)}, f32[1,16,64,128]{3,2,1,0:T(8,128)S(1)}, f32[1,16]{1,0:T(1,128)S(1)}, f32[6,1,16,64,128]{4,3,2,1,0:T(8,128)}, f32[6,1,16]{2,0,1:T(8,...) while((s32[]{:T(128)}, ...), condition=%wide.region_15.16_spmd.clone, body=%wide.region_14.15_spmd.clone.sunk | while | flops 524323 | bytes 2622649 | solution.py:311
  351.6 1.5 fusion.129
  353.1 5.3 fusion.70
  358.3 8.9 %reshape.602 = f32[6,256,1,16,64]{1,0,4,3,2:T(8,128)} reshape(f32[1536,1024]{0,1:T(8,128)} %get-tuple-element.160) | data formatting | bytes 12582912 | tf_op jit(solution)/shard_map/convert_element_type | solution.py:119
  367.3 14.5 %collective-permute-done.5 = f32[1,16]{1,0:T(1,128)S(1)} collective-permute-done((f32[1,16]{1,0:T(1,128)S(1)}, f32[1,16]{1,0:T(1,128)S(1)}, u32[]{:S(2)}, u32[]{:S(2)}) %collective-permute-start.5) | collective-permute-done | bytes 96 | tf_op jit(solution)/shard_map/ppermute | solution.py:15
  381.8 44.7 %collective-permute-done.6 = f32[1,16,64,128]{3,2,1,0:T(8,128)} collective-permute-done((f32[1,16,64,128]{3,2,1,0:T(8,128)S(1)}, f32[1,16,64,128]{3,2,1,0:T(8,128)}, u32[]{:S(2)}, u32[]{:S(2)}) %collective-permute-start.6) | collective-permute-done | bytes 524320 | tf_op jit(solution)/shard_map/ppermute | solution.py:15
  428.0 5.3 fusion.28
  433.4 16.8 %fusion.19 = f32[6,256,1,16,64]{1,4,3,0,2:T(8,128)} fusion(f32[6,256,1,16,64]{1,0,4,3,2:T(8,128)} %reshape.602, f32[6,256,16,64]{1,3,2,0:T(8,128)S(1)} %fusion.28, f32[6,256,16,64]{1,3,2,0:T(8,128)S(1)} %copy-done.7, f32[6,256,16]{1,2,0:T(8,128)S(1)} %copy-done.14, f32[16]{0:T(128)S(1)} %dynamic_slice.166, f32[6,256,16]{1,2,0:T(8,128)S(1)} %copy-done.13, ...), kind=kOutput, calls=%fused_computation.39 | convolution fusion | flops 852492288 | bytes 30670912 | tf_op jit(solution)/shard_map/cghqs,csghp->cqghp/dot_general | solution.py:20
  450.2 11.3 %copy.242 = f32[6,256,1,16,64]{4,3,1,0,2:T(8,128)} copy(f32[6,256,1,16,64]{1,4,3,0,2:T(8,128)} %fusion.19) | data formatting | bytes 12582912 | tf_op jit(solution)/shard_map/reshape | solution.py:323
  461.5 11.6 %reshape.626 = f32[1536,1024]{1,0:T(8,128)} reshape(f32[6,256,1,16,64]{4,3,1,0,2:T(8,128)} %copy.242) | data formatting | bytes 12582912 | tf_op jit(solution)/shard_map/reshape | solution.py:323
  473.1 38.5 %all-gather.5.cloned.1.call-done = bf16[4096,2048]{1,0:T(8,128)(2,1)} async-done(((bf16[512,2048]{1,0:T(8,128)(2,1)}), bf16[4096,2048]{1,0:T(8,128)(2,1)}) %all-gather.5.cloned.1.call-update) | async-done | bytes 16777232 | tf_op jit(solution)/shard_map/all_gather | solution.py:231
  511.6 26.2 %multiply_reduce_fusion = (f32[1536]{0:T(1024)S(1)}, f32[1536,1024]{1,0:T(8,128)}) fusion(f32[1536,1024]{1,0:T(8,128)} %reshape.626, bf16[4096,2048]{1,0:T(8,128)(2,1)} %all-gather.5.cloned.1.call-done, bf16[768,4096]{1,0:T(8,128)(2,1)} %bitcast_select_fusion, bf16[768,4096]{1,0:T(8,128)(2,1)} %copy-done.4, pred[]{:T(512)S(6)} %eq.208), kind=kOutput, calls=%fused_computation.43 | convolution fusion | flops 12955678720 | bytes 33560576 | tf_op jit(solution)/shard_map/dot_general | solution.py:236
  537.8 3.3 broadcast_multiply_fusion
  542.1 5.8 convolution_convert_fusion.4
  547.9 4.6 convolution_convert_fusion.3
  553.0 4.0 convolution_convert_fusion.2
  557.1 3.5 convolution_convert_fusion.1
  561.2 3.9 convert_add_fusion.3
  565.2 1.5 collective-permute-start.10
  566.7 3.5 convert_add_fusion.2
  571.0 3.7 convert_add_fusion.1
  574.9 1.5 collective-permute-start.14
  576.4 3.5 convert_add_fusion
  580.6 5.1 collective-permute-done.10
  585.9 16.6 %collective-permute-done.12 = bf16[384,1024]{1,0:T(8,128)(2,1)S(1)} collective-permute-done((bf16[384,1024]{1,0:T(8,128)(2,1)S(1)}, bf16[384,1024]{1,0:T(8,128)(2,1)S(1)}, u32[]{:S(2)}, u32[]{:S(2)}) %collective-permute-start.12) | collective-permute-done | bytes 786464 | tf_op jit(solution)/shard_map/ppermute | solution.py:127
  602.8 16.6 %collective-permute-done.14 = bf16[384,1024]{1,0:T(8,128)(2,1)S(1)} collective-permute-done((bf16[384,1024]{1,0:T(8,128)(2,1)S(1)}, bf16[384,1024]{1,0:T(8,128)(2,1)S(1)}, u32[]{:S(2)}, u32[]{:S(2)}) %collective-permute-start.14) | collective-permute-done | bytes 786464 | tf_op jit(solution)/shard_map/ppermute | solution.py:127
  619.6 15.7 %collective-permute-done.16 = bf16[384,1024]{1,0:T(8,128)(2,1)S(1)} collective-permute-done((bf16[384,1024]{1,0:T(8,128)(2,1)S(1)}, bf16[384,1024]{1,0:T(8,128)(2,1)S(1)}, u32[]{:S(2)}, u32[]{:S(2)}) %collective-permute-start.16) | collective-permute-done | bytes 786464 | tf_op jit(solution)/shard_map/ppermute | solution.py:127
  635.6 1.8 pad_maximum_fusion.3
  (220 shorter events, 49.4 us)
Async XLA Ops:
  6.5 262.8 %copy-start = (f32[32,64,128]{2,1,0:T(8,128)S(1)}, f32[32,64,128]{2,1,0:T(8,128)}, u32[]{:S(2)}) copy-start(f32[32,64,128]{2,1,0:T(8,128)} %param.35) | copy-start | bytes 3145732
  6.5 5.4 copy-start.5
  6.5 199.2 %all-gather.3.cloned.1.call-start = ((), (), s32[]{:S(2)}) async-start(), calls=%async_computation | async-start | bytes 12976128 | tf_op jit(solution)/shard_map/all_gather | solution.py:211
  20.3 16.8 %collective-permute-start.2 = (bf16[256,1296]{0,1:T(8,128)(2,1)S(1)}, bf16[256,1296]{0,1:T(8,128)(2,1)}, u32[]{:S(2)}, u32[]{:S(2)}) collective-permute-start(bf16[256,1296]{0,1:T(8,128)(2,1)S(1)} %copy.214), channel_id=1, source_target_pairs={{0,2},{2,0},{1,3},{3,1},{4,6},{6,4},{5,7},{7,5},{8,10},{10,8},{9,1... | collective-permute-start | bytes 1990664 | tf_op jit(solution)/shard_map/ppermute | solution.py:127
  43.9 4.3 copy-start.16
  44.0 467.7 %all-gather.5.cloned.1.call-start = ((), (), s32[]{:S(2)}) async-start(), calls=%async_computation.1 | async-start | bytes 18874368 | tf_op jit(solution)/shard_map/all_gather | solution.py:231
  53.6 2.8 copy-start.4
  56.4 69.7 %copy-start.6 = (bf16[256,1,2048]{2,1,0:T(2,128)(2,1)S(1)}, bf16[256,1,2048]{2,1,0:T(2,128)(2,1)}, u32[]{:S(2)}) copy-start(bf16[256,1,2048]{2,1,0:T(2,128)(2,1)} %get-tuple-element.166) | copy-start | bytes 3145732
  56.8 69.2 %collective-permute-start = (bf16[384,4096]{1,0:T(8,128)(2,1)S(1)}, bf16[384,4096]{1,0:T(8,128)(2,1)}, u32[]{:S(2)}, u32[]{:S(2)}) collective-permute-start(bf16[384,4096]{1,0:T(8,128)(2,1)S(1)} %constant_dynamic-slice_fusion.20), channel_id=1, source_target_pairs={{0,2},{2,0},{1,3},{3,1},{4,6},{6,4},{5,7},{7,5},{8,10},{10,8},{9,1... | collective-permute-start | bytes 9437192 | tf_op jit(solution)/shard_map/ppermute | solution.py:127
  126.0 6.0 collective-permute-start.1
  153.2 76.6 %copy-start.8 = (bf16[256,1,2048]{2,0,1:T(8,128)(2,1)S(1)}, bf16[256,1,2048]{2,0,1:T(8,128)(2,1)}, u32[]{:S(2)}) copy-start(bf16[256,1,2048]{2,0,1:T(8,128)(2,1)} %copy.297) | copy-start | bytes 3145732
  230.6 15.0 %collective-permute-start.7 = (bf16[256,1024]{1,0:T(8,128)(2,1)}, bf16[256,1024]{1,0:T(8,128)(2,1)S(1)}, u32[]{:S(2)}, u32[]{:S(2)}) collective-permute-start(bf16[256,1024]{1,0:T(8,128)(2,1)} %get-tuple-element.168), channel_id=1, source_target_pairs={{0,2},{2,0},{1,3},{3,1},{4,6},{6,4},{5,7},{7,5},{8,10},{10,8},{9,1... | collective-permute-start | bytes 1572872 | tf_op jit(solution)/shard_map/ppermute | solution.py:127
  233.7 22.2 %collective-permute-start.8 = (bf16[1024,256]{0,1:T(8,128)(2,1)S(1)}, bf16[1024,256]{0,1:T(8,128)(2,1)S(1)}, u32[]{:S(2)}, u32[]{:S(2)}) collective-permute-start(bf16[1024,256]{0,1:T(8,128)(2,1)S(1)} %get-tuple-element.170), channel_id=1, source_target_pairs={{0,2},{2,0},{1,3},{3,1},{4,6},{6,4},{5,7},{7,5},{8,10},{10,8},{9,1... | collective-permute-start | bytes 1572872 | tf_op jit(solution)/shard_map/ppermute | solution.py:127
  256.0 2.8 copy-start.21
  256.0 2.8 copy-start.22
  256.0 5.4 copy-start.17
  256.0 5.4 copy-start.18
  256.0 5.5 copy-start.23
  256.0 5.6 copy-start.24
  256.0 7.9 %copy-start.25 = (f32[32]{0:T(128)S(1)}, f32[32]{0:T(128)}, u32[]{:S(2)}) copy-start(f32[32]{0:T(128)} %param.29) | copy-start | bytes 388
  256.0 12.9 %copy-start.19 = (bf16[4,2048]{1,0:T(4,128)(2,1)S(1)}, bf16[4,2048]{1,0:T(4,128)(2,1)}, u32[]{:S(2)}) copy-start(bf16[4,2048]{1,0:T(4,128)(2,1)} %param.25) | copy-start | bytes 49156
  256.0 13.0 %copy-start.20 = (bf16[3,2048]{1,0:T(4,128)(2,1)S(1)}, bf16[3,2048]{1,0:T(4,128)(2,1)}, u32[]{:S(2)}) copy-start(bf16[3,2048]{1,0:T(4,128)(2,1)} %param.36) | copy-start | bytes 36868
  272.4 18.9 %collective-permute-start.3 = (bf16[3,1280]{0,1:T(8,128)(2,1)S(1)}, bf16[3,1280]{0,1:T(8,128)(2,1)S(1)}, u32[]{:S(2)}, u32[]{:S(2)}) collective-permute-start(bf16[3,1280]{0,1:T(8,128)(2,1)S(1)} %slice.174), channel_id=1, source_target_pairs={{0,4},{4,8},{8,12},{12,16},{16,20},{20,24},{24,28},{1,5},{5,9},{9,... | collective-permute-start | bytes 23048 | tf_op jit(solution)/shard_map/ppermute | solution.py:15
  312.8 1.9 copy-start.3
  347.5 34.4 %collective-permute-start.4 = (f32[1,16,64,128]{3,2,1,0:T(8,128)S(1)}, f32[1,16,64,128]{3,2,1,0:T(8,128)}, u32[]{:S(2)}, u32[]{:S(2)}) collective-permute-start(f32[1,16,64,128]{3,2,1,0:T(8,128)S(1)} %get-tuple-element.48), channel_id=1, source_target_pairs={{0,4},{4,8},{8,12},{12,16},{16,20},{20,24},{24,28},{1,5},{5,9},{9,... | collective-permute-start | bytes 1572872 | tf_op jit(solution)/shard_map/ppermute | solution.py:15
  348.8 77.7 %collective-permute-start.6 = (f32[1,16,64,128]{3,2,1,0:T(8,128)S(1)}, f32[1,16,64,128]{3,2,1,0:T(8,128)}, u32[]{:S(2)}, u32[]{:S(2)}) collective-permute-start(f32[1,16,64,128]{3,2,1,0:T(8,128)S(1)} %get-tuple-element.48), channel_id=1, source_target_pairs={{0,8},{4,12},{8,16},{12,20},{16,24},{20,28},{1,9},{5,13},{9,17},{1... | collective-permute-start | bytes 1572872 | tf_op jit(solution)/shard_map/ppermute | solution.py:15
  350.3 31.5 %collective-permute-start.5 = (f32[1,16]{1,0:T(1,128)S(1)}, f32[1,16]{1,0:T(1,128)S(1)}, u32[]{:S(2)}, u32[]{:S(2)}) collective-permute-start(f32[1,16]{1,0:T(1,128)S(1)} %get-tuple-element.49), channel_id=1, source_target_pairs={{0,4},{4,8},{8,12},{12,16},{16,20},{20,24},{24,28},{1,5},{5,9},{9,... | collective-permute-start | bytes 200 | tf_op jit(solution)/shard_map/ppermute | solution.py:15
  358.3 75.0 %copy-start.11 = (f32[6,256,256]{2,1,0:T(8,128)S(1)}, f32[6,256,256]{2,1,0:T(8,128)}, u32[]{:S(2)}) copy-start(f32[6,256,256]{2,1,0:T(8,128)} %fusion.129) | copy-start | bytes 4718596
  426.5 6.9 %copy-start.7 = (f32[6,256,16,64]{1,3,2,0:T(8,128)S(1)}, f32[6,256,16,64]{1,3,2,0:T(8,128)}, u32[]{:S(2)}) copy-start(f32[6,256,16,64]{1,3,2,0:T(8,128)} %fusion.70) | copy-start | bytes 18874372
  427.9 5.4 copy-start.2
  428.0 5.4 copy-start.12
  428.0 5.4 copy-start.13
  428.0 5.4 copy-start.14
  428.0 5.4 copy-start.15
  537.8 3.3 dynamic-slice-start
  542.1 5.8 copy-start.9
  547.9 13.3 %collective-permute-start.9 = (bf16[2,384,1024]{2,1,0:T(8,128)(2,1)}, bf16[2,384,1024]{2,1,0:T(8,128)(2,1)}, u32[]{:S(2)}, u32[]{:S(2)}) collective-permute-start(bf16[2,384,1024]{2,1,0:T(8,128)(2,1)} %convolution_convert_fusion.4), channel_id=1, source_target_pairs={{0,1},{1,0},{2,3},{3,2},{4,5},{5,4},{6,7},{7,6},{8,9},{9,8},{10,11... | collective-permute-start | bytes 4718600 | tf_op jit(solution)/shard_map/ppermute | solution.py:345
  552.5 14.2 %collective-permute-start.11 = (bf16[2,384,1024]{2,1,0:T(8,128)(2,1)}, bf16[2,384,1024]{2,1,0:T(8,128)(2,1)S(1)}, u32[]{:S(2)}, u32[]{:S(2)}) collective-permute-start(bf16[2,384,1024]{2,1,0:T(8,128)(2,1)} %convolution_convert_fusion.3), channel_id=1, source_target_pairs={{0,1},{1,0},{2,3},{3,2},{4,5},{5,4},{6,7},{7,6},{8,9},{9,8},{10,11... | collective-permute-start | bytes 4718600 | tf_op jit(solution)/shard_map/ppermute | solution.py:345
  553.0 4.1 copy-start.10
  557.1 13.9 %collective-permute-start.13 = (bf16[2,384,1024]{2,1,0:T(8,128)(2,1)S(1)}, bf16[2,384,1024]{2,1,0:T(8,128)(2,1)S(1)}, u32[]{:S(2)}, u32[]{:S(2)}) collective-permute-start(bf16[2,384,1024]{2,1,0:T(8,128)(2,1)S(1)} %convolution_convert_fusion.2), channel_id=1, source_target_pairs={{0,1},{1,0},{2,3},{3,2},{4,5},{5,4},{6,7},{7,6},{8,9},{9,8},{10,11... | collective-permute-start | bytes 4718600 | tf_op jit(solution)/shard_map/ppermute | solution.py:345
  560.6 15.8 %collective-permute-start.15 = (bf16[2,384,1024]{2,1,0:T(8,128)(2,1)S(1)}, bf16[2,384,1024]{2,1,0:T(8,128)(2,1)S(1)}, u32[]{:S(2)}, u32[]{:S(2)}) collective-permute-start(bf16[2,384,1024]{2,1,0:T(8,128)(2,1)S(1)} %convolution_convert_fusion.1), channel_id=1, source_target_pairs={{0,1},{1,0},{2,3},{3,2},{4,5},{5,4},{6,7},{7,6},{8,9},{9,8},{10,11... | collective-permute-start | bytes 4718600 | tf_op jit(solution)/shard_map/ppermute | solution.py:345
  565.2 20.5 %collective-permute-start.10 = (bf16[384,1024]{1,0:T(8,128)(2,1)S(1)}, bf16[384,1024]{1,0:T(8,128)(2,1)S(1)}, u32[]{:S(2)}, u32[]{:S(2)}) collective-permute-start(bf16[384,1024]{1,0:T(8,128)(2,1)S(1)} %fusion.66), channel_id=1, source_target_pairs={{0,2},{2,0},{1,3},{3,1},{4,6},{6,4},{5,7},{7,5},{8,10},{10,8},{9,1... | collective-permute-start | bytes 2359304 | tf_op jit(solution)/shard_map/ppermute | solution.py:127
  570.3 32.2 %collective-permute-start.12 = (bf16[384,1024]{1,0:T(8,128)(2,1)S(1)}, bf16[384,1024]{1,0:T(8,128)(2,1)S(1)}, u32[]{:S(2)}, u32[]{:S(2)}) collective-permute-start(bf16[384,1024]{1,0:T(8,128)(2,1)S(1)} %fusion.67), channel_id=1, source_target_pairs={{0,2},{2,0},{1,3},{3,1},{4,6},{6,4},{5,7},{7,5},{8,10},{10,8},{9,1... | collective-permute-start | bytes 2359304 | tf_op jit(solution)/shard_map/ppermute | solution.py:127
  574.9 44.5 %collective-permute-start.14 = (bf16[384,1024]{1,0:T(8,128)(2,1)S(1)}, bf16[384,1024]{1,0:T(8,128)(2,1)S(1)}, u32[]{:S(2)}, u32[]{:S(2)}) collective-permute-start(bf16[384,1024]{1,0:T(8,128)(2,1)S(1)} %fusion.68), channel_id=1, source_target_pairs={{0,2},{2,0},{1,3},{3,1},{4,6},{6,4},{5,7},{7,5},{8,10},{10,8},{9,1... | collective-permute-start | bytes 2359304 | tf_op jit(solution)/shard_map/ppermute | solution.py:127
  580.0 55.3 %collective-permute-start.16 = (bf16[384,1024]{1,0:T(8,128)(2,1)S(1)}, bf16[384,1024]{1,0:T(8,128)(2,1)S(1)}, u32[]{:S(2)}, u32[]{:S(2)}) collective-permute-start(bf16[384,1024]{1,0:T(8,128)(2,1)S(1)} %fusion.69), channel_id=1, source_target_pairs={{0,2},{2,0},{1,3},{3,1},{4,6},{6,4},{5,7},{7,5},{8,10},{10,8},{9,1... | collective-permute-start | bytes 2359304 | tf_op jit(solution)/shard_map/ppermute | solution.py:127
  635.3 2.1 copy-start.1
Sparse Core Ops, SparseCore 0:
  44.1 161.6 all-gather.2
  258.2 253.3 all-gather.4

commit v12 on v9

--- a/solution.py
+++ b/solution.py
@@ -347,7 +347,9 @@
             total = part if total is None else total + part
         mine = lax.dynamic_index_in_dim(total, half, 0, keepdims=False)
         theirs = lax.dynamic_index_in_dim(total, 1 - half, 0, keepdims=False)
-        theirs = swap_half(theirs.astype(jnp.bfloat16))
+        theirs = theirs.astype(jnp.bfloat16)
+        by_owner, theirs = lax.optimization_barrier((by_owner, theirs))
+        theirs = swap_half(theirs)
         results.append((mine + theirs.astype(jnp.float32)).astype(jnp.bfloat16))
     return jnp.concatenate(results, axis=1)
 

time: 638 us -> 647 us (1.014)
  waiting for transfers between devices: 276 us -> 286 us
    ppermute x4, waiting for transfers between devices: 0.01 us -> 9.44 us  [body(): lax.ppermute(part.astype(jnp.bfloat16), 'fsdp', [(j, (j + shift) % core_c...]
  transfers between devices with their start and end apart: 20 -> 20, of which waited for: 9 -> 12; matrix products, arithmetic and copies ran while one was open for 39% -> 36% of each run, Pallas kernels for 0% -> 0%
where the time goes in v12:
time: 647 us; the launch traced here: 639 us
  waiting for transfers between devices  286 us (44%)
  other arithmetic  113 us (17%)
  matrix products  105 us (16%)
  local copies, waits for them, and re-layouts  87.1 us (13%)
  starting transfers between devices  32.2 us (5%)
  between operations  15.3 us (2%)
    ppermute x8, waiting for transfers between devices, swap_half(): lax.ppermute(value, 'half', [(k, count - 1 - k) for k in range(count)])  146 us
    all_gather x1, waiting for transfers between devices, body(): out_full = lax.all_gather(out_local, 'pair', axis=1, tiled=True)  78.6 us
    all_gather x1, waiting for transfers between devices, body(): first_full = lax.all_gather(first_local, 'pair', axis=0, tiled=True)  51.9 us
    dot_general x1, matrix products, body(): jnp.dot(normed, z_full, preferred_element_type=jnp.float32)  27 us
    dot_general x1, matrix products, body(): jnp.dot(normed, first_full, preferred_element_type=jnp.float32)  24 us
    reshape x2, local copies, waits for them, and re-layouts, body(): (direct + state_gain[..., None] * from_state).reshape(row_count, inner_lo...  22.9 us
    dot_general x8, matrix products, body(): jnp.einsum('hrc,cd->hrd', rows, columns, preferred_element_type=jnp.float32)  22.2 us
    convert_element_type x1, other arithmetic, conv_rows(): return jax.nn.silu(summed).astype(jnp.bfloat16)  21.5 us
  transfers between devices with their start and end apart: 20, of which 12 were waited for; matrix products, arithmetic and copies ran while one was open for 36% of the time, Pallas kernels for 0%

profile of v12, /device:TPU:0, one launch (start us, length us, event | category | flops | bytes accessed | tf_op | source)
XLA Modules:
  0.0 638.6 jit_solution(15139627736585423153)
XLA Ops:
  8.1 1.5 fusion.118
  11.4 6.9 %fusion.117 = (bf16[256,1,2048]{2,1,0:T(2,128)(2,1)}, bf16[256,1,2048]{2,1,0:T(2,128)(2,1)}) fusion(bf16[256,2,2048]{2,1,0:T(2,128)(2,1)} %param.22), kind=kLoop, calls=%fused_computation.258 | loop fusion | bytes 4194304 | tf_op jit(solution)/shard_map/slice | solution.py:218
  18.4 3.7 constant_dynamic-slice_fusion.19
  24.3 2.9 collective-permute-start.2
  29.7 12.7 %collective-permute-done.2 = bf16[256,1296]{0,1:T(8,128)(2,1)S(1)} collective-permute-done((bf16[256,1296]{0,1:T(8,128)(2,1)}, bf16[256,1296]{0,1:T(8,128)(2,1)S(1)}, u32[]{:S(2)}, u32[]{:S(2)}) %collective-permute-start.2) | collective-permute-done | bytes 663584 | tf_op jit(solution)/shard_map/ppermute | solution.py:127
  42.7 6.3 maximum_select_fusion.3
  49.2 4.1 fusion.3
  53.3 5.3 fusion.5
  58.6 2.9 copy-done.4
  61.8 1.8 collective-permute-start
  63.6 67.6 %collective-permute-done = bf16[384,4096]{1,0:T(8,128)(2,1)} collective-permute-done((bf16[384,4096]{1,0:T(8,128)(2,1)S(1)}, bf16[384,4096]{1,0:T(8,128)(2,1)}, u32[]{:S(2)}, u32[]{:S(2)}) %collective-permute-start) | collective-permute-done | bytes 3145760 | tf_op jit(solution)/shard_map/ppermute | solution.py:127
  134.5 1.8 reduce-window.30
  139.2 2.2 copy.282
  141.5 5.0 fusion.20
  146.4 4.3 gather_fusion.1
  150.7 4.3 gather_fusion
  155.0 3.6 pad_maximum_fusion
  158.7 3.7 bitcast_select_fusion
  162.4 51.9 %all-gather.4.cloned.1.call-done = bf16[4096,1296]{1,0:T(8,128)(2,1)} async-done(((bf16[512,1296]{1,0:T(8,128)(2,1)}), bf16[4096,1296]{1,0:T(8,128)(2,1)}) %all-gather.4.cloned.1.call-update) | async-done | bytes 10616848 | tf_op jit(solution)/shard_map/all_gather | solution.py:211
  214.3 24.0 %convolution_convert_fusion = bf16[1536,1296]{0,1:T(8,128)(2,1)} fusion(bf16[4096,1296]{1,0:T(8,128)(2,1)} %all-gather.4.cloned.1.call-done, bf16[768,4096]{1,0:T(8,128)(2,1)} %bitcast_select_fusion, bf16[768,4096]{1,0:T(8,128)(2,1)} %copy-done.4, pred[]{:T(512)S(6)} %eq.208), kind=kOutput, calls=%fused_computation.27 | convolution fusion | flops 16366067712 | bytes 27181056 | tf_op jit(solution)/shard_map/dot_general | solution.py:212
  238.4 1.5 collective-permute-start.7
  245.6 6.1 collective-permute-done.7
  251.7 1.5 maximum_select_fusion.4
  261.3 1.9 slice.165
  263.2 3.2 collective-permute-start.3
  268.1 3.8 reduce-window.21
  279.1 4.4 slice.160
  283.8 1.5 collective-permute-start.8
  286.2 21.5 %multiply_convert_fusion.3 = bf16[1536,1280]{0,1:T(8,128)(2,1)S(1)} fusion(bf16[1536,1280]{0,1:T(8,128)(2,1)} %slice.160, bf16[3,1280]{0,1:T(8,128)(2,1)} %collective-permute-done.3, f32[1280]{0:T(1024)S(1)} %copy-done.22, f32[1280]{0:T(1024)S(1)} %copy-done.23, f32[1280]{0:T(1024)S(1)} %copy-done.24, f32[1280]{0:T(1024)S(1)} %copy-done.21, ...), kind=kLoop, calls=%fused_computation.26 | loop fusion | flops 104202240 | bytes 7933952 | tf_op jit(solution)/shard_map/convert_element_type | solution.py:68
  307.7 5.3 fusion.115
  315.7 7.5 %reshape.580 = bf16[6,256,16,64]{1,0,3,2:T(8,128)(2,1)} reshape(bf16[1536,1024]{0,1:T(8,128)(2,1)} %get-tuple-element.173) | data formatting | bytes 6291456 | tf_op jit(solution)/shard_map/reshape.48
  323.2 3.2 multiply_convert_fusion.2
  326.4 2.7 add_bitcast_fusion
  329.1 12.6 %while.17 = (s32[]{:T(128)}, f32[1,16,64,128]{3,2,1,0:T(8,128)S(1)}, f32[1,16]{1,0:T(1,128)S(1)}, f32[6,1,16,64,128]{4,3,2,1,0:T(8,128)}, f32[6,1,16]{2,0,1:T(8,...) while((s32[]{:T(128)}, ...), condition=%wide.region_15.16_spmd.clone, body=%wide.region_14.15_spmd.clone.sunk | while | flops 524323 | bytes 2622149 | solution.py:308
  341.7 2.3 collective-permute-start.4
  343.9 6.9 %collective-permute-start.6 = (f32[1,16,64,128]{3,2,1,0:T(8,128)S(1)}, f32[1,16,64,128]{3,2,1,0:T(8,128)}, u32[]{:S(2)}, u32[]{:S(2)}) collective-permute-start(f32[1,16,64,128]{3,2,1,0:T(8,128)S(1)} %get-tuple-element.55), channel_id=1, source_target_pairs={{0,8},{4,12},{8,16},{12,20},{16,24},{20,28},{1,9},{5,13},{9,17},{1... | collective-permute-start | bytes 1572872 | tf_op jit(solution)/shard_map/ppermute | solution.py:15
  351.1 5.4 collective-permute-start.5
  356.4 1.5 fusion.121
  358.0 5.3 fusion.62
  363.2 9.0 %reshape.602 = f32[6,256,1,16,64]{1,0,4,3,2:T(8,128)} reshape(f32[1536,1024]{0,1:T(8,128)} %get-tuple-element.174) | data formatting | bytes 12582912 | tf_op jit(solution)/shard_map/convert_element_type | solution.py:119
  373.7 5.3 fusion.21
  379.2 16.7 %fusion.17 = f32[6,256,1,16,64]{1,4,3,0,2:T(8,128)} fusion(f32[6,256,1,16,64]{1,0,4,3,2:T(8,128)} %reshape.602, f32[6,256,16,64]{1,3,2,0:T(8,128)S(1)} %fusion.21, f32[6,256,16,64]{1,3,2,0:T(8,128)S(1)} %copy-done.5, f32[6,256,16]{1,2,0:T(8,128)S(1)} %copy-done.17, f32[16]{0:T(128)S(1)} %copy-done.55, f32[6,256,16]{1,2,0:T(8,128)S(1)} %copy-done.16, ...), kind=kOutput, calls=%fused_computation.37 | convolution fusion | flops 852492288 | bytes 30670912 | tf_op jit(solution)/shard_map/cghqs,csghp->cqghp/dot_general | solution.py:20
  395.8 11.3 %copy.227 = f32[6,256,1,16,64]{4,3,1,0,2:T(8,128)} copy(f32[6,256,1,16,64]{1,4,3,0,2:T(8,128)} %fusion.17) | data formatting | bytes 12582912 | tf_op jit(solution)/shard_map/reshape | solution.py:320
  407.2 11.6 %reshape.626 = f32[1536,1024]{1,0:T(8,128)} reshape(f32[6,256,1,16,64]{4,3,1,0,2:T(8,128)} %copy.227) | data formatting | bytes 12582912 | tf_op jit(solution)/shard_map/reshape | solution.py:320
  418.7 27.0 %multiply_reduce_fusion = (f32[1536]{0:T(1024)S(1)}, f32[1536,1024]{1,0:T(8,128)}) fusion(f32[1536,1024]{1,0:T(8,128)} %reshape.626, bf16[4096,1024]{1,0:T(8,128)(2,1)} %all-gather.6.cloned.1.call-done, bf16[768,4096]{1,0:T(8,128)(2,1)} %bitcast_select_fusion, bf16[768,4096]{1,0:T(8,128)(2,1)} %copy-done.4, pred[]{:T(512)S(6)} %eq.208), kind=kOutput, calls=%fused_computation.41 | convolution fusion | flops 12955678720 | bytes 33560576 | tf_op jit(solution)/shard_map/dot_general | solution.py:233
  445.7 3.3 broadcast_multiply_fusion
  449.0 2.6 multiply_convert_fusion.4
  451.7 78.6 %all-gather.8.cloned.1.call-done = bf16[1024,4096]{1,0:T(8,128)(2,1)} async-done(((bf16[1024,512]{1,0:T(8,128)(2,1)}), bf16[1024,4096]{1,0:T(8,128)(2,1)}) %all-gather.8.cloned.1.call-update) | async-done | bytes 8388624 | tf_op jit(solution)/shard_map/all_gather | solution.py:232
  530.3 3.9 convolution_convert_fusion.5
  534.3 3.4 collective-permute-done.9
  537.7 3.9 convert_add_fusion.3
  541.7 1.8 convolution_convert_fusion.4
  544.0 3.0 collective-permute-done.11
  547.0 1.8 convert_add_fusion.2
  549.0 1.8 convolution_convert_fusion.3
  551.2 3.0 collective-permute-done.13
  554.3 1.8 convert_add_fusion.1
  556.2 3.0 convolution_convert_fusion.2
  563.1 4.3 convert_add_fusion
  569.0 11.0 %collective-permute-done.10 = bf16[384,1024]{1,0:T(8,128)(2,1)S(1)} collective-permute-done((bf16[384,1024]{1,0:T(8,128)(2,1)S(1)}, bf16[384,1024]{1,0:T(8,128)(2,1)S(1)}, u32[]{:S(2)}, u32[]{:S(2)}) %collective-permute-start.10) | collective-permute-done | bytes 786464 | tf_op jit(solution)/shard_map/ppermute | solution.py:127
  580.3 16.6 %collective-permute-done.12 = bf16[384,1024]{1,0:T(8,128)(2,1)S(1)} collective-permute-done((bf16[384,1024]{1,0:T(8,128)(2,1)S(1)}, bf16[384,1024]{1,0:T(8,128)(2,1)S(1)}, u32[]{:S(2)}, u32[]{:S(2)}) %collective-permute-start.12) | collective-permute-done | bytes 786464 | tf_op jit(solution)/shard_map/ppermute | solution.py:127
  597.1 16.6 %collective-permute-done.14 = bf16[384,1024]{1,0:T(8,128)(2,1)S(1)} collective-permute-done((bf16[384,1024]{1,0:T(8,128)(2,1)S(1)}, bf16[384,1024]{1,0:T(8,128)(2,1)S(1)}, u32[]{:S(2)}, u32[]{:S(2)}) %collective-permute-start.14) | collective-permute-done | bytes 786464 | tf_op jit(solution)/shard_map/ppermute | solution.py:127
  614.0 15.8 %collective-permute-done.16 = bf16[384,1024]{1,0:T(8,128)(2,1)S(1)} collective-permute-done((bf16[384,1024]{1,0:T(8,128)(2,1)S(1)}, bf16[384,1024]{1,0:T(8,128)(2,1)S(1)}, u32[]{:S(2)}, u32[]{:S(2)}) %collective-permute-start.16) | collective-permute-done | bytes 786464 | tf_op jit(solution)/shard_map/ppermute | solution.py:127
  630.0 1.8 pad_maximum_fusion.3
  (281 shorter events, 62.4 us)
Async XLA Ops:
  6.5 251.4 %copy-start = (f32[32,64,128]{2,1,0:T(8,128)S(1)}, f32[32,64,128]{2,1,0:T(8,128)}, u32[]{:S(2)}) copy-start(f32[32,64,128]{2,1,0:T(8,128)} %param.35) | copy-start | bytes 3145732
  6.5 207.7 %all-gather.4.cloned.1.call-start = ((), (), s32[]{:S(2)}) async-start(), calls=%async_computation | async-start | bytes 12976128 | tf_op jit(solution)/shard_map/all_gather | solution.py:211
  24.3 18.1 %collective-permute-start.2 = (bf16[256,1296]{0,1:T(8,128)(2,1)}, bf16[256,1296]{0,1:T(8,128)(2,1)S(1)}, u32[]{:S(2)}, u32[]{:S(2)}) collective-permute-start(bf16[256,1296]{0,1:T(8,128)(2,1)} %copy.201), channel_id=1, source_target_pairs={{0,2},{2,0},{1,3},{3,1},{4,6},{6,4},{5,7},{7,5},{8,10},{10,8},{9,1... | collective-permute-start | bytes 1990664 | tf_op jit(solution)/shard_map/ppermute | solution.py:127
  49.0 369.7 %all-gather.6.cloned.1.call-start = ((), (), s32[]{:S(2)}) async-start(), calls=%async_computation.1 | async-start | bytes 9437184 | tf_op jit(solution)/shard_map/all_gather | solution.py:231
  61.5 70.4 %copy-start.50 = (s32[8]{0:T(128)S(1)}, s32[8]{0:T(128)}, u32[]{:S(2)}) copy-start(s32[8]{0:T(128)} %param.32) | copy-start | bytes 100
  61.5 70.4 %copy-start.51 = (s32[8]{0:T(128)S(1)}, s32[8]{0:T(128)}, u32[]{:S(2)}) copy-start(s32[8]{0:T(128)} %param.33) | copy-start | bytes 100
  61.5 72.8 %copy-start.26 = (bf16[4,2,256]{2,1,0:T(2,128)(2,1)S(1)}, bf16[4,2,256]{2,1,0:T(2,128)(2,1)}, u32[]{:S(2)}) copy-start(bf16[4,2,256]{2,1,0:T(2,128)(2,1)} %param.26) | copy-start | bytes 12292
  61.5 72.9 %copy-start.28 = (bf16[3,2,256]{2,1,0:T(2,128)(2,1)S(1)}, bf16[3,2,256]{2,1,0:T(2,128)(2,1)}, u32[]{:S(2)}) copy-start(bf16[3,2,256]{2,1,0:T(2,128)(2,1)} %param.37) | copy-start | bytes 9220
  61.5 75.8 %copy-start.52 = (f32[32]{0:T(128)S(1)}, f32[32]{0:T(128)}, u32[]{:S(2)}) copy-start(f32[32]{0:T(128)} %param.27) | copy-start | bytes 388
  61.5 76.5 %copy-start.53 = (f32[32]{0:T(128)S(1)}, f32[32]{0:T(128)}, u32[]{:S(2)}) copy-start(f32[32]{0:T(128)} %param.28) | copy-start | bytes 388
  61.6 77.0 %copy-start.54 = (f32[32]{0:T(128)S(1)}, f32[32]{0:T(128)}, u32[]{:S(2)}) copy-start(f32[32]{0:T(128)} %param.29) | copy-start | bytes 388
  61.8 69.5 %collective-permute-start = (bf16[384,4096]{1,0:T(8,128)(2,1)S(1)}, bf16[384,4096]{1,0:T(8,128)(2,1)}, u32[]{:S(2)}, u32[]{:S(2)}) collective-permute-start(bf16[384,4096]{1,0:T(8,128)(2,1)S(1)} %constant_dynamic-slice_fusion.20), channel_id=1, source_target_pairs={{0,2},{2,0},{1,3},{3,1},{4,6},{6,4},{5,7},{7,5},{8,10},{10,8},{9,1... | collective-permute-start | bytes 9437192 | tf_op jit(solution)/shard_map/ppermute | solution.py:127
  131.3 10.2 %collective-permute-start.1 = (bf16[384,4096]{1,0:T(8,128)(2,1)}, bf16[384,4096]{1,0:T(8,128)(2,1)}, u32[]{:S(2)}, u32[]{:S(2)}) collective-permute-start(bf16[384,4096]{1,0:T(8,128)(2,1)} %collective-permute-done), channel_id=1, source_target_pairs={{0,1},{1,0},{2,3},{3,2},{4,5},{5,4},{6,7},{7,6},{8,9},{9,8},{10,11... | collective-permute-start | bytes 9437192 | tf_op jit(solution)/shard_map/ppermute | solution.py:186
  238.3 17.6 %copy-start.47 = (bf16[4,2048]{1,0:T(4,128)(2,1)S(1)}, bf16[4,2048]{1,0:T(4,128)(2,1)}, u32[]{:S(2)}) copy-start(bf16[4,2048]{1,0:T(4,128)(2,1)} %param.25) | copy-start | bytes 49156
  238.3 17.6 %copy-start.48 = (bf16[3,2048]{1,0:T(4,128)(2,1)S(1)}, bf16[3,2048]{1,0:T(4,128)(2,1)}, u32[]{:S(2)}) copy-start(bf16[3,2048]{1,0:T(4,128)(2,1)} %param.36) | copy-start | bytes 36868
  238.4 13.3 %collective-permute-start.7 = (bf16[256,1024]{1,0:T(8,128)(2,1)S(1)}, bf16[256,1024]{1,0:T(8,128)(2,1)S(1)}, u32[]{:S(2)}, u32[]{:S(2)}) collective-permute-start(bf16[256,1024]{1,0:T(8,128)(2,1)S(1)} %get-tuple-element.184), channel_id=1, source_target_pairs={{0,2},{2,0},{1,3},{3,1},{4,6},{6,4},{5,7},{7,5},{8,10},{10,8},{9,1... | collective-permute-start | bytes 1572872 | tf_op jit(solution)/shard_map/ppermute | solution.py:127
  251.7 23.3 %copy-start.14 = (bf16[2048,256]{1,0:T(8,128)(2,1)S(1)}, bf16[2048,256]{1,0:T(8,128)(2,1)}, u32[]{:S(2)}) copy-start(bf16[2048,256]{1,0:T(8,128)(2,1)} %param.31) | copy-start | bytes 3145732
  253.3 277.1 %all-gather.8.cloned.1.call-start = ((), (), s32[]{:S(2)}) async-start(), calls=%async_computation.2 | async-start | bytes 9437184 | tf_op jit(solution)/shard_map/all_gather | solution.py:232
  263.2 22.8 %collective-permute-start.3 = (bf16[3,1280]{0,1:T(8,128)(2,1)}, bf16[3,1280]{0,1:T(8,128)(2,1)}, u32[]{:S(2)}, u32[]{:S(2)}) collective-permute-start(bf16[3,1280]{0,1:T(8,128)(2,1)} %slice.165), channel_id=1, source_target_pairs={{0,4},{4,8},{8,12},{12,16},{16,20},{20,24},{24,28},{1,5},{5,9},{9,... | collective-permute-start | bytes 23048 | tf_op jit(solution)/shard_map/ppermute | solution.py:15
  278.8 7.1 %copy-start.19 = (f32[1280]{0:T(1024)S(1)}, f32[1280]{0:T(1024)}, u32[]{:S(2)}) copy-start(f32[1280]{0:T(1024)} %get-tuple-element.143) | copy-start | bytes 15364
  278.9 7.1 %copy-start.20 = (f32[1280]{0:T(1024)S(1)}, f32[1280]{0:T(1024)}, u32[]{:S(2)}) copy-start(f32[1280]{0:T(1024)} %get-tuple-element.144) | copy-start | bytes 15364
  278.9 7.1 %copy-start.21 = (f32[1280]{0:T(1024)S(1)}, f32[1280]{0:T(1024)}, u32[]{:S(2)}) copy-start(f32[1280]{0:T(1024)} %get-tuple-element.145) | copy-start | bytes 15364
  278.9 7.1 %copy-start.22 = (f32[1280]{0:T(1024)S(1)}, f32[1280]{0:T(1024)}, u32[]{:S(2)}) copy-start(f32[1280]{0:T(1024)} %get-tuple-element.146) | copy-start | bytes 15364
  278.9 7.1 %copy-start.23 = (f32[1280]{0:T(1024)S(1)}, f32[1280]{0:T(1024)}, u32[]{:S(2)}) copy-start(f32[1280]{0:T(1024)} %get-tuple-element.147) | copy-start | bytes 15364
  278.9 7.1 %copy-start.24 = (f32[1280]{0:T(1024)S(1)}, f32[1280]{0:T(1024)}, u32[]{:S(2)}) copy-start(f32[1280]{0:T(1024)} %get-tuple-element.148) | copy-start | bytes 15364
  278.9 7.1 %copy-start.29 = (pred[1536]{0:T(1024)(128)(4,1)S(1)}, pred[1536]{0:T(1024)(128)(4,1)}, u32[]{:S(2)}) copy-start(pred[1536]{0:T(1024)(128)(4,1)} %get-tuple-element.197) | copy-start | bytes 4612
  278.9 7.1 %copy-start.30 = (pred[1536]{0:T(1024)(128)(4,1)S(1)}, pred[1536]{0:T(1024)(128)(4,1)}, u32[]{:S(2)}) copy-start(pred[1536]{0:T(1024)(128)(4,1)} %get-tuple-element.198) | copy-start | bytes 4612
  278.9 7.1 %copy-start.31 = (pred[1536]{0:T(1024)(128)(4,1)S(1)}, pred[1536]{0:T(1024)(128)(4,1)}, u32[]{:S(2)}) copy-start(pred[1536]{0:T(1024)(128)(4,1)} %get-tuple-element.199) | copy-start | bytes 4612
  278.9 7.1 %copy-start.32 = (pred[1536]{0:T(1024)(128)(4,1)S(1)}, pred[1536]{0:T(1024)(128)(4,1)}, u32[]{:S(2)}) copy-start(pred[1536]{0:T(1024)(128)(4,1)} %get-tuple-element.200) | copy-start | bytes 4612
  278.9 7.1 %copy-start.33 = (pred[1536]{0:T(1024)(128)(4,1)S(1)}, pred[1536]{0:T(1024)(128)(4,1)}, u32[]{:S(2)}) copy-start(pred[1536]{0:T(1024)(128)(4,1)} %get-tuple-element.225) | copy-start | bytes 4612
  279.0 7.1 %copy-start.34 = (pred[1536]{0:T(1024)(128)(4,1)S(1)}, pred[1536]{0:T(1024)(128)(4,1)}, u32[]{:S(2)}) copy-start(pred[1536]{0:T(1024)(128)(4,1)} %get-tuple-element.226) | copy-start | bytes 4612
  279.0 7.1 %copy-start.35 = (pred[1536]{0:T(1024)(128)(4,1)S(1)}, pred[1536]{0:T(1024)(128)(4,1)}, u32[]{:S(2)}) copy-start(pred[1536]{0:T(1024)(128)(4,1)} %get-tuple-element.209) | copy-start | bytes 4612
  279.0 7.1 %copy-start.36 = (pred[1536]{0:T(1024)(128)(4,1)S(1)}, pred[1536]{0:T(1024)(128)(4,1)}, u32[]{:S(2)}) copy-start(pred[1536]{0:T(1024)(128)(4,1)} %get-tuple-element.210) | copy-start | bytes 4612
  279.0 7.1 %copy-start.37 = (pred[1536]{0:T(1024)(128)(4,1)S(1)}, pred[1536]{0:T(1024)(128)(4,1)}, u32[]{:S(2)}) copy-start(pred[1536]{0:T(1024)(128)(4,1)} %get-tuple-element.223) | copy-start | bytes 4612
  279.0 7.1 %copy-start.38 = (pred[1536]{0:T(1024)(128)(4,1)S(1)}, pred[1536]{0:T(1024)(128)(4,1)}, u32[]{:S(2)}) copy-start(pred[1536]{0:T(1024)(128)(4,1)} %get-tuple-element.224) | copy-start | bytes 4612
  279.0 7.1 %copy-start.39 = (pred[1536]{0:T(1024)(128)(4,1)S(1)}, pred[1536]{0:T(1024)(128)(4,1)}, u32[]{:S(2)}) copy-start(pred[1536]{0:T(1024)(128)(4,1)} %get-tuple-element.221) | copy-start | bytes 4612
  279.0 7.1 %copy-start.40 = (pred[1536]{0:T(1024)(128)(4,1)S(1)}, pred[1536]{0:T(1024)(128)(4,1)}, u32[]{:S(2)}) copy-start(pred[1536]{0:T(1024)(128)(4,1)} %get-tuple-element.222) | copy-start | bytes 4612
  279.0 7.1 %copy-start.41 = (pred[1536]{0:T(1024)(128)(4,1)S(1)}, pred[1536]{0:T(1024)(128)(4,1)}, u32[]{:S(2)}) copy-start(pred[1536]{0:T(1024)(128)(4,1)} %get-tuple-element.207) | copy-start | bytes 4612
  279.0 7.1 %copy-start.42 = (pred[1536]{0:T(1024)(128)(4,1)S(1)}, pred[1536]{0:T(1024)(128)(4,1)}, u32[]{:S(2)}) copy-start(pred[1536]{0:T(1024)(128)(4,1)} %get-tuple-element.208) | copy-start | bytes 4612
  279.0 7.1 %copy-start.43 = (pred[1536]{0:T(1024)(128)(4,1)S(1)}, pred[1536]{0:T(1024)(128)(4,1)}, u32[]{:S(2)}) copy-start(pred[1536]{0:T(1024)(128)(4,1)} %get-tuple-element.219) | copy-start | bytes 4612
  279.1 7.1 %copy-start.44 = (pred[1536]{0:T(1024)(128)(4,1)S(1)}, pred[1536]{0:T(1024)(128)(4,1)}, u32[]{:S(2)}) copy-start(pred[1536]{0:T(1024)(128)(4,1)} %get-tuple-element.220) | copy-start | bytes 4612
  279.1 7.1 %copy-start.45 = (pred[1536]{0:T(1024)(128)(4,1)S(1)}, pred[1536]{0:T(1024)(128)(4,1)}, u32[]{:S(2)}) copy-start(pred[1536]{0:T(1024)(128)(4,1)} %broadcast_compare_fusion.1) | copy-start | bytes 4612
  283.8 29.2 %collective-permute-start.8 = (bf16[1024,256]{1,0:T(8,128)(2,1)S(1)}, bf16[1024,256]{1,0:T(8,128)(2,1)S(1)}, u32[]{:S(2)}, u32[]{:S(2)}) collective-permute-start(bf16[1024,256]{1,0:T(8,128)(2,1)S(1)} %copy-done.15), channel_id=1, source_target_pairs={{0,2},{2,0},{1,3},{3,1},{4,6},{6,4},{5,7},{7,5},{8,10},{10,8},{9,1... | collective-permute-start | bytes 1572872 | tf_op jit(solution)/shard_map/ppermute | solution.py:127
  341.7 30.6 %collective-permute-start.4 = (f32[1,16,64,128]{3,2,1,0:T(8,128)S(1)}, f32[1,16,64,128]{3,2,1,0:T(8,128)}, u32[]{:S(2)}, u32[]{:S(2)}) collective-permute-start(f32[1,16,64,128]{3,2,1,0:T(8,128)S(1)} %get-tuple-element.55), channel_id=1, source_target_pairs={{0,4},{4,8},{8,12},{12,16},{16,20},{20,24},{24,28},{1,5},{5,9},{9,... | collective-permute-start | bytes 1572872 | tf_op jit(solution)/shard_map/ppermute | solution.py:15
  343.9 28.3 %collective-permute-start.6 = (f32[1,16,64,128]{3,2,1,0:T(8,128)S(1)}, f32[1,16,64,128]{3,2,1,0:T(8,128)}, u32[]{:S(2)}, u32[]{:S(2)}) collective-permute-start(f32[1,16,64,128]{3,2,1,0:T(8,128)S(1)} %get-tuple-element.55), channel_id=1, source_target_pairs={{0,8},{4,12},{8,16},{12,20},{16,24},{20,28},{1,9},{5,13},{9,17},{1... | collective-permute-start | bytes 1572872 | tf_op jit(solution)/shard_map/ppermute | solution.py:15
  351.1 21.1 %collective-permute-start.5 = (f32[1,16]{1,0:T(1,128)S(1)}, f32[1,16]{1,0:T(1,128)S(1)}, u32[]{:S(2)}, u32[]{:S(2)}) collective-permute-start(f32[1,16]{1,0:T(1,128)S(1)} %get-tuple-element.56), channel_id=1, source_target_pairs={{0,4},{4,8},{8,12},{12,16},{16,20},{20,24},{24,28},{1,5},{5,9},{9,... | collective-permute-start | bytes 200 | tf_op jit(solution)/shard_map/ppermute | solution.py:15
  363.2 15.9 %copy-start.13 = (f32[6,256,256]{2,1,0:T(8,128)S(1)}, f32[6,256,256]{2,1,0:T(8,128)}, u32[]{:S(2)}) copy-start(f32[6,256,256]{2,1,0:T(8,128)} %fusion.121) | copy-start | bytes 4718596
  372.2 6.9 %copy-start.5 = (f32[6,256,16,64]{1,3,2,0:T(8,128)S(1)}, f32[6,256,16,64]{1,3,2,0:T(8,128)}, u32[]{:S(2)}) copy-start(f32[6,256,16,64]{1,3,2,0:T(8,128)} %fusion.62) | copy-start | bytes 18874372
  373.7 5.4 copy-start.2
  373.7 5.4 copy-start.16
  373.7 5.4 copy-start.17
  534.2 3.5 collective-permute-start.9
  534.3 7.4 %copy-start.6 = (bf16[2,2,384,1024]{3,2,1,0:T(8,128)(2,1)S(1)}, bf16[2,2,384,1024]{3,2,1,0:T(8,128)(2,1)}, u32[]{:S(2)}) copy-start(bf16[2,2,384,1024]{3,2,1,0:T(8,128)(2,1)} %multiply_convert_fusion.4) | copy-start | bytes 9437188
  534.3 7.4 %copy-start.49 = (bf16[1024,4096]{1,0:T(8,128)(2,1)S(1)}, bf16[1024,4096]{1,0:T(8,128)(2,1)}, u32[]{:S(2)}) copy-start(bf16[1024,4096]{1,0:T(8,128)(2,1)} %all-gather.8.cloned.1.call-done) | copy-start | bytes 25165828
  543.5 3.5 collective-permute-start.11
  550.8 3.5 collective-permute-start.13
  559.2 3.9 collective-permute-start.15
  559.6 20.4 %collective-permute-start.10 = (bf16[384,1024]{1,0:T(8,128)(2,1)S(1)}, bf16[384,1024]{1,0:T(8,128)(2,1)S(1)}, u32[]{:S(2)}, u32[]{:S(2)}) collective-permute-start(bf16[384,1024]{1,0:T(8,128)(2,1)S(1)} %fusion.58), channel_id=1, source_target_pairs={{0,2},{2,0},{1,3},{3,1},{4,6},{6,4},{5,7},{7,5},{8,10},{10,8},{9,1... | collective-permute-start | bytes 2359304 | tf_op jit(solution)/shard_map/ppermute | solution.py:127
  561.1 18.9 %copy-start.8 = (f32[2,384,1024]{2,1,0:T(8,128)S(1)}, f32[2,384,1024]{2,1,0:T(8,128)}, u32[]{:S(2)}) copy-start(f32[2,384,1024]{2,1,0:T(8,128)} %copy-done.7) | copy-start | bytes 9437188
  561.1 35.8 %collective-permute-start.12 = (bf16[384,1024]{1,0:T(8,128)(2,1)S(1)}, bf16[384,1024]{1,0:T(8,128)(2,1)S(1)}, u32[]{:S(2)}, u32[]{:S(2)}) collective-permute-start(bf16[384,1024]{1,0:T(8,128)(2,1)S(1)} %fusion.59), channel_id=1, source_target_pairs={{0,2},{2,0},{1,3},{3,1},{4,6},{6,4},{5,7},{7,5},{8,10},{10,8},{9,1... | collective-permute-start | bytes 2359304 | tf_op jit(solution)/shard_map/ppermute | solution.py:127
  561.6 52.1 %collective-permute-start.14 = (bf16[384,1024]{1,0:T(8,128)(2,1)S(1)}, bf16[384,1024]{1,0:T(8,128)(2,1)S(1)}, u32[]{:S(2)}, u32[]{:S(2)}) collective-permute-start(bf16[384,1024]{1,0:T(8,128)(2,1)S(1)} %fusion.60), channel_id=1, source_target_pairs={{0,2},{2,0},{1,3},{3,1},{4,6},{6,4},{5,7},{7,5},{8,10},{10,8},{9,1... | collective-permute-start | bytes 2359304 | tf_op jit(solution)/shard_map/ppermute | solution.py:127
  567.4 29.4 %copy-start.10 = (f32[2,384,1024]{2,1,0:T(8,128)S(1)}, f32[2,384,1024]{2,1,0:T(8,128)}, u32[]{:S(2)}) copy-start(f32[2,384,1024]{2,1,0:T(8,128)} %copy-done.9) | copy-start | bytes 9437188
  567.4 46.3 %copy-start.12 = (f32[2,384,1024]{2,1,0:T(8,128)S(1)}, f32[2,384,1024]{2,1,0:T(8,128)}, u32[]{:S(2)}) copy-start(f32[2,384,1024]{2,1,0:T(8,128)} %copy-done.11) | copy-start | bytes 9437188
  567.6 62.2 %collective-permute-start.16 = (bf16[384,1024]{1,0:T(8,128)(2,1)S(1)}, bf16[384,1024]{1,0:T(8,128)(2,1)S(1)}, u32[]{:S(2)}, u32[]{:S(2)}) collective-permute-start(bf16[384,1024]{1,0:T(8,128)(2,1)S(1)} %fusion.61), channel_id=1, source_target_pairs={{0,2},{2,0},{1,3},{3,1},{4,6},{6,4},{5,7},{7,5},{8,10},{10,8},{9,1... | collective-permute-start | bytes 2359304 | tf_op jit(solution)/shard_map/ppermute | solution.py:127
  (13 other events, 46.1 us)
Sparse Core Ops, SparseCore 0:
  49.1 165.1 all-gather.3
  253.4 139.7 all-gather.5
  395.2 135.0 all-gather.7

commit v13 on v9

--- a/solution.py
+++ b/solution.py
@@ -207,11 +207,18 @@
     first_theirs = swap_half(
         first_cols(other * inner_local, (other * head_local) // per_group * state_width, other * head_local)
     )
-    first_local = ordered_pair(first_mine, first_theirs, half, 0)
-    first_full = lax.all_gather(first_local, "pair", axis=0, tiled=True)
-    proj_first = jnp.dot(normed, first_full, preferred_element_type=jnp.float32).astype(
-        jnp.bfloat16
-    )
+    mine_full = lax.all_gather(first_mine, "pair", axis=0, tiled=True)
+    theirs_full = lax.all_gather(first_theirs, "pair", axis=0, tiled=True)
+    block_rows = first_mine.shape[0]
+    by_block = normed.reshape(row_count, lax.axis_size("pair"), 2, block_rows)
+    normed_mine = lax.dynamic_index_in_dim(by_block, half, 2, keepdims=False)
+    normed_theirs = lax.dynamic_index_in_dim(by_block, 1 - half, 2, keepdims=False)
+    proj_first = (
+        jnp.dot(normed_mine.reshape(row_count, -1), mine_full, preferred_element_type=jnp.float32)
+        + jnp.dot(
+            normed_theirs.reshape(row_count, -1), theirs_full, preferred_element_type=jnp.float32
+        )
+    ).astype(jnp.bfloat16)
     conv_width = inner_local + 2 * state_cols
     conv_in = proj_first[:, :conv_width]
     proj_dt = proj_first[:, conv_width:]

time: 638 us -> 697 us (1.092)
  local copies, waits for them, and re-layouts: 86.5 us -> 186 us
  waiting for transfers between devices: 276 us -> 213 us
  other arithmetic: 114 us -> 128 us
    gather x2 -> x5, local copies, waits for them, and re-layouts: 8.62 us -> 86.3 us  [body(): jnp.take(arrived, owners, axis=0).reshape(own_rows, tokens.shape[1])]
    all_gather x1 -> x2, waiting for transfers between devices: 51.8 us -> 0.01 us  [the longest x1 0.01 us: body(): mine_full = lax.all_gather(first_mine, 'pair', axis=0, tiled=True)]
    all_gather x1, waiting for transfers between devices: 78.6 us -> 65.7 us  [body(): out_full = lax.all_gather(out_local, 'pair', axis=1, tiled=True)]
    dynamic_slice x0 -> x1, local copies, waits for them, and re-layouts: none -> 10.2 us  [body(): lax.dynamic_index_in_dim(by_block, 1 - half, 2, keepdims=False)]
    unnamed x118 -> x121, local copies, waits for them, and re-layouts: 9.28 us -> 18.5 us
    dot_general x1 -> x2, matrix products: 23.8 us -> 29.2 us  [the longest x1 14.7 us: body(): jnp.dot(normed_theirs.reshape(row_count, -1), theirs_full, preferred_elem...]
  transfers between devices with their start and end apart: 20 -> 21, of which waited for: 9 -> 7; matrix products, arithmetic and copies ran while one was open for 39% -> 56% of each run, Pallas kernels for 0% -> 0%
where the time goes in v13:
time: 697 us; the launch traced here: 687 us
  waiting for transfers between devices  213 us (31%)
  local copies, waits for them, and re-layouts  186 us (27%)
  other arithmetic  128 us (18%)
  matrix products  113 us (16%)
  starting transfers between devices  31.4 us (5%)
  between operations  15.2 us (2%)
    ppermute x8, waiting for transfers between devices, swap_half(): lax.ppermute(value, 'half', [(k, count - 1 - k) for k in range(count)])  147 us
    gather x5, local copies, waits for them, and re-layouts, body(): jnp.take(arrived, owners, axis=0).reshape(own_rows, tokens.shape[1])  86.3 us
    all_gather x1, waiting for transfers between devices, body(): out_full = lax.all_gather(out_local, 'pair', axis=1, tiled=True)  65.7 us
    dot_general x8, matrix products, body(): jnp.einsum('hrc,cd->hrd', rows, columns, preferred_element_type=jnp.float32)  27.2 us
    dot_general x1, matrix products, body(): jnp.dot(normed, z_full, preferred_element_type=jnp.float32)  25.4 us
    reshape x2, local copies, waits for them, and re-layouts, body(): (direct + state_gain[..., None] * from_state).reshape(row_count, inner_lo...  23 us
    convert_element_type x1, other arithmetic, conv_rows(): return jax.nn.silu(summed).astype(jnp.bfloat16)  21.7 us
    dot_general x3, matrix products, product_of(): return jnp.einsum(form, left, right, preferred_element_type=jnp.float32)  20.8 us
  transfers between devices with their start and end apart: 21, of which 7 were waited for; matrix products, arithmetic and copies ran while one was open for 56% of the time, Pallas kernels for 0%

profile of v13, /device:TPU:0, one launch (start us, length us, event | category | flops | bytes accessed | tf_op | source)
XLA Modules:
  0.0 687.0 jit_solution(9664421600400396940)
XLA Ops:
  6.5 2.3 fusion.127
  8.9 2.1 constant_dynamic-slice_fusion.13
  11.9 4.2 fusion.126
  16.1 3.7 constant_dynamic-slice_fusion.15
  21.0 8.6 %copy.206 = bf16[768,4096]{0,1:T(8,128)(2,1)} copy(bf16[768,4096]{1,0:T(8,128)(2,1)} %param.20) | data formatting | bytes 12582912 | tf_op args[0]
  29.6 4.8 fusion.3
  35.0 2.1 fusion.5
  37.0 2.6 copy-done.3
  39.7 2.0 constant_dynamic-slice_fusion.22
  41.7 2.8 collective-permute-start
  48.4 78.7 %collective-permute-done.2 = bf16[256,1296]{0,1:T(8,128)(2,1)S(1)} collective-permute-done((bf16[256,1296]{0,1:T(8,128)(2,1)S(1)}, bf16[256,1296]{0,1:T(8,128)(2,1)S(1)}, u32[]{:S(2)}, u32[]{:S(2)}) %collective-permute-start.2) | collective-permute-done | bytes 663584 | tf_op jit(solution)/shard_map/ppermute | solution.py:127
  128.2 2.2 copy.297
  130.7 2.3 reduce-window.30
  141.6 4.9 fusion.29
  146.5 4.5 gather_fusion
  151.0 4.6 gather_fusion.1
  155.5 7.1 %fusion.122 = (bf16[2,512,8,384]{3,2,1,0:T(8,128)(2,1)}, bf16[2,384,4096]{1,2,0:T(8,128)(2,1)S(1)}) fusion(bf16[2,384,2048]{1,2,0:T(8,128)(2,1)} %gather_fusion.1, bf16[2,384,2048]{1,2,0:T(8,128)(2,1)} %gather_fusion), kind=kLoop, calls=%fused_computation.267 | loop fusion | flops 12582912 | bytes 18874368
  162.6 59.2 %copy.239 = bf16[2,384,4096]{1,0,2:T(2,128)(2,1)} copy(bf16[2,384,4096]{1,2,0:T(8,128)(2,1)S(1)} %get-tuple-element.160) | data formatting | bytes 12582912 | tf_op jit(solution)/shard_map/jit(_take)/gather | solution.py:191
  221.8 14.6 %reshape.647 = bf16[768,8,2,256]{0,3,2,1:T(8,128)(2,1)} reshape(bf16[2,384,4096]{1,0,2:T(2,128)(2,1)} %copy.239) | data formatting | bytes 12582912 | tf_op jit(solution)/shard_map/jit(_take)/gather | solution.py:191
  236.4 3.4 broadcast_select_fusion.2
  239.8 11.6 %maximum_select_fusion = bf16[1536,8,2,256]{0,3,2,1:T(8,128)(2,1)} fusion(bf16[768,8,2,256]{0,3,2,1:T(8,128)(2,1)S(1)} %broadcast_select_fusion.2, bf16[768,8,2,256]{0,3,2,1:T(8,128)(2,1)} %bitcast.229, pred[]{:T(512)S(6)} %eq.207), kind=kLoop, calls=%fused_computation.16 | loop fusion | flops 56623104 | bytes 25165824 | tf_op jit(solution)/shard_map/jit(_where)/select_n | solution.py:131
  251.4 10.2 %constant_dynamic-slice_fusion.16 = (bf16[1536,8,1,256]{0,3,2,1:T(8,128)(2,1)}, bf16[1536,8,1,256]{0,3,2,1:T(8,128)(2,1)}) fusion(bf16[1536,8,2,256]{0,3,2,1:T(8,128)(2,1)} %maximum_select_fusion, s32[]{:T(128)S(6)} %select_n.308, s32[]{:T(128)S(6)} %select_n.303), kind=kLoop, calls=%fused_computation.188 | loop fusion | bytes 25165832 | tf_op jit(solution)/shard_map/jit(dynamic_index_in_dim)/dynamic_slice | solution.py:215
  261.6 14.5 %fusion.130 = f32[1536,1296]{0,1:T(8,128)} fusion(bf16[1536,2048]{0,1:T(8,128)(2,1)} %bitcast.236, bf16[2048,1296]{1,0:T(8,128)(2,1)} %all-gather.5.cloned.1.call-done), kind=kOutput, calls=%fused_computation.274 | convolution fusion | flops 8153726976 | bytes 19562496 | tf_op jit(solution)/shard_map/dot_general | solution.py:217
  276.2 14.7 %fusion.19 = bf16[1536,1296]{0,1:T(8,128)(2,1)} fusion(f32[1536,1296]{0,1:T(8,128)} %fusion.130, bf16[2048,1296]{0,1:T(8,128)(2,1)} %all-gather.7.cloned.1.call-done, bf16[1536,2048]{0,1:T(8,128)(2,1)} %bitcast.235), kind=kOutput, calls=%fused_computation.36 | convolution fusion | flops 8157708288 | bytes 23543808 | tf_op jit(solution)/shard_map/dot_general | solution.py:218
  295.8 9.5 %collective-permute-done.7 = bf16[256,1024]{1,0:T(8,128)(2,1)S(1)} collective-permute-done((bf16[256,1024]{1,0:T(8,128)(2,1)S(1)}, bf16[256,1024]{1,0:T(8,128)(2,1)S(1)}, u32[]{:S(2)}, u32[]{:S(2)}) %collective-permute-start.7) | collective-permute-done | bytes 524320 | tf_op jit(solution)/shard_map/ppermute | solution.py:127
  311.1 3.4 copy.267
  314.6 3.4 broadcast_select_fusion.1
  318.0 1.9 slice.165
  319.9 4.4 collective-permute-start.3
  325.4 3.6 reduce-window.21
  338.8 4.3 slice.160
  344.2 21.7 %multiply_convert_fusion.3 = bf16[1536,1280]{0,1:T(8,128)(2,1)S(1)} fusion(bf16[1536,1280]{0,1:T(8,128)(2,1)} %slice.160, bf16[3,1280]{0,1:T(8,128)(2,1)} %collective-permute-done.3, f32[1280]{0:T(1024)S(1)} %get-tuple-element.132, f32[1280]{0:T(1024)S(1)} %get-tuple-element.133, f32[1280]{0:T(1024)S(1)} %copy-done.18, f32[1280]{0:T(1024)S(1)} %get-tuple-element.131, ...), kind=kLoop, calls=%fused_computation.35 | loop fusion | flops 104202240 | bytes 7933952 | tf_op jit(solution)/shard_map/convert_element_type | solution.py:68
  366.0 2.2 copy-done.5
  368.4 6.7 fusion.124
  375.2 7.5 %reshape.601 = bf16[6,256,16,64]{1,0,3,2:T(8,128)(2,1)} reshape(bf16[1536,1024]{0,1:T(8,128)(2,1)} %get-tuple-element.163) | data formatting | bytes 6291456 | tf_op jit(solution)/shard_map/reshape.53
  384.0 3.2 multiply_convert_fusion.2
  387.2 2.7 add_bitcast_fusion
  389.9 19.9 %while.17 = (s32[]{:T(128)}, f32[1,16,64,128]{3,2,1,0:T(8,128)S(1)}, f32[1,16]{1,0:T(1,128)S(1)}, f32[6,1,16,64,128]{4,3,2,1,0:T(8,128)}, f32[6,1,16]{2,0,1:T(8,...) while((s32[]{:T(128)}, ...), condition=%wide.region_15.16_spmd.clone, body=%wide.region_14.15_spmd.clone.sunk | while | flops 524323 | bytes 2622649 | solution.py:315
  409.8 3.5 collective-permute-start.4
  413.3 4.8 collective-permute-start.6
  418.3 6.7 collective-permute-start.5
  426.5 5.3 fusion.71
  431.8 9.2 %reshape.623 = f32[6,256,1,16,64]{1,0,4,3,2:T(8,128)} reshape(f32[1536,1024]{0,1:T(8,128)} %get-tuple-element.164) | data formatting | bytes 12582912 | tf_op jit(solution)/shard_map/convert_element_type | solution.py:119
  442.5 5.3 fusion.30
  447.9 16.7 %fusion.25 = f32[6,256,1,16,64]{1,4,3,0,2:T(8,128)} fusion(f32[6,256,1,16,64]{1,0,4,3,2:T(8,128)} %reshape.623, f32[6,256,16,64]{1,3,2,0:T(8,128)S(1)} %fusion.30, f32[6,256,16,64]{1,3,2,0:T(8,128)S(1)} %copy-done.7, f32[6,256,16]{1,2,0:T(8,128)S(1)} %copy-done.16, f32[16]{0:T(128)S(1)} %copy-done.50, f32[6,256,16]{1,2,0:T(8,128)S(1)} %fusion.142, ...), kind=kOutput, calls=%fused_computation.46 | convolution fusion | flops 852492288 | bytes 30670912 | tf_op jit(solution)/shard_map/cghqs,csghp->cqghp/dot_general | solution.py:20
  464.6 11.4 %copy.240 = f32[6,256,1,16,64]{4,3,1,0,2:T(8,128)} copy(f32[6,256,1,16,64]{1,4,3,0,2:T(8,128)} %fusion.25) | data formatting | bytes 12582912 | tf_op jit(solution)/shard_map/reshape | solution.py:327
  476.0 11.6 %reshape.648 = f32[1536,1024]{1,0:T(8,128)} reshape(f32[6,256,1,16,64]{4,3,1,0,2:T(8,128)} %copy.240) | data formatting | bytes 12582912 | tf_op jit(solution)/shard_map/reshape | solution.py:327
  487.6 25.4 %multiply_reduce_fusion = (f32[1536]{0:T(1024)S(1)}, f32[1536,1024]{1,0:T(8,128)}) fusion(f32[1536,1024]{1,0:T(8,128)} %reshape.648, bf16[4096,1024]{1,0:T(8,128)(2,1)} %all-gather.9.cloned.1.call-done, bf16[768,4096]{0,1:T(8,128)(2,1)} %broadcast_select_fusion.1, bf16[768,4096]{0,1:T(8,128)(2,1)} %copy-done.3, pred[]{:T(512)S(6)} %eq.207), kind=kOutput, calls=%fused_computation.49 | convolution fusion | flops 12955678720 | bytes 33560576 | tf_op jit(solution)/shard_map/dot_general | solution.py:240
  513.1 3.5 broadcast_multiply_fusion
  516.6 2.6 multiply_convert_fusion.4
  519.3 65.7 %all-gather.11.cloned.1.call-done = bf16[1024,4096]{1,0:T(8,128)(2,1)} async-done(((bf16[1024,512]{1,0:T(8,128)(2,1)}), bf16[1024,4096]{1,0:T(8,128)(2,1)}) %all-gather.11.cloned.1.call-update) | async-done | bytes 8388624 | tf_op jit(solution)/shard_map/all_gather | solution.py:239
  585.0 5.1 convolution_convert_fusion.3
  590.1 4.6 convolution_convert_fusion.2
  595.2 3.9 convolution_convert_fusion.1
  599.2 4.0 convolution_convert_fusion
  603.9 4.1 convert_add_fusion.3
  609.7 1.8 convert_add_fusion.2
  612.3 1.8 convert_add_fusion.1
  615.8 1.8 convert_add_fusion
  618.3 10.3 %collective-permute-done.10 = bf16[384,1024]{1,0:T(8,128)(2,1)S(1)} collective-permute-done((bf16[384,1024]{1,0:T(8,128)(2,1)S(1)}, bf16[384,1024]{1,0:T(8,128)(2,1)S(1)}, u32[]{:S(2)}, u32[]{:S(2)}) %collective-permute-start.10) | collective-permute-done | bytes 786464 | tf_op jit(solution)/shard_map/ppermute | solution.py:127
  628.9 16.6 %collective-permute-done.12 = bf16[384,1024]{1,0:T(8,128)(2,1)S(1)} collective-permute-done((bf16[384,1024]{1,0:T(8,128)(2,1)S(1)}, bf16[384,1024]{1,0:T(8,128)(2,1)S(1)}, u32[]{:S(2)}, u32[]{:S(2)}) %collective-permute-start.12) | collective-permute-done | bytes 786464 | tf_op jit(solution)/shard_map/ppermute | solution.py:127
  645.8 16.6 %collective-permute-done.14 = bf16[384,1024]{1,0:T(8,128)(2,1)S(1)} collective-permute-done((bf16[384,1024]{1,0:T(8,128)(2,1)S(1)}, bf16[384,1024]{1,0:T(8,128)(2,1)S(1)}, u32[]{:S(2)}, u32[]{:S(2)}) %collective-permute-start.14) | collective-permute-done | bytes 786464 | tf_op jit(solution)/shard_map/ppermute | solution.py:127
  662.6 15.5 %collective-permute-done.16 = bf16[384,1024]{1,0:T(8,128)(2,1)S(1)} collective-permute-done((bf16[384,1024]{1,0:T(8,128)(2,1)S(1)}, bf16[384,1024]{1,0:T(8,128)(2,1)S(1)}, u32[]{:S(2)}, u32[]{:S(2)}) %collective-permute-start.16) | collective-permute-done | bytes 786464 | tf_op jit(solution)/shard_map/ppermute | solution.py:127
  678.4 1.8 pad_maximum_fusion.3
  (286 shorter events, 70.0 us)
Async XLA Ops:
  6.5 288.0 %copy-start = (f32[32,64,128]{2,1,0:T(8,128)S(1)}, f32[32,64,128]{2,1,0:T(8,128)}, u32[]{:S(2)}) copy-start(f32[32,64,128]{2,1,0:T(8,128)} %param.35) | copy-start | bytes 3145732
  6.5 5.4 copy-start.6
  6.5 255.1 %all-gather.5.cloned.1.call-start = ((), (), s32[]{:S(2)}) async-start(), calls=%async_computation | async-start | bytes 6488064 | tf_op jit(solution)/shard_map/all_gather | solution.py:210
  20.9 255.2 %all-gather.7.cloned.1.call-start = ((), (), s32[]{:S(2)}) async-start(), calls=%async_computation.1 | async-start | bytes 5971968 | tf_op jit(solution)/shard_map/all_gather | solution.py:211
  21.0 13.4 %copy-start.19 = (f32[4096]{0:T(1024)S(1)}, f32[4096]{0:T(1024)}, u32[]{:S(2)}) copy-start(f32[4096]{0:T(1024)} %param.21) | copy-start | bytes 49156
  39.6 6.2 copy-start.45
  39.6 6.2 copy-start.46
  39.7 8.8 %copy-start.20 = (bf16[4,2,256]{2,1,0:T(2,128)(2,1)S(1)}, bf16[4,2,256]{2,1,0:T(2,128)(2,1)}, u32[]{:S(2)}) copy-start(bf16[4,2,256]{2,1,0:T(2,128)(2,1)} %param.26) | copy-start | bytes 12292
  41.6 88.8 %copy-start.22 = (bf16[3,2,256]{2,1,0:T(2,128)(2,1)S(1)}, bf16[3,2,256]{2,1,0:T(2,128)(2,1)}, u32[]{:S(2)}) copy-start(bf16[3,2,256]{2,1,0:T(2,128)(2,1)} %param.37) | copy-start | bytes 9220
  41.6 88.9 %copy-start.47 = (f32[32]{0:T(128)S(1)}, f32[32]{0:T(128)}, u32[]{:S(2)}) copy-start(f32[32]{0:T(128)} %param.27) | copy-start | bytes 388
  41.6 89.0 %copy-start.48 = (f32[32]{0:T(128)S(1)}, f32[32]{0:T(128)}, u32[]{:S(2)}) copy-start(f32[32]{0:T(128)} %param.28) | copy-start | bytes 388
  41.7 92.4 %copy-start.49 = (f32[32]{0:T(128)S(1)}, f32[32]{0:T(128)}, u32[]{:S(2)}) copy-start(f32[32]{0:T(128)} %param.29) | copy-start | bytes 388
  41.7 99.2 %copy-start.41 = (bf16[4,2048]{1,0:T(4,128)(2,1)S(1)}, bf16[4,2048]{1,0:T(4,128)(2,1)}, u32[]{:S(2)}) copy-start(bf16[4,2048]{1,0:T(4,128)(2,1)} %param.25) | copy-start | bytes 49156
  41.7 99.2 %copy-start.42 = (bf16[3,2048]{1,0:T(4,128)(2,1)S(1)}, bf16[3,2048]{1,0:T(4,128)(2,1)}, u32[]{:S(2)}) copy-start(bf16[3,2048]{1,0:T(4,128)(2,1)} %param.36) | copy-start | bytes 36868
  41.7 86.3 %collective-permute-start = (bf16[384,4096]{0,1:T(8,128)(2,1)}, bf16[384,4096]{0,1:T(8,128)(2,1)}, u32[]{:S(2)}, u32[]{:S(2)}) collective-permute-start(bf16[384,4096]{0,1:T(8,128)(2,1)} %constant_dynamic-slice_fusion.22), channel_id=1, source_target_pairs={{0,2},{2,0},{1,3},{3,1},{4,6},{6,4},{5,7},{7,5},{8,10},{10,8},{9,1... | collective-permute-start | bytes 9437192 | tf_op jit(solution)/shard_map/ppermute | solution.py:127
  45.1 82.0 %collective-permute-start.2 = (bf16[256,1296]{0,1:T(8,128)(2,1)S(1)}, bf16[256,1296]{0,1:T(8,128)(2,1)S(1)}, u32[]{:S(2)}, u32[]{:S(2)}) collective-permute-start(bf16[256,1296]{0,1:T(8,128)(2,1)S(1)} %copy.214), channel_id=1, source_target_pairs={{0,2},{2,0},{1,3},{3,1},{4,6},{6,4},{5,7},{7,5},{8,10},{10,8},{9,1... | collective-permute-start | bytes 1990664 | tf_op jit(solution)/shard_map/ppermute | solution.py:127
  128.0 359.6 %all-gather.9.cloned.1.call-start = ((), (), s32[]{:S(2)}) async-start(), calls=%async_computation.2 | async-start | bytes 9437184 | tf_op jit(solution)/shard_map/all_gather | solution.py:238
  128.0 13.6 %collective-permute-start.1 = (bf16[384,4096]{0,1:T(8,128)(2,1)}, bf16[384,4096]{0,1:T(8,128)(2,1)}, u32[]{:S(2)}, u32[]{:S(2)}) collective-permute-start(bf16[384,4096]{0,1:T(8,128)(2,1)} %collective-permute-done), channel_id=1, source_target_pairs={{0,1},{1,0},{2,3},{3,2},{4,5},{5,4},{6,7},{7,6},{8,9},{9,8},{10,11... | collective-permute-start | bytes 9437192 | tf_op jit(solution)/shard_map/ppermute | solution.py:186
  130.7 194.6 %copy-start.44 = (f32[16]{0:T(128)}, f32[16]{0:T(128)S(1)}, u32[]{:S(2)}) copy-start(f32[16]{0:T(128)S(1)} %dynamic_slice.173) | copy-start | bytes 196
  290.9 14.4 %collective-permute-start.7 = (bf16[256,1024]{1,0:T(8,128)(2,1)S(1)}, bf16[256,1024]{1,0:T(8,128)(2,1)S(1)}, u32[]{:S(2)}, u32[]{:S(2)}) collective-permute-start(bf16[256,1024]{1,0:T(8,128)(2,1)S(1)} %get-tuple-element.172), channel_id=1, source_target_pairs={{0,2},{2,0},{1,3},{3,1},{4,6},{6,4},{5,7},{7,5},{8,10},{10,8},{9,1... | collective-permute-start | bytes 1572872 | tf_op jit(solution)/shard_map/ppermute | solution.py:127
  306.8 278.2 %all-gather.11.cloned.1.call-start = ((), (), s32[]{:S(2)}) async-start(), calls=%async_computation.3 | async-start | bytes 9437184 | tf_op jit(solution)/shard_map/all_gather | solution.py:239
  314.6 15.9 %copy-start.11 = (bf16[2048,256]{1,0:T(8,128)(2,1)S(1)}, bf16[2048,256]{1,0:T(8,128)(2,1)}, u32[]{:S(2)}) copy-start(bf16[2048,256]{1,0:T(8,128)(2,1)} %param.31) | copy-start | bytes 3145732
  319.9 24.2 %collective-permute-start.3 = (bf16[3,1280]{0,1:T(8,128)(2,1)}, bf16[3,1280]{0,1:T(8,128)(2,1)}, u32[]{:S(2)}, u32[]{:S(2)}) collective-permute-start(bf16[3,1280]{0,1:T(8,128)(2,1)} %slice.165), channel_id=1, source_target_pairs={{0,4},{4,8},{8,12},{12,16},{16,20},{20,24},{24,28},{1,5},{5,9},{9,... | collective-permute-start | bytes 23048 | tf_op jit(solution)/shard_map/ppermute | solution.py:15
  331.3 12.8 %copy-start.18 = (f32[1280]{0:T(1024)S(1)}, f32[1280]{0:T(1024)}, u32[]{:S(2)}) copy-start(f32[1280]{0:T(1024)} %get-tuple-element.134) | copy-start | bytes 15364
  331.3 12.8 %copy-start.23 = (pred[1536]{0:T(1024)(128)(4,1)S(1)}, pred[1536]{0:T(1024)(128)(4,1)}, u32[]{:S(2)}) copy-start(pred[1536]{0:T(1024)(128)(4,1)} %get-tuple-element.187) | copy-start | bytes 4612
  331.3 12.8 %copy-start.24 = (pred[1536]{0:T(1024)(128)(4,1)S(1)}, pred[1536]{0:T(1024)(128)(4,1)}, u32[]{:S(2)}) copy-start(pred[1536]{0:T(1024)(128)(4,1)} %get-tuple-element.188) | copy-start | bytes 4612
  331.3 12.8 %copy-start.25 = (pred[1536]{0:T(1024)(128)(4,1)S(1)}, pred[1536]{0:T(1024)(128)(4,1)}, u32[]{:S(2)}) copy-start(pred[1536]{0:T(1024)(128)(4,1)} %get-tuple-element.189) | copy-start | bytes 4612
  331.3 12.8 %copy-start.26 = (pred[1536]{0:T(1024)(128)(4,1)S(1)}, pred[1536]{0:T(1024)(128)(4,1)}, u32[]{:S(2)}) copy-start(pred[1536]{0:T(1024)(128)(4,1)} %get-tuple-element.190) | copy-start | bytes 4612
  331.3 12.8 %copy-start.27 = (pred[1536]{0:T(1024)(128)(4,1)S(1)}, pred[1536]{0:T(1024)(128)(4,1)}, u32[]{:S(2)}) copy-start(pred[1536]{0:T(1024)(128)(4,1)} %get-tuple-element.197) | copy-start | bytes 4612
  331.3 12.8 %copy-start.28 = (pred[1536]{0:T(1024)(128)(4,1)S(1)}, pred[1536]{0:T(1024)(128)(4,1)}, u32[]{:S(2)}) copy-start(pred[1536]{0:T(1024)(128)(4,1)} %get-tuple-element.198) | copy-start | bytes 4612
  331.3 12.8 %copy-start.29 = (pred[1536]{0:T(1024)(128)(4,1)S(1)}, pred[1536]{0:T(1024)(128)(4,1)}, u32[]{:S(2)}) copy-start(pred[1536]{0:T(1024)(128)(4,1)} %get-tuple-element.199) | copy-start | bytes 4612
  331.3 12.8 %copy-start.30 = (pred[1536]{0:T(1024)(128)(4,1)S(1)}, pred[1536]{0:T(1024)(128)(4,1)}, u32[]{:S(2)}) copy-start(pred[1536]{0:T(1024)(128)(4,1)} %get-tuple-element.200) | copy-start | bytes 4612
  331.4 12.8 %copy-start.31 = (pred[1536]{0:T(1024)(128)(4,1)S(1)}, pred[1536]{0:T(1024)(128)(4,1)}, u32[]{:S(2)}) copy-start(pred[1536]{0:T(1024)(128)(4,1)} %get-tuple-element.209) | copy-start | bytes 4612
  331.4 12.8 %copy-start.32 = (pred[1536]{0:T(1024)(128)(4,1)S(1)}, pred[1536]{0:T(1024)(128)(4,1)}, u32[]{:S(2)}) copy-start(pred[1536]{0:T(1024)(128)(4,1)} %get-tuple-element.210) | copy-start | bytes 4612
  331.4 12.8 %copy-start.33 = (pred[1536]{0:T(1024)(128)(4,1)S(1)}, pred[1536]{0:T(1024)(128)(4,1)}, u32[]{:S(2)}) copy-start(pred[1536]{0:T(1024)(128)(4,1)} %get-tuple-element.211) | copy-start | bytes 4612
  331.4 12.8 %copy-start.34 = (pred[1536]{0:T(1024)(128)(4,1)S(1)}, pred[1536]{0:T(1024)(128)(4,1)}, u32[]{:S(2)}) copy-start(pred[1536]{0:T(1024)(128)(4,1)} %get-tuple-element.212) | copy-start | bytes 4612
  331.4 12.8 %copy-start.35 = (pred[1536]{0:T(1024)(128)(4,1)S(1)}, pred[1536]{0:T(1024)(128)(4,1)}, u32[]{:S(2)}) copy-start(pred[1536]{0:T(1024)(128)(4,1)} %get-tuple-element.213) | copy-start | bytes 4612
  331.4 12.8 %copy-start.36 = (pred[1536]{0:T(1024)(128)(4,1)S(1)}, pred[1536]{0:T(1024)(128)(4,1)}, u32[]{:S(2)}) copy-start(pred[1536]{0:T(1024)(128)(4,1)} %get-tuple-element.214) | copy-start | bytes 4612
  331.4 12.8 %copy-start.37 = (pred[1536]{0:T(1024)(128)(4,1)S(1)}, pred[1536]{0:T(1024)(128)(4,1)}, u32[]{:S(2)}) copy-start(pred[1536]{0:T(1024)(128)(4,1)} %get-tuple-element.215) | copy-start | bytes 4612
  331.4 12.8 %copy-start.38 = (pred[1536]{0:T(1024)(128)(4,1)S(1)}, pred[1536]{0:T(1024)(128)(4,1)}, u32[]{:S(2)}) copy-start(pred[1536]{0:T(1024)(128)(4,1)} %get-tuple-element.216) | copy-start | bytes 4612
  331.4 12.8 %copy-start.39 = (pred[1536]{0:T(1024)(128)(4,1)S(1)}, pred[1536]{0:T(1024)(128)(4,1)}, u32[]{:S(2)}) copy-start(pred[1536]{0:T(1024)(128)(4,1)} %broadcast_compare_fusion.1) | copy-start | bytes 4612
  331.4 51.3 %collective-permute-start.8 = (bf16[1024,256]{1,0:T(8,128)(2,1)}, bf16[1024,256]{1,0:T(8,128)(2,1)S(1)}, u32[]{:S(2)}, u32[]{:S(2)}) collective-permute-start(bf16[1024,256]{1,0:T(8,128)(2,1)} %get-tuple-element.174), channel_id=1, source_target_pairs={{0,2},{2,0},{1,3},{3,1},{4,6},{6,4},{5,7},{7,5},{8,10},{10,8},{9,1... | collective-permute-start | bytes 1572872 | tf_op jit(solution)/shard_map/ppermute | solution.py:127
  409.8 31.2 %collective-permute-start.4 = (f32[1,16,64,128]{3,2,1,0:T(8,128)S(1)}, f32[1,16,64,128]{3,2,1,0:T(8,128)}, u32[]{:S(2)}, u32[]{:S(2)}) collective-permute-start(f32[1,16,64,128]{3,2,1,0:T(8,128)S(1)} %get-tuple-element.48), channel_id=1, source_target_pairs={{0,4},{4,8},{8,12},{12,16},{16,20},{20,24},{24,28},{1,5},{5,9},{9,... | collective-permute-start | bytes 1572872 | tf_op jit(solution)/shard_map/ppermute | solution.py:15
  413.3 27.7 %collective-permute-start.6 = (f32[1,16,64,128]{3,2,1,0:T(8,128)S(1)}, f32[1,16,64,128]{3,2,1,0:T(8,128)}, u32[]{:S(2)}, u32[]{:S(2)}) collective-permute-start(f32[1,16,64,128]{3,2,1,0:T(8,128)S(1)} %get-tuple-element.48), channel_id=1, source_target_pairs={{0,8},{4,12},{8,16},{12,20},{16,24},{20,28},{1,9},{5,13},{9,17},{1... | collective-permute-start | bytes 1572872 | tf_op jit(solution)/shard_map/ppermute | solution.py:15
  418.3 22.7 %collective-permute-start.5 = (f32[1,16]{1,0:T(1,128)S(1)}, f32[1,16]{1,0:T(1,128)S(1)}, u32[]{:S(2)}, u32[]{:S(2)}) collective-permute-start(f32[1,16]{1,0:T(1,128)S(1)} %get-tuple-element.49), channel_id=1, source_target_pairs={{0,4},{4,8},{8,12},{12,16},{16,20},{20,24},{24,28},{1,5},{5,9},{9,... | collective-permute-start | bytes 200 | tf_op jit(solution)/shard_map/ppermute | solution.py:15
  431.8 16.1 %copy-start.10 = (f32[6,256,256]{2,1,0:T(8,128)S(1)}, f32[6,256,256]{2,1,0:T(8,128)}, u32[]{:S(2)}) copy-start(f32[6,256,256]{2,1,0:T(8,128)} %fusion.131) | copy-start | bytes 4718596
  441.0 6.9 %copy-start.7 = (f32[6,256,16,64]{1,3,2,0:T(8,128)S(1)}, f32[6,256,16,64]{1,3,2,0:T(8,128)}, u32[]{:S(2)}) copy-start(f32[6,256,16,64]{1,3,2,0:T(8,128)} %fusion.71) | copy-start | bytes 18874372
  442.4 5.4 copy-start.4
  442.5 5.4 copy-start.14
  442.5 5.4 copy-start.15
  442.5 5.4 copy-start.16
  442.5 5.4 copy-start.17
  442.5 5.4 copy-start.50
  590.1 13.8 %collective-permute-start.9 = (bf16[2,384,1024]{2,1,0:T(8,128)(2,1)}, bf16[2,384,1024]{2,1,0:T(8,128)(2,1)}, u32[]{:S(2)}, u32[]{:S(2)}) collective-permute-start(bf16[2,384,1024]{2,1,0:T(8,128)(2,1)} %convolution_convert_fusion.3), channel_id=1, source_target_pairs={{0,1},{1,0},{2,3},{3,2},{4,5},{5,4},{6,7},{7,6},{8,9},{9,8},{10,11... | collective-permute-start | bytes 4718600 | tf_op jit(solution)/shard_map/ppermute | solution.py:349
  594.7 15.0 %collective-permute-start.11 = (bf16[2,384,1024]{2,1,0:T(8,128)(2,1)}, bf16[2,384,1024]{2,1,0:T(8,128)(2,1)S(1)}, u32[]{:S(2)}, u32[]{:S(2)}) collective-permute-start(bf16[2,384,1024]{2,1,0:T(8,128)(2,1)} %convolution_convert_fusion.2), channel_id=1, source_target_pairs={{0,1},{1,0},{2,3},{3,2},{4,5},{5,4},{6,7},{7,6},{8,9},{9,8},{10,11... | collective-permute-start | bytes 4718600 | tf_op jit(solution)/shard_map/ppermute | solution.py:349
  599.1 13.2 %collective-permute-start.13 = (bf16[2,384,1024]{2,1,0:T(8,128)(2,1)S(1)}, bf16[2,384,1024]{2,1,0:T(8,128)(2,1)S(1)}, u32[]{:S(2)}, u32[]{:S(2)}) collective-permute-start(bf16[2,384,1024]{2,1,0:T(8,128)(2,1)S(1)} %convolution_convert_fusion.1), channel_id=1, source_target_pairs={{0,1},{1,0},{2,3},{3,2},{4,5},{5,4},{6,7},{7,6},{8,9},{9,8},{10,11... | collective-permute-start | bytes 4718600 | tf_op jit(solution)/shard_map/ppermute | solution.py:349
  599.2 10.5 %slice-start = ((s8[8388608]{0:T(1024)(128)(4,1)}), s8[4194304]{0:T(1024)(128)(4,1)S(1)}, s32[]{:S(2)}) async-start(s8[8388608]{0:T(1024)(128)(4,1)} %bitcast.258), calls=%async_computation.5 | async-start | bytes 8388608
  603.2 6.5 slice-start.1
  603.2 12.6 %collective-permute-start.15 = (bf16[2,384,1024]{2,1,0:T(8,128)(2,1)S(1)}, bf16[2,384,1024]{2,1,0:T(8,128)(2,1)S(1)}, u32[]{:S(2)}, u32[]{:S(2)}) collective-permute-start(bf16[2,384,1024]{2,1,0:T(8,128)(2,1)S(1)} %convolution_convert_fusion), channel_id=1, source_target_pairs={{0,1},{1,0},{2,3},{3,2},{4,5},{5,4},{6,7},{7,6},{8,9},{9,8},{10,11... | collective-permute-start | bytes 4718600 | tf_op jit(solution)/shard_map/ppermute | solution.py:349
  608.2 20.5 %collective-permute-start.10 = (bf16[384,1024]{1,0:T(8,128)(2,1)S(1)}, bf16[384,1024]{1,0:T(8,128)(2,1)S(1)}, u32[]{:S(2)}, u32[]{:S(2)}) collective-permute-start(bf16[384,1024]{1,0:T(8,128)(2,1)S(1)} %fusion.67), channel_id=1, source_target_pairs={{0,2},{2,0},{1,3},{3,1},{4,6},{6,4},{5,7},{7,5},{8,10},{10,8},{9,1... | collective-permute-start | bytes 2359304 | tf_op jit(solution)/shard_map/ppermute | solution.py:127
  611.7 33.8 %collective-permute-start.12 = (bf16[384,1024]{1,0:T(8,128)(2,1)S(1)}, bf16[384,1024]{1,0:T(8,128)(2,1)S(1)}, u32[]{:S(2)}, u32[]{:S(2)}) collective-permute-start(bf16[384,1024]{1,0:T(8,128)(2,1)S(1)} %fusion.68), channel_id=1, source_target_pairs={{0,2},{2,0},{1,3},{3,1},{4,6},{6,4},{5,7},{7,5},{8,10},{10,8},{9,1... | collective-permute-start | bytes 2359304 | tf_op jit(solution)/shard_map/ppermute | solution.py:127
  614.3 48.1 %collective-permute-start.14 = (bf16[384,1024]{1,0:T(8,128)(2,1)S(1)}, bf16[384,1024]{1,0:T(8,128)(2,1)S(1)}, u32[]{:S(2)}, u32[]{:S(2)}) collective-permute-start(bf16[384,1024]{1,0:T(8,128)(2,1)S(1)} %fusion.69), channel_id=1, source_target_pairs={{0,2},{2,0},{1,3},{3,1},{4,6},{6,4},{5,7},{7,5},{8,10},{10,8},{9,1... | collective-permute-start | bytes 2359304 | tf_op jit(solution)/shard_map/ppermute | solution.py:127
  617.7 60.4 %collective-permute-start.16 = (bf16[384,1024]{1,0:T(8,128)(2,1)S(1)}, bf16[384,1024]{1,0:T(8,128)(2,1)S(1)}, u32[]{:S(2)}, u32[]{:S(2)}) collective-permute-start(bf16[384,1024]{1,0:T(8,128)(2,1)S(1)} %fusion.70), channel_id=1, source_target_pairs={{0,2},{2,0},{1,3},{3,1},{4,6},{6,4},{5,7},{7,5},{8,10},{10,8},{9,1... | collective-permute-start | bytes 2359304 | tf_op jit(solution)/shard_map/ppermute | solution.py:127
  662.4 17.9 %copy-start.1 = (f32[32,64,128]{2,1,0:T(8,128)S(1)}, f32[32,64,128]{2,1,0:T(8,128)}, u32[]{:S(2)}) copy-start(f32[32,64,128]{2,1,0:T(8,128)} %param.35) | copy-start | bytes 3145732
  (11 other events, 37.9 us)
Sparse Core Ops, SparseCore 0:
  21.0 95.3 all-gather.4
  128.1 89.4 all-gather.6
  307.0 141.3 all-gather.8
  450.2 134.7 all-gather.10

commit v14 on v9

--- a/solution.py
+++ b/solution.py
@@ -329,7 +329,7 @@
     ).astype(jnp.bfloat16)
     piece = own_rows // core_count
     by_owner = normed_y.reshape(2, core_count, piece, inner_local)
-    chunk_count = 4
+    chunk_count = 8
     chunk = out_full.shape[1] // chunk_count
     results = []
     for index in range(chunk_count):

time: 638 us -> 639 us (level)
  starting transfers between devices: 31.2 us -> 38.7 us
    ppermute x8 -> x12, starting transfers between devices: 12.2 us -> 17.2 us  [swap_half(): lax.ppermute(value, 'half', [(k, count - 1 - k) for k in range(count)])]
    dot_general x8 -> x16, matrix products: 24.5 us -> 20.4 us  [body(): jnp.einsum('hrc,cd->hrd', rows, columns, preferred_element_type=jnp.float32)]
    ppermute x8 -> x12, waiting for transfers between devices: 145 us -> 144 us  [swap_half(): lax.ppermute(value, 'half', [(k, count - 1 - k) for k in range(count)])]
  transfers between devices with their start and end apart: 20 -> 28, of which waited for: 9 -> 9; matrix products, arithmetic and copies ran while one was open for 39% -> 39% of each run, Pallas kernels for 0% -> 0%
where the time goes in v14:
time: 639 us; the launch traced here: 630 us
  waiting for transfers between devices  274 us (43%)
  other arithmetic  111 us (17%)
  matrix products  103 us (16%)
  local copies, waits for them, and re-layouts  88 us (14%)
  starting transfers between devices  38.7 us (6%)
  between operations  15.8 us (2%)
    ppermute x12, waiting for transfers between devices, swap_half(): lax.ppermute(value, 'half', [(k, count - 1 - k) for k in range(count)])  144 us
    all_gather x1, waiting for transfers between devices, body(): out_full = lax.all_gather(out_local, 'pair', axis=1, tiled=True)  77.8 us
    all_gather x1, waiting for transfers between devices, body(): first_full = lax.all_gather(first_local, 'pair', axis=0, tiled=True)  51.9 us
    dot_general x1, matrix products, body(): jnp.dot(normed, z_full, preferred_element_type=jnp.float32)  27 us
    dot_general x1, matrix products, body(): jnp.dot(normed, first_full, preferred_element_type=jnp.float32)  23.8 us
    reshape x2, local copies, waits for them, and re-layouts, body(): (direct + state_gain[..., None] * from_state).reshape(row_count, inner_lo...  23.1 us
    convert_element_type x1, other arithmetic, conv_rows(): return jax.nn.silu(summed).astype(jnp.bfloat16)  21.8 us
    dot_general x3, matrix products, product_of(): return jnp.einsum(form, left, right, preferred_element_type=jnp.float32)  20.8 us
  transfers between devices with their start and end apart: 28, of which 9 were waited for; matrix products, arithmetic and copies ran while one was open for 39% of the time, Pallas kernels for 0%

profile of v14, /device:TPU:0, one launch (start us, length us, event | category | flops | bytes accessed | tf_op | source)
XLA Modules:
  0.0 630.3 jit_solution(16596327570275416113)
XLA Ops:
  6.5 1.6 fusion.210
  11.4 6.9 %fusion.209 = (bf16[256,1,2048]{2,1,0:T(2,128)(2,1)}, bf16[256,1,2048]{2,1,0:T(2,128)(2,1)}) fusion(bf16[256,2,2048]{2,1,0:T(2,128)(2,1)} %param.22), kind=kLoop, calls=%fused_computation.329 | loop fusion | bytes 4194304 | tf_op jit(solution)/shard_map/slice | solution.py:197
  18.3 3.7 constant_dynamic-slice_fusion.19
  24.2 2.9 collective-permute-start.2
  29.0 13.3 %collective-permute-done.2 = bf16[256,1296]{0,1:T(8,128)(2,1)S(1)} collective-permute-done((bf16[256,1296]{0,1:T(8,128)(2,1)}, bf16[256,1296]{0,1:T(8,128)(2,1)S(1)}, u32[]{:S(2)}, u32[]{:S(2)}) %collective-permute-start.2) | collective-permute-done | bytes 663584 | tf_op jit(solution)/shard_map/ppermute | solution.py:127
  42.6 6.1 maximum_select_fusion.3
  49.0 4.1 fusion.3
  53.1 5.3 fusion.5
  58.8 2.6 copy-done.4
  61.4 1.8 collective-permute-start
  63.1 67.7 %collective-permute-done = bf16[384,4096]{1,0:T(8,128)(2,1)} collective-permute-done((bf16[384,4096]{1,0:T(8,128)(2,1)S(1)}, bf16[384,4096]{1,0:T(8,128)(2,1)}, u32[]{:S(2)}, u32[]{:S(2)}) %collective-permute-start) | collective-permute-done | bytes 3145760 | tf_op jit(solution)/shard_map/ppermute | solution.py:127
  135.4 1.8 reduce-window.30
  138.9 2.2 copy.282
  141.2 5.0 fusion.20
  146.2 4.3 gather_fusion
  150.5 4.3 gather_fusion.1
  154.8 3.6 pad_maximum_fusion
  158.4 3.7 bitcast_select_fusion
  162.2 51.9 %all-gather.4.cloned.1.call-done = bf16[4096,1296]{1,0:T(8,128)(2,1)} async-done(((bf16[512,1296]{1,0:T(8,128)(2,1)}), bf16[4096,1296]{1,0:T(8,128)(2,1)}) %all-gather.4.cloned.1.call-update) | async-done | bytes 10616848 | tf_op jit(solution)/shard_map/all_gather | solution.py:211
  214.1 23.8 %convolution_convert_fusion = bf16[1536,1296]{0,1:T(8,128)(2,1)} fusion(bf16[4096,1296]{1,0:T(8,128)(2,1)} %all-gather.4.cloned.1.call-done, bf16[768,4096]{1,0:T(8,128)(2,1)} %bitcast_select_fusion, bf16[768,4096]{1,0:T(8,128)(2,1)} %copy-done.4, pred[]{:T(512)S(6)} %eq.216), kind=kOutput, calls=%fused_computation.27 | convolution fusion | flops 16366067712 | bytes 27181056 | tf_op jit(solution)/shard_map/dot_general | solution.py:212
  238.0 1.5 collective-permute-start.7
  245.4 5.9 collective-permute-done.7
  251.3 1.5 maximum_select_fusion.4
  252.9 1.3 fusion.169
  261.2 1.9 slice.181
  263.1 3.2 collective-permute-start.3
  268.1 3.9 reduce-window.21
  272.7 1.3 select_bitcast_fusion
  277.9 4.3 slice.176
  282.6 1.5 collective-permute-start.8
  285.0 21.8 %multiply_convert_fusion.3 = bf16[1536,1280]{0,1:T(8,128)(2,1)S(1)} fusion(bf16[1536,1280]{0,1:T(8,128)(2,1)} %slice.176, bf16[3,1280]{0,1:T(8,128)(2,1)} %collective-permute-done.3, f32[1280]{0:T(1024)S(1)} %copy-done.17, f32[1280]{0:T(1024)S(1)} %copy-done.18, f32[1280]{0:T(1024)S(1)} %copy-done.19, f32[1280]{0:T(1024)S(1)} %copy-done.16, ...), kind=kLoop, calls=%fused_computation.26 | loop fusion | flops 104202240 | bytes 7933952 | tf_op jit(solution)/shard_map/convert_element_type | solution.py:68
  306.9 5.3 fusion.207
  314.8 7.5 %reshape.584 = bf16[6,256,16,64]{1,0,3,2:T(8,128)(2,1)} reshape(bf16[1536,1024]{0,1:T(8,128)(2,1)} %get-tuple-element.159) | data formatting | bytes 6291456 | tf_op jit(solution)/shard_map/reshape.48
  322.4 3.2 multiply_convert_fusion.2
  325.6 2.7 add_bitcast_fusion
  328.3 12.5 %while.17 = (s32[]{:T(128)}, f32[1,16,64,128]{3,2,1,0:T(8,128)S(1)}, f32[1,16]{1,0:T(1,128)S(1)}, f32[6,1,16,64,128]{4,3,2,1,0:T(8,128)}, f32[6,1,16]{2,0,1:T(8,...) while((s32[]{:T(128)}, ...), condition=%wide.region_15.16_spmd.clone, body=%wide.region_14.15_spmd.clone.sunk | while | flops 524323 | bytes 2622649 | solution.py:308
  340.8 2.3 collective-permute-start.4
  343.1 7.8 %collective-permute-start.6 = (f32[1,16,64,128]{3,2,1,0:T(8,128)S(1)}, f32[1,16,64,128]{3,2,1,0:T(8,128)}, u32[]{:S(2)}, u32[]{:S(2)}) collective-permute-start(f32[1,16,64,128]{3,2,1,0:T(8,128)S(1)} %get-tuple-element.48), channel_id=1, source_target_pairs={{0,8},{4,12},{8,16},{12,20},{16,24},{20,28},{1,9},{5,13},{9,17},{1... | collective-permute-start | bytes 1572872 | tf_op jit(solution)/shard_map/ppermute | solution.py:15
  351.2 5.3 collective-permute-start.5
  356.5 1.5 fusion.213
  358.0 5.3 fusion.114
  363.3 9.0 %reshape.606 = f32[6,256,1,16,64]{1,0,4,3,2:T(8,128)} reshape(f32[1536,1024]{0,1:T(8,128)} %get-tuple-element.160) | data formatting | bytes 12582912 | tf_op jit(solution)/shard_map/convert_element_type | solution.py:119
  372.3 1.5 add_bitcast_fusion.1
  373.8 5.3 fusion.21
  379.2 16.7 %fusion.17 = f32[6,256,1,16,64]{1,4,3,0,2:T(8,128)} fusion(f32[6,256,1,16,64]{1,0,4,3,2:T(8,128)} %reshape.606, f32[6,256,16,64]{1,3,2,0:T(8,128)S(1)} %fusion.21, f32[6,256,16,64]{1,3,2,0:T(8,128)S(1)} %copy-done.5, f32[6,256,16]{1,2,0:T(8,128)S(1)} %copy-done.11, f32[16]{0:T(128)S(1)} %copy-done.52, f32[6,256,16]{1,2,0:T(8,128)S(1)} %copy-done.10, ...), kind=kOutput, calls=%fused_computation.37 | convolution fusion | flops 852492288 | bytes 30670912 | tf_op jit(solution)/shard_map/cghqs,csghp->cqghp/dot_general | solution.py:20
  395.9 11.3 %copy.227 = f32[6,256,1,16,64]{4,3,1,0,2:T(8,128)} copy(f32[6,256,1,16,64]{1,4,3,0,2:T(8,128)} %fusion.17) | data formatting | bytes 12582912 | tf_op jit(solution)/shard_map/reshape | solution.py:320
  407.2 11.8 %reshape.634 = f32[1536,1024]{1,0:T(8,128)} reshape(f32[6,256,1,16,64]{4,3,1,0,2:T(8,128)} %copy.227) | data formatting | bytes 12582912 | tf_op jit(solution)/shard_map/reshape | solution.py:320
  419.0 27.0 %multiply_reduce_fusion = (f32[1536]{0:T(1024)S(1)}, f32[1536,1024]{1,0:T(8,128)}) fusion(f32[1536,1024]{1,0:T(8,128)} %reshape.634, bf16[4096,1024]{1,0:T(8,128)(2,1)} %all-gather.6.cloned.1.call-done, bf16[768,4096]{1,0:T(8,128)(2,1)} %bitcast_select_fusion, bf16[768,4096]{1,0:T(8,128)(2,1)} %copy-done.4, pred[]{:T(512)S(6)} %eq.216), kind=kOutput, calls=%fused_computation.41 | convolution fusion | flops 12955678720 | bytes 33560576 | tf_op jit(solution)/shard_map/dot_general | solution.py:233
  446.0 3.3 broadcast_multiply_fusion
  449.3 2.6 multiply_convert_fusion.4
  452.0 77.8 %all-gather.8.cloned.1.call-done = bf16[1024,4096]{1,0:T(8,128)(2,1)} async-done(((bf16[1024,512]{1,0:T(8,128)(2,1)}), bf16[1024,4096]{1,0:T(8,128)(2,1)}) %all-gather.8.cloned.1.call-update) | async-done | bytes 8388624 | tf_op jit(solution)/shard_map/all_gather | solution.py:232
  529.8 2.8 fusion.87
  532.7 2.4 fusion.84
  535.6 2.2 fusion.81
  547.9 1.5 collective-permute-start.24
  552.4 1.5 collective-permute-start.20
  556.6 1.5 collective-permute-start.10
  559.3 33.6 %collective-permute-done.10 = bf16[384,512]{1,0:T(8,128)(2,1)S(1)} collective-permute-done((bf16[384,512]{1,0:T(8,128)(2,1)S(1)}, bf16[384,512]{1,0:T(8,128)(2,1)S(1)}, u32[]{:S(2)}, u32[]{:S(2)}) %collective-permute-start.10) | collective-permute-done | bytes 393248 | tf_op jit(solution)/shard_map/ppermute | solution.py:127
  593.0 1.5 collective-permute-start.14
  595.3 9.7 %collective-permute-done.14 = bf16[384,512]{1,0:T(8,128)(2,1)S(1)} collective-permute-done((bf16[384,512]{1,0:T(8,128)(2,1)S(1)}, bf16[384,512]{1,0:T(8,128)(2,1)S(1)}, u32[]{:S(2)}, u32[]{:S(2)}) %collective-permute-start.14) | collective-permute-done | bytes 393248 | tf_op jit(solution)/shard_map/ppermute | solution.py:127
  605.0 1.5 collective-permute-start.18
  606.6 6.8 %collective-permute-done.16 = bf16[384,512]{1,0:T(8,128)(2,1)S(1)} collective-permute-done((bf16[384,512]{1,0:T(8,128)(2,1)S(1)}, bf16[384,512]{1,0:T(8,128)(2,1)S(1)}, u32[]{:S(2)}, u32[]{:S(2)}) %collective-permute-start.16) | collective-permute-done | bytes 393248 | tf_op jit(solution)/shard_map/ppermute | solution.py:127
  613.6 6.7 %collective-permute-done.18 = bf16[384,512]{1,0:T(8,128)(2,1)S(1)} collective-permute-done((bf16[384,512]{1,0:T(8,128)(2,1)S(1)}, bf16[384,512]{1,0:T(8,128)(2,1)S(1)}, u32[]{:S(2)}, u32[]{:S(2)}) %collective-permute-start.18) | collective-permute-done | bytes 393248 | tf_op jit(solution)/shard_map/ppermute | solution.py:127
  620.8 1.6 copy-done.13
  (306 shorter events, 68.7 us)
Async XLA Ops:
  6.5 251.2 %copy-start = (f32[32,64,128]{2,1,0:T(8,128)S(1)}, f32[32,64,128]{2,1,0:T(8,128)}, u32[]{:S(2)}) copy-start(f32[32,64,128]{2,1,0:T(8,128)} %param.35) | copy-start | bytes 3145732
  6.5 207.5 %all-gather.4.cloned.1.call-start = ((), (), s32[]{:S(2)}) async-start(), calls=%async_computation | async-start | bytes 12976128 | tf_op jit(solution)/shard_map/all_gather | solution.py:211
  24.2 18.1 %collective-permute-start.2 = (bf16[256,1296]{0,1:T(8,128)(2,1)}, bf16[256,1296]{0,1:T(8,128)(2,1)S(1)}, u32[]{:S(2)}, u32[]{:S(2)}) collective-permute-start(bf16[256,1296]{0,1:T(8,128)(2,1)} %copy.201), channel_id=1, source_target_pairs={{0,2},{2,0},{1,3},{3,1},{4,6},{6,4},{5,7},{7,5},{8,10},{10,8},{9,1... | collective-permute-start | bytes 1990664 | tf_op jit(solution)/shard_map/ppermute | solution.py:127
  48.8 370.2 %all-gather.6.cloned.1.call-start = ((), (), s32[]{:S(2)}) async-start(), calls=%async_computation.1 | async-start | bytes 9437184 | tf_op jit(solution)/shard_map/all_gather | solution.py:231
  58.5 73.0 %copy-start.47 = (s32[8]{0:T(128)S(1)}, s32[8]{0:T(128)}, u32[]{:S(2)}) copy-start(s32[8]{0:T(128)} %param.32) | copy-start | bytes 100
  58.5 73.0 %copy-start.48 = (s32[8]{0:T(128)S(1)}, s32[8]{0:T(128)}, u32[]{:S(2)}) copy-start(s32[8]{0:T(128)} %param.33) | copy-start | bytes 100
  58.5 75.6 %copy-start.22 = (bf16[4,2,256]{2,1,0:T(2,128)(2,1)S(1)}, bf16[4,2,256]{2,1,0:T(2,128)(2,1)}, u32[]{:S(2)}) copy-start(bf16[4,2,256]{2,1,0:T(2,128)(2,1)} %param.26) | copy-start | bytes 12292
  58.5 75.6 %copy-start.24 = (bf16[3,2,256]{2,1,0:T(2,128)(2,1)S(1)}, bf16[3,2,256]{2,1,0:T(2,128)(2,1)}, u32[]{:S(2)}) copy-start(bf16[3,2,256]{2,1,0:T(2,128)(2,1)} %param.37) | copy-start | bytes 9220
  58.5 75.7 %copy-start.49 = (f32[32]{0:T(128)S(1)}, f32[32]{0:T(128)}, u32[]{:S(2)}) copy-start(f32[32]{0:T(128)} %param.27) | copy-start | bytes 388
  58.5 76.2 %copy-start.50 = (f32[32]{0:T(128)S(1)}, f32[32]{0:T(128)}, u32[]{:S(2)}) copy-start(f32[32]{0:T(128)} %param.28) | copy-start | bytes 388
  58.6 79.7 %copy-start.51 = (f32[32]{0:T(128)S(1)}, f32[32]{0:T(128)}, u32[]{:S(2)}) copy-start(f32[32]{0:T(128)} %param.29) | copy-start | bytes 388
  61.4 69.4 %collective-permute-start = (bf16[384,4096]{1,0:T(8,128)(2,1)S(1)}, bf16[384,4096]{1,0:T(8,128)(2,1)}, u32[]{:S(2)}, u32[]{:S(2)}) collective-permute-start(bf16[384,4096]{1,0:T(8,128)(2,1)S(1)} %constant_dynamic-slice_fusion.20), channel_id=1, source_target_pairs={{0,2},{2,0},{1,3},{3,1},{4,6},{6,4},{5,7},{7,5},{8,10},{10,8},{9,1... | collective-permute-start | bytes 9437192 | tf_op jit(solution)/shard_map/ppermute | solution.py:127
  130.8 10.4 %collective-permute-start.1 = (bf16[384,4096]{1,0:T(8,128)(2,1)}, bf16[384,4096]{1,0:T(8,128)(2,1)}, u32[]{:S(2)}, u32[]{:S(2)}) collective-permute-start(bf16[384,4096]{1,0:T(8,128)(2,1)} %collective-permute-done), channel_id=1, source_target_pairs={{0,1},{1,0},{2,3},{3,2},{4,5},{5,4},{6,7},{7,6},{8,9},{9,8},{10,11... | collective-permute-start | bytes 9437192 | tf_op jit(solution)/shard_map/ppermute | solution.py:186
  237.9 17.7 %copy-start.44 = (bf16[4,2048]{1,0:T(4,128)(2,1)S(1)}, bf16[4,2048]{1,0:T(4,128)(2,1)}, u32[]{:S(2)}) copy-start(bf16[4,2048]{1,0:T(4,128)(2,1)} %param.25) | copy-start | bytes 49156
  237.9 17.7 %copy-start.45 = (bf16[3,2048]{1,0:T(4,128)(2,1)S(1)}, bf16[3,2048]{1,0:T(4,128)(2,1)}, u32[]{:S(2)}) copy-start(bf16[3,2048]{1,0:T(4,128)(2,1)} %param.36) | copy-start | bytes 36868
  238.0 13.3 %collective-permute-start.7 = (bf16[256,1024]{1,0:T(8,128)(2,1)S(1)}, bf16[256,1024]{1,0:T(8,128)(2,1)S(1)}, u32[]{:S(2)}, u32[]{:S(2)}) collective-permute-start(bf16[256,1024]{1,0:T(8,128)(2,1)S(1)} %get-tuple-element.168), channel_id=1, source_target_pairs={{0,2},{2,0},{1,3},{3,1},{4,6},{6,4},{5,7},{7,5},{8,10},{10,8},{9,1... | collective-permute-start | bytes 1572872 | tf_op jit(solution)/shard_map/ppermute | solution.py:127
  252.8 22.2 %copy-start.8 = (bf16[2048,256]{1,0:T(8,128)(2,1)S(1)}, bf16[2048,256]{1,0:T(8,128)(2,1)}, u32[]{:S(2)}) copy-start(bf16[2048,256]{1,0:T(8,128)(2,1)} %param.31) | copy-start | bytes 3145732
  252.9 276.9 %all-gather.8.cloned.1.call-start = ((), (), s32[]{:S(2)}) async-start(), calls=%async_computation.2 | async-start | bytes 9437184 | tf_op jit(solution)/shard_map/all_gather | solution.py:232
  257.8 16.4 %copy-start.25 = (pred[6,256]{1,0:T(8,128)(4,1)S(1)}, pred[6,256]{1,0:T(8,128)(4,1)}, u32[]{:S(2)}) copy-start(pred[6,256]{1,0:T(8,128)(4,1)} %get-tuple-element.203) | copy-start | bytes 4612
  263.1 21.7 %collective-permute-start.3 = (bf16[3,1280]{0,1:T(8,128)(2,1)}, bf16[3,1280]{0,1:T(8,128)(2,1)}, u32[]{:S(2)}, u32[]{:S(2)}) collective-permute-start(bf16[3,1280]{0,1:T(8,128)(2,1)} %slice.181), channel_id=1, source_target_pairs={{0,4},{4,8},{8,12},{12,16},{16,20},{20,24},{24,28},{1,5},{5,9},{9,... | collective-permute-start | bytes 23048 | tf_op jit(solution)/shard_map/ppermute | solution.py:15
  277.7 7.1 %copy-start.14 = (f32[1280]{0:T(1024)S(1)}, f32[1280]{0:T(1024)}, u32[]{:S(2)}) copy-start(f32[1280]{0:T(1024)} %get-tuple-element.129) | copy-start | bytes 15364
  277.7 7.1 %copy-start.15 = (f32[1280]{0:T(1024)S(1)}, f32[1280]{0:T(1024)}, u32[]{:S(2)}) copy-start(f32[1280]{0:T(1024)} %get-tuple-element.130) | copy-start | bytes 15364
  277.7 7.1 %copy-start.16 = (f32[1280]{0:T(1024)S(1)}, f32[1280]{0:T(1024)}, u32[]{:S(2)}) copy-start(f32[1280]{0:T(1024)} %get-tuple-element.131) | copy-start | bytes 15364
  277.7 7.1 %copy-start.17 = (f32[1280]{0:T(1024)S(1)}, f32[1280]{0:T(1024)}, u32[]{:S(2)}) copy-start(f32[1280]{0:T(1024)} %get-tuple-element.132) | copy-start | bytes 15364
  277.7 7.1 %copy-start.18 = (f32[1280]{0:T(1024)S(1)}, f32[1280]{0:T(1024)}, u32[]{:S(2)}) copy-start(f32[1280]{0:T(1024)} %get-tuple-element.133) | copy-start | bytes 15364
  277.7 7.1 %copy-start.19 = (f32[1280]{0:T(1024)S(1)}, f32[1280]{0:T(1024)}, u32[]{:S(2)}) copy-start(f32[1280]{0:T(1024)} %get-tuple-element.134) | copy-start | bytes 15364
  277.7 7.1 %copy-start.26 = (pred[1536]{0:T(1024)(128)(4,1)S(1)}, pred[1536]{0:T(1024)(128)(4,1)}, u32[]{:S(2)}) copy-start(pred[1536]{0:T(1024)(128)(4,1)} %get-tuple-element.183) | copy-start | bytes 4612
  277.7 7.1 %copy-start.27 = (pred[1536]{0:T(1024)(128)(4,1)S(1)}, pred[1536]{0:T(1024)(128)(4,1)}, u32[]{:S(2)}) copy-start(pred[1536]{0:T(1024)(128)(4,1)} %get-tuple-element.184) | copy-start | bytes 4612
  277.8 7.1 %copy-start.28 = (pred[1536]{0:T(1024)(128)(4,1)S(1)}, pred[1536]{0:T(1024)(128)(4,1)}, u32[]{:S(2)}) copy-start(pred[1536]{0:T(1024)(128)(4,1)} %get-tuple-element.185) | copy-start | bytes 4612
  277.8 7.1 %copy-start.29 = (pred[1536]{0:T(1024)(128)(4,1)S(1)}, pred[1536]{0:T(1024)(128)(4,1)}, u32[]{:S(2)}) copy-start(pred[1536]{0:T(1024)(128)(4,1)} %get-tuple-element.186) | copy-start | bytes 4612
  277.8 7.1 %copy-start.30 = (pred[1536]{0:T(1024)(128)(4,1)S(1)}, pred[1536]{0:T(1024)(128)(4,1)}, u32[]{:S(2)}) copy-start(pred[1536]{0:T(1024)(128)(4,1)} %get-tuple-element.193) | copy-start | bytes 4612
  277.8 7.1 %copy-start.31 = (pred[1536]{0:T(1024)(128)(4,1)S(1)}, pred[1536]{0:T(1024)(128)(4,1)}, u32[]{:S(2)}) copy-start(pred[1536]{0:T(1024)(128)(4,1)} %get-tuple-element.194) | copy-start | bytes 4612
  277.8 7.1 %copy-start.32 = (pred[1536]{0:T(1024)(128)(4,1)S(1)}, pred[1536]{0:T(1024)(128)(4,1)}, u32[]{:S(2)}) copy-start(pred[1536]{0:T(1024)(128)(4,1)} %get-tuple-element.195) | copy-start | bytes 4612
  277.8 7.1 %copy-start.33 = (pred[1536]{0:T(1024)(128)(4,1)S(1)}, pred[1536]{0:T(1024)(128)(4,1)}, u32[]{:S(2)}) copy-start(pred[1536]{0:T(1024)(128)(4,1)} %get-tuple-element.196) | copy-start | bytes 4612
  277.8 7.1 %copy-start.34 = (pred[1536]{0:T(1024)(128)(4,1)S(1)}, pred[1536]{0:T(1024)(128)(4,1)}, u32[]{:S(2)}) copy-start(pred[1536]{0:T(1024)(128)(4,1)} %get-tuple-element.205) | copy-start | bytes 4612
  277.8 7.1 %copy-start.35 = (pred[1536]{0:T(1024)(128)(4,1)S(1)}, pred[1536]{0:T(1024)(128)(4,1)}, u32[]{:S(2)}) copy-start(pred[1536]{0:T(1024)(128)(4,1)} %get-tuple-element.206) | copy-start | bytes 4612
  277.8 7.1 %copy-start.36 = (pred[1536]{0:T(1024)(128)(4,1)S(1)}, pred[1536]{0:T(1024)(128)(4,1)}, u32[]{:S(2)}) copy-start(pred[1536]{0:T(1024)(128)(4,1)} %get-tuple-element.207) | copy-start | bytes 4612
  277.8 7.1 %copy-start.37 = (pred[1536]{0:T(1024)(128)(4,1)S(1)}, pred[1536]{0:T(1024)(128)(4,1)}, u32[]{:S(2)}) copy-start(pred[1536]{0:T(1024)(128)(4,1)} %get-tuple-element.208) | copy-start | bytes 4612
  277.9 7.1 %copy-start.38 = (pred[1536]{0:T(1024)(128)(4,1)S(1)}, pred[1536]{0:T(1024)(128)(4,1)}, u32[]{:S(2)}) copy-start(pred[1536]{0:T(1024)(128)(4,1)} %get-tuple-element.209) | copy-start | bytes 4612
  277.9 7.1 %copy-start.39 = (pred[1536]{0:T(1024)(128)(4,1)S(1)}, pred[1536]{0:T(1024)(128)(4,1)}, u32[]{:S(2)}) copy-start(pred[1536]{0:T(1024)(128)(4,1)} %get-tuple-element.210) | copy-start | bytes 4612
  277.9 7.1 %copy-start.40 = (pred[1536]{0:T(1024)(128)(4,1)S(1)}, pred[1536]{0:T(1024)(128)(4,1)}, u32[]{:S(2)}) copy-start(pred[1536]{0:T(1024)(128)(4,1)} %get-tuple-element.211) | copy-start | bytes 4612
  277.9 7.1 %copy-start.41 = (pred[1536]{0:T(1024)(128)(4,1)S(1)}, pred[1536]{0:T(1024)(128)(4,1)}, u32[]{:S(2)}) copy-start(pred[1536]{0:T(1024)(128)(4,1)} %get-tuple-element.212) | copy-start | bytes 4612
  282.6 29.6 %collective-permute-start.8 = (bf16[1024,256]{1,0:T(8,128)(2,1)S(1)}, bf16[1024,256]{1,0:T(8,128)(2,1)S(1)}, u32[]{:S(2)}, u32[]{:S(2)}) collective-permute-start(bf16[1024,256]{1,0:T(8,128)(2,1)S(1)} %copy-done.9), channel_id=1, source_target_pairs={{0,2},{2,0},{1,3},{3,1},{4,6},{6,4},{5,7},{7,5},{8,10},{10,8},{9,1... | collective-permute-start | bytes 1572872 | tf_op jit(solution)/shard_map/ppermute | solution.py:127
  340.8 31.5 %collective-permute-start.4 = (f32[1,16,64,128]{3,2,1,0:T(8,128)S(1)}, f32[1,16,64,128]{3,2,1,0:T(8,128)}, u32[]{:S(2)}, u32[]{:S(2)}) collective-permute-start(f32[1,16,64,128]{3,2,1,0:T(8,128)S(1)} %get-tuple-element.48), channel_id=1, source_target_pairs={{0,4},{4,8},{8,12},{12,16},{16,20},{20,24},{24,28},{1,5},{5,9},{9,... | collective-permute-start | bytes 1572872 | tf_op jit(solution)/shard_map/ppermute | solution.py:15
  343.1 29.2 %collective-permute-start.6 = (f32[1,16,64,128]{3,2,1,0:T(8,128)S(1)}, f32[1,16,64,128]{3,2,1,0:T(8,128)}, u32[]{:S(2)}, u32[]{:S(2)}) collective-permute-start(f32[1,16,64,128]{3,2,1,0:T(8,128)S(1)} %get-tuple-element.48), channel_id=1, source_target_pairs={{0,8},{4,12},{8,16},{12,20},{16,24},{20,28},{1,9},{5,13},{9,17},{1... | collective-permute-start | bytes 1572872 | tf_op jit(solution)/shard_map/ppermute | solution.py:15
  351.2 21.1 %collective-permute-start.5 = (f32[1,16]{1,0:T(1,128)S(1)}, f32[1,16]{1,0:T(1,128)S(1)}, u32[]{:S(2)}, u32[]{:S(2)}) collective-permute-start(f32[1,16]{1,0:T(1,128)S(1)} %get-tuple-element.49), channel_id=1, source_target_pairs={{0,4},{4,8},{8,12},{12,16},{16,20},{20,24},{24,28},{1,5},{5,9},{9,... | collective-permute-start | bytes 200 | tf_op jit(solution)/shard_map/ppermute | solution.py:15
  363.3 15.9 %copy-start.7 = (f32[6,256,256]{2,1,0:T(8,128)S(1)}, f32[6,256,256]{2,1,0:T(8,128)}, u32[]{:S(2)}) copy-start(f32[6,256,256]{2,1,0:T(8,128)} %fusion.213) | copy-start | bytes 4718596
  532.6 11.2 %collective-permute-start.23 = (bf16[2,384,512]{2,1,0:T(8,128)(2,1)S(1)}, bf16[2,384,512]{2,1,0:T(8,128)(2,1)S(1)}, u32[]{:S(2)}, u32[]{:S(2)}) collective-permute-start(bf16[2,384,512]{2,1,0:T(8,128)(2,1)S(1)} %fusion.87), channel_id=1, source_target_pairs={{0,1},{1,0},{2,3},{3,2},{4,5},{5,4},{6,7},{7,6},{8,9},{9,8},{10,11... | collective-permute-start | bytes 2359304 | tf_op jit(solution)/shard_map/ppermute | solution.py:342
  535.1 10.0 %collective-permute-start.21 = (bf16[2,384,512]{2,1,0:T(8,128)(2,1)S(1)}, bf16[2,384,512]{2,1,0:T(8,128)(2,1)S(1)}, u32[]{:S(2)}, u32[]{:S(2)}) collective-permute-start(bf16[2,384,512]{2,1,0:T(8,128)(2,1)S(1)} %fusion.84), channel_id=1, source_target_pairs={{0,1},{1,0},{2,3},{3,2},{4,5},{5,4},{6,7},{7,6},{8,9},{9,8},{10,11... | collective-permute-start | bytes 2359304 | tf_op jit(solution)/shard_map/ppermute | solution.py:342
  537.8 8.7 %collective-permute-start.19 = (bf16[2,384,512]{2,1,0:T(8,128)(2,1)S(1)}, bf16[2,384,512]{2,1,0:T(8,128)(2,1)S(1)}, u32[]{:S(2)}, u32[]{:S(2)}) collective-permute-start(bf16[2,384,512]{2,1,0:T(8,128)(2,1)S(1)} %fusion.81), channel_id=1, source_target_pairs={{0,1},{1,0},{2,3},{3,2},{4,5},{5,4},{6,7},{7,6},{8,9},{9,8},{10,11... | collective-permute-start | bytes 2359304 | tf_op jit(solution)/shard_map/ppermute | solution.py:342
  539.2 13.3 %collective-permute-start.17 = (bf16[2,384,512]{2,1,0:T(8,128)(2,1)S(1)}, bf16[2,384,512]{2,1,0:T(8,128)(2,1)S(1)}, u32[]{:S(2)}, u32[]{:S(2)}) collective-permute-start(bf16[2,384,512]{2,1,0:T(8,128)(2,1)S(1)} %fusion.78), channel_id=1, source_target_pairs={{0,1},{1,0},{2,3},{3,2},{4,5},{5,4},{6,7},{7,6},{8,9},{9,8},{10,11... | collective-permute-start | bytes 2359304 | tf_op jit(solution)/shard_map/ppermute | solution.py:342
  540.4 14.5 %collective-permute-start.15 = (bf16[2,384,512]{2,1,0:T(8,128)(2,1)S(1)}, bf16[2,384,512]{2,1,0:T(8,128)(2,1)S(1)}, u32[]{:S(2)}, u32[]{:S(2)}) collective-permute-start(bf16[2,384,512]{2,1,0:T(8,128)(2,1)S(1)} %fusion.75), channel_id=1, source_target_pairs={{0,1},{1,0},{2,3},{3,2},{4,5},{5,4},{6,7},{7,6},{8,9},{9,8},{10,11... | collective-permute-start | bytes 2359304 | tf_op jit(solution)/shard_map/ppermute | solution.py:342
  543.8 4.1 collective-permute-start.11
  545.1 5.3 collective-permute-start.9
  546.5 10.1 %collective-permute-start.13 = (bf16[2,384,512]{2,1,0:T(8,128)(2,1)S(1)}, bf16[2,384,512]{2,1,0:T(8,128)(2,1)S(1)}, u32[]{:S(2)}, u32[]{:S(2)}) collective-permute-start(bf16[2,384,512]{2,1,0:T(8,128)(2,1)S(1)} %fusion.72), channel_id=1, source_target_pairs={{0,1},{1,0},{2,3},{3,2},{4,5},{5,4},{6,7},{7,6},{8,9},{9,8},{10,11... | collective-permute-start | bytes 2359304 | tf_op jit(solution)/shard_map/ppermute | solution.py:342
  547.9 72.9 %collective-permute-start.24 = (bf16[384,512]{1,0:T(8,128)(2,1)S(1)}, bf16[384,512]{1,0:T(8,128)(2,1)S(1)}, u32[]{:S(2)}, u32[]{:S(2)}) collective-permute-start(bf16[384,512]{1,0:T(8,128)(2,1)S(1)} %fusion.123), channel_id=1, source_target_pairs={{0,2},{2,0},{1,3},{3,1},{4,6},{6,4},{5,7},{7,5},{8,10},{10,8},{9,1... | collective-permute-start | bytes 1179656 | tf_op jit(solution)/shard_map/ppermute | solution.py:127
  550.4 70.2 %collective-permute-start.22 = (bf16[384,512]{1,0:T(8,128)(2,1)S(1)}, bf16[384,512]{1,0:T(8,128)(2,1)S(1)}, u32[]{:S(2)}, u32[]{:S(2)}) collective-permute-start(bf16[384,512]{1,0:T(8,128)(2,1)S(1)} %fusion.122), channel_id=1, source_target_pairs={{0,2},{2,0},{1,3},{3,1},{4,6},{6,4},{5,7},{7,5},{8,10},{10,8},{9,1... | collective-permute-start | bytes 1179656 | tf_op jit(solution)/shard_map/ppermute | solution.py:127
  552.4 68.0 %collective-permute-start.20 = (bf16[384,512]{1,0:T(8,128)(2,1)S(1)}, bf16[384,512]{1,0:T(8,128)(2,1)S(1)}, u32[]{:S(2)}, u32[]{:S(2)}) collective-permute-start(bf16[384,512]{1,0:T(8,128)(2,1)S(1)} %fusion.121), channel_id=1, source_target_pairs={{0,2},{2,0},{1,3},{3,1},{4,6},{6,4},{5,7},{7,5},{8,10},{10,8},{9,1... | collective-permute-start | bytes 1179656 | tf_op jit(solution)/shard_map/ppermute | solution.py:127
  555.0 39.6 %collective-permute-start.12 = (bf16[384,512]{1,0:T(8,128)(2,1)S(1)}, bf16[384,512]{1,0:T(8,128)(2,1)S(1)}, u32[]{:S(2)}, u32[]{:S(2)}) collective-permute-start(bf16[384,512]{1,0:T(8,128)(2,1)S(1)} %fusion.117), channel_id=1, source_target_pairs={{0,2},{2,0},{1,3},{3,1},{4,6},{6,4},{5,7},{7,5},{8,10},{10,8},{9,1... | collective-permute-start | bytes 1179656 | tf_op jit(solution)/shard_map/ppermute | solution.py:127
  556.6 36.4 %collective-permute-start.10 = (bf16[384,512]{1,0:T(8,128)(2,1)S(1)}, bf16[384,512]{1,0:T(8,128)(2,1)S(1)}, u32[]{:S(2)}, u32[]{:S(2)}) collective-permute-start(bf16[384,512]{1,0:T(8,128)(2,1)S(1)} %fusion.116), channel_id=1, source_target_pairs={{0,2},{2,0},{1,3},{3,1},{4,6},{6,4},{5,7},{7,5},{8,10},{10,8},{9,1... | collective-permute-start | bytes 1179656 | tf_op jit(solution)/shard_map/ppermute | solution.py:127
  593.0 12.1 %collective-permute-start.14 = (bf16[384,512]{1,0:T(8,128)(2,1)S(1)}, bf16[384,512]{1,0:T(8,128)(2,1)S(1)}, u32[]{:S(2)}, u32[]{:S(2)}) collective-permute-start(bf16[384,512]{1,0:T(8,128)(2,1)S(1)} %fusion.118), channel_id=1, source_target_pairs={{0,2},{2,0},{1,3},{3,1},{4,6},{6,4},{5,7},{7,5},{8,10},{10,8},{9,1... | collective-permute-start | bytes 1179656 | tf_op jit(solution)/shard_map/ppermute | solution.py:127
  594.6 18.9 %collective-permute-start.16 = (bf16[384,512]{1,0:T(8,128)(2,1)S(1)}, bf16[384,512]{1,0:T(8,128)(2,1)S(1)}, u32[]{:S(2)}, u32[]{:S(2)}) collective-permute-start(bf16[384,512]{1,0:T(8,128)(2,1)S(1)} %fusion.119), channel_id=1, source_target_pairs={{0,2},{2,0},{1,3},{3,1},{4,6},{6,4},{5,7},{7,5},{8,10},{10,8},{9,1... | collective-permute-start | bytes 1179656 | tf_op jit(solution)/shard_map/ppermute | solution.py:127
  605.0 15.3 %collective-permute-start.18 = (bf16[384,512]{1,0:T(8,128)(2,1)S(1)}, bf16[384,512]{1,0:T(8,128)(2,1)S(1)}, u32[]{:S(2)}, u32[]{:S(2)}) collective-permute-start(bf16[384,512]{1,0:T(8,128)(2,1)S(1)} %fusion.120), channel_id=1, source_target_pairs={{0,2},{2,0},{1,3},{3,1},{4,6},{6,4},{5,7},{7,5},{8,10},{10,8},{9,1... | collective-permute-start | bytes 1179656 | tf_op jit(solution)/shard_map/ppermute | solution.py:127
  613.4 9.9 %copy-start.1 = (f32[32,64,128]{2,1,0:T(8,128)S(1)}, f32[32,64,128]{2,1,0:T(8,128)}, u32[]{:S(2)}) copy-start(f32[32,64,128]{2,1,0:T(8,128)} %param.35) | copy-start | bytes 3145732
  (18 other events, 81.3 us)
Sparse Core Ops, SparseCore 0:
  48.9 165.1 all-gather.3
  253.0 139.9 all-gather.5
  395.0 134.6 all-gather.7
